TPU v7x, 256 devices: a whole 4x4x8 slice. The times are simulated.
256 devices in a mesh: gx: 16 (over z, core), gy: 16 (over y, x).
Axes of the slice: x: 4, y: 4, z: 8, core: 2. Of those that a mesh axis runs over, the one named last changes fastest.
Arguments:
- right_side: float32 [256, 128, 1024], P('gx', 'gy'), may hold values from -340 to 340
- start_guess: float32 [256, 128, 1024], P('gx', 'gy'), may hold values from -1.8 to 1.8
- couple_x: float32 [256, 128, 64], P('gx', 'gy'), may hold values from 0.3 to 3
- couple_y: float32 [256, 128, 64], P('gx', 'gy'), may hold values from 0.3 to 3
- couple_z: float32 [256, 128, 64], P('gx', 'gy'), may hold values from 0.3 to 3
- reaction: float32 [256, 128, 64], P('gx', 'gy'), may hold values from 0.01 to 0.1
Outputs:
- solution: float32 [256, 128, 1024], P('gx', 'gy')
- residual: float32 [256, 128, 1024], P('gx', 'gy')
All inputs are finite; a program needn't handle non-finite values.
Results may differ from a plain program's by a relative error of at most 0.0003.
Values sent between devices are 32-bit elements; how exact they have to be, the bound alone decides.
No kernel may reach another device: no remote copies, remote signals or barrier semaphores. Data moves between devices by JAX's collectives and lax.ppermute only.
A program may use at most 64 MiB of HBM per device.

v0:
```python
import jax
import jax.numpy as jnp
from jax import lax
from jax.sharding import PartitionSpec as P

ITERS = 2
SWEEPS = 4
FACT_SWEEPS = 3
SHIFT = 1.0


HIGH = lax.Precision.HIGHEST


def mesh_sum(block):
    for axis in ("gx", "gy"):
        count = lax.axis_size(axis)
        if count & (count - 1):
            block = lax.psum(block, axis)
            continue
        step = 1
        while step < count:
            radix = 4 if count % (step * 4) == 0 else 2
            parts = [block] + [
                lax.ppermute(block, axis, [(i, i ^ (step * m)) for i in range(count)])
                for m in range(1, radix)
            ]
            while len(parts) > 1:
                parts = [parts[i] + parts[i + 1] for i in range(0, len(parts), 2)]
            block = parts[0]
            step *= radix
    return block


def low_along(values, axis, width):
    count = values.shape[axis]
    blank = jnp.zeros_like(lax.slice_in_dim(values, 0, width, axis=axis))
    return jnp.concatenate([blank, lax.slice_in_dim(values, 0, count - width, axis=axis)], axis=axis)


def up_along(values, axis, width):
    count = values.shape[axis]
    blank = jnp.zeros_like(lax.slice_in_dim(values, 0, width, axis=axis))
    return jnp.concatenate([lax.slice_in_dim(values, width, count, axis=axis), blank], axis=axis)


def block_gram(former, latter):
    return jnp.einsum("sxl,txl->st", former, latter, precision=HIGH)


def mix_block(values, matrix):
    return jnp.einsum("ts,sxl->txl", matrix.T, values, precision=HIGH)


def chol_factor(gram_mat):
    low_factor = jnp.linalg.cholesky(gram_mat)
    eye_mat = jnp.eye(gram_mat.shape[0], dtype=gram_mat.dtype)
    inverse = lax.linalg.triangular_solve(low_factor, eye_mat, left_side=True, lower=True)
    return (low_factor.T, inverse.T)


def solve_small(columns, first_factor):
    hessen = jnp.concatenate(columns, axis=1)
    count_rhs = first_factor.shape[0]
    target = jnp.dot(hessen[:count_rhs].T, first_factor, precision=HIGH)
    normal = jnp.dot(hessen.T, hessen, precision=HIGH)
    low_factor = jnp.linalg.cholesky(normal)
    partial_sol = lax.linalg.triangular_solve(low_factor, target, left_side=True, lower=True)
    return lax.linalg.triangular_solve(
        low_factor, partial_sol, left_side=True, lower=True, transpose_a=True
    )


def body(right_side, start_guess, couple_x, couple_y, couple_z, reaction):
    rows_x, rows_y, flat_len = right_side.shape
    layers = couple_z.shape[2]
    count_rhs = flat_len // layers
    plane = rows_y * layers
    depth = jnp.arange(plane, dtype=jnp.int32) % layers
    keep_first = (depth != 0).astype(jnp.float32)
    keep_last = (depth != layers - 1).astype(jnp.float32)

    def inward(values):
        split = values.reshape(rows_x, rows_y, count_rhs, layers)
        return jnp.transpose(split, (2, 0, 1, 3)).reshape(count_rhs, rows_x, plane)

    def outward(values):
        split = values.reshape(count_rhs, rows_x, rows_y, layers)
        return jnp.transpose(split, (1, 2, 0, 3)).reshape(rows_x, rows_y, flat_len)

    def coef(values):
        return values.reshape(1, rows_x, plane)

    def low_x(values):
        return low_along(values, 1, 1)

    def up_x(values):
        return up_along(values, 1, 1)

    def low_y(values):
        return low_along(values, 2, layers)

    def up_y(values):
        return up_along(values, 2, layers)

    def low_z(values):
        return low_along(values, 2, 1) * keep_first

    def up_z(values):
        return up_along(values, 2, 1) * keep_last

    def forward(block, axis):
        count = lax.axis_size(axis)
        return lax.ppermute(block, axis, [(i, i + 1) for i in range(count - 1)])

    def backward(block, axis):
        count = lax.axis_size(axis)
        return lax.ppermute(block, axis, [(i + 1, i) for i in range(count - 1)])

    after_x = coef(couple_x)
    after_y = coef(couple_y)
    after_z = coef(couple_z)
    edge_x = forward(after_x[:, -1:], "gx")
    edge_y = forward(after_y[:, :, plane - layers :], "gy")
    before_x = jnp.concatenate([edge_x, after_x[:, :-1]], axis=1)
    before_y = jnp.concatenate([edge_y, after_y[:, :, : plane - layers]], axis=2)
    before_z = low_z(after_z)
    diagonal = coef(reaction) + after_x + before_x + after_y + before_y + after_z + before_z

    def halos(values):
        return (
            forward(values[:, -1:], "gx"),
            backward(values[:, :1], "gx"),
            forward(values[:, :, plane - layers :], "gy"),
            backward(values[:, :, :layers], "gy"),
        )

    def apply_op(values, edges):
        from_low_x, from_high_x, from_low_y, from_high_y = edges
        next_x = jnp.concatenate([values[:, 1:], from_high_x], axis=1)
        prev_x = jnp.concatenate([from_low_x, values[:, :-1]], axis=1)
        next_y = jnp.concatenate([values[:, :, layers:], from_high_y], axis=2)
        prev_y = jnp.concatenate([from_low_y, values[:, :, : plane - layers]], axis=2)
        return (
            diagonal * values
            - after_x * next_x
            - before_x * prev_x
            - after_y * next_y
            - before_y * prev_y
            - after_z * up_z(values)
            - before_z * low_z(values)
        )

    lows = (low_x(after_x), low_y(after_y), before_z)
    ups = (
        up_x(jnp.ones_like(after_x)) * after_x,
        up_y(jnp.ones_like(after_y)) * after_y,
        after_z,
    )
    pivots = diagonal
    for repeat in range(FACT_SWEEPS):
        inv_now = 1.0 / pivots
        pivots = (
            diagonal
            - lows[0] * lows[0] * low_x(inv_now)
            - lows[1] * lows[1] * low_y(inv_now)
            - lows[2] * lows[2] * low_z(inv_now)
        )
    inv_piv = 1.0 / pivots

    def total_gram(former, latter):
        return mesh_sum(block_gram(former, latter))

    rhs_in = inward(right_side)
    start_in = inward(start_guess)
    def precondition(source):
        lower_sol = inv_piv * source
        for precondition_repeat in range(SWEEPS):
            lower_sol = inv_piv * (
                source
                + lows[0] * low_x(lower_sol)
                + lows[1] * low_y(lower_sol)
                + lows[2] * low_z(lower_sol)
            )
        upper_sol = lower_sol
        for precondition_repeat in range(SWEEPS):
            upper_sol = lower_sol + inv_piv * (
                ups[0] * up_x(upper_sol)
                + ups[1] * up_y(upper_sol)
                + ups[2] * up_z(upper_sol)
            )
        return upper_sol

    start_edges = halos(start_in)
    start_res = rhs_in - apply_op(start_in, start_edges)
    krylov = [start_res]
    precond_set = []
    edge_set = []
    for column in range(ITERS):
        turned = precondition(krylov[-1])
        turned_edges = halos(turned)
        precond_set.append(turned)
        edge_set.append(turned_edges)
        krylov.append(apply_op(turned, turned_edges) - SHIFT * krylov[-1])
    stacked = jnp.concatenate(krylov, axis=0)
    span_gram = mesh_sum(block_gram(stacked, stacked))
    width = span_gram.shape[0]

    def inner(left, right):
        return jnp.dot(left.T, jnp.dot(span_gram, right, precision=HIGH), precision=HIGH)

    def advance(weights):
        moved = jnp.concatenate([jnp.zeros_like(weights[:count_rhs]), weights[:-count_rhs]], axis=0)
        return moved + SHIFT * weights

    first_factor, first_inv = chol_factor(inner(*(2 * [jnp.eye(width, count_rhs, dtype=jnp.float32)])))
    basis_set = [jnp.dot(jnp.eye(width, count_rhs, dtype=jnp.float32), first_inv, precision=HIGH)]
    columns = []
    for column in range(ITERS):
        image = advance(basis_set[column])
        projections = [inner(member, image) for member in basis_set]
        perp = image - sum(
            jnp.dot(member, proj, precision=HIGH) for member, proj in zip(basis_set, projections)
        )
        next_factor, next_inv = chol_factor(inner(perp, perp))
        if column + 1 < ITERS:
            basis_set.append(jnp.dot(perp, next_inv, precision=HIGH))
        blank = jnp.zeros(((ITERS - 1 - column) * count_rhs, count_rhs), dtype=next_factor.dtype)
        columns.append(jnp.concatenate(projections + [next_factor, blank], axis=0))
    coeffs = solve_small(columns, first_factor)
    combined = sum(
        jnp.dot(basis_set[column], coeffs[column * count_rhs : (column + 1) * count_rhs], precision=HIGH)
        for column in range(ITERS)
    )
    solution = start_in
    solution_edges = start_edges
    for column in range(ITERS):
        weights = combined[column * count_rhs : (column + 1) * count_rhs]
        solution = solution + mix_block(precond_set[column], weights)
        solution_edges = tuple(
            have + mix_block(extra, weights)
            for have, extra in zip(solution_edges, edge_set[column])
        )
    residual = rhs_in - apply_op(solution, solution_edges)
    return (outward(solution), outward(residual))


def solution(mesh):
    return jax.shard_map(
        body,
        mesh=mesh,
        in_specs=(
            P("gx", "gy", None),
            P("gx", "gy", None),
            P("gx", "gy", None),
            P("gx", "gy", None),
            P("gx", "gy", None),
            P("gx", "gy", None),
        ),
        out_specs=(P("gx", "gy", None), P("gx", "gy", None)),
        check_vma=False,
    )
```

profile of v0, /device:TPU:40, one launch (start us, length us, event | category | flops | bytes accessed | tf_op | source)
XLA Modules:
  0.0 159.7 jit_solution(14015445854135187705)
XLA Ops:
  2.2 3.4 %collective-permute-start.1 = (f32[1,16,64]{2,1,0:T(8,128)}, f32[1,16,64]{2,1,0:T(8,128)S(1)}, u32[]{:S(2)}, u32[]{:S(2)}) collective-permute-start(f32[1,16,64]{2,1,0:T(8,128)} %slice.444), channel_id=1, source_target_pairs={{0,1},{1,2},{2,3},{3,4},{4,5},{5,6},{6,7},{7,8},{8,9},{9,10},{10,1... | collective-permute-start | bytes 12296 | tf_op jit(solution)/shard_map/ppermute | solution.py:114
  11.7 4.5 %collective-permute-start.4 = (f32[16,16,64]{2,0,1:T(8,128)}, f32[16,16,64]{2,0,1:T(8,128)}, u32[]{:S(2)}, u32[]{:S(2)}) collective-permute-start(f32[16,16,64]{2,0,1:T(8,128)} %get-tuple-element.42), channel_id=1, source_target_pairs={{1,0},{2,1},{3,2},{4,3},{5,4},{6,5},{7,6},{8,7},{9,8},{10,9},{11,1... | collective-permute-start | bytes 196616 | tf_op jit(solution)/shard_map/ppermute | solution.py:118
  18.8 3.3 %collective-permute-start.2 = (f32[16,1,512]{2,0,1:T(8,128)}, f32[16,1,512]{2,0,1:T(8,128)S(1)}, u32[]{:S(2)}, u32[]{:S(2)}) collective-permute-start(f32[16,1,512]{2,0,1:T(8,128)} %get-tuple-element.38), channel_id=1, source_target_pairs={{16,0},{32,16},{48,32},{64,48},{80,64},{96,80},{112,96},{128,112},... | collective-permute-start | bytes 98312 | tf_op jit(solution)/shard_map/ppermute | solution.py:118
  28.7 2.3 %collective-permute-start.3 = (f32[16,1,512]{2,0,1:T(8,128)}, f32[16,1,512]{2,0,1:T(8,128)S(1)}, u32[]{:S(2)}, u32[]{:S(2)}) collective-permute-start(f32[16,1,512]{2,0,1:T(8,128)} %get-tuple-element.39), channel_id=1, source_target_pairs={{0,16},{16,32},{32,48},{48,64},{64,80},{80,96},{96,112},{112,128},... | collective-permute-start | bytes 98312 | tf_op jit(solution)/shard_map/ppermute | solution.py:114
  32.2 2.1 %collective-permute-done.3 = f32[16,1,512]{2,0,1:T(8,128)S(1)} collective-permute-done((f32[16,1,512]{2,0,1:T(8,128)}, f32[16,1,512]{2,0,1:T(8,128)S(1)}, u32[]{:S(2)}, u32[]{:S(2)}) %collective-permute-start.3) | collective-permute-done | bytes 32800 | tf_op jit(solution)/shard_map/ppermute | solution.py:114
  34.3 2.1 %broadcast_multiply_fusion.1 = (f32[16,16,512]{2,0,1:T(8,128)S(1)}, f32[16,16,512]{2,0,1:T(8,128)S(1)}) fusion(f32[16,512]{1,0:T(8,128)S(1)} %divide_bitcast_fusion, f32[16,16,512]{2,0,1:T(8,128)S(1)} %reshape.213, f32[512]{0:T(512)S(1)} %get-tuple-element.54, f32[16,16,511]{2,0,1:T(8,128)S(1)} %copy-done.1, f32[16,512]{1,0:T(8,128)S(1)} %get-tuple-element.48, ...), kind=kLoop, calls=%fused_computation.88 | loop fusion | flops 2752512 | bytes 5507072 | tf_op jit(solution)/shard_map/mul | solution.py:177
  41.9 5.8 %collective-permute-start.8 = (f32[16,16,64]{2,0,1:T(8,128)S(1)}, f32[16,16,64]{2,0,1:T(8,128)S(1)}, u32[]{:S(2)}, u32[]{:S(2)}) collective-permute-start(f32[16,16,64]{2,0,1:T(8,128)S(1)} %get-tuple-element.32), channel_id=1, source_target_pairs={{1,0},{2,1},{3,2},{4,3},{5,4},{6,5},{7,6},{8,7},{9,8},{10,9},{11,1... | collective-permute-start | bytes 196616 | tf_op jit(solution)/shard_map/ppermute | solution.py:118
  51.5 2.6 %collective-permute-start.7 = (f32[16,1,512]{2,0,1:T(8,128)S(1)}, f32[16,1,512]{2,0,1:T(8,128)S(1)}, u32[]{:S(2)}, u32[]{:S(2)}) collective-permute-start(f32[16,1,512]{2,0,1:T(8,128)S(1)} %get-tuple-element.29), channel_id=1, source_target_pairs={{0,16},{16,32},{32,48},{48,64},{64,80},{80,96},{96,112},{112,128},... | collective-permute-start | bytes 98312 | tf_op jit(solution)/shard_map/ppermute | solution.py:114
  54.3 2.5 %collective-permute-done.7 = f32[16,1,512]{2,0,1:T(8,128)S(1)} collective-permute-done((f32[16,1,512]{2,0,1:T(8,128)S(1)}, f32[16,1,512]{2,0,1:T(8,128)S(1)}, u32[]{:S(2)}, u32[]{:S(2)}) %collective-permute-start.7) | collective-permute-done | bytes 32800 | tf_op jit(solution)/shard_map/ppermute | solution.py:114
  63.1 6.0 %collective-permute-start.12 = (f32[16,16,64]{2,0,1:T(8,128)S(1)}, f32[16,16,64]{2,0,1:T(8,128)S(1)}, u32[]{:S(2)}, u32[]{:S(2)}) collective-permute-start(f32[16,16,64]{2,0,1:T(8,128)S(1)} %get-tuple-element.19), channel_id=1, source_target_pairs={{1,0},{2,1},{3,2},{4,3},{5,4},{6,5},{7,6},{8,7},{9,8},{10,9},{11,1... | collective-permute-start | bytes 196616 | tf_op jit(solution)/shard_map/ppermute | solution.py:118
  73.0 2.4 %collective-permute-start.11 = (f32[16,1,512]{2,0,1:T(8,128)S(1)}, f32[16,1,512]{2,0,1:T(8,128)S(1)}, u32[]{:S(2)}, u32[]{:S(2)}) collective-permute-start(f32[16,1,512]{2,0,1:T(8,128)S(1)} %get-tuple-element.22), channel_id=1, source_target_pairs={{0,16},{16,32},{32,48},{48,64},{64,80},{80,96},{96,112},{112,128},... | collective-permute-start | bytes 98312 | tf_op jit(solution)/shard_map/ppermute | solution.py:114
  75.5 2.7 %collective-permute-done.11 = f32[16,1,512]{2,0,1:T(8,128)S(1)} collective-permute-done((f32[16,1,512]{2,0,1:T(8,128)S(1)}, f32[16,1,512]{2,0,1:T(8,128)S(1)}, u32[]{:S(2)}, u32[]{:S(2)}) %collective-permute-start.11) | collective-permute-done | bytes 32800 | tf_op jit(solution)/shard_map/ppermute | solution.py:114
  82.4 2.0 %collective-permute-done.15 = f32[48,48]{1,0:T(8,128)S(1)} collective-permute-done((f32[48,48]{1,0:T(8,128)S(1)}, f32[48,48]{1,0:T(8,128)S(1)}, u32[]{:S(2)}, u32[]{:S(2)}) %collective-permute-start.15) | collective-permute-done | bytes 9248 | tf_op jit(solution)/shard_map/ppermute | solution.py:25
  84.4 7.8 %collective-permute-start.17 = (f32[48,48]{1,0:T(8,128)S(1)}, f32[48,48]{1,0:T(8,128)S(1)}, u32[]{:S(2)}, u32[]{:S(2)}) collective-permute-start(f32[48,48]{1,0:T(8,128)S(1)} %add_add_fusion.4), channel_id=1, source_target_pairs={{0,64},{16,80},{32,96},{48,112},{64,0},{80,16},{96,32},{112,48},{1... | collective-permute-start | bytes 27656 | tf_op jit(solution)/shard_map/ppermute | solution.py:25
  92.2 3.9 %collective-permute-start.18 = (f32[48,48]{1,0:T(8,128)S(1)}, f32[48,48]{1,0:T(8,128)S(1)}, u32[]{:S(2)}, u32[]{:S(2)}) collective-permute-start(f32[48,48]{1,0:T(8,128)S(1)} %add_add_fusion.4), channel_id=1, source_target_pairs={{0,128},{16,144},{32,160},{48,176},{64,192},{80,208},{96,224},{112... | collective-permute-start | bytes 27656 | tf_op jit(solution)/shard_map/ppermute | solution.py:25
  96.7 3.5 %collective-permute-done.18 = f32[48,48]{1,0:T(8,128)S(1)} collective-permute-done((f32[48,48]{1,0:T(8,128)S(1)}, f32[48,48]{1,0:T(8,128)S(1)}, u32[]{:S(2)}, u32[]{:S(2)}) %collective-permute-start.18) | collective-permute-done | bytes 9248 | tf_op jit(solution)/shard_map/ppermute | solution.py:25
  100.2 2.2 %collective-permute-done.19 = f32[48,48]{1,0:T(8,128)S(1)} collective-permute-done((f32[48,48]{1,0:T(8,128)S(1)}, f32[48,48]{1,0:T(8,128)S(1)}, u32[]{:S(2)}, u32[]{:S(2)}) %collective-permute-start.19) | collective-permute-done | bytes 9248 | tf_op jit(solution)/shard_map/ppermute | solution.py:25
  102.5 5.7 %collective-permute-start.21 = (f32[48,48]{1,0:T(8,128)S(1)}, f32[48,48]{1,0:T(8,128)S(1)}, u32[]{:S(2)}, u32[]{:S(2)}) collective-permute-start(f32[48,48]{1,0:T(8,128)S(1)} %add_add_fusion.3), channel_id=1, source_target_pairs={{0,2},{1,3},{2,0},{3,1},{4,6},{5,7},{6,4},{7,5},{8,10},{9,11},{10,... | collective-permute-start | bytes 27656 | tf_op jit(solution)/shard_map/ppermute | solution.py:25
  108.2 2.1 %collective-permute-done.21 = f32[48,48]{1,0:T(8,128)S(1)} collective-permute-done((f32[48,48]{1,0:T(8,128)S(1)}, f32[48,48]{1,0:T(8,128)S(1)}, u32[]{:S(2)}, u32[]{:S(2)}) %collective-permute-start.21) | collective-permute-done | bytes 9248 | tf_op jit(solution)/shard_map/ppermute | solution.py:25
  110.3 3.0 %collective-permute-done.22 = f32[48,48]{1,0:T(8,128)S(1)} collective-permute-done((f32[48,48]{1,0:T(8,128)S(1)}, f32[48,48]{1,0:T(8,128)S(1)}, u32[]{:S(2)}, u32[]{:S(2)}) %collective-permute-start.22) | collective-permute-done | bytes 9248 | tf_op jit(solution)/shard_map/ppermute | solution.py:25
  113.8 2.3 %collective-permute-start.24 = (f32[48,48]{1,0:T(8,128)S(1)}, f32[48,48]{1,0:T(8,128)S(1)}, u32[]{:S(2)}, u32[]{:S(2)}) collective-permute-start(f32[48,48]{1,0:T(8,128)S(1)} %add_add_fusion.2), channel_id=1, source_target_pairs={{0,8},{1,9},{2,10},{3,11},{4,12},{5,13},{6,14},{7,15},{8,0},{9,1},... | collective-permute-start | bytes 27656 | tf_op jit(solution)/shard_map/ppermute | solution.py:25
  135.2 2.9 %cholesky.41 = f32[32,32]{1,0:T(8,128)S(1)} custom-call(f32[32,32]{1,0:T(8,128)S(1)} %fusion.61), custom_call_target="Cholesky" | custom-call | tf_op jit(solution)/shard_map/jit(cholesky)/cholesky | solution.py:67
  139.4 2.4 %custom-call.13 = f32[1,32,32]{1,2,0:T(8,128)S(1)} custom-call(f32[1,32,32]{2,1,0:T(8,128)S(1)} %fusion.54), custom_call_target="InvertDiagBlocksLowerTriangular" | custom-call | tf_op jit(solution)/shard_map/triangular_solve | solution.py:69
  156.1 2.3 %reshape.225 = f32[16,8,1024]{2,1,0:T(8,128)} reshape(f32[16,8,16,64]{3,2,1,0:T(8,128)} %copy.15) | data formatting | bytes 1048576 | tf_op jit(solution)/shard_map/reshape | solution.py:89
  (234 shorter events, 78.1 us)
Async XLA Ops:
  2.2 28.9 %collective-permute-start.1 = (f32[1,16,64]{2,1,0:T(8,128)}, f32[1,16,64]{2,1,0:T(8,128)S(1)}, u32[]{:S(2)}, u32[]{:S(2)}) collective-permute-start(f32[1,16,64]{2,1,0:T(8,128)} %slice.444), channel_id=1, source_target_pairs={{0,1},{1,2},{2,3},{3,4},{4,5},{5,6},{6,7},{7,8},{8,9},{9,10},{10,1... | collective-permute-start | bytes 12296 | tf_op jit(solution)/shard_map/ppermute | solution.py:114
  7.1 21.6 %collective-permute-start = (f32[1,1,512]{2,1,0:T(1,128)}, f32[1,1,512]{2,1,0:T(1,128)}, u32[]{:S(2)}, u32[]{:S(2)}) collective-permute-start(f32[1,1,512]{2,1,0:T(1,128)} %slice.442), channel_id=1, source_target_pairs={{0,16},{16,32},{32,48},{48,64},{64,80},{80,96},{96,112},{112,128},... | collective-permute-start | bytes 6152 | tf_op jit(solution)/shard_map/ppermute | solution.py:114
  11.7 22.6 %collective-permute-start.4 = (f32[16,16,64]{2,0,1:T(8,128)}, f32[16,16,64]{2,0,1:T(8,128)}, u32[]{:S(2)}, u32[]{:S(2)}) collective-permute-start(f32[16,16,64]{2,0,1:T(8,128)} %get-tuple-element.42), channel_id=1, source_target_pairs={{1,0},{2,1},{3,2},{4,3},{5,4},{6,5},{7,6},{8,7},{9,8},{10,9},{11,1... | collective-permute-start | bytes 196616 | tf_op jit(solution)/shard_map/ppermute | solution.py:118
  16.3 18.0 %collective-permute-start.5 = (f32[16,16,64]{2,0,1:T(8,128)}, f32[16,16,64]{2,0,1:T(8,128)}, u32[]{:S(2)}, u32[]{:S(2)}) collective-permute-start(f32[16,16,64]{2,0,1:T(8,128)} %get-tuple-element.43), channel_id=1, source_target_pairs={{0,1},{1,2},{2,3},{3,4},{4,5},{5,6},{6,7},{7,8},{8,9},{9,10},{10,1... | collective-permute-start | bytes 196616 | tf_op jit(solution)/shard_map/ppermute | solution.py:114
  18.8 13.4 %collective-permute-start.2 = (f32[16,1,512]{2,0,1:T(8,128)}, f32[16,1,512]{2,0,1:T(8,128)S(1)}, u32[]{:S(2)}, u32[]{:S(2)}) collective-permute-start(f32[16,1,512]{2,0,1:T(8,128)} %get-tuple-element.38), channel_id=1, source_target_pairs={{16,0},{32,16},{48,32},{64,48},{80,64},{96,80},{112,96},{128,112},... | collective-permute-start | bytes 98312 | tf_op jit(solution)/shard_map/ppermute | solution.py:118
  28.7 5.6 %collective-permute-start.3 = (f32[16,1,512]{2,0,1:T(8,128)}, f32[16,1,512]{2,0,1:T(8,128)S(1)}, u32[]{:S(2)}, u32[]{:S(2)}) collective-permute-start(f32[16,1,512]{2,0,1:T(8,128)} %get-tuple-element.39), channel_id=1, source_target_pairs={{0,16},{16,32},{32,48},{48,64},{64,80},{80,96},{96,112},{112,128},... | collective-permute-start | bytes 98312 | tf_op jit(solution)/shard_map/ppermute | solution.py:114
  41.9 14.9 %collective-permute-start.8 = (f32[16,16,64]{2,0,1:T(8,128)S(1)}, f32[16,16,64]{2,0,1:T(8,128)S(1)}, u32[]{:S(2)}, u32[]{:S(2)}) collective-permute-start(f32[16,16,64]{2,0,1:T(8,128)S(1)} %get-tuple-element.32), channel_id=1, source_target_pairs={{1,0},{2,1},{3,2},{4,3},{5,4},{6,5},{7,6},{8,7},{9,8},{10,9},{11,1... | collective-permute-start | bytes 196616 | tf_op jit(solution)/shard_map/ppermute | solution.py:118
  47.7 9.1 %collective-permute-start.9 = (f32[16,16,64]{2,0,1:T(8,128)S(1)}, f32[16,16,64]{2,0,1:T(8,128)S(1)}, u32[]{:S(2)}, u32[]{:S(2)}) collective-permute-start(f32[16,16,64]{2,0,1:T(8,128)S(1)} %get-tuple-element.33), channel_id=1, source_target_pairs={{0,1},{1,2},{2,3},{3,4},{4,5},{5,6},{6,7},{7,8},{8,9},{9,10},{10,1... | collective-permute-start | bytes 196616 | tf_op jit(solution)/shard_map/ppermute | solution.py:114
  49.6 4.6 %collective-permute-start.6 = (f32[16,1,512]{2,0,1:T(8,128)S(1)}, f32[16,1,512]{2,0,1:T(8,128)S(1)}, u32[]{:S(2)}, u32[]{:S(2)}) collective-permute-start(f32[16,1,512]{2,0,1:T(8,128)S(1)} %get-tuple-element.28), channel_id=1, source_target_pairs={{16,0},{32,16},{48,32},{64,48},{80,64},{96,80},{112,96},{128,112},... | collective-permute-start | bytes 98312 | tf_op jit(solution)/shard_map/ppermute | solution.py:118
  51.5 5.2 %collective-permute-start.7 = (f32[16,1,512]{2,0,1:T(8,128)S(1)}, f32[16,1,512]{2,0,1:T(8,128)S(1)}, u32[]{:S(2)}, u32[]{:S(2)}) collective-permute-start(f32[16,1,512]{2,0,1:T(8,128)S(1)} %get-tuple-element.29), channel_id=1, source_target_pairs={{0,16},{16,32},{32,48},{48,64},{64,80},{80,96},{96,112},{112,128},... | collective-permute-start | bytes 98312 | tf_op jit(solution)/shard_map/ppermute | solution.py:114
  63.1 15.1 %collective-permute-start.12 = (f32[16,16,64]{2,0,1:T(8,128)S(1)}, f32[16,16,64]{2,0,1:T(8,128)S(1)}, u32[]{:S(2)}, u32[]{:S(2)}) collective-permute-start(f32[16,16,64]{2,0,1:T(8,128)S(1)} %get-tuple-element.19), channel_id=1, source_target_pairs={{1,0},{2,1},{3,2},{4,3},{5,4},{6,5},{7,6},{8,7},{9,8},{10,9},{11,1... | collective-permute-start | bytes 196616 | tf_op jit(solution)/shard_map/ppermute | solution.py:118
  69.1 9.1 %collective-permute-start.13 = (f32[16,16,64]{2,0,1:T(8,128)S(1)}, f32[16,16,64]{2,0,1:T(8,128)S(1)}, u32[]{:S(2)}, u32[]{:S(2)}) collective-permute-start(f32[16,16,64]{2,0,1:T(8,128)S(1)} %get-tuple-element.18), channel_id=1, source_target_pairs={{0,1},{1,2},{2,3},{3,4},{4,5},{5,6},{6,7},{7,8},{8,9},{9,10},{10,1... | collective-permute-start | bytes 196616 | tf_op jit(solution)/shard_map/ppermute | solution.py:114
  71.0 4.5 %collective-permute-start.10 = (f32[16,1,512]{2,0,1:T(8,128)S(1)}, f32[16,1,512]{2,0,1:T(8,128)S(1)}, u32[]{:S(2)}, u32[]{:S(2)}) collective-permute-start(f32[16,1,512]{2,0,1:T(8,128)S(1)} %get-tuple-element.23), channel_id=1, source_target_pairs={{16,0},{32,16},{48,32},{64,48},{80,64},{96,80},{112,96},{128,112},... | collective-permute-start | bytes 98312 | tf_op jit(solution)/shard_map/ppermute | solution.py:118
  73.0 5.2 %collective-permute-start.11 = (f32[16,1,512]{2,0,1:T(8,128)S(1)}, f32[16,1,512]{2,0,1:T(8,128)S(1)}, u32[]{:S(2)}, u32[]{:S(2)}) collective-permute-start(f32[16,1,512]{2,0,1:T(8,128)S(1)} %get-tuple-element.22), channel_id=1, source_target_pairs={{0,16},{16,32},{32,48},{48,64},{64,80},{80,96},{96,112},{112,128},... | collective-permute-start | bytes 98312 | tf_op jit(solution)/shard_map/ppermute | solution.py:114
  80.5 3.9 %collective-permute-start.15 = (f32[48,48]{1,0:T(8,128)S(1)}, f32[48,48]{1,0:T(8,128)S(1)}, u32[]{:S(2)}, u32[]{:S(2)}) collective-permute-start(f32[48,48]{1,0:T(8,128)S(1)} %fusion.12), channel_id=1, source_target_pairs={{0,32},{16,48},{32,0},{48,16},{64,96},{80,112},{96,64},{112,80},{1... | collective-permute-start | bytes 27656 | tf_op jit(solution)/shard_map/ppermute | solution.py:25
  84.4 12.2 %collective-permute-start.17 = (f32[48,48]{1,0:T(8,128)S(1)}, f32[48,48]{1,0:T(8,128)S(1)}, u32[]{:S(2)}, u32[]{:S(2)}) collective-permute-start(f32[48,48]{1,0:T(8,128)S(1)} %add_add_fusion.4), channel_id=1, source_target_pairs={{0,64},{16,80},{32,96},{48,112},{64,0},{80,16},{96,32},{112,48},{1... | collective-permute-start | bytes 27656 | tf_op jit(solution)/shard_map/ppermute | solution.py:25
  92.2 7.9 %collective-permute-start.18 = (f32[48,48]{1,0:T(8,128)S(1)}, f32[48,48]{1,0:T(8,128)S(1)}, u32[]{:S(2)}, u32[]{:S(2)}) collective-permute-start(f32[48,48]{1,0:T(8,128)S(1)} %add_add_fusion.4), channel_id=1, source_target_pairs={{0,128},{16,144},{32,160},{48,176},{64,192},{80,208},{96,224},{112... | collective-permute-start | bytes 27656 | tf_op jit(solution)/shard_map/ppermute | solution.py:25
  96.2 6.2 %collective-permute-start.19 = (f32[48,48]{1,0:T(8,128)S(1)}, f32[48,48]{1,0:T(8,128)S(1)}, u32[]{:S(2)}, u32[]{:S(2)}) collective-permute-start(f32[48,48]{1,0:T(8,128)S(1)} %add_add_fusion.4), channel_id=1, source_target_pairs={{0,192},{16,208},{32,224},{48,240},{64,128},{80,144},{96,160},{112... | collective-permute-start | bytes 27656 | tf_op jit(solution)/shard_map/ppermute | solution.py:25
  102.4 5.8 %collective-permute-start.20 = (f32[48,48]{1,0:T(8,128)S(1)}, f32[48,48]{1,0:T(8,128)S(1)}, u32[]{:S(2)}, u32[]{:S(2)}) collective-permute-start(f32[48,48]{1,0:T(8,128)S(1)} %add_add_fusion.3), channel_id=1, source_target_pairs={{0,1},{1,0},{2,3},{3,2},{4,5},{5,4},{6,7},{7,6},{8,9},{9,8},{10,11... | collective-permute-start | bytes 27656 | tf_op jit(solution)/shard_map/ppermute | solution.py:25
  102.5 7.8 %collective-permute-start.21 = (f32[48,48]{1,0:T(8,128)S(1)}, f32[48,48]{1,0:T(8,128)S(1)}, u32[]{:S(2)}, u32[]{:S(2)}) collective-permute-start(f32[48,48]{1,0:T(8,128)S(1)} %add_add_fusion.3), channel_id=1, source_target_pairs={{0,2},{1,3},{2,0},{3,1},{4,6},{5,7},{6,4},{7,5},{8,10},{9,11},{10,... | collective-permute-start | bytes 27656 | tf_op jit(solution)/shard_map/ppermute | solution.py:25
  108.2 5.0 %collective-permute-start.22 = (f32[48,48]{1,0:T(8,128)S(1)}, f32[48,48]{1,0:T(8,128)S(1)}, u32[]{:S(2)}, u32[]{:S(2)}) collective-permute-start(f32[48,48]{1,0:T(8,128)S(1)} %add_add_fusion.3), channel_id=1, source_target_pairs={{0,3},{1,2},{2,1},{3,0},{4,7},{5,6},{6,5},{7,4},{8,11},{9,10},{10,... | collective-permute-start | bytes 27656 | tf_op jit(solution)/shard_map/ppermute | solution.py:25
  113.2 3.9 %collective-permute-start.23 = (f32[48,48]{1,0:T(8,128)S(1)}, f32[48,48]{1,0:T(8,128)S(1)}, u32[]{:S(2)}, u32[]{:S(2)}) collective-permute-start(f32[48,48]{1,0:T(8,128)S(1)} %add_add_fusion.2), channel_id=1, source_target_pairs={{0,4},{1,5},{2,6},{3,7},{4,0},{5,1},{6,2},{7,3},{8,12},{9,13},{10,... | collective-permute-start | bytes 27656 | tf_op jit(solution)/shard_map/ppermute | solution.py:25
  113.8 5.3 %collective-permute-start.24 = (f32[48,48]{1,0:T(8,128)S(1)}, f32[48,48]{1,0:T(8,128)S(1)}, u32[]{:S(2)}, u32[]{:S(2)}) collective-permute-start(f32[48,48]{1,0:T(8,128)S(1)} %add_add_fusion.2), channel_id=1, source_target_pairs={{0,8},{1,9},{2,10},{3,11},{4,12},{5,13},{6,14},{7,15},{8,0},{9,1},... | collective-permute-start | bytes 27656 | tf_op jit(solution)/shard_map/ppermute | solution.py:25
  116.1 3.8 %collective-permute-start.25 = (f32[48,48]{1,0:T(8,128)S(1)}, f32[48,48]{1,0:T(8,128)S(1)}, u32[]{:S(2)}, u32[]{:S(2)}) collective-permute-start(f32[48,48]{1,0:T(8,128)S(1)} %add_add_fusion.2), channel_id=1, source_target_pairs={{0,12},{1,13},{2,14},{3,15},{4,8},{5,9},{6,10},{7,11},{8,4},{9,5},... | collective-permute-start | bytes 27656 | tf_op jit(solution)/shard_map/ppermute | solution.py:25
  (22 other events, 67.2 us)
where the time goes:
time: 162 us; the launch traced here: 160 us
  starting transfers between devices  65.4 us (40%)
  other arithmetic  30.3 us (19%)
  local copies, waits for them, and re-layouts  26.7 us (16%)
  waiting for transfers between devices  23.2 us (14%)
  matrix products  12.5 us (8%)
  between operations  1.64 us (1%)
    ppermute x12, starting transfers between devices, mesh_sum(): lax.ppermute(block, axis, [(i, i ^ step * m) for i in range(count)])  23.5 us
    ppermute x6, starting transfers between devices, backward(): return lax.ppermute(block, axis, [(i + 1, i) for i in range(count - 1)])  23.5 us
    ppermute x8, starting transfers between devices, forward(): return lax.ppermute(block, axis, [(i, i + 1) for i in range(count - 1)])  18.4 us
    ppermute x12, waiting for transfers between devices, mesh_sum(): lax.ppermute(block, axis, [(i, i ^ step * m) for i in range(count)])  15.9 us
    ppermute x8, waiting for transfers between devices, forward(): return lax.ppermute(block, axis, [(i, i + 1) for i in range(count - 1)])  7.27 us
    another operation x9, other arithmetic, chol_factor(): low_factor = jnp.linalg.cholesky(gram_mat)  6.44 us
    dot_general x10, matrix products, mix_block(): return jnp.einsum('ts,sxl->txl', matrix.T, values, precision=HIGH)  6.43 us
    slice x28, local copies, waits for them, and re-layouts, up_along(): lax.slice_in_dim(values, width, count, axis=axis)  6.06 us
  transfers between devices with their start and end apart: 26, of which 11 were waited for; matrix products, arithmetic and copies ran while one was open for 8% of the time, Pallas kernels for 0%

commit v1 on v0

--- a/solution.py
+++ b/solution.py
@@ -127,12 +127,18 @@
     before_z = low_z(after_z)
     diagonal = coef(reaction) + after_x + before_x + after_y + before_y + after_z + before_z
 
+    def packed(slab):
+        return slab.reshape(count_rhs, rows_x * layers // 128, 128)
+
+    def unpacked(slab):
+        return slab.reshape(count_rhs, rows_x, layers)
+
     def halos(values):
         return (
             forward(values[:, -1:], "gx"),
             backward(values[:, :1], "gx"),
-            forward(values[:, :, plane - layers :], "gy"),
-            backward(values[:, :, :layers], "gy"),
+            unpacked(forward(packed(values[:, :, plane - layers :]), "gy")),
+            unpacked(backward(packed(values[:, :, :layers]), "gy")),
         )
 
     def apply_op(values, edges):
@@ -203,7 +209,27 @@
         edge_set.append(turned_edges)
         krylov.append(apply_op(turned, turned_edges) - SHIFT * krylov[-1])
     stacked = jnp.concatenate(krylov, axis=0)
-    span_gram = mesh_sum(block_gram(stacked, stacked))
+    local_gram = block_gram(stacked, stacked)
+    count_blocks = len(krylov)
+    pairs = [(i, k) for i in range(count_blocks) for k in range(i, count_blocks)]
+    upper = mesh_sum(
+        jnp.stack(
+            [
+                local_gram[i * count_rhs : (i + 1) * count_rhs, k * count_rhs : (k + 1) * count_rhs]
+                for i, k in pairs
+            ]
+        )
+    )
+    span_gram = jnp.concatenate(
+        [
+            jnp.concatenate(
+                [upper[pairs.index((i, k))] if i <= k else upper[pairs.index((k, i))].T for k in range(count_blocks)],
+                axis=1,
+            )
+            for i in range(count_blocks)
+        ],
+        axis=0,
+    )
     width = span_gram.shape[0]
 
     def inner(left, right):

time: 162 us -> 186 us (1.15)
  local copies, waits for them, and re-layouts: 26.7 us -> 48 us
  waiting for transfers between devices: 23.2 us -> 18.9 us
  other arithmetic: 30.3 us -> 34.2 us
    reshape x0 -> x18, local copies, waits for them, and re-layouts: none -> 12.7 us  [the longest x12 7.89 us: unpacked(): return slab.reshape(count_rhs, rows_x, layers)]
    ppermute x8, waiting for transfers between devices: 7.27 us -> 1.42 us  [forward(): return lax.ppermute(block, axis, [(i, i + 1) for i in range(count - 1)])]
    slice x1 -> x4, local copies, waits for them, and re-layouts: 0.1 us -> 2.48 us  [halos(): values[:, :, plane - layers:]]
    reshape x4, local copies, waits for them, and re-layouts: 4.51 us -> 2.27 us  [inward(): split = values.reshape(rows_x, rows_y, count_rhs, layers)]
    mul x2, other arithmetic: 2.89 us -> 4.9 us  [precondition(): lower_sol = inv_piv * source]
  transfers between devices with their start and end apart: 26 -> 26, of which waited for: 11 -> 9; matrix products, arithmetic and copies ran while one was open for 8% -> 13% of each run, Pallas kernels for 0% -> 0%
where the time goes in v1:
time: 186 us; the launch traced here: 183 us
  starting transfers between devices  66.9 us (36%)
  local copies, waits for them, and re-layouts  48 us (26%)
  other arithmetic  34.2 us (18%)
  waiting for transfers between devices  18.9 us (10%)
  matrix products  13.8 us (7%)
    ppermute x12, starting transfers between devices, mesh_sum(): lax.ppermute(block, axis, [(i, i ^ step * m) for i in range(count)])  24.4 us
    ppermute x6, starting transfers between devices, backward(): return lax.ppermute(block, axis, [(i + 1, i) for i in range(count - 1)])  24.4 us
    ppermute x8, starting transfers between devices, forward(): return lax.ppermute(block, axis, [(i, i + 1) for i in range(count - 1)])  18 us
    ppermute x12, waiting for transfers between devices, mesh_sum(): lax.ppermute(block, axis, [(i, i ^ step * m) for i in range(count)])  17.5 us
    slice x28, local copies, waits for them, and re-layouts, up_along(): lax.slice_in_dim(values, width, count, axis=axis)  7.89 us
    reshape x12, local copies, waits for them, and re-layouts, unpacked(): return slab.reshape(count_rhs, rows_x, layers)  7.89 us
    dot_general x10, matrix products, mix_block(): return jnp.einsum('ts,sxl->txl', matrix.T, values, precision=HIGH)  7.84 us
    another operation x9, other arithmetic, chol_factor(): low_factor = jnp.linalg.cholesky(gram_mat)  6.44 us
  transfers between devices with their start and end apart: 26, of which 9 were waited for; matrix products, arithmetic and copies ran while one was open for 13% of the time, Pallas kernels for 0%

profile of v1, /device:TPU:40, one launch (start us, length us, event | category | flops | bytes accessed | tf_op | source)
XLA Modules:
  0.0 183.5 jit_solution(2932039072031952339)
XLA Ops:
  2.2 3.4 %collective-permute-start.1 = (f32[1,16,64]{2,1,0:T(8,128)}, f32[1,16,64]{2,1,0:T(8,128)S(1)}, u32[]{:S(2)}, u32[]{:S(2)}) collective-permute-start(f32[1,16,64]{2,1,0:T(8,128)} %slice.495), channel_id=1, source_target_pairs={{0,1},{1,2},{2,3},{3,4},{4,5},{5,6},{6,7},{7,8},{8,9},{9,10},{10,1... | collective-permute-start | bytes 12296 | tf_op jit(solution)/shard_map/ppermute | solution.py:114
  11.9 4.5 %collective-permute-start.4 = (f32[16,8,128]{2,1,0:T(8,128)}, f32[16,8,128]{2,1,0:T(8,128)}, u32[]{:S(2)}, u32[]{:S(2)}) collective-permute-start(f32[16,8,128]{2,1,0:T(8,128)} %reshape.254), channel_id=1, source_target_pairs={{1,0},{2,1},{3,2},{4,3},{5,4},{6,5},{7,6},{8,7},{9,8},{10,9},{11,1... | collective-permute-start | bytes 196616 | tf_op jit(solution)/shard_map/ppermute | solution.py:118
  19.7 3.4 %collective-permute-start.2 = (f32[16,1,512]{2,0,1:T(8,128)}, f32[16,1,512]{2,0,1:T(8,128)}, u32[]{:S(2)}, u32[]{:S(2)}) collective-permute-start(f32[16,1,512]{2,0,1:T(8,128)} %get-tuple-element.38), channel_id=1, source_target_pairs={{16,0},{32,16},{48,32},{64,48},{80,64},{96,80},{112,96},{128,112},... | collective-permute-start | bytes 98312 | tf_op jit(solution)/shard_map/ppermute | solution.py:118
  28.1 2.2 %collective-permute-start.3 = (f32[16,1,512]{2,0,1:T(8,128)S(1)}, f32[16,1,512]{2,0,1:T(8,128)S(1)}, u32[]{:S(2)}, u32[]{:S(2)}) collective-permute-start(f32[16,1,512]{2,0,1:T(8,128)S(1)} %copy-done.26), channel_id=1, source_target_pairs={{0,16},{16,32},{32,48},{48,64},{64,80},{80,96},{96,112},{112,128},... | collective-permute-start | bytes 98312 | tf_op jit(solution)/shard_map/ppermute | solution.py:114
  34.1 2.4 %broadcast_multiply_fusion.1 = (f32[16,16,512]{2,0,1:T(8,128)S(1)}, f32[16,16,512]{2,0,1:T(8,128)S(1)}) fusion(f32[16,512]{1,0:T(8,128)S(1)} %divide_bitcast_fusion, f32[16,16,512]{2,0,1:T(8,128)S(1)} %reshape.249, f32[512]{0:T(512)S(1)} %get-tuple-element.63, f32[16,16,511]{2,0,1:T(8,128)} %get-tuple-element.45, f32[16,512]{1,0:T(8,128)S(1)} %get-tuple-element.57, ...), kind=kLoop, calls=%fused_computation.88 | loop fusion | flops 2752512 | bytes 5507072 | tf_op jit(solution)/shard_map/mul | solution.py:183
  43.8 5.8 %collective-permute-start.8 = (f32[16,8,128]{2,1,0:T(8,128)S(1)}, f32[16,8,128]{2,1,0:T(8,128)S(1)}, u32[]{:S(2)}, u32[]{:S(2)}) collective-permute-start(f32[16,8,128]{2,1,0:T(8,128)S(1)} %reshape.258), channel_id=1, source_target_pairs={{1,0},{2,1},{3,2},{4,3},{5,4},{6,5},{7,6},{8,7},{9,8},{10,9},{11,1... | collective-permute-start | bytes 196616 | tf_op jit(solution)/shard_map/ppermute | solution.py:118
  51.6 3.1 %collective-permute-start.6 = (f32[16,1,512]{2,0,1:T(8,128)S(1)}, f32[16,1,512]{2,0,1:T(8,128)S(1)}, u32[]{:S(2)}, u32[]{:S(2)}) collective-permute-start(f32[16,1,512]{2,0,1:T(8,128)S(1)} %get-tuple-element.28), channel_id=1, source_target_pairs={{16,0},{32,16},{48,32},{64,48},{80,64},{96,80},{112,96},{128,112},... | collective-permute-start | bytes 98312 | tf_op jit(solution)/shard_map/ppermute | solution.py:118
  54.7 2.4 %collective-permute-start.7 = (f32[16,1,512]{2,0,1:T(8,128)S(1)}, f32[16,1,512]{2,0,1:T(8,128)S(1)}, u32[]{:S(2)}, u32[]{:S(2)}) collective-permute-start(f32[16,1,512]{2,0,1:T(8,128)S(1)} %get-tuple-element.29), channel_id=1, source_target_pairs={{0,16},{16,32},{32,48},{48,64},{64,80},{80,96},{96,112},{112,128},... | collective-permute-start | bytes 98312 | tf_op jit(solution)/shard_map/ppermute | solution.py:114
  60.0 2.5 %broadcast_multiply_fusion = (f32[16,16,512]{2,0,1:T(8,128)S(1)}, f32[16,16,512]{2,0,1:T(8,128)S(1)}) fusion(f32[16,512]{1,0:T(8,128)S(1)} %divide_bitcast_fusion, f32[16,16,512]{2,0,1:T(8,128)S(1)} %get-tuple-element.7, f32[512]{0:T(512)S(1)} %get-tuple-element.63, f32[16,16,511]{2,0,1:T(8,128)} %get-tuple-element.35, f32[16,512]{1,0:T(8,128)S(1)} %get-tuple-element.57, ...), kind=kLoop, calls=%fused_computation.87 | loop fusion | flops 2752512 | bytes 5507072 | tf_op jit(solution)/shard_map/mul | solution.py:183
  72.9 5.7 %collective-permute-start.12 = (f32[16,8,128]{2,1,0:T(8,128)}, f32[16,8,128]{2,1,0:T(8,128)}, u32[]{:S(2)}, u32[]{:S(2)}) collective-permute-start(f32[16,8,128]{2,1,0:T(8,128)} %reshape.262), channel_id=1, source_target_pairs={{1,0},{2,1},{3,2},{4,3},{5,4},{6,5},{7,6},{8,7},{9,8},{10,9},{11,1... | collective-permute-start | bytes 196616 | tf_op jit(solution)/shard_map/ppermute | solution.py:118
  85.7 2.4 %collective-permute-start.11 = (f32[16,1,512]{2,0,1:T(8,128)S(1)}, f32[16,1,512]{2,0,1:T(8,128)S(1)}, u32[]{:S(2)}, u32[]{:S(2)}) collective-permute-start(f32[16,1,512]{2,0,1:T(8,128)S(1)} %get-tuple-element.22), channel_id=1, source_target_pairs={{0,16},{16,32},{32,48},{48,64},{64,80},{80,96},{96,112},{112,128},... | collective-permute-start | bytes 98312 | tf_op jit(solution)/shard_map/ppermute | solution.py:114
  95.0 2.6 %fusion.36 = f32[16,16,512]{2,0,1:T(8,128)S(1)} fusion(f32[16,16,512]{2,0,1:T(8,128)S(1)} %get-tuple-element.5, f32[16,1,512]{2,0,1:T(8,128)S(1)} %collective-permute-done.10, f32[16,15,512]{2,0,1:T(8,128)} %get-tuple-element.25, f32[16,15,512]{2,0,1:T(8,128)} %get-tuple-element.24, f32[16,1,512]{2,0,1:T(8,128)S(1)} %collective-permute-done.11, ...), kind=kLoop, calls=%fused_computation.56 | loop fusion | flops 2621440 | bytes 4950016 | tf_op jit(solution)/shard_map/sub | solution.py:210
  102.3 2.8 %collective-permute-done.15 = f32[6,16,16]{2,1,0:T(8,128)S(1)} collective-permute-done((f32[6,16,16]{2,1,0:T(8,128)S(1)}, f32[6,16,16]{2,1,0:T(8,128)S(1)}, u32[]{:S(2)}, u32[]{:S(2)}) %collective-permute-start.15) | collective-permute-done | bytes 6176 | tf_op jit(solution)/shard_map/ppermute | solution.py:25
  105.1 8.2 %collective-permute-start.17 = (f32[6,16,16]{2,1,0:T(8,128)S(1)}, f32[6,16,16]{2,1,0:T(8,128)S(1)}, u32[]{:S(2)}, u32[]{:S(2)}) collective-permute-start(f32[6,16,16]{2,1,0:T(8,128)S(1)} %add_add_fusion.3), channel_id=1, source_target_pairs={{0,64},{16,80},{32,96},{48,112},{64,0},{80,16},{96,32},{112,48},{1... | collective-permute-start | bytes 18440 | tf_op jit(solution)/shard_map/ppermute | solution.py:25
  114.2 2.8 %collective-permute-start.19 = (f32[6,16,16]{2,1,0:T(8,128)S(1)}, f32[6,16,16]{2,1,0:T(8,128)S(1)}, u32[]{:S(2)}, u32[]{:S(2)}) collective-permute-start(f32[6,16,16]{2,1,0:T(8,128)S(1)} %add_add_fusion.3), channel_id=1, source_target_pairs={{0,192},{16,208},{32,224},{48,240},{64,128},{80,144},{96,160},{112... | collective-permute-start | bytes 18440 | tf_op jit(solution)/shard_map/ppermute | solution.py:25
  117.0 5.2 %collective-permute-done.18 = f32[6,16,16]{2,1,0:T(8,128)S(1)} collective-permute-done((f32[6,16,16]{2,1,0:T(8,128)S(1)}, f32[6,16,16]{2,1,0:T(8,128)S(1)}, u32[]{:S(2)}, u32[]{:S(2)}) %collective-permute-start.18) | collective-permute-done | bytes 6176 | tf_op jit(solution)/shard_map/ppermute | solution.py:25
  123.4 5.7 %collective-permute-start.21 = (f32[6,16,16]{2,1,0:T(8,128)S(1)}, f32[6,16,16]{2,1,0:T(8,128)S(1)}, u32[]{:S(2)}, u32[]{:S(2)}) collective-permute-start(f32[6,16,16]{2,1,0:T(8,128)S(1)} %add_add_fusion.2), channel_id=1, source_target_pairs={{0,2},{1,3},{2,0},{3,1},{4,6},{5,7},{6,4},{7,5},{8,10},{9,11},{10,... | collective-permute-start | bytes 18440 | tf_op jit(solution)/shard_map/ppermute | solution.py:25
  129.1 2.6 %collective-permute-done.21 = f32[6,16,16]{2,1,0:T(8,128)S(1)} collective-permute-done((f32[6,16,16]{2,1,0:T(8,128)S(1)}, f32[6,16,16]{2,1,0:T(8,128)S(1)}, u32[]{:S(2)}, u32[]{:S(2)}) %collective-permute-start.21) | collective-permute-done | bytes 6176 | tf_op jit(solution)/shard_map/ppermute | solution.py:25
  131.7 2.7 %collective-permute-done.22 = f32[6,16,16]{2,1,0:T(8,128)S(1)} collective-permute-done((f32[6,16,16]{2,1,0:T(8,128)S(1)}, f32[6,16,16]{2,1,0:T(8,128)S(1)}, u32[]{:S(2)}, u32[]{:S(2)}) %collective-permute-start.22) | collective-permute-done | bytes 6176 | tf_op jit(solution)/shard_map/ppermute | solution.py:25
  134.9 2.3 %collective-permute-start.24 = (f32[6,16,16]{2,1,0:T(8,128)S(1)}, f32[6,16,16]{2,1,0:T(8,128)S(1)}, u32[]{:S(2)}, u32[]{:S(2)}) collective-permute-start(f32[6,16,16]{2,1,0:T(8,128)S(1)} %add_add_fusion.1), channel_id=1, source_target_pairs={{0,8},{1,9},{2,10},{3,11},{4,12},{5,13},{6,14},{7,15},{8,0},{9,1},... | collective-permute-start | bytes 18440 | tf_op jit(solution)/shard_map/ppermute | solution.py:25
  156.9 2.9 %cholesky.41 = f32[32,32]{1,0:T(8,128)S(1)} custom-call(f32[32,32]{1,0:T(8,128)S(1)} %fusion.61), custom_call_target="Cholesky" | custom-call | tf_op jit(solution)/shard_map/jit(cholesky)/cholesky | solution.py:67
  161.1 2.4 %custom-call.13 = f32[1,32,32]{1,2,0:T(8,128)S(1)} custom-call(f32[1,32,32]{2,1,0:T(8,128)S(1)} %fusion.54), custom_call_target="InvertDiagBlocksLowerTriangular" | custom-call | tf_op jit(solution)/shard_map/triangular_solve | solution.py:69
  176.4 2.1 %fusion.43 = f32[16,16,512]{2,0,1:T(8,128)S(1)} fusion(f32[16,16,512]{2,0,1:T(8,128)S(1)} %reshape.249, f32[16,1,512]{2,0,1:T(8,128)S(1)} %fusion.9, f32[16,15,512]{2,0,1:T(8,128)} %get-tuple-element.15, f32[16,15,512]{2,0,1:T(8,128)} %get-tuple-element.14, f32[16,1,512]{2,0,1:T(8,128)S(1)} %fusion.11, f32[16,16,64]{2,0,1:T(8,128)S(1)} %fusion.6, ...), kind=kLoop, calls=%fused_computation.67 | loop fusion | flops 2621440 | bytes 4950016 | tf_op jit(solution)/shard_map/sub | solution.py:270
  179.9 2.3 %reshape.273 = f32[16,8,1024]{2,1,0:T(8,128)} reshape(f32[16,8,16,64]{3,2,1,0:T(8,128)} %copy.82) | data formatting | bytes 1048576 | tf_op jit(solution)/shard_map/reshape | solution.py:89
  (283 shorter events, 99.4 us)
Async XLA Ops:
  2.2 28.1 %collective-permute-start.1 = (f32[1,16,64]{2,1,0:T(8,128)}, f32[1,16,64]{2,1,0:T(8,128)S(1)}, u32[]{:S(2)}, u32[]{:S(2)}) collective-permute-start(f32[1,16,64]{2,1,0:T(8,128)} %slice.495), channel_id=1, source_target_pairs={{0,1},{1,2},{2,3},{3,4},{4,5},{5,6},{6,7},{7,8},{8,9},{9,10},{10,1... | collective-permute-start | bytes 12296 | tf_op jit(solution)/shard_map/ppermute | solution.py:114
  7.1 21.0 %collective-permute-start = (f32[1,1,512]{2,1,0:T(1,128)}, f32[1,1,512]{2,1,0:T(1,128)}, u32[]{:S(2)}, u32[]{:S(2)}) collective-permute-start(f32[1,1,512]{2,1,0:T(1,128)} %slice.493), channel_id=1, source_target_pairs={{0,16},{16,32},{32,48},{48,64},{64,80},{80,96},{96,112},{112,128},... | collective-permute-start | bytes 6152 | tf_op jit(solution)/shard_map/ppermute | solution.py:114
  11.9 19.6 %collective-permute-start.4 = (f32[16,8,128]{2,1,0:T(8,128)}, f32[16,8,128]{2,1,0:T(8,128)}, u32[]{:S(2)}, u32[]{:S(2)}) collective-permute-start(f32[16,8,128]{2,1,0:T(8,128)} %reshape.254), channel_id=1, source_target_pairs={{1,0},{2,1},{3,2},{4,3},{5,4},{6,5},{7,6},{8,7},{9,8},{10,9},{11,1... | collective-permute-start | bytes 196616 | tf_op jit(solution)/shard_map/ppermute | solution.py:118
  17.2 15.3 %collective-permute-start.5 = (f32[16,8,128]{2,1,0:T(8,128)}, f32[16,8,128]{2,1,0:T(8,128)}, u32[]{:S(2)}, u32[]{:S(2)}) collective-permute-start(f32[16,8,128]{2,1,0:T(8,128)} %reshape.256), channel_id=1, source_target_pairs={{0,1},{1,2},{2,3},{3,4},{4,5},{5,6},{6,7},{7,8},{8,9},{9,10},{10,1... | collective-permute-start | bytes 196616 | tf_op jit(solution)/shard_map/ppermute | solution.py:114
  19.7 13.7 %collective-permute-start.2 = (f32[16,1,512]{2,0,1:T(8,128)}, f32[16,1,512]{2,0,1:T(8,128)}, u32[]{:S(2)}, u32[]{:S(2)}) collective-permute-start(f32[16,1,512]{2,0,1:T(8,128)} %get-tuple-element.38), channel_id=1, source_target_pairs={{16,0},{32,16},{48,32},{64,48},{80,64},{96,80},{112,96},{128,112},... | collective-permute-start | bytes 98312 | tf_op jit(solution)/shard_map/ppermute | solution.py:118
  28.1 5.3 %collective-permute-start.3 = (f32[16,1,512]{2,0,1:T(8,128)S(1)}, f32[16,1,512]{2,0,1:T(8,128)S(1)}, u32[]{:S(2)}, u32[]{:S(2)}) collective-permute-start(f32[16,1,512]{2,0,1:T(8,128)S(1)} %copy-done.26), channel_id=1, source_target_pairs={{0,16},{16,32},{32,48},{48,64},{64,80},{80,96},{96,112},{112,128},... | collective-permute-start | bytes 98312 | tf_op jit(solution)/shard_map/ppermute | solution.py:114
  43.8 14.4 %collective-permute-start.8 = (f32[16,8,128]{2,1,0:T(8,128)S(1)}, f32[16,8,128]{2,1,0:T(8,128)S(1)}, u32[]{:S(2)}, u32[]{:S(2)}) collective-permute-start(f32[16,8,128]{2,1,0:T(8,128)S(1)} %reshape.258), channel_id=1, source_target_pairs={{1,0},{2,1},{3,2},{4,3},{5,4},{6,5},{7,6},{8,7},{9,8},{10,9},{11,1... | collective-permute-start | bytes 196616 | tf_op jit(solution)/shard_map/ppermute | solution.py:118
  49.7 8.7 %collective-permute-start.9 = (f32[16,8,128]{2,1,0:T(8,128)S(1)}, f32[16,8,128]{2,1,0:T(8,128)S(1)}, u32[]{:S(2)}, u32[]{:S(2)}) collective-permute-start(f32[16,8,128]{2,1,0:T(8,128)S(1)} %reshape.260), channel_id=1, source_target_pairs={{0,1},{1,2},{2,3},{3,4},{4,5},{5,6},{6,7},{7,8},{8,9},{9,10},{10,1... | collective-permute-start | bytes 196616 | tf_op jit(solution)/shard_map/ppermute | solution.py:114
  51.6 6.9 %collective-permute-start.6 = (f32[16,1,512]{2,0,1:T(8,128)S(1)}, f32[16,1,512]{2,0,1:T(8,128)S(1)}, u32[]{:S(2)}, u32[]{:S(2)}) collective-permute-start(f32[16,1,512]{2,0,1:T(8,128)S(1)} %get-tuple-element.28), channel_id=1, source_target_pairs={{16,0},{32,16},{48,32},{64,48},{80,64},{96,80},{112,96},{128,112},... | collective-permute-start | bytes 98312 | tf_op jit(solution)/shard_map/ppermute | solution.py:118
  54.7 5.2 %collective-permute-start.7 = (f32[16,1,512]{2,0,1:T(8,128)S(1)}, f32[16,1,512]{2,0,1:T(8,128)S(1)}, u32[]{:S(2)}, u32[]{:S(2)}) collective-permute-start(f32[16,1,512]{2,0,1:T(8,128)S(1)} %get-tuple-element.29), channel_id=1, source_target_pairs={{0,16},{16,32},{32,48},{48,64},{64,80},{80,96},{96,112},{112,128},... | collective-permute-start | bytes 98312 | tf_op jit(solution)/shard_map/ppermute | solution.py:114
  72.9 16.3 %collective-permute-start.12 = (f32[16,8,128]{2,1,0:T(8,128)}, f32[16,8,128]{2,1,0:T(8,128)}, u32[]{:S(2)}, u32[]{:S(2)}) collective-permute-start(f32[16,8,128]{2,1,0:T(8,128)} %reshape.262), channel_id=1, source_target_pairs={{1,0},{2,1},{3,2},{4,3},{5,4},{6,5},{7,6},{8,7},{9,8},{10,9},{11,1... | collective-permute-start | bytes 196616 | tf_op jit(solution)/shard_map/ppermute | solution.py:118
  81.9 10.5 %collective-permute-start.13 = (f32[16,8,128]{2,1,0:T(8,128)}, f32[16,8,128]{2,1,0:T(8,128)}, u32[]{:S(2)}, u32[]{:S(2)}) collective-permute-start(f32[16,8,128]{2,1,0:T(8,128)} %reshape.264), channel_id=1, source_target_pairs={{0,1},{1,2},{2,3},{3,4},{4,5},{5,6},{6,7},{7,8},{8,9},{9,10},{10,1... | collective-permute-start | bytes 196616 | tf_op jit(solution)/shard_map/ppermute | solution.py:114
  83.8 11.2 %collective-permute-start.10 = (f32[16,1,512]{2,0,1:T(8,128)S(1)}, f32[16,1,512]{2,0,1:T(8,128)S(1)}, u32[]{:S(2)}, u32[]{:S(2)}) collective-permute-start(f32[16,1,512]{2,0,1:T(8,128)S(1)} %get-tuple-element.23), channel_id=1, source_target_pairs={{16,0},{32,16},{48,32},{64,48},{80,64},{96,80},{112,96},{128,112},... | collective-permute-start | bytes 98312 | tf_op jit(solution)/shard_map/ppermute | solution.py:118
  85.7 9.2 %collective-permute-start.11 = (f32[16,1,512]{2,0,1:T(8,128)S(1)}, f32[16,1,512]{2,0,1:T(8,128)S(1)}, u32[]{:S(2)}, u32[]{:S(2)}) collective-permute-start(f32[16,1,512]{2,0,1:T(8,128)S(1)} %get-tuple-element.22), channel_id=1, source_target_pairs={{0,16},{16,32},{32,48},{48,64},{64,80},{80,96},{96,112},{112,128},... | collective-permute-start | bytes 98312 | tf_op jit(solution)/shard_map/ppermute | solution.py:114
  100.8 4.3 %collective-permute-start.15 = (f32[6,16,16]{2,1,0:T(8,128)S(1)}, f32[6,16,16]{2,1,0:T(8,128)S(1)}, u32[]{:S(2)}, u32[]{:S(2)}) collective-permute-start(f32[6,16,16]{2,1,0:T(8,128)S(1)} %constant_dynamic-update-slice_fusion), channel_id=1, source_target_pairs={{0,32},{16,48},{32,0},{48,16},{64,96},{80,112},{96,64},{112,80},{1... | collective-permute-start | bytes 18440 | tf_op jit(solution)/shard_map/ppermute | solution.py:25
  100.9 4.2 %collective-permute-start.16 = (f32[6,16,16]{2,1,0:T(8,128)S(1)}, f32[6,16,16]{2,1,0:T(8,128)S(1)}, u32[]{:S(2)}, u32[]{:S(2)}) collective-permute-start(f32[6,16,16]{2,1,0:T(8,128)S(1)} %constant_dynamic-update-slice_fusion), channel_id=1, source_target_pairs={{0,48},{16,32},{32,16},{48,0},{64,112},{80,96},{96,80},{112,64},{1... | collective-permute-start | bytes 18440 | tf_op jit(solution)/shard_map/ppermute | solution.py:25
  105.1 11.9 %collective-permute-start.17 = (f32[6,16,16]{2,1,0:T(8,128)S(1)}, f32[6,16,16]{2,1,0:T(8,128)S(1)}, u32[]{:S(2)}, u32[]{:S(2)}) collective-permute-start(f32[6,16,16]{2,1,0:T(8,128)S(1)} %add_add_fusion.3), channel_id=1, source_target_pairs={{0,64},{16,80},{32,96},{48,112},{64,0},{80,16},{96,32},{112,48},{1... | collective-permute-start | bytes 18440 | tf_op jit(solution)/shard_map/ppermute | solution.py:25
  113.3 8.9 %collective-permute-start.18 = (f32[6,16,16]{2,1,0:T(8,128)S(1)}, f32[6,16,16]{2,1,0:T(8,128)S(1)}, u32[]{:S(2)}, u32[]{:S(2)}) collective-permute-start(f32[6,16,16]{2,1,0:T(8,128)S(1)} %add_add_fusion.3), channel_id=1, source_target_pairs={{0,128},{16,144},{32,160},{48,176},{64,192},{80,208},{96,224},{112... | collective-permute-start | bytes 18440 | tf_op jit(solution)/shard_map/ppermute | solution.py:25
  114.2 8.8 %collective-permute-start.19 = (f32[6,16,16]{2,1,0:T(8,128)S(1)}, f32[6,16,16]{2,1,0:T(8,128)S(1)}, u32[]{:S(2)}, u32[]{:S(2)}) collective-permute-start(f32[6,16,16]{2,1,0:T(8,128)S(1)} %add_add_fusion.3), channel_id=1, source_target_pairs={{0,192},{16,208},{32,224},{48,240},{64,128},{80,144},{96,160},{112... | collective-permute-start | bytes 18440 | tf_op jit(solution)/shard_map/ppermute | solution.py:25
  123.0 6.0 %collective-permute-start.20 = (f32[6,16,16]{2,1,0:T(8,128)S(1)}, f32[6,16,16]{2,1,0:T(8,128)S(1)}, u32[]{:S(2)}, u32[]{:S(2)}) collective-permute-start(f32[6,16,16]{2,1,0:T(8,128)S(1)} %add_add_fusion.2), channel_id=1, source_target_pairs={{0,1},{1,0},{2,3},{3,2},{4,5},{5,4},{6,7},{7,6},{8,9},{9,8},{10,11... | collective-permute-start | bytes 18440 | tf_op jit(solution)/shard_map/ppermute | solution.py:25
  123.4 8.3 %collective-permute-start.21 = (f32[6,16,16]{2,1,0:T(8,128)S(1)}, f32[6,16,16]{2,1,0:T(8,128)S(1)}, u32[]{:S(2)}, u32[]{:S(2)}) collective-permute-start(f32[6,16,16]{2,1,0:T(8,128)S(1)} %add_add_fusion.2), channel_id=1, source_target_pairs={{0,2},{1,3},{2,0},{3,1},{4,6},{5,7},{6,4},{7,5},{8,10},{9,11},{10,... | collective-permute-start | bytes 18440 | tf_op jit(solution)/shard_map/ppermute | solution.py:25
  129.1 5.3 %collective-permute-start.22 = (f32[6,16,16]{2,1,0:T(8,128)S(1)}, f32[6,16,16]{2,1,0:T(8,128)S(1)}, u32[]{:S(2)}, u32[]{:S(2)}) collective-permute-start(f32[6,16,16]{2,1,0:T(8,128)S(1)} %add_add_fusion.2), channel_id=1, source_target_pairs={{0,3},{1,2},{2,1},{3,0},{4,7},{5,6},{6,5},{7,4},{8,11},{9,10},{10,... | collective-permute-start | bytes 18440 | tf_op jit(solution)/shard_map/ppermute | solution.py:25
  134.4 4.2 %collective-permute-start.23 = (f32[6,16,16]{2,1,0:T(8,128)S(1)}, f32[6,16,16]{2,1,0:T(8,128)S(1)}, u32[]{:S(2)}, u32[]{:S(2)}) collective-permute-start(f32[6,16,16]{2,1,0:T(8,128)S(1)} %add_add_fusion.1), channel_id=1, source_target_pairs={{0,4},{1,5},{2,6},{3,7},{4,0},{5,1},{6,2},{7,3},{8,12},{9,13},{10,... | collective-permute-start | bytes 18440 | tf_op jit(solution)/shard_map/ppermute | solution.py:25
  134.9 5.6 %collective-permute-start.24 = (f32[6,16,16]{2,1,0:T(8,128)S(1)}, f32[6,16,16]{2,1,0:T(8,128)S(1)}, u32[]{:S(2)}, u32[]{:S(2)}) collective-permute-start(f32[6,16,16]{2,1,0:T(8,128)S(1)} %add_add_fusion.1), channel_id=1, source_target_pairs={{0,8},{1,9},{2,10},{3,11},{4,12},{5,13},{6,14},{7,15},{8,0},{9,1},... | collective-permute-start | bytes 18440 | tf_op jit(solution)/shard_map/ppermute | solution.py:25
  (29 other events, 157.3 us)

commit v2 on v0

--- a/solution.py
+++ b/solution.py
@@ -127,12 +127,21 @@
     before_z = low_z(after_z)
     diagonal = coef(reaction) + after_x + before_x + after_y + before_y + after_z + before_z
 
+    def split_send(move, slab, axis):
+        pieces = max(1, slab.size * 4 // 32768)
+        if count_rhs % pieces:
+            return move(slab, axis)
+        share = count_rhs // pieces
+        return jnp.concatenate(
+            [move(slab[i * share : (i + 1) * share], axis) for i in range(pieces)], axis=0
+        )
+
     def halos(values):
         return (
-            forward(values[:, -1:], "gx"),
-            backward(values[:, :1], "gx"),
-            forward(values[:, :, plane - layers :], "gy"),
-            backward(values[:, :, :layers], "gy"),
+            split_send(forward, values[:, -1:], "gx"),
+            split_send(backward, values[:, :1], "gx"),
+            split_send(forward, values[:, :, plane - layers :], "gy"),
+            split_send(backward, values[:, :, :layers], "gy"),
         )
 
     def apply_op(values, edges):

time: 162 us -> 179 us (1.10)
  starting transfers between devices: 65.4 us -> 81.4 us
  waiting for transfers between devices: 23.2 us -> 20.5 us
  local copies, waits for them, and re-layouts: 26.7 us -> 28.6 us
    ppermute x8 -> x11, starting transfers between devices: 18.4 us -> 30.8 us  [forward(): return lax.ppermute(block, axis, [(i, i + 1) for i in range(count - 1)])]
    ppermute x6 -> x9, starting transfers between devices: 23.5 us -> 28.1 us  [backward(): return lax.ppermute(block, axis, [(i + 1, i) for i in range(count - 1)])]
    unnamed x40 -> x60, local copies, waits for them, and re-layouts: 0.55 us -> 3.08 us
    reshape x4, local copies, waits for them, and re-layouts: 4.51 us -> 2.27 us  [inward(): split = values.reshape(rows_x, rows_y, count_rhs, layers)]
    ppermute x8 -> x11, waiting for transfers between devices: 7.27 us -> 5.9 us  [forward(): return lax.ppermute(block, axis, [(i, i + 1) for i in range(count - 1)])]
  transfers between devices with their start and end apart: 26 -> 32, of which waited for: 11 -> 12; matrix products, arithmetic and copies ran while one was open for 8% -> 7% of each run, Pallas kernels for 0% -> 0%
where the time goes in v2:
time: 179 us; the launch traced here: 176 us
  starting transfers between devices  81.4 us (45%)
  other arithmetic  30.2 us (17%)
  local copies, waits for them, and re-layouts  28.6 us (16%)
  waiting for transfers between devices  20.5 us (11%)
  matrix products  13.1 us (7%)
  between operations  1.79 us (1%)
    ppermute x11, starting transfers between devices, forward(): return lax.ppermute(block, axis, [(i, i + 1) for i in range(count - 1)])  30.8 us
    ppermute x9, starting transfers between devices, backward(): return lax.ppermute(block, axis, [(i + 1, i) for i in range(count - 1)])  28.1 us
    ppermute x12, starting transfers between devices, mesh_sum(): lax.ppermute(block, axis, [(i, i ^ step * m) for i in range(count)])  22.5 us
    ppermute x12, waiting for transfers between devices, mesh_sum(): lax.ppermute(block, axis, [(i, i ^ step * m) for i in range(count)])  14.6 us
    dot_general x10, matrix products, mix_block(): return jnp.einsum('ts,sxl->txl', matrix.T, values, precision=HIGH)  7.05 us
    another operation x9, other arithmetic, chol_factor(): low_factor = jnp.linalg.cholesky(gram_mat)  6.44 us
    slice x28, local copies, waits for them, and re-layouts, up_along(): lax.slice_in_dim(values, width, count, axis=axis)  6.06 us
    ppermute x11, waiting for transfers between devices, forward(): return lax.ppermute(block, axis, [(i, i + 1) for i in range(count - 1)])  5.9 us
  transfers between devices with their start and end apart: 32, of which 12 were waited for; matrix products, arithmetic and copies ran while one was open for 7% of the time, Pallas kernels for 0%

profile of v2, /device:TPU:40, one launch (start us, length us, event | category | flops | bytes accessed | tf_op | source)
XLA Modules:
  0.0 175.6 jit_solution(12666832079528326055)
XLA Ops:
  2.2 3.4 %collective-permute-start.1 = (f32[1,16,64]{2,1,0:T(8,128)}, f32[1,16,64]{2,1,0:T(8,128)S(1)}, u32[]{:S(2)}, u32[]{:S(2)}) collective-permute-start(f32[1,16,64]{2,1,0:T(8,128)} %slice.486), channel_id=1, source_target_pairs={{0,1},{1,2},{2,3},{3,4},{4,5},{5,6},{6,7},{7,8},{8,9},{9,10},{10,1... | collective-permute-start | bytes 12296 | tf_op jit(solution)/shard_map/ppermute | solution.py:114
  11.7 4.5 %collective-permute-start.4 = (f32[8,16,64]{2,0,1:T(8,128)}, f32[8,16,64]{2,0,1:T(8,128)}, u32[]{:S(2)}, u32[]{:S(2)}) collective-permute-start(f32[8,16,64]{2,0,1:T(8,128)} %get-tuple-element.49), channel_id=1, source_target_pairs={{1,0},{2,1},{3,2},{4,3},{5,4},{6,5},{7,6},{8,7},{9,8},{10,9},{11,1... | collective-permute-start | bytes 98312 | tf_op jit(solution)/shard_map/ppermute | solution.py:118
  16.3 2.4 %collective-permute-start.5 = (f32[8,16,64]{2,0,1:T(8,128)}, f32[8,16,64]{2,0,1:T(8,128)}, u32[]{:S(2)}, u32[]{:S(2)}) collective-permute-start(f32[8,16,64]{2,0,1:T(8,128)} %get-tuple-element.46), channel_id=1, source_target_pairs={{1,0},{2,1},{3,2},{4,3},{5,4},{6,5},{7,6},{8,7},{9,8},{10,9},{11,1... | collective-permute-start | bytes 98312 | tf_op jit(solution)/shard_map/ppermute | solution.py:118
  18.7 3.4 %collective-permute-start.6 = (f32[8,16,64]{2,0,1:T(8,128)}, f32[8,16,64]{2,0,1:T(8,128)}, u32[]{:S(2)}, u32[]{:S(2)}) collective-permute-start(f32[8,16,64]{2,0,1:T(8,128)} %get-tuple-element.48), channel_id=1, source_target_pairs={{0,1},{1,2},{2,3},{3,4},{4,5},{5,6},{6,7},{7,8},{8,9},{9,10},{10,1... | collective-permute-start | bytes 98312 | tf_op jit(solution)/shard_map/ppermute | solution.py:114
  29.9 2.8 %collective-permute-start.2 = (f32[16,1,512]{2,0,1:T(8,128)S(1)}, f32[16,1,512]{2,0,1:T(8,128)S(1)}, u32[]{:S(2)}, u32[]{:S(2)}) collective-permute-start(f32[16,1,512]{2,0,1:T(8,128)S(1)} %copy-done.26), channel_id=1, source_target_pairs={{16,0},{32,16},{48,32},{64,48},{80,64},{96,80},{112,96},{128,112},... | collective-permute-start | bytes 98312 | tf_op jit(solution)/shard_map/ppermute | solution.py:118
  46.6 5.8 %collective-permute-start.10 = (f32[8,16,64]{2,0,1:T(8,128)S(1)}, f32[8,16,64]{2,0,1:T(8,128)S(1)}, u32[]{:S(2)}, u32[]{:S(2)}) collective-permute-start(f32[8,16,64]{2,0,1:T(8,128)S(1)} %get-tuple-element.37), channel_id=1, source_target_pairs={{1,0},{2,1},{3,2},{4,3},{5,4},{6,5},{7,6},{8,7},{9,8},{10,9},{11,1... | collective-permute-start | bytes 98312 | tf_op jit(solution)/shard_map/ppermute | solution.py:118
  52.4 2.4 %collective-permute-start.11 = (f32[8,16,64]{2,0,1:T(8,128)S(1)}, f32[8,16,64]{2,0,1:T(8,128)S(1)}, u32[]{:S(2)}, u32[]{:S(2)}) collective-permute-start(f32[8,16,64]{2,0,1:T(8,128)S(1)} %get-tuple-element.34), channel_id=1, source_target_pairs={{1,0},{2,1},{3,2},{4,3},{5,4},{6,5},{7,6},{8,7},{9,8},{10,9},{11,1... | collective-permute-start | bytes 98312 | tf_op jit(solution)/shard_map/ppermute | solution.py:118
  54.9 3.4 %collective-permute-start.12 = (f32[8,16,64]{2,0,1:T(8,128)S(1)}, f32[8,16,64]{2,0,1:T(8,128)S(1)}, u32[]{:S(2)}, u32[]{:S(2)}) collective-permute-start(f32[8,16,64]{2,0,1:T(8,128)S(1)} %get-tuple-element.36), channel_id=1, source_target_pairs={{0,1},{1,2},{2,3},{3,4},{4,5},{5,6},{6,7},{7,8},{8,9},{9,10},{10,1... | collective-permute-start | bytes 98312 | tf_op jit(solution)/shard_map/ppermute | solution.py:114
  62.4 2.4 %collective-permute-start.9 = (f32[16,1,512]{2,0,1:T(8,128)S(1)}, f32[16,1,512]{2,0,1:T(8,128)S(1)}, u32[]{:S(2)}, u32[]{:S(2)}) collective-permute-start(f32[16,1,512]{2,0,1:T(8,128)S(1)} %get-tuple-element.31), channel_id=1, source_target_pairs={{0,16},{16,32},{32,48},{48,64},{64,80},{80,96},{96,112},{112,128},... | collective-permute-start | bytes 98312 | tf_op jit(solution)/shard_map/ppermute | solution.py:114
  76.2 5.6 %collective-permute-start.19 = (f32[8,16,64]{2,0,1:T(8,128)S(1)}, f32[8,16,64]{2,0,1:T(8,128)S(1)}, u32[]{:S(2)}, u32[]{:S(2)}) collective-permute-start(f32[8,16,64]{2,0,1:T(8,128)S(1)} %get-tuple-element.18), channel_id=1, source_target_pairs={{0,1},{1,2},{2,3},{3,4},{4,5},{5,6},{6,7},{7,8},{8,9},{9,10},{10,1... | collective-permute-start | bytes 98312 | tf_op jit(solution)/shard_map/ppermute | solution.py:114
  81.8 2.4 %collective-permute-start.16 = (f32[8,16,64]{2,0,1:T(8,128)S(1)}, f32[8,16,64]{2,0,1:T(8,128)S(1)}, u32[]{:S(2)}, u32[]{:S(2)}) collective-permute-start(f32[8,16,64]{2,0,1:T(8,128)S(1)} %get-tuple-element.21), channel_id=1, source_target_pairs={{1,0},{2,1},{3,2},{4,3},{5,4},{6,5},{7,6},{8,7},{9,8},{10,9},{11,1... | collective-permute-start | bytes 98312 | tf_op jit(solution)/shard_map/ppermute | solution.py:118
  84.2 3.6 %collective-permute-start.17 = (f32[8,16,64]{2,0,1:T(8,128)S(1)}, f32[8,16,64]{2,0,1:T(8,128)S(1)}, u32[]{:S(2)}, u32[]{:S(2)}) collective-permute-start(f32[8,16,64]{2,0,1:T(8,128)S(1)} %get-tuple-element.20), channel_id=1, source_target_pairs={{1,0},{2,1},{3,2},{4,3},{5,4},{6,5},{7,6},{8,7},{9,8},{10,9},{11,1... | collective-permute-start | bytes 98312 | tf_op jit(solution)/shard_map/ppermute | solution.py:118
  89.8 2.4 %collective-permute-start.15 = (f32[16,1,512]{2,0,1:T(8,128)S(1)}, f32[16,1,512]{2,0,1:T(8,128)S(1)}, u32[]{:S(2)}, u32[]{:S(2)}) collective-permute-start(f32[16,1,512]{2,0,1:T(8,128)S(1)} %get-tuple-element.24), channel_id=1, source_target_pairs={{0,16},{16,32},{32,48},{48,64},{64,80},{80,96},{96,112},{112,128},... | collective-permute-start | bytes 98312 | tf_op jit(solution)/shard_map/ppermute | solution.py:114
  92.3 2.7 %collective-permute-done.15 = f32[16,1,512]{2,0,1:T(8,128)S(1)} collective-permute-done((f32[16,1,512]{2,0,1:T(8,128)S(1)}, f32[16,1,512]{2,0,1:T(8,128)S(1)}, u32[]{:S(2)}, u32[]{:S(2)}) %collective-permute-start.15) | collective-permute-done | bytes 32800 | tf_op jit(solution)/shard_map/ppermute | solution.py:114
  101.2 7.8 %collective-permute-start.23 = (f32[48,48]{1,0:T(8,128)S(1)}, f32[48,48]{1,0:T(8,128)S(1)}, u32[]{:S(2)}, u32[]{:S(2)}) collective-permute-start(f32[48,48]{1,0:T(8,128)S(1)} %add_add_fusion.4), channel_id=1, source_target_pairs={{0,64},{16,80},{32,96},{48,112},{64,0},{80,16},{96,32},{112,48},{1... | collective-permute-start | bytes 27656 | tf_op jit(solution)/shard_map/ppermute | solution.py:25
  109.0 3.9 %collective-permute-start.24 = (f32[48,48]{1,0:T(8,128)S(1)}, f32[48,48]{1,0:T(8,128)S(1)}, u32[]{:S(2)}, u32[]{:S(2)}) collective-permute-start(f32[48,48]{1,0:T(8,128)S(1)} %add_add_fusion.4), channel_id=1, source_target_pairs={{0,128},{16,144},{32,160},{48,176},{64,192},{80,208},{96,224},{112... | collective-permute-start | bytes 27656 | tf_op jit(solution)/shard_map/ppermute | solution.py:25
  113.4 3.5 %collective-permute-done.24 = f32[48,48]{1,0:T(8,128)S(1)} collective-permute-done((f32[48,48]{1,0:T(8,128)S(1)}, f32[48,48]{1,0:T(8,128)S(1)}, u32[]{:S(2)}, u32[]{:S(2)}) %collective-permute-start.24) | collective-permute-done | bytes 9248 | tf_op jit(solution)/shard_map/ppermute | solution.py:25
  116.9 2.2 %collective-permute-done.25 = f32[48,48]{1,0:T(8,128)S(1)} collective-permute-done((f32[48,48]{1,0:T(8,128)S(1)}, f32[48,48]{1,0:T(8,128)S(1)}, u32[]{:S(2)}, u32[]{:S(2)}) %collective-permute-start.25) | collective-permute-done | bytes 9248 | tf_op jit(solution)/shard_map/ppermute | solution.py:25
  119.6 3.1 %collective-permute-start.27 = (f32[48,48]{1,0:T(8,128)S(1)}, f32[48,48]{1,0:T(8,128)S(1)}, u32[]{:S(2)}, u32[]{:S(2)}) collective-permute-start(f32[48,48]{1,0:T(8,128)S(1)} %add_add_fusion.3), channel_id=1, source_target_pairs={{0,2},{1,3},{2,0},{3,1},{4,6},{5,7},{6,4},{7,5},{8,10},{9,11},{10,... | collective-permute-start | bytes 27656 | tf_op jit(solution)/shard_map/ppermute | solution.py:25
  124.9 2.8 %collective-permute-done.28 = f32[48,48]{1,0:T(8,128)S(1)} collective-permute-done((f32[48,48]{1,0:T(8,128)S(1)}, f32[48,48]{1,0:T(8,128)S(1)}, u32[]{:S(2)}, u32[]{:S(2)}) %collective-permute-start.28) | collective-permute-done | bytes 9248 | tf_op jit(solution)/shard_map/ppermute | solution.py:25
  128.2 2.3 %collective-permute-start.30 = (f32[48,48]{1,0:T(8,128)S(1)}, f32[48,48]{1,0:T(8,128)S(1)}, u32[]{:S(2)}, u32[]{:S(2)}) collective-permute-start(f32[48,48]{1,0:T(8,128)S(1)} %add_add_fusion.2), channel_id=1, source_target_pairs={{0,8},{1,9},{2,10},{3,11},{4,12},{5,13},{6,14},{7,15},{8,0},{9,1},... | collective-permute-start | bytes 27656 | tf_op jit(solution)/shard_map/ppermute | solution.py:25
  149.6 2.9 %cholesky.41 = f32[32,32]{1,0:T(8,128)S(1)} custom-call(f32[32,32]{1,0:T(8,128)S(1)} %fusion.61), custom_call_target="Cholesky" | custom-call | tf_op jit(solution)/shard_map/jit(cholesky)/cholesky | solution.py:67
  153.9 2.4 %custom-call.13 = f32[1,32,32]{1,2,0:T(8,128)S(1)} custom-call(f32[1,32,32]{2,1,0:T(8,128)S(1)} %fusion.54), custom_call_target="InvertDiagBlocksLowerTriangular" | custom-call | tf_op jit(solution)/shard_map/triangular_solve | solution.py:69
  172.0 2.3 %reshape.225 = f32[16,8,1024]{2,1,0:T(8,128)} reshape(f32[16,8,16,64]{3,2,1,0:T(8,128)} %copy.15) | data formatting | bytes 1048576 | tf_op jit(solution)/shard_map/reshape | solution.py:89
  (272 shorter events, 93.2 us)
Async XLA Ops:
  2.2 27.7 %collective-permute-start.1 = (f32[1,16,64]{2,1,0:T(8,128)}, f32[1,16,64]{2,1,0:T(8,128)S(1)}, u32[]{:S(2)}, u32[]{:S(2)}) collective-permute-start(f32[1,16,64]{2,1,0:T(8,128)} %slice.486), channel_id=1, source_target_pairs={{0,1},{1,2},{2,3},{3,4},{4,5},{5,6},{6,7},{7,8},{8,9},{9,10},{10,1... | collective-permute-start | bytes 12296 | tf_op jit(solution)/shard_map/ppermute | solution.py:114
  7.1 20.7 %collective-permute-start = (f32[1,1,512]{2,1,0:T(1,128)}, f32[1,1,512]{2,1,0:T(1,128)}, u32[]{:S(2)}, u32[]{:S(2)}) collective-permute-start(f32[1,1,512]{2,1,0:T(1,128)} %slice.484), channel_id=1, source_target_pairs={{0,16},{16,32},{32,48},{48,64},{64,80},{80,96},{96,112},{112,128},... | collective-permute-start | bytes 6152 | tf_op jit(solution)/shard_map/ppermute | solution.py:114
  11.7 22.1 %collective-permute-start.4 = (f32[8,16,64]{2,0,1:T(8,128)}, f32[8,16,64]{2,0,1:T(8,128)}, u32[]{:S(2)}, u32[]{:S(2)}) collective-permute-start(f32[8,16,64]{2,0,1:T(8,128)} %get-tuple-element.49), channel_id=1, source_target_pairs={{1,0},{2,1},{3,2},{4,3},{5,4},{6,5},{7,6},{8,7},{9,8},{10,9},{11,1... | collective-permute-start | bytes 98312 | tf_op jit(solution)/shard_map/ppermute | solution.py:118
  16.3 21.5 %collective-permute-start.5 = (f32[8,16,64]{2,0,1:T(8,128)}, f32[8,16,64]{2,0,1:T(8,128)}, u32[]{:S(2)}, u32[]{:S(2)}) collective-permute-start(f32[8,16,64]{2,0,1:T(8,128)} %get-tuple-element.46), channel_id=1, source_target_pairs={{1,0},{2,1},{3,2},{4,3},{5,4},{6,5},{7,6},{8,7},{9,8},{10,9},{11,1... | collective-permute-start | bytes 98312 | tf_op jit(solution)/shard_map/ppermute | solution.py:118
  18.7 18.2 %collective-permute-start.6 = (f32[8,16,64]{2,0,1:T(8,128)}, f32[8,16,64]{2,0,1:T(8,128)}, u32[]{:S(2)}, u32[]{:S(2)}) collective-permute-start(f32[8,16,64]{2,0,1:T(8,128)} %get-tuple-element.48), channel_id=1, source_target_pairs={{0,1},{1,2},{2,3},{3,4},{4,5},{5,6},{6,7},{7,8},{8,9},{9,10},{10,1... | collective-permute-start | bytes 98312 | tf_op jit(solution)/shard_map/ppermute | solution.py:114
  27.9 10.8 %collective-permute-start.7 = (f32[8,16,64]{2,0,1:T(8,128)S(1)}, f32[8,16,64]{2,0,1:T(8,128)S(1)}, u32[]{:S(2)}, u32[]{:S(2)}) collective-permute-start(f32[8,16,64]{2,0,1:T(8,128)S(1)} %copy-done.23), channel_id=1, source_target_pairs={{0,1},{1,2},{2,3},{3,4},{4,5},{5,6},{6,7},{7,8},{8,9},{9,10},{10,1... | collective-permute-start | bytes 98312 | tf_op jit(solution)/shard_map/ppermute | solution.py:114
  29.9 8.7 %collective-permute-start.2 = (f32[16,1,512]{2,0,1:T(8,128)S(1)}, f32[16,1,512]{2,0,1:T(8,128)S(1)}, u32[]{:S(2)}, u32[]{:S(2)}) collective-permute-start(f32[16,1,512]{2,0,1:T(8,128)S(1)} %copy-done.26), channel_id=1, source_target_pairs={{16,0},{32,16},{48,32},{64,48},{80,64},{96,80},{112,96},{128,112},... | collective-permute-start | bytes 98312 | tf_op jit(solution)/shard_map/ppermute | solution.py:118
  33.9 5.2 %collective-permute-start.3 = (f32[16,1,512]{2,0,1:T(8,128)S(1)}, f32[16,1,512]{2,0,1:T(8,128)S(1)}, u32[]{:S(2)}, u32[]{:S(2)}) collective-permute-start(f32[16,1,512]{2,0,1:T(8,128)S(1)} %get-tuple-element.43), channel_id=1, source_target_pairs={{0,16},{16,32},{32,48},{48,64},{64,80},{80,96},{96,112},{112,128},... | collective-permute-start | bytes 98312 | tf_op jit(solution)/shard_map/ppermute | solution.py:114
  46.6 15.7 %collective-permute-start.10 = (f32[8,16,64]{2,0,1:T(8,128)S(1)}, f32[8,16,64]{2,0,1:T(8,128)S(1)}, u32[]{:S(2)}, u32[]{:S(2)}) collective-permute-start(f32[8,16,64]{2,0,1:T(8,128)S(1)} %get-tuple-element.37), channel_id=1, source_target_pairs={{1,0},{2,1},{3,2},{4,3},{5,4},{6,5},{7,6},{8,7},{9,8},{10,9},{11,1... | collective-permute-start | bytes 98312 | tf_op jit(solution)/shard_map/ppermute | solution.py:118
  52.4 12.4 %collective-permute-start.11 = (f32[8,16,64]{2,0,1:T(8,128)S(1)}, f32[8,16,64]{2,0,1:T(8,128)S(1)}, u32[]{:S(2)}, u32[]{:S(2)}) collective-permute-start(f32[8,16,64]{2,0,1:T(8,128)S(1)} %get-tuple-element.34), channel_id=1, source_target_pairs={{1,0},{2,1},{3,2},{4,3},{5,4},{6,5},{7,6},{8,7},{9,8},{10,9},{11,1... | collective-permute-start | bytes 98312 | tf_op jit(solution)/shard_map/ppermute | solution.py:118
  54.9 9.9 %collective-permute-start.12 = (f32[8,16,64]{2,0,1:T(8,128)S(1)}, f32[8,16,64]{2,0,1:T(8,128)S(1)}, u32[]{:S(2)}, u32[]{:S(2)}) collective-permute-start(f32[8,16,64]{2,0,1:T(8,128)S(1)} %get-tuple-element.36), channel_id=1, source_target_pairs={{0,1},{1,2},{2,3},{3,4},{4,5},{5,6},{6,7},{7,8},{8,9},{9,10},{10,1... | collective-permute-start | bytes 98312 | tf_op jit(solution)/shard_map/ppermute | solution.py:114
  58.3 8.5 %collective-permute-start.13 = (f32[8,16,64]{2,0,1:T(8,128)S(1)}, f32[8,16,64]{2,0,1:T(8,128)S(1)}, u32[]{:S(2)}, u32[]{:S(2)}) collective-permute-start(f32[8,16,64]{2,0,1:T(8,128)S(1)} %get-tuple-element.35), channel_id=1, source_target_pairs={{0,1},{1,2},{2,3},{3,4},{4,5},{5,6},{6,7},{7,8},{8,9},{9,10},{10,1... | collective-permute-start | bytes 98312 | tf_op jit(solution)/shard_map/ppermute | solution.py:114
  60.2 6.6 %collective-permute-start.8 = (f32[16,1,512]{2,0,1:T(8,128)S(1)}, f32[16,1,512]{2,0,1:T(8,128)S(1)}, u32[]{:S(2)}, u32[]{:S(2)}) collective-permute-start(f32[16,1,512]{2,0,1:T(8,128)S(1)} %get-tuple-element.30), channel_id=1, source_target_pairs={{16,0},{32,16},{48,32},{64,48},{80,64},{96,80},{112,96},{128,112},... | collective-permute-start | bytes 98312 | tf_op jit(solution)/shard_map/ppermute | solution.py:118
  62.4 5.2 %collective-permute-start.9 = (f32[16,1,512]{2,0,1:T(8,128)S(1)}, f32[16,1,512]{2,0,1:T(8,128)S(1)}, u32[]{:S(2)}, u32[]{:S(2)}) collective-permute-start(f32[16,1,512]{2,0,1:T(8,128)S(1)} %get-tuple-element.31), channel_id=1, source_target_pairs={{0,16},{16,32},{32,48},{48,64},{64,80},{80,96},{96,112},{112,128},... | collective-permute-start | bytes 98312 | tf_op jit(solution)/shard_map/ppermute | solution.py:114
  74.0 15.8 %collective-permute-start.18 = (f32[8,16,64]{2,0,1:T(8,128)S(1)}, f32[8,16,64]{2,0,1:T(8,128)S(1)}, u32[]{:S(2)}, u32[]{:S(2)}) collective-permute-start(f32[8,16,64]{2,0,1:T(8,128)S(1)} %get-tuple-element.19), channel_id=1, source_target_pairs={{0,1},{1,2},{2,3},{3,4},{4,5},{5,6},{6,7},{7,8},{8,9},{9,10},{10,1... | collective-permute-start | bytes 98312 | tf_op jit(solution)/shard_map/ppermute | solution.py:114
  76.2 16.0 %collective-permute-start.19 = (f32[8,16,64]{2,0,1:T(8,128)S(1)}, f32[8,16,64]{2,0,1:T(8,128)S(1)}, u32[]{:S(2)}, u32[]{:S(2)}) collective-permute-start(f32[8,16,64]{2,0,1:T(8,128)S(1)} %get-tuple-element.18), channel_id=1, source_target_pairs={{0,1},{1,2},{2,3},{3,4},{4,5},{5,6},{6,7},{7,8},{8,9},{9,10},{10,1... | collective-permute-start | bytes 98312 | tf_op jit(solution)/shard_map/ppermute | solution.py:114
  81.8 10.4 %collective-permute-start.16 = (f32[8,16,64]{2,0,1:T(8,128)S(1)}, f32[8,16,64]{2,0,1:T(8,128)S(1)}, u32[]{:S(2)}, u32[]{:S(2)}) collective-permute-start(f32[8,16,64]{2,0,1:T(8,128)S(1)} %get-tuple-element.21), channel_id=1, source_target_pairs={{1,0},{2,1},{3,2},{4,3},{5,4},{6,5},{7,6},{8,7},{9,8},{10,9},{11,1... | collective-permute-start | bytes 98312 | tf_op jit(solution)/shard_map/ppermute | solution.py:118
  84.2 8.1 %collective-permute-start.17 = (f32[8,16,64]{2,0,1:T(8,128)S(1)}, f32[8,16,64]{2,0,1:T(8,128)S(1)}, u32[]{:S(2)}, u32[]{:S(2)}) collective-permute-start(f32[8,16,64]{2,0,1:T(8,128)S(1)} %get-tuple-element.20), channel_id=1, source_target_pairs={{1,0},{2,1},{3,2},{4,3},{5,4},{6,5},{7,6},{8,7},{9,8},{10,9},{11,1... | collective-permute-start | bytes 98312 | tf_op jit(solution)/shard_map/ppermute | solution.py:118
  89.8 5.2 %collective-permute-start.15 = (f32[16,1,512]{2,0,1:T(8,128)S(1)}, f32[16,1,512]{2,0,1:T(8,128)S(1)}, u32[]{:S(2)}, u32[]{:S(2)}) collective-permute-start(f32[16,1,512]{2,0,1:T(8,128)S(1)} %get-tuple-element.24), channel_id=1, source_target_pairs={{0,16},{16,32},{32,48},{48,64},{64,80},{80,96},{96,112},{112,128},... | collective-permute-start | bytes 98312 | tf_op jit(solution)/shard_map/ppermute | solution.py:114
  101.2 12.2 %collective-permute-start.23 = (f32[48,48]{1,0:T(8,128)S(1)}, f32[48,48]{1,0:T(8,128)S(1)}, u32[]{:S(2)}, u32[]{:S(2)}) collective-permute-start(f32[48,48]{1,0:T(8,128)S(1)} %add_add_fusion.4), channel_id=1, source_target_pairs={{0,64},{16,80},{32,96},{48,112},{64,0},{80,16},{96,32},{112,48},{1... | collective-permute-start | bytes 27656 | tf_op jit(solution)/shard_map/ppermute | solution.py:25
  109.0 7.9 %collective-permute-start.24 = (f32[48,48]{1,0:T(8,128)S(1)}, f32[48,48]{1,0:T(8,128)S(1)}, u32[]{:S(2)}, u32[]{:S(2)}) collective-permute-start(f32[48,48]{1,0:T(8,128)S(1)} %add_add_fusion.4), channel_id=1, source_target_pairs={{0,128},{16,144},{32,160},{48,176},{64,192},{80,208},{96,224},{112... | collective-permute-start | bytes 27656 | tf_op jit(solution)/shard_map/ppermute | solution.py:25
  113.0 6.2 %collective-permute-start.25 = (f32[48,48]{1,0:T(8,128)S(1)}, f32[48,48]{1,0:T(8,128)S(1)}, u32[]{:S(2)}, u32[]{:S(2)}) collective-permute-start(f32[48,48]{1,0:T(8,128)S(1)} %add_add_fusion.4), channel_id=1, source_target_pairs={{0,192},{16,208},{32,224},{48,240},{64,128},{80,144},{96,160},{112... | collective-permute-start | bytes 27656 | tf_op jit(solution)/shard_map/ppermute | solution.py:25
  119.6 5.4 %collective-permute-start.27 = (f32[48,48]{1,0:T(8,128)S(1)}, f32[48,48]{1,0:T(8,128)S(1)}, u32[]{:S(2)}, u32[]{:S(2)}) collective-permute-start(f32[48,48]{1,0:T(8,128)S(1)} %add_add_fusion.3), channel_id=1, source_target_pairs={{0,2},{1,3},{2,0},{3,1},{4,6},{5,7},{6,4},{7,5},{8,10},{9,11},{10,... | collective-permute-start | bytes 27656 | tf_op jit(solution)/shard_map/ppermute | solution.py:25
  128.2 5.3 %collective-permute-start.30 = (f32[48,48]{1,0:T(8,128)S(1)}, f32[48,48]{1,0:T(8,128)S(1)}, u32[]{:S(2)}, u32[]{:S(2)}) collective-permute-start(f32[48,48]{1,0:T(8,128)S(1)} %add_add_fusion.2), channel_id=1, source_target_pairs={{0,8},{1,9},{2,10},{3,11},{4,12},{5,13},{6,14},{7,15},{8,0},{9,1},... | collective-permute-start | bytes 27656 | tf_op jit(solution)/shard_map/ppermute | solution.py:25
  (35 other events, 115.4 us)

commit v3 on v0

--- a/solution.py
+++ b/solution.py
@@ -195,13 +195,13 @@
     start_res = rhs_in - apply_op(start_in, start_edges)
     krylov = [start_res]
     precond_set = []
-    edge_set = []
+    applied_set = []
     for column in range(ITERS):
         turned = precondition(krylov[-1])
         turned_edges = halos(turned)
         precond_set.append(turned)
-        edge_set.append(turned_edges)
-        krylov.append(apply_op(turned, turned_edges) - SHIFT * krylov[-1])
+        applied_set.append(apply_op(turned, turned_edges))
+        krylov.append(applied_set[-1] - SHIFT * krylov[-1])
     stacked = jnp.concatenate(krylov, axis=0)
     span_gram = mesh_sum(block_gram(stacked, stacked))
     width = span_gram.shape[0]
@@ -233,15 +233,11 @@
         for column in range(ITERS)
     )
     solution = start_in
-    solution_edges = start_edges
+    residual = start_res
     for column in range(ITERS):
         weights = combined[column * count_rhs : (column + 1) * count_rhs]
         solution = solution + mix_block(precond_set[column], weights)
-        solution_edges = tuple(
-            have + mix_block(extra, weights)
-            for have, extra in zip(solution_edges, edge_set[column])
-        )
-    residual = rhs_in - apply_op(solution, solution_edges)
+        residual = residual - mix_block(applied_set[column], weights)
     return (outward(solution), outward(residual))
 
 

time: 162 us -> 149 us (0.920)
  local copies, waits for them, and re-layouts: 26.7 us -> 19.9 us
  matrix products: 12.5 us -> 9.25 us
  other arithmetic: 30.3 us -> 28.3 us
    dot_general x10 -> x4, matrix products: 6.43 us -> 3.2 us  [mix_block(): return jnp.einsum('ts,sxl->txl', matrix.T, values, precision=HIGH)]
    slice x6 -> x0, local copies, waits for them, and re-layouts: 2.66 us -> none  [the longest x2 1.34 us: apply_op(): values[:, :, :plane - layers]]
    reshape x4, local copies, waits for them, and re-layouts: 4.51 us -> 2.27 us  [inward(): split = values.reshape(rows_x, rows_y, count_rhs, layers)]
    sub x2 -> x1, other arithmetic: 2.76 us -> 0.78 us  [body(): krylov.append(applied_set[-1] - SHIFT * krylov[-1])]
    slice x28 -> x27, local copies, waits for them, and re-layouts: 6.06 us -> 5.09 us  [up_along(): lax.slice_in_dim(values, width, count, axis=axis)]
  transfers between devices with their start and end apart: 26 -> 26, of which waited for: 11 -> 11; matrix products, arithmetic and copies ran while one was open for 8% -> 7% of each run, Pallas kernels for 0% -> 0%
where the time goes in v3:
time: 149 us; the launch traced here: 147 us
  starting transfers between devices  65.4 us (44%)
  other arithmetic  28.3 us (19%)
  waiting for transfers between devices  23 us (15%)
  local copies, waits for them, and re-layouts  19.9 us (13%)
  matrix products  9.25 us (6%)
    ppermute x12, starting transfers between devices, mesh_sum(): lax.ppermute(block, axis, [(i, i ^ step * m) for i in range(count)])  23.5 us
    ppermute x6, starting transfers between devices, backward(): return lax.ppermute(block, axis, [(i + 1, i) for i in range(count - 1)])  23.5 us
    ppermute x8, starting transfers between devices, forward(): return lax.ppermute(block, axis, [(i, i + 1) for i in range(count - 1)])  18.4 us
    ppermute x12, waiting for transfers between devices, mesh_sum(): lax.ppermute(block, axis, [(i, i ^ step * m) for i in range(count)])  15.9 us
    ppermute x8, waiting for transfers between devices, forward(): return lax.ppermute(block, axis, [(i, i + 1) for i in range(count - 1)])  7.06 us
    another operation x9, other arithmetic, chol_factor(): low_factor = jnp.linalg.cholesky(gram_mat)  6.44 us
    slice x27, local copies, waits for them, and re-layouts, up_along(): lax.slice_in_dim(values, width, count, axis=axis)  5.09 us
    another operation x3, other arithmetic, solve_small(): low_factor = jnp.linalg.cholesky(normal)  3.6 us
  transfers between devices with their start and end apart: 26, of which 11 were waited for; matrix products, arithmetic and copies ran while one was open for 7% of the time, Pallas kernels for 0%

profile of v3, /device:TPU:40, one launch (start us, length us, event | category | flops | bytes accessed | tf_op | source)
XLA Modules:
  0.0 147.3 jit_solution(8195371544257867422)
XLA Ops:
  2.2 3.4 %collective-permute-start.1 = (f32[1,16,64]{2,1,0:T(8,128)}, f32[1,16,64]{2,1,0:T(8,128)S(1)}, u32[]{:S(2)}, u32[]{:S(2)}) collective-permute-start(f32[1,16,64]{2,1,0:T(8,128)} %slice.420), channel_id=1, source_target_pairs={{0,1},{1,2},{2,3},{3,4},{4,5},{5,6},{6,7},{7,8},{8,9},{9,10},{10,1... | collective-permute-start | bytes 12296 | tf_op jit(solution)/shard_map/ppermute | solution.py:114
  11.7 4.5 %collective-permute-start.4 = (f32[16,16,64]{2,0,1:T(8,128)}, f32[16,16,64]{2,0,1:T(8,128)S(1)}, u32[]{:S(2)}, u32[]{:S(2)}) collective-permute-start(f32[16,16,64]{2,0,1:T(8,128)} %get-tuple-element.39), channel_id=1, source_target_pairs={{1,0},{2,1},{3,2},{4,3},{5,4},{6,5},{7,6},{8,7},{9,8},{10,9},{11,1... | collective-permute-start | bytes 196616 | tf_op jit(solution)/shard_map/ppermute | solution.py:118
  16.3 1.9 %collective-permute-start.5 = (f32[16,16,64]{2,0,1:T(8,128)}, f32[16,16,64]{2,0,1:T(8,128)}, u32[]{:S(2)}, u32[]{:S(2)}) collective-permute-start(f32[16,16,64]{2,0,1:T(8,128)} %get-tuple-element.40), channel_id=1, source_target_pairs={{0,1},{1,2},{2,3},{3,4},{4,5},{5,6},{6,7},{7,8},{8,9},{9,10},{10,1... | collective-permute-start | bytes 196616 | tf_op jit(solution)/shard_map/ppermute | solution.py:114
  18.8 3.3 %collective-permute-start.2 = (f32[16,1,512]{2,0,1:T(8,128)}, f32[16,1,512]{2,0,1:T(8,128)S(1)}, u32[]{:S(2)}, u32[]{:S(2)}) collective-permute-start(f32[16,1,512]{2,0,1:T(8,128)} %get-tuple-element.35), channel_id=1, source_target_pairs={{16,0},{32,16},{48,32},{64,48},{80,64},{96,80},{112,96},{128,112},... | collective-permute-start | bytes 98312 | tf_op jit(solution)/shard_map/ppermute | solution.py:118
  27.5 2.3 %collective-permute-start.3 = (f32[16,1,512]{2,0,1:T(8,128)S(1)}, f32[16,1,512]{2,0,1:T(8,128)S(1)}, u32[]{:S(2)}, u32[]{:S(2)}) collective-permute-start(f32[16,1,512]{2,0,1:T(8,128)S(1)} %copy-done.11), channel_id=1, source_target_pairs={{0,16},{16,32},{32,48},{48,64},{64,80},{80,96},{96,112},{112,128},... | collective-permute-start | bytes 98312 | tf_op jit(solution)/shard_map/ppermute | solution.py:114
  32.9 2.1 %broadcast_multiply_fusion.1 = (f32[16,16,512]{2,0,1:T(8,128)S(1)}, f32[16,16,512]{2,0,1:T(8,128)S(1)}) fusion(f32[16,512]{1,0:T(8,128)S(1)} %divide_bitcast_fusion, f32[16,16,512]{2,0,1:T(8,128)S(1)} %reshape.197, f32[512]{0:T(512)S(1)} %get-tuple-element.51, f32[16,16,511]{2,0,1:T(8,128)} %get-tuple-element.42, f32[16,512]{1,0:T(8,128)S(1)} %get-tuple-element.45, ...), kind=kLoop, calls=%fused_computation.65 | loop fusion | flops 2752512 | bytes 5507072 | tf_op jit(solution)/shard_map/mul | solution.py:177
  40.5 5.8 %collective-permute-start.8 = (f32[16,16,64]{2,0,1:T(8,128)S(1)}, f32[16,16,64]{2,0,1:T(8,128)S(1)}, u32[]{:S(2)}, u32[]{:S(2)}) collective-permute-start(f32[16,16,64]{2,0,1:T(8,128)S(1)} %get-tuple-element.29), channel_id=1, source_target_pairs={{1,0},{2,1},{3,2},{4,3},{5,4},{6,5},{7,6},{8,7},{9,8},{10,9},{11,1... | collective-permute-start | bytes 196616 | tf_op jit(solution)/shard_map/ppermute | solution.py:118
  50.1 2.6 %collective-permute-start.7 = (f32[16,1,512]{2,0,1:T(8,128)S(1)}, f32[16,1,512]{2,0,1:T(8,128)S(1)}, u32[]{:S(2)}, u32[]{:S(2)}) collective-permute-start(f32[16,1,512]{2,0,1:T(8,128)S(1)} %get-tuple-element.26), channel_id=1, source_target_pairs={{0,16},{16,32},{32,48},{48,64},{64,80},{80,96},{96,112},{112,128},... | collective-permute-start | bytes 98312 | tf_op jit(solution)/shard_map/ppermute | solution.py:114
  52.9 2.5 %collective-permute-done.7 = f32[16,1,512]{2,0,1:T(8,128)S(1)} collective-permute-done((f32[16,1,512]{2,0,1:T(8,128)S(1)}, f32[16,1,512]{2,0,1:T(8,128)S(1)}, u32[]{:S(2)}, u32[]{:S(2)}) %collective-permute-start.7) | collective-permute-done | bytes 32800 | tf_op jit(solution)/shard_map/ppermute | solution.py:114
  61.5 6.0 %collective-permute-start.12 = (f32[16,16,64]{2,0,1:T(8,128)S(1)}, f32[16,16,64]{2,0,1:T(8,128)S(1)}, u32[]{:S(2)}, u32[]{:S(2)}) collective-permute-start(f32[16,16,64]{2,0,1:T(8,128)S(1)} %get-tuple-element.19), channel_id=1, source_target_pairs={{1,0},{2,1},{3,2},{4,3},{5,4},{6,5},{7,6},{8,7},{9,8},{10,9},{11,1... | collective-permute-start | bytes 196616 | tf_op jit(solution)/shard_map/ppermute | solution.py:118
  71.4 2.4 %collective-permute-start.11 = (f32[16,1,512]{2,0,1:T(8,128)S(1)}, f32[16,1,512]{2,0,1:T(8,128)S(1)}, u32[]{:S(2)}, u32[]{:S(2)}) collective-permute-start(f32[16,1,512]{2,0,1:T(8,128)S(1)} %get-tuple-element.16), channel_id=1, source_target_pairs={{0,16},{16,32},{32,48},{48,64},{64,80},{80,96},{96,112},{112,128},... | collective-permute-start | bytes 98312 | tf_op jit(solution)/shard_map/ppermute | solution.py:114
  74.0 2.7 %collective-permute-done.11 = f32[16,1,512]{2,0,1:T(8,128)S(1)} collective-permute-done((f32[16,1,512]{2,0,1:T(8,128)S(1)}, f32[16,1,512]{2,0,1:T(8,128)S(1)}, u32[]{:S(2)}, u32[]{:S(2)}) %collective-permute-start.11) | collective-permute-done | bytes 32800 | tf_op jit(solution)/shard_map/ppermute | solution.py:114
  80.8 2.0 %collective-permute-done.15 = f32[48,48]{1,0:T(8,128)S(1)} collective-permute-done((f32[48,48]{1,0:T(8,128)S(1)}, f32[48,48]{1,0:T(8,128)S(1)}, u32[]{:S(2)}, u32[]{:S(2)}) %collective-permute-start.15) | collective-permute-done | bytes 9248 | tf_op jit(solution)/shard_map/ppermute | solution.py:25
  82.8 7.8 %collective-permute-start.17 = (f32[48,48]{1,0:T(8,128)S(1)}, f32[48,48]{1,0:T(8,128)S(1)}, u32[]{:S(2)}, u32[]{:S(2)}) collective-permute-start(f32[48,48]{1,0:T(8,128)S(1)} %add_add_fusion.4), channel_id=1, source_target_pairs={{0,64},{16,80},{32,96},{48,112},{64,0},{80,16},{96,32},{112,48},{1... | collective-permute-start | bytes 27656 | tf_op jit(solution)/shard_map/ppermute | solution.py:25
  90.7 3.9 %collective-permute-start.18 = (f32[48,48]{1,0:T(8,128)S(1)}, f32[48,48]{1,0:T(8,128)S(1)}, u32[]{:S(2)}, u32[]{:S(2)}) collective-permute-start(f32[48,48]{1,0:T(8,128)S(1)} %add_add_fusion.4), channel_id=1, source_target_pairs={{0,128},{16,144},{32,160},{48,176},{64,192},{80,208},{96,224},{112... | collective-permute-start | bytes 27656 | tf_op jit(solution)/shard_map/ppermute | solution.py:25
  95.1 3.5 %collective-permute-done.18 = f32[48,48]{1,0:T(8,128)S(1)} collective-permute-done((f32[48,48]{1,0:T(8,128)S(1)}, f32[48,48]{1,0:T(8,128)S(1)}, u32[]{:S(2)}, u32[]{:S(2)}) %collective-permute-start.18) | collective-permute-done | bytes 9248 | tf_op jit(solution)/shard_map/ppermute | solution.py:25
  98.6 2.2 %collective-permute-done.19 = f32[48,48]{1,0:T(8,128)S(1)} collective-permute-done((f32[48,48]{1,0:T(8,128)S(1)}, f32[48,48]{1,0:T(8,128)S(1)}, u32[]{:S(2)}, u32[]{:S(2)}) %collective-permute-start.19) | collective-permute-done | bytes 9248 | tf_op jit(solution)/shard_map/ppermute | solution.py:25
  100.9 5.7 %collective-permute-start.21 = (f32[48,48]{1,0:T(8,128)S(1)}, f32[48,48]{1,0:T(8,128)S(1)}, u32[]{:S(2)}, u32[]{:S(2)}) collective-permute-start(f32[48,48]{1,0:T(8,128)S(1)} %add_add_fusion.3), channel_id=1, source_target_pairs={{0,2},{1,3},{2,0},{3,1},{4,6},{5,7},{6,4},{7,5},{8,10},{9,11},{10,... | collective-permute-start | bytes 27656 | tf_op jit(solution)/shard_map/ppermute | solution.py:25
  106.6 2.1 %collective-permute-done.21 = f32[48,48]{1,0:T(8,128)S(1)} collective-permute-done((f32[48,48]{1,0:T(8,128)S(1)}, f32[48,48]{1,0:T(8,128)S(1)}, u32[]{:S(2)}, u32[]{:S(2)}) %collective-permute-start.21) | collective-permute-done | bytes 9248 | tf_op jit(solution)/shard_map/ppermute | solution.py:25
  108.7 3.0 %collective-permute-done.22 = f32[48,48]{1,0:T(8,128)S(1)} collective-permute-done((f32[48,48]{1,0:T(8,128)S(1)}, f32[48,48]{1,0:T(8,128)S(1)}, u32[]{:S(2)}, u32[]{:S(2)}) %collective-permute-start.22) | collective-permute-done | bytes 9248 | tf_op jit(solution)/shard_map/ppermute | solution.py:25
  112.2 2.3 %collective-permute-start.24 = (f32[48,48]{1,0:T(8,128)S(1)}, f32[48,48]{1,0:T(8,128)S(1)}, u32[]{:S(2)}, u32[]{:S(2)}) collective-permute-start(f32[48,48]{1,0:T(8,128)S(1)} %add_add_fusion.2), channel_id=1, source_target_pairs={{0,8},{1,9},{2,10},{3,11},{4,12},{5,13},{6,14},{7,15},{8,0},{9,1},... | collective-permute-start | bytes 27656 | tf_op jit(solution)/shard_map/ppermute | solution.py:25
  115.6 2.0 %collective-permute-done.24 = f32[48,48]{1,0:T(8,128)S(1)} collective-permute-done((f32[48,48]{1,0:T(8,128)S(1)}, f32[48,48]{1,0:T(8,128)S(1)}, u32[]{:S(2)}, u32[]{:S(2)}) %collective-permute-start.24) | collective-permute-done | bytes 9248 | tf_op jit(solution)/shard_map/ppermute | solution.py:25
  133.6 2.9 %cholesky.41 = f32[32,32]{1,0:T(8,128)S(1)} custom-call(f32[32,32]{1,0:T(8,128)S(1)} %fusion.42), custom_call_target="Cholesky" | custom-call | tf_op jit(solution)/shard_map/jit(cholesky)/cholesky | solution.py:67
  137.8 2.4 %custom-call.13 = f32[1,32,32]{1,2,0:T(8,128)S(1)} custom-call(f32[1,32,32]{2,1,0:T(8,128)S(1)} %fusion.35), custom_call_target="InvertDiagBlocksLowerTriangular" | custom-call | tf_op jit(solution)/shard_map/triangular_solve | solution.py:69
  (208 shorter events, 66.3 us)
Async XLA Ops:
  2.2 27.6 %collective-permute-start.1 = (f32[1,16,64]{2,1,0:T(8,128)}, f32[1,16,64]{2,1,0:T(8,128)S(1)}, u32[]{:S(2)}, u32[]{:S(2)}) collective-permute-start(f32[1,16,64]{2,1,0:T(8,128)} %slice.420), channel_id=1, source_target_pairs={{0,1},{1,2},{2,3},{3,4},{4,5},{5,6},{6,7},{7,8},{8,9},{9,10},{10,1... | collective-permute-start | bytes 12296 | tf_op jit(solution)/shard_map/ppermute | solution.py:114
  7.1 20.3 %collective-permute-start = (f32[1,1,512]{2,1,0:T(1,128)}, f32[1,1,512]{2,1,0:T(1,128)}, u32[]{:S(2)}, u32[]{:S(2)}) collective-permute-start(f32[1,1,512]{2,1,0:T(1,128)} %slice.418), channel_id=1, source_target_pairs={{0,16},{16,32},{32,48},{48,64},{64,80},{80,96},{96,112},{112,128},... | collective-permute-start | bytes 6152 | tf_op jit(solution)/shard_map/ppermute | solution.py:114
  11.7 21.1 %collective-permute-start.4 = (f32[16,16,64]{2,0,1:T(8,128)}, f32[16,16,64]{2,0,1:T(8,128)S(1)}, u32[]{:S(2)}, u32[]{:S(2)}) collective-permute-start(f32[16,16,64]{2,0,1:T(8,128)} %get-tuple-element.39), channel_id=1, source_target_pairs={{1,0},{2,1},{3,2},{4,3},{5,4},{6,5},{7,6},{8,7},{9,8},{10,9},{11,1... | collective-permute-start | bytes 196616 | tf_op jit(solution)/shard_map/ppermute | solution.py:118
  16.3 16.6 %collective-permute-start.5 = (f32[16,16,64]{2,0,1:T(8,128)}, f32[16,16,64]{2,0,1:T(8,128)}, u32[]{:S(2)}, u32[]{:S(2)}) collective-permute-start(f32[16,16,64]{2,0,1:T(8,128)} %get-tuple-element.40), channel_id=1, source_target_pairs={{0,1},{1,2},{2,3},{3,4},{4,5},{5,6},{6,7},{7,8},{8,9},{9,10},{10,1... | collective-permute-start | bytes 196616 | tf_op jit(solution)/shard_map/ppermute | solution.py:114
  18.8 12.1 %collective-permute-start.2 = (f32[16,1,512]{2,0,1:T(8,128)}, f32[16,1,512]{2,0,1:T(8,128)S(1)}, u32[]{:S(2)}, u32[]{:S(2)}) collective-permute-start(f32[16,1,512]{2,0,1:T(8,128)} %get-tuple-element.35), channel_id=1, source_target_pairs={{16,0},{32,16},{48,32},{64,48},{80,64},{96,80},{112,96},{128,112},... | collective-permute-start | bytes 98312 | tf_op jit(solution)/shard_map/ppermute | solution.py:118
  27.5 5.4 %collective-permute-start.3 = (f32[16,1,512]{2,0,1:T(8,128)S(1)}, f32[16,1,512]{2,0,1:T(8,128)S(1)}, u32[]{:S(2)}, u32[]{:S(2)}) collective-permute-start(f32[16,1,512]{2,0,1:T(8,128)S(1)} %copy-done.11), channel_id=1, source_target_pairs={{0,16},{16,32},{32,48},{48,64},{64,80},{80,96},{96,112},{112,128},... | collective-permute-start | bytes 98312 | tf_op jit(solution)/shard_map/ppermute | solution.py:114
  40.5 14.9 %collective-permute-start.8 = (f32[16,16,64]{2,0,1:T(8,128)S(1)}, f32[16,16,64]{2,0,1:T(8,128)S(1)}, u32[]{:S(2)}, u32[]{:S(2)}) collective-permute-start(f32[16,16,64]{2,0,1:T(8,128)S(1)} %get-tuple-element.29), channel_id=1, source_target_pairs={{1,0},{2,1},{3,2},{4,3},{5,4},{6,5},{7,6},{8,7},{9,8},{10,9},{11,1... | collective-permute-start | bytes 196616 | tf_op jit(solution)/shard_map/ppermute | solution.py:118
  46.3 9.1 %collective-permute-start.9 = (f32[16,16,64]{2,0,1:T(8,128)S(1)}, f32[16,16,64]{2,0,1:T(8,128)S(1)}, u32[]{:S(2)}, u32[]{:S(2)}) collective-permute-start(f32[16,16,64]{2,0,1:T(8,128)S(1)} %get-tuple-element.30), channel_id=1, source_target_pairs={{0,1},{1,2},{2,3},{3,4},{4,5},{5,6},{6,7},{7,8},{8,9},{9,10},{10,1... | collective-permute-start | bytes 196616 | tf_op jit(solution)/shard_map/ppermute | solution.py:114
  48.2 4.7 %collective-permute-start.6 = (f32[16,1,512]{2,0,1:T(8,128)S(1)}, f32[16,1,512]{2,0,1:T(8,128)S(1)}, u32[]{:S(2)}, u32[]{:S(2)}) collective-permute-start(f32[16,1,512]{2,0,1:T(8,128)S(1)} %get-tuple-element.25), channel_id=1, source_target_pairs={{16,0},{32,16},{48,32},{64,48},{80,64},{96,80},{112,96},{128,112},... | collective-permute-start | bytes 98312 | tf_op jit(solution)/shard_map/ppermute | solution.py:118
  50.1 5.2 %collective-permute-start.7 = (f32[16,1,512]{2,0,1:T(8,128)S(1)}, f32[16,1,512]{2,0,1:T(8,128)S(1)}, u32[]{:S(2)}, u32[]{:S(2)}) collective-permute-start(f32[16,1,512]{2,0,1:T(8,128)S(1)} %get-tuple-element.26), channel_id=1, source_target_pairs={{0,16},{16,32},{32,48},{48,64},{64,80},{80,96},{96,112},{112,128},... | collective-permute-start | bytes 98312 | tf_op jit(solution)/shard_map/ppermute | solution.py:114
  61.5 15.1 %collective-permute-start.12 = (f32[16,16,64]{2,0,1:T(8,128)S(1)}, f32[16,16,64]{2,0,1:T(8,128)S(1)}, u32[]{:S(2)}, u32[]{:S(2)}) collective-permute-start(f32[16,16,64]{2,0,1:T(8,128)S(1)} %get-tuple-element.19), channel_id=1, source_target_pairs={{1,0},{2,1},{3,2},{4,3},{5,4},{6,5},{7,6},{8,7},{9,8},{10,9},{11,1... | collective-permute-start | bytes 196616 | tf_op jit(solution)/shard_map/ppermute | solution.py:118
  67.6 9.1 %collective-permute-start.13 = (f32[16,16,64]{2,0,1:T(8,128)S(1)}, f32[16,16,64]{2,0,1:T(8,128)S(1)}, u32[]{:S(2)}, u32[]{:S(2)}) collective-permute-start(f32[16,16,64]{2,0,1:T(8,128)S(1)} %get-tuple-element.20), channel_id=1, source_target_pairs={{0,1},{1,2},{2,3},{3,4},{4,5},{5,6},{6,7},{7,8},{8,9},{9,10},{10,1... | collective-permute-start | bytes 196616 | tf_op jit(solution)/shard_map/ppermute | solution.py:114
  69.5 4.5 %collective-permute-start.10 = (f32[16,1,512]{2,0,1:T(8,128)S(1)}, f32[16,1,512]{2,0,1:T(8,128)S(1)}, u32[]{:S(2)}, u32[]{:S(2)}) collective-permute-start(f32[16,1,512]{2,0,1:T(8,128)S(1)} %get-tuple-element.15), channel_id=1, source_target_pairs={{16,0},{32,16},{48,32},{64,48},{80,64},{96,80},{112,96},{128,112},... | collective-permute-start | bytes 98312 | tf_op jit(solution)/shard_map/ppermute | solution.py:118
  71.4 5.2 %collective-permute-start.11 = (f32[16,1,512]{2,0,1:T(8,128)S(1)}, f32[16,1,512]{2,0,1:T(8,128)S(1)}, u32[]{:S(2)}, u32[]{:S(2)}) collective-permute-start(f32[16,1,512]{2,0,1:T(8,128)S(1)} %get-tuple-element.16), channel_id=1, source_target_pairs={{0,16},{16,32},{32,48},{48,64},{64,80},{80,96},{96,112},{112,128},... | collective-permute-start | bytes 98312 | tf_op jit(solution)/shard_map/ppermute | solution.py:114
  78.9 3.9 %collective-permute-start.15 = (f32[48,48]{1,0:T(8,128)S(1)}, f32[48,48]{1,0:T(8,128)S(1)}, u32[]{:S(2)}, u32[]{:S(2)}) collective-permute-start(f32[48,48]{1,0:T(8,128)S(1)} %fusion.6), channel_id=1, source_target_pairs={{0,32},{16,48},{32,0},{48,16},{64,96},{80,112},{96,64},{112,80},{1... | collective-permute-start | bytes 27656 | tf_op jit(solution)/shard_map/ppermute | solution.py:25
  82.8 12.2 %collective-permute-start.17 = (f32[48,48]{1,0:T(8,128)S(1)}, f32[48,48]{1,0:T(8,128)S(1)}, u32[]{:S(2)}, u32[]{:S(2)}) collective-permute-start(f32[48,48]{1,0:T(8,128)S(1)} %add_add_fusion.4), channel_id=1, source_target_pairs={{0,64},{16,80},{32,96},{48,112},{64,0},{80,16},{96,32},{112,48},{1... | collective-permute-start | bytes 27656 | tf_op jit(solution)/shard_map/ppermute | solution.py:25
  90.7 7.9 %collective-permute-start.18 = (f32[48,48]{1,0:T(8,128)S(1)}, f32[48,48]{1,0:T(8,128)S(1)}, u32[]{:S(2)}, u32[]{:S(2)}) collective-permute-start(f32[48,48]{1,0:T(8,128)S(1)} %add_add_fusion.4), channel_id=1, source_target_pairs={{0,128},{16,144},{32,160},{48,176},{64,192},{80,208},{96,224},{112... | collective-permute-start | bytes 27656 | tf_op jit(solution)/shard_map/ppermute | solution.py:25
  94.6 6.2 %collective-permute-start.19 = (f32[48,48]{1,0:T(8,128)S(1)}, f32[48,48]{1,0:T(8,128)S(1)}, u32[]{:S(2)}, u32[]{:S(2)}) collective-permute-start(f32[48,48]{1,0:T(8,128)S(1)} %add_add_fusion.4), channel_id=1, source_target_pairs={{0,192},{16,208},{32,224},{48,240},{64,128},{80,144},{96,160},{112... | collective-permute-start | bytes 27656 | tf_op jit(solution)/shard_map/ppermute | solution.py:25
  100.8 5.8 %collective-permute-start.20 = (f32[48,48]{1,0:T(8,128)S(1)}, f32[48,48]{1,0:T(8,128)S(1)}, u32[]{:S(2)}, u32[]{:S(2)}) collective-permute-start(f32[48,48]{1,0:T(8,128)S(1)} %add_add_fusion.3), channel_id=1, source_target_pairs={{0,1},{1,0},{2,3},{3,2},{4,5},{5,4},{6,7},{7,6},{8,9},{9,8},{10,11... | collective-permute-start | bytes 27656 | tf_op jit(solution)/shard_map/ppermute | solution.py:25
  100.9 7.8 %collective-permute-start.21 = (f32[48,48]{1,0:T(8,128)S(1)}, f32[48,48]{1,0:T(8,128)S(1)}, u32[]{:S(2)}, u32[]{:S(2)}) collective-permute-start(f32[48,48]{1,0:T(8,128)S(1)} %add_add_fusion.3), channel_id=1, source_target_pairs={{0,2},{1,3},{2,0},{3,1},{4,6},{5,7},{6,4},{7,5},{8,10},{9,11},{10,... | collective-permute-start | bytes 27656 | tf_op jit(solution)/shard_map/ppermute | solution.py:25
  106.6 5.0 %collective-permute-start.22 = (f32[48,48]{1,0:T(8,128)S(1)}, f32[48,48]{1,0:T(8,128)S(1)}, u32[]{:S(2)}, u32[]{:S(2)}) collective-permute-start(f32[48,48]{1,0:T(8,128)S(1)} %add_add_fusion.3), channel_id=1, source_target_pairs={{0,3},{1,2},{2,1},{3,0},{4,7},{5,6},{6,5},{7,4},{8,11},{9,10},{10,... | collective-permute-start | bytes 27656 | tf_op jit(solution)/shard_map/ppermute | solution.py:25
  111.6 3.9 %collective-permute-start.23 = (f32[48,48]{1,0:T(8,128)S(1)}, f32[48,48]{1,0:T(8,128)S(1)}, u32[]{:S(2)}, u32[]{:S(2)}) collective-permute-start(f32[48,48]{1,0:T(8,128)S(1)} %add_add_fusion.2), channel_id=1, source_target_pairs={{0,4},{1,5},{2,6},{3,7},{4,0},{5,1},{6,2},{7,3},{8,12},{9,13},{10,... | collective-permute-start | bytes 27656 | tf_op jit(solution)/shard_map/ppermute | solution.py:25
  112.2 5.3 %collective-permute-start.24 = (f32[48,48]{1,0:T(8,128)S(1)}, f32[48,48]{1,0:T(8,128)S(1)}, u32[]{:S(2)}, u32[]{:S(2)}) collective-permute-start(f32[48,48]{1,0:T(8,128)S(1)} %add_add_fusion.2), channel_id=1, source_target_pairs={{0,8},{1,9},{2,10},{3,11},{4,12},{5,13},{6,14},{7,15},{8,0},{9,1},... | collective-permute-start | bytes 27656 | tf_op jit(solution)/shard_map/ppermute | solution.py:25
  114.5 3.8 %collective-permute-start.25 = (f32[48,48]{1,0:T(8,128)S(1)}, f32[48,48]{1,0:T(8,128)S(1)}, u32[]{:S(2)}, u32[]{:S(2)}) collective-permute-start(f32[48,48]{1,0:T(8,128)S(1)} %add_add_fusion.2), channel_id=1, source_target_pairs={{0,12},{1,13},{2,14},{3,15},{4,8},{5,9},{6,10},{7,11},{8,4},{9,5},... | collective-permute-start | bytes 27656 | tf_op jit(solution)/shard_map/ppermute | solution.py:25
  (14 other events, 32.9 us)

commit v4 on v3

--- a/solution.py
+++ b/solution.py
@@ -50,13 +50,6 @@
 
 def mix_block(values, matrix):
     return jnp.einsum("ts,sxl->txl", matrix.T, values, precision=HIGH)
-
-
-def chol_factor(gram_mat):
-    low_factor = jnp.linalg.cholesky(gram_mat)
-    eye_mat = jnp.eye(gram_mat.shape[0], dtype=gram_mat.dtype)
-    inverse = lax.linalg.triangular_solve(low_factor, eye_mat, left_side=True, lower=True)
-    return (low_factor.T, inverse.T)
 
 
 def solve_small(columns, first_factor):
@@ -206,32 +199,17 @@
     span_gram = mesh_sum(block_gram(stacked, stacked))
     width = span_gram.shape[0]
 
-    def inner(left, right):
-        return jnp.dot(left.T, jnp.dot(span_gram, right, precision=HIGH), precision=HIGH)
-
-    def advance(weights):
-        moved = jnp.concatenate([jnp.zeros_like(weights[:count_rhs]), weights[:-count_rhs]], axis=0)
-        return moved + SHIFT * weights
-
-    first_factor, first_inv = chol_factor(inner(*(2 * [jnp.eye(width, count_rhs, dtype=jnp.float32)])))
-    basis_set = [jnp.dot(jnp.eye(width, count_rhs, dtype=jnp.float32), first_inv, precision=HIGH)]
-    columns = []
-    for column in range(ITERS):
-        image = advance(basis_set[column])
-        projections = [inner(member, image) for member in basis_set]
-        perp = image - sum(
-            jnp.dot(member, proj, precision=HIGH) for member, proj in zip(basis_set, projections)
-        )
-        next_factor, next_inv = chol_factor(inner(perp, perp))
-        if column + 1 < ITERS:
-            basis_set.append(jnp.dot(perp, next_inv, precision=HIGH))
-        blank = jnp.zeros(((ITERS - 1 - column) * count_rhs, count_rhs), dtype=next_factor.dtype)
-        columns.append(jnp.concatenate(projections + [next_factor, blank], axis=0))
-    coeffs = solve_small(columns, first_factor)
-    combined = sum(
-        jnp.dot(basis_set[column], coeffs[column * count_rhs : (column + 1) * count_rhs], precision=HIGH)
-        for column in range(ITERS)
-    )
+    full_low = jnp.linalg.cholesky(span_gram)
+    upper = full_low.T
+    head = ITERS * count_rhs
+    head_inv = lax.linalg.triangular_solve(
+        full_low[:head, :head], jnp.eye(head, dtype=jnp.float32), left_side=True, lower=True
+    ).T
+    advance = jnp.eye(width, head, k=-count_rhs, dtype=jnp.float32) + SHIFT * jnp.eye(width, head, dtype=jnp.float32)
+    hessen = jnp.dot(jnp.dot(upper, advance, precision=HIGH), head_inv, precision=HIGH)
+    first_factor = upper[:count_rhs, :count_rhs]
+    coeffs = solve_small([hessen], first_factor)
+    combined = jnp.dot(head_inv, coeffs, precision=HIGH)
     solution = start_in
     residual = start_res
     for column in range(ITERS):

time: 149 us -> 142 us (0.953)
  matrix products: 9.25 us -> 6.08 us
  other arithmetic: 28.3 us -> 25.5 us
  local copies, waits for them, and re-layouts: 19.9 us -> 17.3 us
    dot_general x18 -> x3, matrix products: 2.91 us -> 0.63 us  [the longest x1 0.26 us: body(): jnp.dot(upper, advance, precision=HIGH)]
    another operation x12 -> x5, other arithmetic: 9.54 us -> 7.49 us  [the longest x3 5.05 us: body(): full_low = jnp.linalg.cholesky(span_gram)]
  transfers between devices with their start and end apart: 26 -> 26, of which waited for: 11 -> 11; matrix products, arithmetic and copies ran while one was open for 7% -> 6% of each run, Pallas kernels for 0% -> 0%
where the time goes in v4:
time: 142 us; the launch traced here: 139 us
  starting transfers between devices  65.5 us (46%)
  other arithmetic  25.5 us (18%)
  waiting for transfers between devices  23.7 us (17%)
  local copies, waits for them, and re-layouts  17.3 us (12%)
  matrix products  6.08 us (4%)
  between operations  1.44 us (1%)
    ppermute x6, starting transfers between devices, backward(): return lax.ppermute(block, axis, [(i + 1, i) for i in range(count - 1)])  23.5 us
    ppermute x12, starting transfers between devices, mesh_sum(): lax.ppermute(block, axis, [(i, i ^ step * m) for i in range(count)])  23.5 us
    ppermute x8, starting transfers between devices, forward(): return lax.ppermute(block, axis, [(i, i + 1) for i in range(count - 1)])  18.4 us
    ppermute x12, waiting for transfers between devices, mesh_sum(): lax.ppermute(block, axis, [(i, i ^ step * m) for i in range(count)])  15.9 us
    ppermute x8, waiting for transfers between devices, forward(): return lax.ppermute(block, axis, [(i, i + 1) for i in range(count - 1)])  7.76 us
    slice x27, local copies, waits for them, and re-layouts, up_along(): lax.slice_in_dim(values, width, count, axis=axis)  5.07 us
    another operation x3, other arithmetic, body(): full_low = jnp.linalg.cholesky(span_gram)  5.05 us
    another operation x3, other arithmetic, solve_small(): low_factor = jnp.linalg.cholesky(normal)  3.6 us
  transfers between devices with their start and end apart: 26, of which 11 were waited for; matrix products, arithmetic and copies ran while one was open for 6% of the time, Pallas kernels for 0%

profile of v4, /device:TPU:40, one launch (start us, length us, event | category | flops | bytes accessed | tf_op | source)
XLA Modules:
  0.0 139.4 jit_solution(7118741589230291426)
XLA Ops:
  1.6 3.4 %collective-permute-start.1 = (f32[1,16,64]{2,1,0:T(8,128)S(1)}, f32[1,16,64]{2,1,0:T(8,128)S(1)}, u32[]{:S(2)}, u32[]{:S(2)}) collective-permute-start(f32[1,16,64]{2,1,0:T(8,128)S(1)} %slice.416), channel_id=1, source_target_pairs={{0,1},{1,2},{2,3},{3,4},{4,5},{5,6},{6,7},{7,8},{8,9},{9,10},{10,1... | collective-permute-start | bytes 12296 | tf_op jit(solution)/shard_map/ppermute | solution.py:107
  9.9 4.6 %collective-permute-start.4 = (f32[16,16,64]{2,0,1:T(8,128)S(1)}, f32[16,16,64]{2,0,1:T(8,128)S(1)}, u32[]{:S(2)}, u32[]{:S(2)}) collective-permute-start(f32[16,16,64]{2,0,1:T(8,128)S(1)} %get-tuple-element.37), channel_id=1, source_target_pairs={{1,0},{2,1},{3,2},{4,3},{5,4},{6,5},{7,6},{8,7},{9,8},{10,9},{11,1... | collective-permute-start | bytes 196616 | tf_op jit(solution)/shard_map/ppermute | solution.py:111
  16.4 3.4 %collective-permute-start.2 = (f32[16,1,512]{2,0,1:T(8,128)S(1)}, f32[16,1,512]{2,0,1:T(8,128)S(1)}, u32[]{:S(2)}, u32[]{:S(2)}) collective-permute-start(f32[16,1,512]{2,0,1:T(8,128)S(1)} %get-tuple-element.33), channel_id=1, source_target_pairs={{16,0},{32,16},{48,32},{64,48},{80,64},{96,80},{112,96},{128,112},... | collective-permute-start | bytes 98312 | tf_op jit(solution)/shard_map/ppermute | solution.py:111
  25.0 2.3 %collective-permute-start.3 = (f32[16,1,512]{2,0,1:T(8,128)S(1)}, f32[16,1,512]{2,0,1:T(8,128)S(1)}, u32[]{:S(2)}, u32[]{:S(2)}) collective-permute-start(f32[16,1,512]{2,0,1:T(8,128)S(1)} %get-tuple-element.34), channel_id=1, source_target_pairs={{0,16},{16,32},{32,48},{48,64},{64,80},{80,96},{96,112},{112,128},... | collective-permute-start | bytes 98312 | tf_op jit(solution)/shard_map/ppermute | solution.py:107
  27.8 2.5 %collective-permute-done.3 = f32[16,1,512]{2,0,1:T(8,128)S(1)} collective-permute-done((f32[16,1,512]{2,0,1:T(8,128)S(1)}, f32[16,1,512]{2,0,1:T(8,128)S(1)}, u32[]{:S(2)}, u32[]{:S(2)}) %collective-permute-start.3) | collective-permute-done | bytes 32800 | tf_op jit(solution)/shard_map/ppermute | solution.py:107
  30.4 2.1 %broadcast_multiply_fusion.1 = (f32[16,16,512]{2,0,1:T(8,128)S(1)}, f32[16,16,512]{2,0,1:T(8,128)S(1)}) fusion(f32[16,512]{1,0:T(8,128)S(1)} %divide_bitcast_fusion, f32[16,16,512]{2,0,1:T(8,128)S(1)} %reshape.194, f32[512]{0:T(512)S(1)} %get-tuple-element.47, f32[16,16,511]{2,0,1:T(8,128)} %get-tuple-element.40, f32[16,512]{1,0:T(8,128)S(1)} %get-tuple-element.43, ...), kind=kLoop, calls=%fused_computation.61 | loop fusion | flops 2752512 | bytes 5507072 | tf_op jit(solution)/shard_map/mul | solution.py:170
  38.0 5.8 %collective-permute-start.8 = (f32[16,16,64]{2,0,1:T(8,128)S(1)}, f32[16,16,64]{2,0,1:T(8,128)S(1)}, u32[]{:S(2)}, u32[]{:S(2)}) collective-permute-start(f32[16,16,64]{2,0,1:T(8,128)S(1)} %get-tuple-element.27), channel_id=1, source_target_pairs={{1,0},{2,1},{3,2},{4,3},{5,4},{6,5},{7,6},{8,7},{9,8},{10,9},{11,1... | collective-permute-start | bytes 196616 | tf_op jit(solution)/shard_map/ppermute | solution.py:111
  47.6 2.6 %collective-permute-start.7 = (f32[16,1,512]{2,0,1:T(8,128)S(1)}, f32[16,1,512]{2,0,1:T(8,128)S(1)}, u32[]{:S(2)}, u32[]{:S(2)}) collective-permute-start(f32[16,1,512]{2,0,1:T(8,128)S(1)} %get-tuple-element.24), channel_id=1, source_target_pairs={{0,16},{16,32},{32,48},{48,64},{64,80},{80,96},{96,112},{112,128},... | collective-permute-start | bytes 98312 | tf_op jit(solution)/shard_map/ppermute | solution.py:107
  50.3 2.5 %collective-permute-done.7 = f32[16,1,512]{2,0,1:T(8,128)S(1)} collective-permute-done((f32[16,1,512]{2,0,1:T(8,128)S(1)}, f32[16,1,512]{2,0,1:T(8,128)S(1)}, u32[]{:S(2)}, u32[]{:S(2)}) %collective-permute-start.7) | collective-permute-done | bytes 32800 | tf_op jit(solution)/shard_map/ppermute | solution.py:107
  59.1 6.0 %collective-permute-start.12 = (f32[16,16,64]{2,0,1:T(8,128)S(1)}, f32[16,16,64]{2,0,1:T(8,128)S(1)}, u32[]{:S(2)}, u32[]{:S(2)}) collective-permute-start(f32[16,16,64]{2,0,1:T(8,128)S(1)} %get-tuple-element.17), channel_id=1, source_target_pairs={{1,0},{2,1},{3,2},{4,3},{5,4},{6,5},{7,6},{8,7},{9,8},{10,9},{11,1... | collective-permute-start | bytes 196616 | tf_op jit(solution)/shard_map/ppermute | solution.py:111
  69.0 2.4 %collective-permute-start.11 = (f32[16,1,512]{2,0,1:T(8,128)S(1)}, f32[16,1,512]{2,0,1:T(8,128)S(1)}, u32[]{:S(2)}, u32[]{:S(2)}) collective-permute-start(f32[16,1,512]{2,0,1:T(8,128)S(1)} %get-tuple-element.14), channel_id=1, source_target_pairs={{0,16},{16,32},{32,48},{48,64},{64,80},{80,96},{96,112},{112,128},... | collective-permute-start | bytes 98312 | tf_op jit(solution)/shard_map/ppermute | solution.py:107
  71.5 2.7 %collective-permute-done.11 = f32[16,1,512]{2,0,1:T(8,128)S(1)} collective-permute-done((f32[16,1,512]{2,0,1:T(8,128)S(1)}, f32[16,1,512]{2,0,1:T(8,128)S(1)}, u32[]{:S(2)}, u32[]{:S(2)}) %collective-permute-start.11) | collective-permute-done | bytes 32800 | tf_op jit(solution)/shard_map/ppermute | solution.py:107
  80.4 7.8 %collective-permute-start.17 = (f32[48,48]{0,1:T(8,128)S(1)}, f32[48,48]{0,1:T(8,128)S(1)}, u32[]{:S(2)}, u32[]{:S(2)}) collective-permute-start(f32[48,48]{0,1:T(8,128)S(1)} %add_add_fusion.4), channel_id=1, source_target_pairs={{0,64},{16,80},{32,96},{48,112},{64,0},{80,16},{96,32},{112,48},{1... | collective-permute-start | bytes 27656 | tf_op jit(solution)/shard_map/ppermute | solution.py:25
  88.2 3.9 %collective-permute-start.18 = (f32[48,48]{0,1:T(8,128)S(1)}, f32[48,48]{0,1:T(8,128)S(1)}, u32[]{:S(2)}, u32[]{:S(2)}) collective-permute-start(f32[48,48]{0,1:T(8,128)S(1)} %add_add_fusion.4), channel_id=1, source_target_pairs={{0,128},{16,144},{32,160},{48,176},{64,192},{80,208},{96,224},{112... | collective-permute-start | bytes 27656 | tf_op jit(solution)/shard_map/ppermute | solution.py:25
  92.6 3.5 %collective-permute-done.18 = f32[48,48]{0,1:T(8,128)S(1)} collective-permute-done((f32[48,48]{0,1:T(8,128)S(1)}, f32[48,48]{0,1:T(8,128)S(1)}, u32[]{:S(2)}, u32[]{:S(2)}) %collective-permute-start.18) | collective-permute-done | bytes 9248 | tf_op jit(solution)/shard_map/ppermute | solution.py:25
  96.1 2.2 %collective-permute-done.19 = f32[48,48]{0,1:T(8,128)S(1)} collective-permute-done((f32[48,48]{0,1:T(8,128)S(1)}, f32[48,48]{0,1:T(8,128)S(1)}, u32[]{:S(2)}, u32[]{:S(2)}) %collective-permute-start.19) | collective-permute-done | bytes 9248 | tf_op jit(solution)/shard_map/ppermute | solution.py:25
  98.5 5.7 %collective-permute-start.21 = (f32[48,48]{0,1:T(8,128)S(1)}, f32[48,48]{0,1:T(8,128)S(1)}, u32[]{:S(2)}, u32[]{:S(2)}) collective-permute-start(f32[48,48]{0,1:T(8,128)S(1)} %add_add_fusion.3), channel_id=1, source_target_pairs={{0,2},{1,3},{2,0},{3,1},{4,6},{5,7},{6,4},{7,5},{8,10},{9,11},{10,... | collective-permute-start | bytes 27656 | tf_op jit(solution)/shard_map/ppermute | solution.py:25
  104.2 2.1 %collective-permute-done.21 = f32[48,48]{0,1:T(8,128)S(1)} collective-permute-done((f32[48,48]{0,1:T(8,128)S(1)}, f32[48,48]{0,1:T(8,128)S(1)}, u32[]{:S(2)}, u32[]{:S(2)}) %collective-permute-start.21) | collective-permute-done | bytes 9248 | tf_op jit(solution)/shard_map/ppermute | solution.py:25
  106.2 3.0 %collective-permute-done.22 = f32[48,48]{0,1:T(8,128)S(1)} collective-permute-done((f32[48,48]{0,1:T(8,128)S(1)}, f32[48,48]{0,1:T(8,128)S(1)}, u32[]{:S(2)}, u32[]{:S(2)}) %collective-permute-start.22) | collective-permute-done | bytes 9248 | tf_op jit(solution)/shard_map/ppermute | solution.py:25
  109.7 2.3 %collective-permute-start.24 = (f32[48,48]{0,1:T(8,128)S(1)}, f32[48,48]{0,1:T(8,128)S(1)}, u32[]{:S(2)}, u32[]{:S(2)}) collective-permute-start(f32[48,48]{0,1:T(8,128)S(1)} %add_add_fusion.2), channel_id=1, source_target_pairs={{0,8},{1,9},{2,10},{3,11},{4,12},{5,13},{6,14},{7,15},{8,0},{9,1},... | collective-permute-start | bytes 27656 | tf_op jit(solution)/shard_map/ppermute | solution.py:25
  116.0 4.4 %cholesky.31 = f32[48,48]{1,0:T(8,128)S(1)} custom-call(f32[48,48]{1,0:T(8,128)S(1)} %fusion.29), custom_call_target="Cholesky" | custom-call | tf_op jit(solution)/shard_map/jit(cholesky)/cholesky | solution.py:202
  122.4 2.4 %custom-call.14 = f32[1,32,32]{1,2,0:T(8,128)S(1)} custom-call(f32[1,32,32]{2,1,0:T(8,128)S(1)} %fusion.39), custom_call_target="InvertDiagBlocksLowerTriangular" | custom-call | tf_op jit(solution)/shard_map/triangular_solve | solution.py:205
  125.7 2.9 %cholesky.59 = f32[32,32]{1,0:T(8,128)S(1)} custom-call(f32[32,32]{1,0:T(8,128)S(1)} %fusion.44), custom_call_target="Cholesky" | custom-call | tf_op jit(solution)/shard_map/jit(cholesky)/cholesky | solution.py:60
  129.9 2.4 %custom-call.15 = f32[1,32,32]{1,2,0:T(8,128)S(1)} custom-call(f32[1,32,32]{2,1,0:T(8,128)S(1)} %fusion.36), custom_call_target="InvertDiagBlocksLowerTriangular" | custom-call | tf_op jit(solution)/shard_map/triangular_solve | solution.py:62
  (178 shorter events, 55.0 us)
Async XLA Ops:
  1.6 25.7 %collective-permute-start.1 = (f32[1,16,64]{2,1,0:T(8,128)S(1)}, f32[1,16,64]{2,1,0:T(8,128)S(1)}, u32[]{:S(2)}, u32[]{:S(2)}) collective-permute-start(f32[1,16,64]{2,1,0:T(8,128)S(1)} %slice.416), channel_id=1, source_target_pairs={{0,1},{1,2},{2,3},{3,4},{4,5},{5,6},{6,7},{7,8},{8,9},{9,10},{10,1... | collective-permute-start | bytes 12296 | tf_op jit(solution)/shard_map/ppermute | solution.py:107
  5.9 19.1 %collective-permute-start = (f32[1,1,512]{2,1,0:T(1,128)S(1)}, f32[1,1,512]{2,1,0:T(1,128)S(1)}, u32[]{:S(2)}, u32[]{:S(2)}) collective-permute-start(f32[1,1,512]{2,1,0:T(1,128)S(1)} %slice.414), channel_id=1, source_target_pairs={{0,16},{16,32},{32,48},{48,64},{64,80},{80,96},{96,112},{112,128},... | collective-permute-start | bytes 6152 | tf_op jit(solution)/shard_map/ppermute | solution.py:107
  9.9 20.5 %collective-permute-start.4 = (f32[16,16,64]{2,0,1:T(8,128)S(1)}, f32[16,16,64]{2,0,1:T(8,128)S(1)}, u32[]{:S(2)}, u32[]{:S(2)}) collective-permute-start(f32[16,16,64]{2,0,1:T(8,128)S(1)} %get-tuple-element.37), channel_id=1, source_target_pairs={{1,0},{2,1},{3,2},{4,3},{5,4},{6,5},{7,6},{8,7},{9,8},{10,9},{11,1... | collective-permute-start | bytes 196616 | tf_op jit(solution)/shard_map/ppermute | solution.py:111
  14.5 15.9 %collective-permute-start.5 = (f32[16,16,64]{2,0,1:T(8,128)S(1)}, f32[16,16,64]{2,0,1:T(8,128)}, u32[]{:S(2)}, u32[]{:S(2)}) collective-permute-start(f32[16,16,64]{2,0,1:T(8,128)S(1)} %get-tuple-element.38), channel_id=1, source_target_pairs={{0,1},{1,2},{2,3},{3,4},{4,5},{5,6},{6,7},{7,8},{8,9},{9,10},{10,1... | collective-permute-start | bytes 196616 | tf_op jit(solution)/shard_map/ppermute | solution.py:107
  16.4 11.4 %collective-permute-start.2 = (f32[16,1,512]{2,0,1:T(8,128)S(1)}, f32[16,1,512]{2,0,1:T(8,128)S(1)}, u32[]{:S(2)}, u32[]{:S(2)}) collective-permute-start(f32[16,1,512]{2,0,1:T(8,128)S(1)} %get-tuple-element.33), channel_id=1, source_target_pairs={{16,0},{32,16},{48,32},{64,48},{80,64},{96,80},{112,96},{128,112},... | collective-permute-start | bytes 98312 | tf_op jit(solution)/shard_map/ppermute | solution.py:111
  25.0 5.4 %collective-permute-start.3 = (f32[16,1,512]{2,0,1:T(8,128)S(1)}, f32[16,1,512]{2,0,1:T(8,128)S(1)}, u32[]{:S(2)}, u32[]{:S(2)}) collective-permute-start(f32[16,1,512]{2,0,1:T(8,128)S(1)} %get-tuple-element.34), channel_id=1, source_target_pairs={{0,16},{16,32},{32,48},{48,64},{64,80},{80,96},{96,112},{112,128},... | collective-permute-start | bytes 98312 | tf_op jit(solution)/shard_map/ppermute | solution.py:107
  38.0 14.9 %collective-permute-start.8 = (f32[16,16,64]{2,0,1:T(8,128)S(1)}, f32[16,16,64]{2,0,1:T(8,128)S(1)}, u32[]{:S(2)}, u32[]{:S(2)}) collective-permute-start(f32[16,16,64]{2,0,1:T(8,128)S(1)} %get-tuple-element.27), channel_id=1, source_target_pairs={{1,0},{2,1},{3,2},{4,3},{5,4},{6,5},{7,6},{8,7},{9,8},{10,9},{11,1... | collective-permute-start | bytes 196616 | tf_op jit(solution)/shard_map/ppermute | solution.py:111
  43.8 9.1 %collective-permute-start.9 = (f32[16,16,64]{2,0,1:T(8,128)S(1)}, f32[16,16,64]{2,0,1:T(8,128)S(1)}, u32[]{:S(2)}, u32[]{:S(2)}) collective-permute-start(f32[16,16,64]{2,0,1:T(8,128)S(1)} %get-tuple-element.28), channel_id=1, source_target_pairs={{0,1},{1,2},{2,3},{3,4},{4,5},{5,6},{6,7},{7,8},{8,9},{9,10},{10,1... | collective-permute-start | bytes 196616 | tf_op jit(solution)/shard_map/ppermute | solution.py:107
  45.7 4.6 %collective-permute-start.6 = (f32[16,1,512]{2,0,1:T(8,128)S(1)}, f32[16,1,512]{2,0,1:T(8,128)S(1)}, u32[]{:S(2)}, u32[]{:S(2)}) collective-permute-start(f32[16,1,512]{2,0,1:T(8,128)S(1)} %get-tuple-element.23), channel_id=1, source_target_pairs={{16,0},{32,16},{48,32},{64,48},{80,64},{96,80},{112,96},{128,112},... | collective-permute-start | bytes 98312 | tf_op jit(solution)/shard_map/ppermute | solution.py:111
  47.6 5.2 %collective-permute-start.7 = (f32[16,1,512]{2,0,1:T(8,128)S(1)}, f32[16,1,512]{2,0,1:T(8,128)S(1)}, u32[]{:S(2)}, u32[]{:S(2)}) collective-permute-start(f32[16,1,512]{2,0,1:T(8,128)S(1)} %get-tuple-element.24), channel_id=1, source_target_pairs={{0,16},{16,32},{32,48},{48,64},{64,80},{80,96},{96,112},{112,128},... | collective-permute-start | bytes 98312 | tf_op jit(solution)/shard_map/ppermute | solution.py:107
  59.1 15.1 %collective-permute-start.12 = (f32[16,16,64]{2,0,1:T(8,128)S(1)}, f32[16,16,64]{2,0,1:T(8,128)S(1)}, u32[]{:S(2)}, u32[]{:S(2)}) collective-permute-start(f32[16,16,64]{2,0,1:T(8,128)S(1)} %get-tuple-element.17), channel_id=1, source_target_pairs={{1,0},{2,1},{3,2},{4,3},{5,4},{6,5},{7,6},{8,7},{9,8},{10,9},{11,1... | collective-permute-start | bytes 196616 | tf_op jit(solution)/shard_map/ppermute | solution.py:111
  65.1 9.1 %collective-permute-start.13 = (f32[16,16,64]{2,0,1:T(8,128)S(1)}, f32[16,16,64]{2,0,1:T(8,128)S(1)}, u32[]{:S(2)}, u32[]{:S(2)}) collective-permute-start(f32[16,16,64]{2,0,1:T(8,128)S(1)} %get-tuple-element.18), channel_id=1, source_target_pairs={{0,1},{1,2},{2,3},{3,4},{4,5},{5,6},{6,7},{7,8},{8,9},{9,10},{10,1... | collective-permute-start | bytes 196616 | tf_op jit(solution)/shard_map/ppermute | solution.py:107
  67.0 4.5 %collective-permute-start.10 = (f32[16,1,512]{2,0,1:T(8,128)S(1)}, f32[16,1,512]{2,0,1:T(8,128)S(1)}, u32[]{:S(2)}, u32[]{:S(2)}) collective-permute-start(f32[16,1,512]{2,0,1:T(8,128)S(1)} %get-tuple-element.13), channel_id=1, source_target_pairs={{16,0},{32,16},{48,32},{64,48},{80,64},{96,80},{112,96},{128,112},... | collective-permute-start | bytes 98312 | tf_op jit(solution)/shard_map/ppermute | solution.py:111
  69.0 5.2 %collective-permute-start.11 = (f32[16,1,512]{2,0,1:T(8,128)S(1)}, f32[16,1,512]{2,0,1:T(8,128)S(1)}, u32[]{:S(2)}, u32[]{:S(2)}) collective-permute-start(f32[16,1,512]{2,0,1:T(8,128)S(1)} %get-tuple-element.14), channel_id=1, source_target_pairs={{0,16},{16,32},{32,48},{48,64},{64,80},{80,96},{96,112},{112,128},... | collective-permute-start | bytes 98312 | tf_op jit(solution)/shard_map/ppermute | solution.py:107
  76.5 3.9 %collective-permute-start.15 = (f32[48,48]{0,1:T(8,128)S(1)}, f32[48,48]{0,1:T(8,128)S(1)}, u32[]{:S(2)}, u32[]{:S(2)}) collective-permute-start(f32[48,48]{0,1:T(8,128)S(1)} %fusion.6), channel_id=1, source_target_pairs={{0,32},{16,48},{32,0},{48,16},{64,96},{80,112},{96,64},{112,80},{1... | collective-permute-start | bytes 27656 | tf_op jit(solution)/shard_map/ppermute | solution.py:25
  80.4 12.2 %collective-permute-start.17 = (f32[48,48]{0,1:T(8,128)S(1)}, f32[48,48]{0,1:T(8,128)S(1)}, u32[]{:S(2)}, u32[]{:S(2)}) collective-permute-start(f32[48,48]{0,1:T(8,128)S(1)} %add_add_fusion.4), channel_id=1, source_target_pairs={{0,64},{16,80},{32,96},{48,112},{64,0},{80,16},{96,32},{112,48},{1... | collective-permute-start | bytes 27656 | tf_op jit(solution)/shard_map/ppermute | solution.py:25
  88.2 7.9 %collective-permute-start.18 = (f32[48,48]{0,1:T(8,128)S(1)}, f32[48,48]{0,1:T(8,128)S(1)}, u32[]{:S(2)}, u32[]{:S(2)}) collective-permute-start(f32[48,48]{0,1:T(8,128)S(1)} %add_add_fusion.4), channel_id=1, source_target_pairs={{0,128},{16,144},{32,160},{48,176},{64,192},{80,208},{96,224},{112... | collective-permute-start | bytes 27656 | tf_op jit(solution)/shard_map/ppermute | solution.py:25
  92.2 6.2 %collective-permute-start.19 = (f32[48,48]{0,1:T(8,128)S(1)}, f32[48,48]{0,1:T(8,128)S(1)}, u32[]{:S(2)}, u32[]{:S(2)}) collective-permute-start(f32[48,48]{0,1:T(8,128)S(1)} %add_add_fusion.4), channel_id=1, source_target_pairs={{0,192},{16,208},{32,224},{48,240},{64,128},{80,144},{96,160},{112... | collective-permute-start | bytes 27656 | tf_op jit(solution)/shard_map/ppermute | solution.py:25
  98.4 5.8 %collective-permute-start.20 = (f32[48,48]{0,1:T(8,128)S(1)}, f32[48,48]{0,1:T(8,128)S(1)}, u32[]{:S(2)}, u32[]{:S(2)}) collective-permute-start(f32[48,48]{0,1:T(8,128)S(1)} %add_add_fusion.3), channel_id=1, source_target_pairs={{0,1},{1,0},{2,3},{3,2},{4,5},{5,4},{6,7},{7,6},{8,9},{9,8},{10,11... | collective-permute-start | bytes 27656 | tf_op jit(solution)/shard_map/ppermute | solution.py:25
  98.5 7.7 %collective-permute-start.21 = (f32[48,48]{0,1:T(8,128)S(1)}, f32[48,48]{0,1:T(8,128)S(1)}, u32[]{:S(2)}, u32[]{:S(2)}) collective-permute-start(f32[48,48]{0,1:T(8,128)S(1)} %add_add_fusion.3), channel_id=1, source_target_pairs={{0,2},{1,3},{2,0},{3,1},{4,6},{5,7},{6,4},{7,5},{8,10},{9,11},{10,... | collective-permute-start | bytes 27656 | tf_op jit(solution)/shard_map/ppermute | solution.py:25
  104.2 5.0 %collective-permute-start.22 = (f32[48,48]{0,1:T(8,128)S(1)}, f32[48,48]{0,1:T(8,128)S(1)}, u32[]{:S(2)}, u32[]{:S(2)}) collective-permute-start(f32[48,48]{0,1:T(8,128)S(1)} %add_add_fusion.3), channel_id=1, source_target_pairs={{0,3},{1,2},{2,1},{3,0},{4,7},{5,6},{6,5},{7,4},{8,11},{9,10},{10,... | collective-permute-start | bytes 27656 | tf_op jit(solution)/shard_map/ppermute | solution.py:25
  109.2 3.9 %collective-permute-start.23 = (f32[48,48]{0,1:T(8,128)S(1)}, f32[48,48]{0,1:T(8,128)S(1)}, u32[]{:S(2)}, u32[]{:S(2)}) collective-permute-start(f32[48,48]{0,1:T(8,128)S(1)} %add_add_fusion.2), channel_id=1, source_target_pairs={{0,4},{1,5},{2,6},{3,7},{4,0},{5,1},{6,2},{7,3},{8,12},{9,13},{10,... | collective-permute-start | bytes 27656 | tf_op jit(solution)/shard_map/ppermute | solution.py:25
  109.7 5.3 %collective-permute-start.24 = (f32[48,48]{0,1:T(8,128)S(1)}, f32[48,48]{0,1:T(8,128)S(1)}, u32[]{:S(2)}, u32[]{:S(2)}) collective-permute-start(f32[48,48]{0,1:T(8,128)S(1)} %add_add_fusion.2), channel_id=1, source_target_pairs={{0,8},{1,9},{2,10},{3,11},{4,12},{5,13},{6,14},{7,15},{8,0},{9,1},... | collective-permute-start | bytes 27656 | tf_op jit(solution)/shard_map/ppermute | solution.py:25
  112.0 3.8 %collective-permute-start.25 = (f32[48,48]{0,1:T(8,128)S(1)}, f32[48,48]{0,1:T(8,128)S(1)}, u32[]{:S(2)}, u32[]{:S(2)}) collective-permute-start(f32[48,48]{0,1:T(8,128)S(1)} %add_add_fusion.2), channel_id=1, source_target_pairs={{0,12},{1,13},{2,14},{3,15},{4,8},{5,9},{6,10},{7,11},{8,4},{9,5},... | collective-permute-start | bytes 27656 | tf_op jit(solution)/shard_map/ppermute | solution.py:25
  (13 other events, 32.1 us)

commit v5 on v4

--- a/solution.py
+++ b/solution.py
@@ -113,8 +113,14 @@
     after_x = coef(couple_x)
     after_y = coef(couple_y)
     after_z = coef(couple_z)
-    edge_x = forward(after_x[:, -1:], "gx")
-    edge_y = forward(after_y[:, :, plane - layers :], "gy")
+    rhs_in = inward(right_side)
+    start_in = inward(start_guess)
+    joint_x = forward(jnp.concatenate([start_in[:, -1:], after_x[:, -1:]], axis=0), "gx")
+    joint_y = forward(
+        jnp.concatenate([start_in[:, :, plane - layers :], after_y[:, :, plane - layers :]], axis=0), "gy"
+    )
+    edge_x = joint_x[count_rhs:]
+    edge_y = joint_y[count_rhs:]
     before_x = jnp.concatenate([edge_x, after_x[:, :-1]], axis=1)
     before_y = jnp.concatenate([edge_y, after_y[:, :, : plane - layers]], axis=2)
     before_z = low_z(after_z)
@@ -164,8 +170,6 @@
     def total_gram(former, latter):
         return mesh_sum(block_gram(former, latter))
 
-    rhs_in = inward(right_side)
-    start_in = inward(start_guess)
     def precondition(source):
         lower_sol = inv_piv * source
         for precondition_repeat in range(SWEEPS):
@@ -184,7 +188,12 @@
             )
         return upper_sol
 
-    start_edges = halos(start_in)
+    start_edges = (
+        joint_x[:count_rhs],
+        backward(start_in[:, :1], "gx"),
+        joint_y[:count_rhs],
+        backward(start_in[:, :, :layers], "gy"),
+    )
     start_res = rhs_in - apply_op(start_in, start_edges)
     krylov = [start_res]
     precond_set = []

time: 142 us -> 134 us (0.944)
  starting transfers between devices: 65.5 us -> 56.7 us
  local copies, waits for them, and re-layouts: 17.3 us -> 20.2 us
  waiting for transfers between devices: 23.7 us -> 21.4 us
    ppermute x6, starting transfers between devices: 23.5 us -> 18.8 us  [backward(): return lax.ppermute(block, axis, [(i + 1, i) for i in range(count - 1)])]
    slice x2 -> x9, local copies, waits for them, and re-layouts: 0.08 us -> 4.2 us  [the longest x1 0.96 us: body(): edge_y = joint_y[count_rhs:]]
    ppermute x8 -> x6, starting transfers between devices: 18.4 us -> 15.6 us  [forward(): return lax.ppermute(block, axis, [(i, i + 1) for i in range(count - 1)])]
    ppermute x8 -> x6, waiting for transfers between devices: 7.76 us -> 5.21 us  [forward(): return lax.ppermute(block, axis, [(i, i + 1) for i in range(count - 1)])]
    reshape x4, local copies, waits for them, and re-layouts: 1.99 us -> 0.39 us  [coef(): return values.reshape(1, rows_x, plane)]
    mul x9 -> x8, other arithmetic: 3.36 us -> 3.31 us  [precondition(): inv_piv * (source + lows[0] * low_x(lower_sol) + lows[1] * low_y(lower_so...]
  transfers between devices with their start and end apart: 26 -> 24, of which waited for: 11 -> 10; matrix products, arithmetic and copies ran while one was open for 6% -> 8% of each run, Pallas kernels for 0% -> 0%
where the time goes in v5:
time: 134 us; the launch traced here: 132 us
  starting transfers between devices  56.7 us (42%)
  other arithmetic  26 us (19%)
  waiting for transfers between devices  21.4 us (16%)
  local copies, waits for them, and re-layouts  20.2 us (15%)
  matrix products  6.07 us (5%)
  between operations  1.56 us (1%)
    ppermute x12, starting transfers between devices, mesh_sum(): lax.ppermute(block, axis, [(i, i ^ step * m) for i in range(count)])  22.3 us
    ppermute x6, starting transfers between devices, backward(): return lax.ppermute(block, axis, [(i + 1, i) for i in range(count - 1)])  18.8 us
    ppermute x12, waiting for transfers between devices, mesh_sum(): lax.ppermute(block, axis, [(i, i ^ step * m) for i in range(count)])  16.2 us
    ppermute x6, starting transfers between devices, forward(): return lax.ppermute(block, axis, [(i, i + 1) for i in range(count - 1)])  15.6 us
    ppermute x6, waiting for transfers between devices, forward(): return lax.ppermute(block, axis, [(i, i + 1) for i in range(count - 1)])  5.21 us
    slice x27, local copies, waits for them, and re-layouts, up_along(): lax.slice_in_dim(values, width, count, axis=axis)  5.1 us
    another operation x3, other arithmetic, body(): full_low = jnp.linalg.cholesky(span_gram)  5.05 us
    another operation x3, other arithmetic, solve_small(): low_factor = jnp.linalg.cholesky(normal)  3.6 us
  transfers between devices with their start and end apart: 24, of which 10 were waited for; matrix products, arithmetic and copies ran while one was open for 8% of the time, Pallas kernels for 0%

profile of v5, /device:TPU:40, one launch (start us, length us, event | category | flops | bytes accessed | tf_op | source)
XLA Modules:
  0.0 131.9 jit_solution(3470976119642969988)
XLA Ops:
  3.3 3.4 %collective-permute-start.1 = (f32[17,16,64]{2,0,1:T(8,128)S(1)}, f32[17,16,64]{2,0,1:T(8,128)}, u32[]{:S(2)}, u32[]{:S(2)}) collective-permute-start(f32[17,16,64]{2,0,1:T(8,128)S(1)} %pad_maximum_fusion), channel_id=1, source_target_pairs={{0,1},{1,2},{2,3},{3,4},{4,5},{5,6},{6,7},{7,8},{8,9},{9,10},{10,1... | collective-permute-start | bytes 208904 | tf_op jit(solution)/shard_map/ppermute | solution.py:107
  9.4 4.6 %collective-permute-start.3 = (f32[16,16,64]{2,0,1:T(8,128)S(1)}, f32[16,16,64]{2,0,1:T(8,128)}, u32[]{:S(2)}, u32[]{:S(2)}) collective-permute-start(f32[16,16,64]{2,0,1:T(8,128)S(1)} %get-tuple-element.39), channel_id=1, source_target_pairs={{1,0},{2,1},{3,2},{4,3},{5,4},{6,5},{7,6},{8,7},{9,8},{10,9},{11,1... | collective-permute-start | bytes 196616 | tf_op jit(solution)/shard_map/ppermute | solution.py:111
  14.0 3.4 %collective-permute-start.2 = (f32[16,1,512]{2,0,1:T(8,128)}, f32[16,1,512]{2,0,1:T(8,128)S(1)}, u32[]{:S(2)}, u32[]{:S(2)}) collective-permute-start(f32[16,1,512]{2,0,1:T(8,128)} %get-tuple-element.35), channel_id=1, source_target_pairs={{16,0},{32,16},{48,32},{64,48},{80,64},{96,80},{112,96},{128,112},... | collective-permute-start | bytes 98312 | tf_op jit(solution)/shard_map/ppermute | solution.py:111
  34.7 2.4 %collective-permute-start.6 = (f32[16,16,64]{2,0,1:T(8,128)S(1)}, f32[16,16,64]{2,0,1:T(8,128)S(1)}, u32[]{:S(2)}, u32[]{:S(2)}) collective-permute-start(f32[16,16,64]{2,0,1:T(8,128)S(1)} %get-tuple-element.29), channel_id=1, source_target_pairs={{1,0},{2,1},{3,2},{4,3},{5,4},{6,5},{7,6},{8,7},{9,8},{10,9},{11,1... | collective-permute-start | bytes 196616 | tf_op jit(solution)/shard_map/ppermute | solution.py:111
  37.2 3.4 %collective-permute-start.7 = (f32[16,16,64]{2,0,1:T(8,128)S(1)}, f32[16,16,64]{2,0,1:T(8,128)S(1)}, u32[]{:S(2)}, u32[]{:S(2)}) collective-permute-start(f32[16,16,64]{2,0,1:T(8,128)S(1)} %get-tuple-element.30), channel_id=1, source_target_pairs={{0,1},{1,2},{2,3},{3,4},{4,5},{5,6},{6,7},{7,8},{8,9},{9,10},{10,1... | collective-permute-start | bytes 196616 | tf_op jit(solution)/shard_map/ppermute | solution.py:107
  42.5 2.6 %collective-permute-start.5 = (f32[16,1,512]{2,0,1:T(8,128)S(1)}, f32[16,1,512]{2,0,1:T(8,128)S(1)}, u32[]{:S(2)}, u32[]{:S(2)}) collective-permute-start(f32[16,1,512]{2,0,1:T(8,128)S(1)} %get-tuple-element.26), channel_id=1, source_target_pairs={{0,16},{16,32},{32,48},{48,64},{64,80},{80,96},{96,112},{112,128},... | collective-permute-start | bytes 98312 | tf_op jit(solution)/shard_map/ppermute | solution.py:107
  45.3 2.5 %collective-permute-done.5 = f32[16,1,512]{2,0,1:T(8,128)S(1)} collective-permute-done((f32[16,1,512]{2,0,1:T(8,128)S(1)}, f32[16,1,512]{2,0,1:T(8,128)S(1)}, u32[]{:S(2)}, u32[]{:S(2)}) %collective-permute-start.5) | collective-permute-done | bytes 32800 | tf_op jit(solution)/shard_map/ppermute | solution.py:107
  54.0 4.6 %collective-permute-start.10 = (f32[16,16,64]{2,0,1:T(8,128)S(1)}, f32[16,16,64]{2,0,1:T(8,128)S(1)}, u32[]{:S(2)}, u32[]{:S(2)}) collective-permute-start(f32[16,16,64]{2,0,1:T(8,128)S(1)} %get-tuple-element.19), channel_id=1, source_target_pairs={{1,0},{2,1},{3,2},{4,3},{5,4},{6,5},{7,6},{8,7},{9,8},{10,9},{11,1... | collective-permute-start | bytes 196616 | tf_op jit(solution)/shard_map/ppermute | solution.py:111
  62.5 2.4 %collective-permute-start.9 = (f32[16,1,512]{2,0,1:T(8,128)S(1)}, f32[16,1,512]{2,0,1:T(8,128)S(1)}, u32[]{:S(2)}, u32[]{:S(2)}) collective-permute-start(f32[16,1,512]{2,0,1:T(8,128)S(1)} %get-tuple-element.16), channel_id=1, source_target_pairs={{0,16},{16,32},{32,48},{48,64},{64,80},{80,96},{96,112},{112,128},... | collective-permute-start | bytes 98312 | tf_op jit(solution)/shard_map/ppermute | solution.py:107
  65.0 2.7 %collective-permute-done.9 = f32[16,1,512]{2,0,1:T(8,128)S(1)} collective-permute-done((f32[16,1,512]{2,0,1:T(8,128)S(1)}, f32[16,1,512]{2,0,1:T(8,128)S(1)}, u32[]{:S(2)}, u32[]{:S(2)}) %collective-permute-start.9) | collective-permute-done | bytes 32800 | tf_op jit(solution)/shard_map/ppermute | solution.py:107
  71.8 2.0 %collective-permute-done.13 = f32[48,48]{0,1:T(8,128)S(1)} collective-permute-done((f32[48,48]{0,1:T(8,128)S(1)}, f32[48,48]{0,1:T(8,128)S(1)}, u32[]{:S(2)}, u32[]{:S(2)}) %collective-permute-start.13) | collective-permute-done | bytes 9248 | tf_op jit(solution)/shard_map/ppermute | solution.py:25
  73.9 6.6 %collective-permute-start.15 = (f32[48,48]{0,1:T(8,128)S(1)}, f32[48,48]{0,1:T(8,128)S(1)}, u32[]{:S(2)}, u32[]{:S(2)}) collective-permute-start(f32[48,48]{0,1:T(8,128)S(1)} %add_add_fusion.4), channel_id=1, source_target_pairs={{0,64},{16,80},{32,96},{48,112},{64,0},{80,16},{96,32},{112,48},{1... | collective-permute-start | bytes 27656 | tf_op jit(solution)/shard_map/ppermute | solution.py:25
  80.5 3.9 %collective-permute-start.16 = (f32[48,48]{0,1:T(8,128)S(1)}, f32[48,48]{0,1:T(8,128)S(1)}, u32[]{:S(2)}, u32[]{:S(2)}) collective-permute-start(f32[48,48]{0,1:T(8,128)S(1)} %add_add_fusion.4), channel_id=1, source_target_pairs={{0,128},{16,144},{32,160},{48,176},{64,192},{80,208},{96,224},{112... | collective-permute-start | bytes 27656 | tf_op jit(solution)/shard_map/ppermute | solution.py:25
  84.9 3.5 %collective-permute-done.16 = f32[48,48]{0,1:T(8,128)S(1)} collective-permute-done((f32[48,48]{0,1:T(8,128)S(1)}, f32[48,48]{0,1:T(8,128)S(1)}, u32[]{:S(2)}, u32[]{:S(2)}) %collective-permute-start.16) | collective-permute-done | bytes 9248 | tf_op jit(solution)/shard_map/ppermute | solution.py:25
  88.4 2.2 %collective-permute-done.17 = f32[48,48]{0,1:T(8,128)S(1)} collective-permute-done((f32[48,48]{0,1:T(8,128)S(1)}, f32[48,48]{0,1:T(8,128)S(1)}, u32[]{:S(2)}, u32[]{:S(2)}) %collective-permute-start.17) | collective-permute-done | bytes 9248 | tf_op jit(solution)/shard_map/ppermute | solution.py:25
  90.7 5.7 %collective-permute-start.19 = (f32[48,48]{0,1:T(8,128)S(1)}, f32[48,48]{0,1:T(8,128)S(1)}, u32[]{:S(2)}, u32[]{:S(2)}) collective-permute-start(f32[48,48]{0,1:T(8,128)S(1)} %add_add_fusion.3), channel_id=1, source_target_pairs={{0,2},{1,3},{2,0},{3,1},{4,6},{5,7},{6,4},{7,5},{8,10},{9,11},{10,... | collective-permute-start | bytes 27656 | tf_op jit(solution)/shard_map/ppermute | solution.py:25
  96.4 2.1 %collective-permute-done.19 = f32[48,48]{0,1:T(8,128)S(1)} collective-permute-done((f32[48,48]{0,1:T(8,128)S(1)}, f32[48,48]{0,1:T(8,128)S(1)}, u32[]{:S(2)}, u32[]{:S(2)}) %collective-permute-start.19) | collective-permute-done | bytes 9248 | tf_op jit(solution)/shard_map/ppermute | solution.py:25
  98.5 3.0 %collective-permute-done.20 = f32[48,48]{0,1:T(8,128)S(1)} collective-permute-done((f32[48,48]{0,1:T(8,128)S(1)}, f32[48,48]{0,1:T(8,128)S(1)}, u32[]{:S(2)}, u32[]{:S(2)}) %collective-permute-start.20) | collective-permute-done | bytes 9248 | tf_op jit(solution)/shard_map/ppermute | solution.py:25
  102.0 2.6 %collective-permute-start.22 = (f32[48,48]{0,1:T(8,128)S(1)}, f32[48,48]{0,1:T(8,128)S(1)}, u32[]{:S(2)}, u32[]{:S(2)}) collective-permute-start(f32[48,48]{0,1:T(8,128)S(1)} %add_add_fusion.2), channel_id=1, source_target_pairs={{0,8},{1,9},{2,10},{3,11},{4,12},{5,13},{6,14},{7,15},{8,0},{9,1},... | collective-permute-start | bytes 27656 | tf_op jit(solution)/shard_map/ppermute | solution.py:25
  105.4 2.0 %collective-permute-done.22 = f32[48,48]{0,1:T(8,128)S(1)} collective-permute-done((f32[48,48]{0,1:T(8,128)S(1)}, f32[48,48]{0,1:T(8,128)S(1)}, u32[]{:S(2)}, u32[]{:S(2)}) %collective-permute-start.22) | collective-permute-done | bytes 9248 | tf_op jit(solution)/shard_map/ppermute | solution.py:25
  108.5 4.4 %cholesky.31 = f32[48,48]{1,0:T(8,128)S(1)} custom-call(f32[48,48]{1,0:T(8,128)S(1)} %fusion.28), custom_call_target="Cholesky" | custom-call | tf_op jit(solution)/shard_map/jit(cholesky)/cholesky | solution.py:211
  114.9 2.4 %custom-call.14 = f32[1,32,32]{1,2,0:T(8,128)S(1)} custom-call(f32[1,32,32]{2,1,0:T(8,128)S(1)} %fusion.36), custom_call_target="InvertDiagBlocksLowerTriangular" | custom-call | tf_op jit(solution)/shard_map/triangular_solve | solution.py:214
  118.2 2.9 %cholesky.59 = f32[32,32]{1,0:T(8,128)S(1)} custom-call(f32[32,32]{1,0:T(8,128)S(1)} %fusion.41), custom_call_target="Cholesky" | custom-call | tf_op jit(solution)/shard_map/jit(cholesky)/cholesky | solution.py:60
  122.5 2.4 %custom-call.15 = f32[1,32,32]{1,2,0:T(8,128)S(1)} custom-call(f32[1,32,32]{2,1,0:T(8,128)S(1)} %fusion.33), custom_call_target="InvertDiagBlocksLowerTriangular" | custom-call | tf_op jit(solution)/shard_map/triangular_solve | solution.py:62
  (193 shorter events, 52.7 us)
Async XLA Ops:
  3.3 20.8 %collective-permute-start.1 = (f32[17,16,64]{2,0,1:T(8,128)S(1)}, f32[17,16,64]{2,0,1:T(8,128)}, u32[]{:S(2)}, u32[]{:S(2)}) collective-permute-start(f32[17,16,64]{2,0,1:T(8,128)S(1)} %pad_maximum_fusion), channel_id=1, source_target_pairs={{0,1},{1,2},{2,3},{3,4},{4,5},{5,6},{6,7},{7,8},{8,9},{9,10},{10,1... | collective-permute-start | bytes 208904 | tf_op jit(solution)/shard_map/ppermute | solution.py:107
  7.5 15.1 %collective-permute-start = (f32[17,1,512]{2,0,1:T(8,128)S(1)}, f32[17,1,512]{2,0,1:T(8,128)}, u32[]{:S(2)}, u32[]{:S(2)}) collective-permute-start(f32[17,1,512]{2,0,1:T(8,128)S(1)} %pad_maximum_fusion.1), channel_id=1, source_target_pairs={{0,16},{16,32},{32,48},{48,64},{64,80},{80,96},{96,112},{112,128},... | collective-permute-start | bytes 104456 | tf_op jit(solution)/shard_map/ppermute | solution.py:107
  9.4 17.9 %collective-permute-start.3 = (f32[16,16,64]{2,0,1:T(8,128)S(1)}, f32[16,16,64]{2,0,1:T(8,128)}, u32[]{:S(2)}, u32[]{:S(2)}) collective-permute-start(f32[16,16,64]{2,0,1:T(8,128)S(1)} %get-tuple-element.39), channel_id=1, source_target_pairs={{1,0},{2,1},{3,2},{4,3},{5,4},{6,5},{7,6},{8,7},{9,8},{10,9},{11,1... | collective-permute-start | bytes 196616 | tf_op jit(solution)/shard_map/ppermute | solution.py:111
  14.0 13.3 %collective-permute-start.2 = (f32[16,1,512]{2,0,1:T(8,128)}, f32[16,1,512]{2,0,1:T(8,128)S(1)}, u32[]{:S(2)}, u32[]{:S(2)}) collective-permute-start(f32[16,1,512]{2,0,1:T(8,128)} %get-tuple-element.35), channel_id=1, source_target_pairs={{16,0},{32,16},{48,32},{64,48},{80,64},{96,80},{112,96},{128,112},... | collective-permute-start | bytes 98312 | tf_op jit(solution)/shard_map/ppermute | solution.py:111
  34.7 13.0 %collective-permute-start.6 = (f32[16,16,64]{2,0,1:T(8,128)S(1)}, f32[16,16,64]{2,0,1:T(8,128)S(1)}, u32[]{:S(2)}, u32[]{:S(2)}) collective-permute-start(f32[16,16,64]{2,0,1:T(8,128)S(1)} %get-tuple-element.29), channel_id=1, source_target_pairs={{1,0},{2,1},{3,2},{4,3},{5,4},{6,5},{7,6},{8,7},{9,8},{10,9},{11,1... | collective-permute-start | bytes 196616 | tf_op jit(solution)/shard_map/ppermute | solution.py:111
  37.2 10.6 %collective-permute-start.7 = (f32[16,16,64]{2,0,1:T(8,128)S(1)}, f32[16,16,64]{2,0,1:T(8,128)S(1)}, u32[]{:S(2)}, u32[]{:S(2)}) collective-permute-start(f32[16,16,64]{2,0,1:T(8,128)S(1)} %get-tuple-element.30), channel_id=1, source_target_pairs={{0,1},{1,2},{2,3},{3,4},{4,5},{5,6},{6,7},{7,8},{8,9},{9,10},{10,1... | collective-permute-start | bytes 196616 | tf_op jit(solution)/shard_map/ppermute | solution.py:107
  40.6 4.6 %collective-permute-start.4 = (f32[16,1,512]{2,0,1:T(8,128)S(1)}, f32[16,1,512]{2,0,1:T(8,128)S(1)}, u32[]{:S(2)}, u32[]{:S(2)}) collective-permute-start(f32[16,1,512]{2,0,1:T(8,128)S(1)} %get-tuple-element.25), channel_id=1, source_target_pairs={{16,0},{32,16},{48,32},{64,48},{80,64},{96,80},{112,96},{128,112},... | collective-permute-start | bytes 98312 | tf_op jit(solution)/shard_map/ppermute | solution.py:111
  42.5 5.2 %collective-permute-start.5 = (f32[16,1,512]{2,0,1:T(8,128)S(1)}, f32[16,1,512]{2,0,1:T(8,128)S(1)}, u32[]{:S(2)}, u32[]{:S(2)}) collective-permute-start(f32[16,1,512]{2,0,1:T(8,128)S(1)} %get-tuple-element.26), channel_id=1, source_target_pairs={{0,16},{16,32},{32,48},{48,64},{64,80},{80,96},{96,112},{112,128},... | collective-permute-start | bytes 98312 | tf_op jit(solution)/shard_map/ppermute | solution.py:107
  54.0 13.7 %collective-permute-start.10 = (f32[16,16,64]{2,0,1:T(8,128)S(1)}, f32[16,16,64]{2,0,1:T(8,128)S(1)}, u32[]{:S(2)}, u32[]{:S(2)}) collective-permute-start(f32[16,16,64]{2,0,1:T(8,128)S(1)} %get-tuple-element.19), channel_id=1, source_target_pairs={{1,0},{2,1},{3,2},{4,3},{5,4},{6,5},{7,6},{8,7},{9,8},{10,9},{11,1... | collective-permute-start | bytes 196616 | tf_op jit(solution)/shard_map/ppermute | solution.py:111
  58.6 9.1 %collective-permute-start.11 = (f32[16,16,64]{2,0,1:T(8,128)S(1)}, f32[16,16,64]{2,0,1:T(8,128)S(1)}, u32[]{:S(2)}, u32[]{:S(2)}) collective-permute-start(f32[16,16,64]{2,0,1:T(8,128)S(1)} %get-tuple-element.20), channel_id=1, source_target_pairs={{0,1},{1,2},{2,3},{3,4},{4,5},{5,6},{6,7},{7,8},{8,9},{9,10},{10,1... | collective-permute-start | bytes 196616 | tf_op jit(solution)/shard_map/ppermute | solution.py:107
  60.5 4.5 %collective-permute-start.8 = (f32[16,1,512]{2,0,1:T(8,128)S(1)}, f32[16,1,512]{2,0,1:T(8,128)S(1)}, u32[]{:S(2)}, u32[]{:S(2)}) collective-permute-start(f32[16,1,512]{2,0,1:T(8,128)S(1)} %get-tuple-element.15), channel_id=1, source_target_pairs={{16,0},{32,16},{48,32},{64,48},{80,64},{96,80},{112,96},{128,112},... | collective-permute-start | bytes 98312 | tf_op jit(solution)/shard_map/ppermute | solution.py:111
  62.5 5.2 %collective-permute-start.9 = (f32[16,1,512]{2,0,1:T(8,128)S(1)}, f32[16,1,512]{2,0,1:T(8,128)S(1)}, u32[]{:S(2)}, u32[]{:S(2)}) collective-permute-start(f32[16,1,512]{2,0,1:T(8,128)S(1)} %get-tuple-element.16), channel_id=1, source_target_pairs={{0,16},{16,32},{32,48},{48,64},{64,80},{80,96},{96,112},{112,128},... | collective-permute-start | bytes 98312 | tf_op jit(solution)/shard_map/ppermute | solution.py:107
  69.9 2.0 %collective-permute-start.12 = (f32[48,48]{0,1:T(8,128)S(1)}, f32[48,48]{0,1:T(8,128)S(1)}, u32[]{:S(2)}, u32[]{:S(2)}) collective-permute-start(f32[48,48]{0,1:T(8,128)S(1)} %fusion.6), channel_id=1, source_target_pairs={{0,16},{16,0},{32,48},{48,32},{64,80},{80,64},{96,112},{112,96},{1... | collective-permute-start | bytes 27656 | tf_op jit(solution)/shard_map/ppermute | solution.py:25
  70.0 3.9 %collective-permute-start.13 = (f32[48,48]{0,1:T(8,128)S(1)}, f32[48,48]{0,1:T(8,128)S(1)}, u32[]{:S(2)}, u32[]{:S(2)}) collective-permute-start(f32[48,48]{0,1:T(8,128)S(1)} %fusion.6), channel_id=1, source_target_pairs={{0,32},{16,48},{32,0},{48,16},{64,96},{80,112},{96,64},{112,80},{1... | collective-permute-start | bytes 27656 | tf_op jit(solution)/shard_map/ppermute | solution.py:25
  70.1 3.8 %collective-permute-start.14 = (f32[48,48]{0,1:T(8,128)S(1)}, f32[48,48]{0,1:T(8,128)S(1)}, u32[]{:S(2)}, u32[]{:S(2)}) collective-permute-start(f32[48,48]{0,1:T(8,128)S(1)} %fusion.6), channel_id=1, source_target_pairs={{0,48},{16,32},{32,16},{48,0},{64,112},{80,96},{96,80},{112,64},{1... | collective-permute-start | bytes 27656 | tf_op jit(solution)/shard_map/ppermute | solution.py:25
  73.9 11.0 %collective-permute-start.15 = (f32[48,48]{0,1:T(8,128)S(1)}, f32[48,48]{0,1:T(8,128)S(1)}, u32[]{:S(2)}, u32[]{:S(2)}) collective-permute-start(f32[48,48]{0,1:T(8,128)S(1)} %add_add_fusion.4), channel_id=1, source_target_pairs={{0,64},{16,80},{32,96},{48,112},{64,0},{80,16},{96,32},{112,48},{1... | collective-permute-start | bytes 27656 | tf_op jit(solution)/shard_map/ppermute | solution.py:25
  80.5 7.9 %collective-permute-start.16 = (f32[48,48]{0,1:T(8,128)S(1)}, f32[48,48]{0,1:T(8,128)S(1)}, u32[]{:S(2)}, u32[]{:S(2)}) collective-permute-start(f32[48,48]{0,1:T(8,128)S(1)} %add_add_fusion.4), channel_id=1, source_target_pairs={{0,128},{16,144},{32,160},{48,176},{64,192},{80,208},{96,224},{112... | collective-permute-start | bytes 27656 | tf_op jit(solution)/shard_map/ppermute | solution.py:25
  84.4 6.2 %collective-permute-start.17 = (f32[48,48]{0,1:T(8,128)S(1)}, f32[48,48]{0,1:T(8,128)S(1)}, u32[]{:S(2)}, u32[]{:S(2)}) collective-permute-start(f32[48,48]{0,1:T(8,128)S(1)} %add_add_fusion.4), channel_id=1, source_target_pairs={{0,192},{16,208},{32,224},{48,240},{64,128},{80,144},{96,160},{112... | collective-permute-start | bytes 27656 | tf_op jit(solution)/shard_map/ppermute | solution.py:25
  90.6 5.8 %collective-permute-start.18 = (f32[48,48]{0,1:T(8,128)S(1)}, f32[48,48]{0,1:T(8,128)S(1)}, u32[]{:S(2)}, u32[]{:S(2)}) collective-permute-start(f32[48,48]{0,1:T(8,128)S(1)} %add_add_fusion.3), channel_id=1, source_target_pairs={{0,1},{1,0},{2,3},{3,2},{4,5},{5,4},{6,7},{7,6},{8,9},{9,8},{10,11... | collective-permute-start | bytes 27656 | tf_op jit(solution)/shard_map/ppermute | solution.py:25
  90.7 7.8 %collective-permute-start.19 = (f32[48,48]{0,1:T(8,128)S(1)}, f32[48,48]{0,1:T(8,128)S(1)}, u32[]{:S(2)}, u32[]{:S(2)}) collective-permute-start(f32[48,48]{0,1:T(8,128)S(1)} %add_add_fusion.3), channel_id=1, source_target_pairs={{0,2},{1,3},{2,0},{3,1},{4,6},{5,7},{6,4},{7,5},{8,10},{9,11},{10,... | collective-permute-start | bytes 27656 | tf_op jit(solution)/shard_map/ppermute | solution.py:25
  96.4 5.0 %collective-permute-start.20 = (f32[48,48]{0,1:T(8,128)S(1)}, f32[48,48]{0,1:T(8,128)S(1)}, u32[]{:S(2)}, u32[]{:S(2)}) collective-permute-start(f32[48,48]{0,1:T(8,128)S(1)} %add_add_fusion.3), channel_id=1, source_target_pairs={{0,3},{1,2},{2,1},{3,0},{4,7},{5,6},{6,5},{7,4},{8,11},{9,10},{10,... | collective-permute-start | bytes 27656 | tf_op jit(solution)/shard_map/ppermute | solution.py:25
  101.5 3.9 %collective-permute-start.21 = (f32[48,48]{0,1:T(8,128)S(1)}, f32[48,48]{0,1:T(8,128)S(1)}, u32[]{:S(2)}, u32[]{:S(2)}) collective-permute-start(f32[48,48]{0,1:T(8,128)S(1)} %add_add_fusion.2), channel_id=1, source_target_pairs={{0,4},{1,5},{2,6},{3,7},{4,0},{5,1},{6,2},{7,3},{8,12},{9,13},{10,... | collective-permute-start | bytes 27656 | tf_op jit(solution)/shard_map/ppermute | solution.py:25
  102.0 5.3 %collective-permute-start.22 = (f32[48,48]{0,1:T(8,128)S(1)}, f32[48,48]{0,1:T(8,128)S(1)}, u32[]{:S(2)}, u32[]{:S(2)}) collective-permute-start(f32[48,48]{0,1:T(8,128)S(1)} %add_add_fusion.2), channel_id=1, source_target_pairs={{0,8},{1,9},{2,10},{3,11},{4,12},{5,13},{6,14},{7,15},{8,0},{9,1},... | collective-permute-start | bytes 27656 | tf_op jit(solution)/shard_map/ppermute | solution.py:25
  104.6 3.8 %collective-permute-start.23 = (f32[48,48]{0,1:T(8,128)S(1)}, f32[48,48]{0,1:T(8,128)S(1)}, u32[]{:S(2)}, u32[]{:S(2)}) collective-permute-start(f32[48,48]{0,1:T(8,128)S(1)} %add_add_fusion.2), channel_id=1, source_target_pairs={{0,12},{1,13},{2,14},{3,15},{4,8},{5,9},{6,10},{7,11},{8,4},{9,5},... | collective-permute-start | bytes 27656 | tf_op jit(solution)/shard_map/ppermute | solution.py:25
  (13 other events, 31.5 us)

commit v6 on v4

--- a/solution.py
+++ b/solution.py
@@ -113,8 +113,18 @@
     after_x = coef(couple_x)
     after_y = coef(couple_y)
     after_z = coef(couple_z)
-    edge_x = forward(after_x[:, -1:], "gx")
-    edge_y = forward(after_y[:, :, plane - layers :], "gy")
+    rhs_in = inward(right_side)
+    start_in = inward(start_guess)
+
+    def slab_in(values):
+        count_a, count_b = values.shape[:2]
+        split = values.reshape(count_a, count_b, count_rhs, layers)
+        return jnp.transpose(split, (2, 0, 1, 3)).reshape(count_rhs, count_a, count_b * layers)
+
+    joint_x = forward(jnp.concatenate([start_guess[-1:], couple_x[-1:]], axis=2), "gx")
+    joint_y = forward(jnp.concatenate([start_guess[:, -1:], couple_y[:, -1:]], axis=2), "gy")
+    edge_x = joint_x[:, :, flat_len:].reshape(1, 1, plane)
+    edge_y = joint_y[:, :, flat_len:].reshape(1, rows_x, layers)
     before_x = jnp.concatenate([edge_x, after_x[:, :-1]], axis=1)
     before_y = jnp.concatenate([edge_y, after_y[:, :, : plane - layers]], axis=2)
     before_z = low_z(after_z)
@@ -164,8 +174,6 @@
     def total_gram(former, latter):
         return mesh_sum(block_gram(former, latter))
 
-    rhs_in = inward(right_side)
-    start_in = inward(start_guess)
     def precondition(source):
         lower_sol = inv_piv * source
         for precondition_repeat in range(SWEEPS):
@@ -184,7 +192,12 @@
             )
         return upper_sol
 
-    start_edges = halos(start_in)
+    start_edges = (
+        slab_in(joint_x[:, :, :flat_len]),
+        slab_in(backward(start_guess[:1], "gx")),
+        slab_in(joint_y[:, :, :flat_len]).reshape(count_rhs, rows_x, layers),
+        slab_in(backward(start_guess[:, :1], "gy")).reshape(count_rhs, rows_x, layers),
+    )
     start_res = rhs_in - apply_op(start_in, start_edges)
     krylov = [start_res]
     precond_set = []

time: 142 us -> 138 us (0.972)
  starting transfers between devices: 65.5 us -> 56.7 us
  local copies, waits for them, and re-layouts: 17.3 us -> 22.2 us
  other arithmetic: 25.5 us -> 28 us
  waiting for transfers between devices: 23.7 us -> 21.4 us
    slice x2 -> x7, local copies, waits for them, and re-layouts: 0.08 us -> 5.73 us  [the longest x1 1.96 us: body(): start_guess[:, :1]]
    ppermute x6, starting transfers between devices: 23.5 us -> 18.8 us  [backward(): return lax.ppermute(block, axis, [(i + 1, i) for i in range(count - 1)])]
    ppermute x8 -> x6, starting transfers between devices: 18.4 us -> 15.6 us  [forward(): return lax.ppermute(block, axis, [(i, i + 1) for i in range(count - 1)])]
    ppermute x8 -> x6, waiting for transfers between devices: 7.76 us -> 5.21 us  [forward(): return lax.ppermute(block, axis, [(i, i + 1) for i in range(count - 1)])]
    reshape x4, local copies, waits for them, and re-layouts: 1.99 us -> 0.31 us  [coef(): return values.reshape(1, rows_x, plane)]
  transfers between devices with their start and end apart: 26 -> 24, of which waited for: 11 -> 10; matrix products, arithmetic and copies ran while one was open for 6% -> 7% of each run, Pallas kernels for 0% -> 0%
where the time goes in v6:
time: 138 us; the launch traced here: 136 us
  starting transfers between devices  56.7 us (41%)
  other arithmetic  28 us (20%)
  local copies, waits for them, and re-layouts  22.2 us (16%)
  waiting for transfers between devices  21.4 us (16%)
  matrix products  6.2 us (4%)
  between operations  1.42 us (1%)
    ppermute x12, starting transfers between devices, mesh_sum(): lax.ppermute(block, axis, [(i, i ^ step * m) for i in range(count)])  22.3 us
    ppermute x6, starting transfers between devices, backward(): return lax.ppermute(block, axis, [(i + 1, i) for i in range(count - 1)])  18.8 us
    ppermute x12, waiting for transfers between devices, mesh_sum(): lax.ppermute(block, axis, [(i, i ^ step * m) for i in range(count)])  16.2 us
    ppermute x6, starting transfers between devices, forward(): return lax.ppermute(block, axis, [(i, i + 1) for i in range(count - 1)])  15.6 us
    ppermute x6, waiting for transfers between devices, forward(): return lax.ppermute(block, axis, [(i, i + 1) for i in range(count - 1)])  5.21 us
    slice x27, local copies, waits for them, and re-layouts, up_along(): lax.slice_in_dim(values, width, count, axis=axis)  5.08 us
    another operation x3, other arithmetic, body(): full_low = jnp.linalg.cholesky(span_gram)  5.05 us
    mul x2, other arithmetic, precondition(): lower_sol = inv_piv * source  3.68 us
  transfers between devices with their start and end apart: 24, of which 10 were waited for; matrix products, arithmetic and copies ran while one was open for 7% of the time, Pallas kernels for 0%

profile of v6, /device:TPU:40, one launch (start us, length us, event | category | flops | bytes accessed | tf_op | source)
XLA Modules:
  0.0 135.8 jit_solution(4039351723385560420)
XLA Ops:
  4.1 3.4 %collective-permute-start.1 = (f32[16,1,1088]{2,0,1:T(8,128)}, f32[16,1,1088]{2,0,1:T(8,128)}, u32[]{:S(2)}, u32[]{:S(2)}) collective-permute-start(f32[16,1,1088]{2,0,1:T(8,128)} %pad_maximum_fusion), channel_id=1, source_target_pairs={{0,1},{1,2},{2,3},{3,4},{4,5},{5,6},{6,7},{7,8},{8,9},{9,10},{10,1... | collective-permute-start | bytes 208904 | tf_op jit(solution)/shard_map/ppermute | solution.py:107
  11.5 4.6 %collective-permute-start.3 = (f32[16,1,1024]{2,1,0:T(1,128)}, f32[16,1,1024]{2,1,0:T(1,128)}, u32[]{:S(2)}, u32[]{:S(2)}) collective-permute-start(f32[16,1,1024]{2,1,0:T(1,128)} %get-tuple-element.37), channel_id=1, source_target_pairs={{1,0},{2,1},{3,2},{4,3},{5,4},{6,5},{7,6},{8,7},{9,8},{10,9},{11,1... | collective-permute-start | bytes 196616 | tf_op jit(solution)/shard_map/ppermute | solution.py:111
  16.1 3.4 %collective-permute-start.2 = (f32[1,8,1024]{2,1,0:T(8,128)}, f32[1,8,1024]{2,1,0:T(8,128)S(1)}, u32[]{:S(2)}, u32[]{:S(2)}) collective-permute-start(f32[1,8,1024]{2,1,0:T(8,128)} %get-tuple-element.33), channel_id=1, source_target_pairs={{16,0},{32,16},{48,32},{64,48},{80,64},{96,80},{112,96},{128,112},... | collective-permute-start | bytes 98312 | tf_op jit(solution)/shard_map/ppermute | solution.py:111
  30.2 2.1 %broadcast_multiply_fusion.1 = (f32[16,16,512]{2,0,1:T(8,128)S(1)}, f32[16,16,512]{2,0,1:T(8,128)S(1)}) fusion(f32[16,512]{1,0:T(8,128)S(1)} %divide_bitcast_fusion, f32[16,16,512]{2,0,1:T(8,128)S(1)} %reshape.228, f32[512]{0:T(512)S(1)} %fusion.53, f32[16,16,511]{2,0,1:T(8,128)} %get-tuple-element.40, f32[16,512]{1,0:T(8,128)S(1)} %get-tuple-element.43, ...), kind=kLoop, calls=%fused_computation.61 | loop fusion | flops 2752512 | bytes 5507072 | tf_op jit(solution)/shard_map/mul | solution.py:178
  37.8 2.4 %collective-permute-start.6 = (f32[16,16,64]{2,0,1:T(8,128)S(1)}, f32[16,16,64]{2,0,1:T(8,128)S(1)}, u32[]{:S(2)}, u32[]{:S(2)}) collective-permute-start(f32[16,16,64]{2,0,1:T(8,128)S(1)} %get-tuple-element.27), channel_id=1, source_target_pairs={{1,0},{2,1},{3,2},{4,3},{5,4},{6,5},{7,6},{8,7},{9,8},{10,9},{11,1... | collective-permute-start | bytes 196616 | tf_op jit(solution)/shard_map/ppermute | solution.py:111
  40.3 3.4 %collective-permute-start.7 = (f32[16,16,64]{2,0,1:T(8,128)S(1)}, f32[16,16,64]{2,0,1:T(8,128)S(1)}, u32[]{:S(2)}, u32[]{:S(2)}) collective-permute-start(f32[16,16,64]{2,0,1:T(8,128)S(1)} %get-tuple-element.28), channel_id=1, source_target_pairs={{0,1},{1,2},{2,3},{3,4},{4,5},{5,6},{6,7},{7,8},{8,9},{9,10},{10,1... | collective-permute-start | bytes 196616 | tf_op jit(solution)/shard_map/ppermute | solution.py:107
  45.6 2.6 %collective-permute-start.5 = (f32[16,1,512]{2,0,1:T(8,128)S(1)}, f32[16,1,512]{2,0,1:T(8,128)S(1)}, u32[]{:S(2)}, u32[]{:S(2)}) collective-permute-start(f32[16,1,512]{2,0,1:T(8,128)S(1)} %get-tuple-element.24), channel_id=1, source_target_pairs={{0,16},{16,32},{32,48},{48,64},{64,80},{80,96},{96,112},{112,128},... | collective-permute-start | bytes 98312 | tf_op jit(solution)/shard_map/ppermute | solution.py:107
  48.4 2.5 %collective-permute-done.5 = f32[16,1,512]{2,0,1:T(8,128)S(1)} collective-permute-done((f32[16,1,512]{2,0,1:T(8,128)S(1)}, f32[16,1,512]{2,0,1:T(8,128)S(1)}, u32[]{:S(2)}, u32[]{:S(2)}) %collective-permute-start.5) | collective-permute-done | bytes 32800 | tf_op jit(solution)/shard_map/ppermute | solution.py:107
  57.8 4.6 %collective-permute-start.10 = (f32[16,16,64]{2,0,1:T(8,128)S(1)}, f32[16,16,64]{2,0,1:T(8,128)S(1)}, u32[]{:S(2)}, u32[]{:S(2)}) collective-permute-start(f32[16,16,64]{2,0,1:T(8,128)S(1)} %get-tuple-element.17), channel_id=1, source_target_pairs={{1,0},{2,1},{3,2},{4,3},{5,4},{6,5},{7,6},{8,7},{9,8},{10,9},{11,1... | collective-permute-start | bytes 196616 | tf_op jit(solution)/shard_map/ppermute | solution.py:111
  66.2 2.4 %collective-permute-start.9 = (f32[16,1,512]{2,0,1:T(8,128)S(1)}, f32[16,1,512]{2,0,1:T(8,128)S(1)}, u32[]{:S(2)}, u32[]{:S(2)}) collective-permute-start(f32[16,1,512]{2,0,1:T(8,128)S(1)} %get-tuple-element.14), channel_id=1, source_target_pairs={{0,16},{16,32},{32,48},{48,64},{64,80},{80,96},{96,112},{112,128},... | collective-permute-start | bytes 98312 | tf_op jit(solution)/shard_map/ppermute | solution.py:107
  68.8 2.7 %collective-permute-done.9 = f32[16,1,512]{2,0,1:T(8,128)S(1)} collective-permute-done((f32[16,1,512]{2,0,1:T(8,128)S(1)}, f32[16,1,512]{2,0,1:T(8,128)S(1)}, u32[]{:S(2)}, u32[]{:S(2)}) %collective-permute-start.9) | collective-permute-done | bytes 32800 | tf_op jit(solution)/shard_map/ppermute | solution.py:107
  75.6 2.0 %collective-permute-done.13 = f32[48,48]{0,1:T(8,128)S(1)} collective-permute-done((f32[48,48]{0,1:T(8,128)S(1)}, f32[48,48]{0,1:T(8,128)S(1)}, u32[]{:S(2)}, u32[]{:S(2)}) %collective-permute-start.13) | collective-permute-done | bytes 9248 | tf_op jit(solution)/shard_map/ppermute | solution.py:25
  77.7 6.6 %collective-permute-start.15 = (f32[48,48]{0,1:T(8,128)S(1)}, f32[48,48]{0,1:T(8,128)S(1)}, u32[]{:S(2)}, u32[]{:S(2)}) collective-permute-start(f32[48,48]{0,1:T(8,128)S(1)} %add_add_fusion.4), channel_id=1, source_target_pairs={{0,64},{16,80},{32,96},{48,112},{64,0},{80,16},{96,32},{112,48},{1... | collective-permute-start | bytes 27656 | tf_op jit(solution)/shard_map/ppermute | solution.py:25
  84.3 3.9 %collective-permute-start.16 = (f32[48,48]{0,1:T(8,128)S(1)}, f32[48,48]{0,1:T(8,128)S(1)}, u32[]{:S(2)}, u32[]{:S(2)}) collective-permute-start(f32[48,48]{0,1:T(8,128)S(1)} %add_add_fusion.4), channel_id=1, source_target_pairs={{0,128},{16,144},{32,160},{48,176},{64,192},{80,208},{96,224},{112... | collective-permute-start | bytes 27656 | tf_op jit(solution)/shard_map/ppermute | solution.py:25
  88.7 3.5 %collective-permute-done.16 = f32[48,48]{0,1:T(8,128)S(1)} collective-permute-done((f32[48,48]{0,1:T(8,128)S(1)}, f32[48,48]{0,1:T(8,128)S(1)}, u32[]{:S(2)}, u32[]{:S(2)}) %collective-permute-start.16) | collective-permute-done | bytes 9248 | tf_op jit(solution)/shard_map/ppermute | solution.py:25
  92.2 2.2 %collective-permute-done.17 = f32[48,48]{0,1:T(8,128)S(1)} collective-permute-done((f32[48,48]{0,1:T(8,128)S(1)}, f32[48,48]{0,1:T(8,128)S(1)}, u32[]{:S(2)}, u32[]{:S(2)}) %collective-permute-start.17) | collective-permute-done | bytes 9248 | tf_op jit(solution)/shard_map/ppermute | solution.py:25
  94.5 5.7 %collective-permute-start.19 = (f32[48,48]{0,1:T(8,128)S(1)}, f32[48,48]{0,1:T(8,128)S(1)}, u32[]{:S(2)}, u32[]{:S(2)}) collective-permute-start(f32[48,48]{0,1:T(8,128)S(1)} %add_add_fusion.3), channel_id=1, source_target_pairs={{0,2},{1,3},{2,0},{3,1},{4,6},{5,7},{6,4},{7,5},{8,10},{9,11},{10,... | collective-permute-start | bytes 27656 | tf_op jit(solution)/shard_map/ppermute | solution.py:25
  100.2 2.1 %collective-permute-done.19 = f32[48,48]{0,1:T(8,128)S(1)} collective-permute-done((f32[48,48]{0,1:T(8,128)S(1)}, f32[48,48]{0,1:T(8,128)S(1)}, u32[]{:S(2)}, u32[]{:S(2)}) %collective-permute-start.19) | collective-permute-done | bytes 9248 | tf_op jit(solution)/shard_map/ppermute | solution.py:25
  102.3 3.0 %collective-permute-done.20 = f32[48,48]{0,1:T(8,128)S(1)} collective-permute-done((f32[48,48]{0,1:T(8,128)S(1)}, f32[48,48]{0,1:T(8,128)S(1)}, u32[]{:S(2)}, u32[]{:S(2)}) %collective-permute-start.20) | collective-permute-done | bytes 9248 | tf_op jit(solution)/shard_map/ppermute | solution.py:25
  105.8 2.6 %collective-permute-start.22 = (f32[48,48]{0,1:T(8,128)S(1)}, f32[48,48]{0,1:T(8,128)S(1)}, u32[]{:S(2)}, u32[]{:S(2)}) collective-permute-start(f32[48,48]{0,1:T(8,128)S(1)} %add_add_fusion.2), channel_id=1, source_target_pairs={{0,8},{1,9},{2,10},{3,11},{4,12},{5,13},{6,14},{7,15},{8,0},{9,1},... | collective-permute-start | bytes 27656 | tf_op jit(solution)/shard_map/ppermute | solution.py:25
  112.3 4.4 %cholesky.31 = f32[48,48]{1,0:T(8,128)S(1)} custom-call(f32[48,48]{1,0:T(8,128)S(1)} %fusion.29), custom_call_target="Cholesky" | custom-call | tf_op jit(solution)/shard_map/jit(cholesky)/cholesky | solution.py:215
  118.7 2.4 %custom-call.14 = f32[1,32,32]{1,2,0:T(8,128)S(1)} custom-call(f32[1,32,32]{2,1,0:T(8,128)S(1)} %fusion.39), custom_call_target="InvertDiagBlocksLowerTriangular" | custom-call | tf_op jit(solution)/shard_map/triangular_solve | solution.py:218
  122.1 2.9 %cholesky.59 = f32[32,32]{1,0:T(8,128)S(1)} custom-call(f32[32,32]{1,0:T(8,128)S(1)} %fusion.44), custom_call_target="Cholesky" | custom-call | tf_op jit(solution)/shard_map/jit(cholesky)/cholesky | solution.py:60
  126.3 2.4 %custom-call.15 = f32[1,32,32]{1,2,0:T(8,128)S(1)} custom-call(f32[1,32,32]{2,1,0:T(8,128)S(1)} %fusion.36), custom_call_target="InvertDiagBlocksLowerTriangular" | custom-call | tf_op jit(solution)/shard_map/triangular_solve | solution.py:62
  (194 shorter events, 56.6 us)
Async XLA Ops:
  4.1 23.3 %collective-permute-start.1 = (f32[16,1,1088]{2,0,1:T(8,128)}, f32[16,1,1088]{2,0,1:T(8,128)}, u32[]{:S(2)}, u32[]{:S(2)}) collective-permute-start(f32[16,1,1088]{2,0,1:T(8,128)} %pad_maximum_fusion), channel_id=1, source_target_pairs={{0,1},{1,2},{2,3},{3,4},{4,5},{5,6},{6,7},{7,8},{8,9},{9,10},{10,1... | collective-permute-start | bytes 208904 | tf_op jit(solution)/shard_map/ppermute | solution.py:107
  9.6 16.4 %collective-permute-start = (f32[1,8,1088]{2,1,0:T(8,128)S(1)}, f32[1,8,1088]{2,1,0:T(8,128)S(1)}, u32[]{:S(2)}, u32[]{:S(2)}) collective-permute-start(f32[1,8,1088]{2,1,0:T(8,128)S(1)} %pad_maximum_fusion.1), channel_id=1, source_target_pairs={{0,16},{16,32},{32,48},{48,64},{64,80},{80,96},{96,112},{112,128},... | collective-permute-start | bytes 104456 | tf_op jit(solution)/shard_map/ppermute | solution.py:107
  11.5 14.8 %collective-permute-start.3 = (f32[16,1,1024]{2,1,0:T(1,128)}, f32[16,1,1024]{2,1,0:T(1,128)}, u32[]{:S(2)}, u32[]{:S(2)}) collective-permute-start(f32[16,1,1024]{2,1,0:T(1,128)} %get-tuple-element.37), channel_id=1, source_target_pairs={{1,0},{2,1},{3,2},{4,3},{5,4},{6,5},{7,6},{8,7},{9,8},{10,9},{11,1... | collective-permute-start | bytes 196616 | tf_op jit(solution)/shard_map/ppermute | solution.py:111
  16.1 9.7 %collective-permute-start.2 = (f32[1,8,1024]{2,1,0:T(8,128)}, f32[1,8,1024]{2,1,0:T(8,128)S(1)}, u32[]{:S(2)}, u32[]{:S(2)}) collective-permute-start(f32[1,8,1024]{2,1,0:T(8,128)} %get-tuple-element.33), channel_id=1, source_target_pairs={{16,0},{32,16},{48,32},{64,48},{80,64},{96,80},{112,96},{128,112},... | collective-permute-start | bytes 98312 | tf_op jit(solution)/shard_map/ppermute | solution.py:111
  37.8 13.0 %collective-permute-start.6 = (f32[16,16,64]{2,0,1:T(8,128)S(1)}, f32[16,16,64]{2,0,1:T(8,128)S(1)}, u32[]{:S(2)}, u32[]{:S(2)}) collective-permute-start(f32[16,16,64]{2,0,1:T(8,128)S(1)} %get-tuple-element.27), channel_id=1, source_target_pairs={{1,0},{2,1},{3,2},{4,3},{5,4},{6,5},{7,6},{8,7},{9,8},{10,9},{11,1... | collective-permute-start | bytes 196616 | tf_op jit(solution)/shard_map/ppermute | solution.py:111
  40.3 10.6 %collective-permute-start.7 = (f32[16,16,64]{2,0,1:T(8,128)S(1)}, f32[16,16,64]{2,0,1:T(8,128)S(1)}, u32[]{:S(2)}, u32[]{:S(2)}) collective-permute-start(f32[16,16,64]{2,0,1:T(8,128)S(1)} %get-tuple-element.28), channel_id=1, source_target_pairs={{0,1},{1,2},{2,3},{3,4},{4,5},{5,6},{6,7},{7,8},{8,9},{9,10},{10,1... | collective-permute-start | bytes 196616 | tf_op jit(solution)/shard_map/ppermute | solution.py:107
  43.7 4.6 %collective-permute-start.4 = (f32[16,1,512]{2,0,1:T(8,128)S(1)}, f32[16,1,512]{2,0,1:T(8,128)S(1)}, u32[]{:S(2)}, u32[]{:S(2)}) collective-permute-start(f32[16,1,512]{2,0,1:T(8,128)S(1)} %get-tuple-element.23), channel_id=1, source_target_pairs={{16,0},{32,16},{48,32},{64,48},{80,64},{96,80},{112,96},{128,112},... | collective-permute-start | bytes 98312 | tf_op jit(solution)/shard_map/ppermute | solution.py:111
  45.6 5.2 %collective-permute-start.5 = (f32[16,1,512]{2,0,1:T(8,128)S(1)}, f32[16,1,512]{2,0,1:T(8,128)S(1)}, u32[]{:S(2)}, u32[]{:S(2)}) collective-permute-start(f32[16,1,512]{2,0,1:T(8,128)S(1)} %get-tuple-element.24), channel_id=1, source_target_pairs={{0,16},{16,32},{32,48},{48,64},{64,80},{80,96},{96,112},{112,128},... | collective-permute-start | bytes 98312 | tf_op jit(solution)/shard_map/ppermute | solution.py:107
  57.8 13.7 %collective-permute-start.10 = (f32[16,16,64]{2,0,1:T(8,128)S(1)}, f32[16,16,64]{2,0,1:T(8,128)S(1)}, u32[]{:S(2)}, u32[]{:S(2)}) collective-permute-start(f32[16,16,64]{2,0,1:T(8,128)S(1)} %get-tuple-element.17), channel_id=1, source_target_pairs={{1,0},{2,1},{3,2},{4,3},{5,4},{6,5},{7,6},{8,7},{9,8},{10,9},{11,1... | collective-permute-start | bytes 196616 | tf_op jit(solution)/shard_map/ppermute | solution.py:111
  62.4 9.1 %collective-permute-start.11 = (f32[16,16,64]{2,0,1:T(8,128)S(1)}, f32[16,16,64]{2,0,1:T(8,128)S(1)}, u32[]{:S(2)}, u32[]{:S(2)}) collective-permute-start(f32[16,16,64]{2,0,1:T(8,128)S(1)} %get-tuple-element.18), channel_id=1, source_target_pairs={{0,1},{1,2},{2,3},{3,4},{4,5},{5,6},{6,7},{7,8},{8,9},{9,10},{10,1... | collective-permute-start | bytes 196616 | tf_op jit(solution)/shard_map/ppermute | solution.py:107
  64.3 4.5 %collective-permute-start.8 = (f32[16,1,512]{2,0,1:T(8,128)S(1)}, f32[16,1,512]{2,0,1:T(8,128)S(1)}, u32[]{:S(2)}, u32[]{:S(2)}) collective-permute-start(f32[16,1,512]{2,0,1:T(8,128)S(1)} %get-tuple-element.13), channel_id=1, source_target_pairs={{16,0},{32,16},{48,32},{64,48},{80,64},{96,80},{112,96},{128,112},... | collective-permute-start | bytes 98312 | tf_op jit(solution)/shard_map/ppermute | solution.py:111
  66.2 5.2 %collective-permute-start.9 = (f32[16,1,512]{2,0,1:T(8,128)S(1)}, f32[16,1,512]{2,0,1:T(8,128)S(1)}, u32[]{:S(2)}, u32[]{:S(2)}) collective-permute-start(f32[16,1,512]{2,0,1:T(8,128)S(1)} %get-tuple-element.14), channel_id=1, source_target_pairs={{0,16},{16,32},{32,48},{48,64},{64,80},{80,96},{96,112},{112,128},... | collective-permute-start | bytes 98312 | tf_op jit(solution)/shard_map/ppermute | solution.py:107
  73.6 2.0 %collective-permute-start.12 = (f32[48,48]{0,1:T(8,128)S(1)}, f32[48,48]{0,1:T(8,128)S(1)}, u32[]{:S(2)}, u32[]{:S(2)}) collective-permute-start(f32[48,48]{0,1:T(8,128)S(1)} %fusion.6), channel_id=1, source_target_pairs={{0,16},{16,0},{32,48},{48,32},{64,80},{80,64},{96,112},{112,96},{1... | collective-permute-start | bytes 27656 | tf_op jit(solution)/shard_map/ppermute | solution.py:25
  73.7 3.9 %collective-permute-start.13 = (f32[48,48]{0,1:T(8,128)S(1)}, f32[48,48]{0,1:T(8,128)S(1)}, u32[]{:S(2)}, u32[]{:S(2)}) collective-permute-start(f32[48,48]{0,1:T(8,128)S(1)} %fusion.6), channel_id=1, source_target_pairs={{0,32},{16,48},{32,0},{48,16},{64,96},{80,112},{96,64},{112,80},{1... | collective-permute-start | bytes 27656 | tf_op jit(solution)/shard_map/ppermute | solution.py:25
  73.8 3.8 %collective-permute-start.14 = (f32[48,48]{0,1:T(8,128)S(1)}, f32[48,48]{0,1:T(8,128)S(1)}, u32[]{:S(2)}, u32[]{:S(2)}) collective-permute-start(f32[48,48]{0,1:T(8,128)S(1)} %fusion.6), channel_id=1, source_target_pairs={{0,48},{16,32},{32,16},{48,0},{64,112},{80,96},{96,80},{112,64},{1... | collective-permute-start | bytes 27656 | tf_op jit(solution)/shard_map/ppermute | solution.py:25
  77.7 11.0 %collective-permute-start.15 = (f32[48,48]{0,1:T(8,128)S(1)}, f32[48,48]{0,1:T(8,128)S(1)}, u32[]{:S(2)}, u32[]{:S(2)}) collective-permute-start(f32[48,48]{0,1:T(8,128)S(1)} %add_add_fusion.4), channel_id=1, source_target_pairs={{0,64},{16,80},{32,96},{48,112},{64,0},{80,16},{96,32},{112,48},{1... | collective-permute-start | bytes 27656 | tf_op jit(solution)/shard_map/ppermute | solution.py:25
  84.3 7.9 %collective-permute-start.16 = (f32[48,48]{0,1:T(8,128)S(1)}, f32[48,48]{0,1:T(8,128)S(1)}, u32[]{:S(2)}, u32[]{:S(2)}) collective-permute-start(f32[48,48]{0,1:T(8,128)S(1)} %add_add_fusion.4), channel_id=1, source_target_pairs={{0,128},{16,144},{32,160},{48,176},{64,192},{80,208},{96,224},{112... | collective-permute-start | bytes 27656 | tf_op jit(solution)/shard_map/ppermute | solution.py:25
  88.2 6.2 %collective-permute-start.17 = (f32[48,48]{0,1:T(8,128)S(1)}, f32[48,48]{0,1:T(8,128)S(1)}, u32[]{:S(2)}, u32[]{:S(2)}) collective-permute-start(f32[48,48]{0,1:T(8,128)S(1)} %add_add_fusion.4), channel_id=1, source_target_pairs={{0,192},{16,208},{32,224},{48,240},{64,128},{80,144},{96,160},{112... | collective-permute-start | bytes 27656 | tf_op jit(solution)/shard_map/ppermute | solution.py:25
  94.4 5.8 %collective-permute-start.18 = (f32[48,48]{0,1:T(8,128)S(1)}, f32[48,48]{0,1:T(8,128)S(1)}, u32[]{:S(2)}, u32[]{:S(2)}) collective-permute-start(f32[48,48]{0,1:T(8,128)S(1)} %add_add_fusion.3), channel_id=1, source_target_pairs={{0,1},{1,0},{2,3},{3,2},{4,5},{5,4},{6,7},{7,6},{8,9},{9,8},{10,11... | collective-permute-start | bytes 27656 | tf_op jit(solution)/shard_map/ppermute | solution.py:25
  94.5 7.8 %collective-permute-start.19 = (f32[48,48]{0,1:T(8,128)S(1)}, f32[48,48]{0,1:T(8,128)S(1)}, u32[]{:S(2)}, u32[]{:S(2)}) collective-permute-start(f32[48,48]{0,1:T(8,128)S(1)} %add_add_fusion.3), channel_id=1, source_target_pairs={{0,2},{1,3},{2,0},{3,1},{4,6},{5,7},{6,4},{7,5},{8,10},{9,11},{10,... | collective-permute-start | bytes 27656 | tf_op jit(solution)/shard_map/ppermute | solution.py:25
  100.2 5.0 %collective-permute-start.20 = (f32[48,48]{0,1:T(8,128)S(1)}, f32[48,48]{0,1:T(8,128)S(1)}, u32[]{:S(2)}, u32[]{:S(2)}) collective-permute-start(f32[48,48]{0,1:T(8,128)S(1)} %add_add_fusion.3), channel_id=1, source_target_pairs={{0,3},{1,2},{2,1},{3,0},{4,7},{5,6},{6,5},{7,4},{8,11},{9,10},{10,... | collective-permute-start | bytes 27656 | tf_op jit(solution)/shard_map/ppermute | solution.py:25
  105.3 3.9 %collective-permute-start.21 = (f32[48,48]{0,1:T(8,128)S(1)}, f32[48,48]{0,1:T(8,128)S(1)}, u32[]{:S(2)}, u32[]{:S(2)}) collective-permute-start(f32[48,48]{0,1:T(8,128)S(1)} %add_add_fusion.2), channel_id=1, source_target_pairs={{0,4},{1,5},{2,6},{3,7},{4,0},{5,1},{6,2},{7,3},{8,12},{9,13},{10,... | collective-permute-start | bytes 27656 | tf_op jit(solution)/shard_map/ppermute | solution.py:25
  105.8 5.3 %collective-permute-start.22 = (f32[48,48]{0,1:T(8,128)S(1)}, f32[48,48]{0,1:T(8,128)S(1)}, u32[]{:S(2)}, u32[]{:S(2)}) collective-permute-start(f32[48,48]{0,1:T(8,128)S(1)} %add_add_fusion.2), channel_id=1, source_target_pairs={{0,8},{1,9},{2,10},{3,11},{4,12},{5,13},{6,14},{7,15},{8,0},{9,1},... | collective-permute-start | bytes 27656 | tf_op jit(solution)/shard_map/ppermute | solution.py:25
  108.4 3.8 %collective-permute-start.23 = (f32[48,48]{0,1:T(8,128)S(1)}, f32[48,48]{0,1:T(8,128)S(1)}, u32[]{:S(2)}, u32[]{:S(2)}) collective-permute-start(f32[48,48]{0,1:T(8,128)S(1)} %add_add_fusion.2), channel_id=1, source_target_pairs={{0,12},{1,13},{2,14},{3,15},{4,8},{5,9},{6,10},{7,11},{8,4},{9,5},... | collective-permute-start | bytes 27656 | tf_op jit(solution)/shard_map/ppermute | solution.py:25
  (12 other events, 40.6 us)

commit v7 on v5

--- a/solution.py
+++ b/solution.py
@@ -13,7 +13,7 @@
 
 
 def mesh_sum(block):
-    for axis in ("gx", "gy"):
+    for axis in ("gy", "gx"):
         count = lax.axis_size(axis)
         if count & (count - 1):
             block = lax.psum(block, axis)

time: 134 us -> 134 us (level)
  no operation moved by 1% of the time
where the time goes in v7:
time: 134 us; the launch traced here: 132 us
  starting transfers between devices  56.8 us (42%)
  other arithmetic  26 us (19%)
  waiting for transfers between devices  21.5 us (16%)
  local copies, waits for them, and re-layouts  20.2 us (15%)
  matrix products  6.07 us (5%)
  between operations  1.56 us (1%)
    ppermute x12, starting transfers between devices, mesh_sum(): lax.ppermute(block, axis, [(i, i ^ step * m) for i in range(count)])  22.5 us
    ppermute x6, starting transfers between devices, backward(): return lax.ppermute(block, axis, [(i + 1, i) for i in range(count - 1)])  18.8 us
    ppermute x12, waiting for transfers between devices, mesh_sum(): lax.ppermute(block, axis, [(i, i ^ step * m) for i in range(count)])  16.3 us
    ppermute x6, starting transfers between devices, forward(): return lax.ppermute(block, axis, [(i, i + 1) for i in range(count - 1)])  15.6 us
    ppermute x6, waiting for transfers between devices, forward(): return lax.ppermute(block, axis, [(i, i + 1) for i in range(count - 1)])  5.21 us
    slice x27, local copies, waits for them, and re-layouts, up_along(): lax.slice_in_dim(values, width, count, axis=axis)  5.1 us
    another operation x3, other arithmetic, body(): full_low = jnp.linalg.cholesky(span_gram)  5.05 us
    another operation x3, other arithmetic, solve_small(): low_factor = jnp.linalg.cholesky(normal)  3.6 us
  transfers between devices with their start and end apart: 24, of which 10 were waited for; matrix products, arithmetic and copies ran while one was open for 8% of the time, Pallas kernels for 0%

profile of v7, /device:TPU:40, one launch (start us, length us, event | category | flops | bytes accessed | tf_op | source)
XLA Modules:
  0.0 132.2 jit_solution(5352032144597181419)
XLA Ops:
  3.3 3.4 %collective-permute-start.1 = (f32[17,16,64]{2,0,1:T(8,128)S(1)}, f32[17,16,64]{2,0,1:T(8,128)}, u32[]{:S(2)}, u32[]{:S(2)}) collective-permute-start(f32[17,16,64]{2,0,1:T(8,128)S(1)} %pad_maximum_fusion), channel_id=1, source_target_pairs={{0,1},{1,2},{2,3},{3,4},{4,5},{5,6},{6,7},{7,8},{8,9},{9,10},{10,1... | collective-permute-start | bytes 208904 | tf_op jit(solution)/shard_map/ppermute | solution.py:107
  7.5 1.9 %collective-permute-start = (f32[17,1,512]{2,0,1:T(8,128)S(1)}, f32[17,1,512]{2,0,1:T(8,128)}, u32[]{:S(2)}, u32[]{:S(2)}) collective-permute-start(f32[17,1,512]{2,0,1:T(8,128)S(1)} %pad_maximum_fusion.1), channel_id=1, source_target_pairs={{0,16},{16,32},{32,48},{48,64},{64,80},{80,96},{96,112},{112,128},... | collective-permute-start | bytes 104456 | tf_op jit(solution)/shard_map/ppermute | solution.py:107
  9.4 4.6 %collective-permute-start.3 = (f32[16,16,64]{2,0,1:T(8,128)S(1)}, f32[16,16,64]{2,0,1:T(8,128)}, u32[]{:S(2)}, u32[]{:S(2)}) collective-permute-start(f32[16,16,64]{2,0,1:T(8,128)S(1)} %get-tuple-element.39), channel_id=1, source_target_pairs={{1,0},{2,1},{3,2},{4,3},{5,4},{6,5},{7,6},{8,7},{9,8},{10,9},{11,1... | collective-permute-start | bytes 196616 | tf_op jit(solution)/shard_map/ppermute | solution.py:111
  14.0 3.4 %collective-permute-start.2 = (f32[16,1,512]{2,0,1:T(8,128)}, f32[16,1,512]{2,0,1:T(8,128)S(1)}, u32[]{:S(2)}, u32[]{:S(2)}) collective-permute-start(f32[16,1,512]{2,0,1:T(8,128)} %get-tuple-element.35), channel_id=1, source_target_pairs={{16,0},{32,16},{48,32},{64,48},{80,64},{96,80},{112,96},{128,112},... | collective-permute-start | bytes 98312 | tf_op jit(solution)/shard_map/ppermute | solution.py:111
  34.7 2.4 %collective-permute-start.6 = (f32[16,16,64]{2,0,1:T(8,128)S(1)}, f32[16,16,64]{2,0,1:T(8,128)S(1)}, u32[]{:S(2)}, u32[]{:S(2)}) collective-permute-start(f32[16,16,64]{2,0,1:T(8,128)S(1)} %get-tuple-element.29), channel_id=1, source_target_pairs={{1,0},{2,1},{3,2},{4,3},{5,4},{6,5},{7,6},{8,7},{9,8},{10,9},{11,1... | collective-permute-start | bytes 196616 | tf_op jit(solution)/shard_map/ppermute | solution.py:111
  37.2 3.4 %collective-permute-start.7 = (f32[16,16,64]{2,0,1:T(8,128)S(1)}, f32[16,16,64]{2,0,1:T(8,128)S(1)}, u32[]{:S(2)}, u32[]{:S(2)}) collective-permute-start(f32[16,16,64]{2,0,1:T(8,128)S(1)} %get-tuple-element.30), channel_id=1, source_target_pairs={{0,1},{1,2},{2,3},{3,4},{4,5},{5,6},{6,7},{7,8},{8,9},{9,10},{10,1... | collective-permute-start | bytes 196616 | tf_op jit(solution)/shard_map/ppermute | solution.py:107
  42.5 2.6 %collective-permute-start.5 = (f32[16,1,512]{2,0,1:T(8,128)S(1)}, f32[16,1,512]{2,0,1:T(8,128)S(1)}, u32[]{:S(2)}, u32[]{:S(2)}) collective-permute-start(f32[16,1,512]{2,0,1:T(8,128)S(1)} %get-tuple-element.26), channel_id=1, source_target_pairs={{0,16},{16,32},{32,48},{48,64},{64,80},{80,96},{96,112},{112,128},... | collective-permute-start | bytes 98312 | tf_op jit(solution)/shard_map/ppermute | solution.py:107
  45.3 2.5 %collective-permute-done.5 = f32[16,1,512]{2,0,1:T(8,128)S(1)} collective-permute-done((f32[16,1,512]{2,0,1:T(8,128)S(1)}, f32[16,1,512]{2,0,1:T(8,128)S(1)}, u32[]{:S(2)}, u32[]{:S(2)}) %collective-permute-start.5) | collective-permute-done | bytes 32800 | tf_op jit(solution)/shard_map/ppermute | solution.py:107
  54.0 4.6 %collective-permute-start.10 = (f32[16,16,64]{2,0,1:T(8,128)S(1)}, f32[16,16,64]{2,0,1:T(8,128)S(1)}, u32[]{:S(2)}, u32[]{:S(2)}) collective-permute-start(f32[16,16,64]{2,0,1:T(8,128)S(1)} %get-tuple-element.19), channel_id=1, source_target_pairs={{1,0},{2,1},{3,2},{4,3},{5,4},{6,5},{7,6},{8,7},{9,8},{10,9},{11,1... | collective-permute-start | bytes 196616 | tf_op jit(solution)/shard_map/ppermute | solution.py:111
  62.5 2.4 %collective-permute-start.9 = (f32[16,1,512]{2,0,1:T(8,128)S(1)}, f32[16,1,512]{2,0,1:T(8,128)S(1)}, u32[]{:S(2)}, u32[]{:S(2)}) collective-permute-start(f32[16,1,512]{2,0,1:T(8,128)S(1)} %get-tuple-element.16), channel_id=1, source_target_pairs={{0,16},{16,32},{32,48},{48,64},{64,80},{80,96},{96,112},{112,128},... | collective-permute-start | bytes 98312 | tf_op jit(solution)/shard_map/ppermute | solution.py:107
  65.0 2.7 %collective-permute-done.9 = f32[16,1,512]{2,0,1:T(8,128)S(1)} collective-permute-done((f32[16,1,512]{2,0,1:T(8,128)S(1)}, f32[16,1,512]{2,0,1:T(8,128)S(1)}, u32[]{:S(2)}, u32[]{:S(2)}) %collective-permute-start.9) | collective-permute-done | bytes 32800 | tf_op jit(solution)/shard_map/ppermute | solution.py:107
  70.0 5.7 %collective-permute-start.13 = (f32[48,48]{0,1:T(8,128)S(1)}, f32[48,48]{0,1:T(8,128)S(1)}, u32[]{:S(2)}, u32[]{:S(2)}) collective-permute-start(f32[48,48]{0,1:T(8,128)S(1)} %fusion.6), channel_id=1, source_target_pairs={{0,2},{1,3},{2,0},{3,1},{4,6},{5,7},{6,4},{7,5},{8,10},{9,11},{10,... | collective-permute-start | bytes 27656 | tf_op jit(solution)/shard_map/ppermute | solution.py:25
  75.7 2.1 %collective-permute-done.13 = f32[48,48]{0,1:T(8,128)S(1)} collective-permute-done((f32[48,48]{0,1:T(8,128)S(1)}, f32[48,48]{0,1:T(8,128)S(1)}, u32[]{:S(2)}, u32[]{:S(2)}) %collective-permute-start.13) | collective-permute-done | bytes 9248 | tf_op jit(solution)/shard_map/ppermute | solution.py:25
  77.7 3.0 %collective-permute-done.14 = f32[48,48]{0,1:T(8,128)S(1)} collective-permute-done((f32[48,48]{0,1:T(8,128)S(1)}, f32[48,48]{0,1:T(8,128)S(1)}, u32[]{:S(2)}, u32[]{:S(2)}) %collective-permute-start.14) | collective-permute-done | bytes 9248 | tf_op jit(solution)/shard_map/ppermute | solution.py:25
  81.2 2.6 %collective-permute-start.16 = (f32[48,48]{0,1:T(8,128)S(1)}, f32[48,48]{0,1:T(8,128)S(1)}, u32[]{:S(2)}, u32[]{:S(2)}) collective-permute-start(f32[48,48]{0,1:T(8,128)S(1)} %add_add_fusion.4), channel_id=1, source_target_pairs={{0,8},{1,9},{2,10},{3,11},{4,12},{5,13},{6,14},{7,15},{8,0},{9,1},... | collective-permute-start | bytes 27656 | tf_op jit(solution)/shard_map/ppermute | solution.py:25
  84.6 1.9 %collective-permute-done.16 = f32[48,48]{0,1:T(8,128)S(1)} collective-permute-done((f32[48,48]{0,1:T(8,128)S(1)}, f32[48,48]{0,1:T(8,128)S(1)}, u32[]{:S(2)}, u32[]{:S(2)}) %collective-permute-start.16) | collective-permute-done | bytes 9248 | tf_op jit(solution)/shard_map/ppermute | solution.py:25
  89.6 2.3 %collective-permute-done.19 = f32[48,48]{0,1:T(8,128)S(1)} collective-permute-done((f32[48,48]{0,1:T(8,128)S(1)}, f32[48,48]{0,1:T(8,128)S(1)}, u32[]{:S(2)}, u32[]{:S(2)}) %collective-permute-start.19) | collective-permute-done | bytes 9248 | tf_op jit(solution)/shard_map/ppermute | solution.py:25
  91.9 3.5 %collective-permute-start.21 = (f32[48,48]{0,1:T(8,128)S(1)}, f32[48,48]{0,1:T(8,128)S(1)}, u32[]{:S(2)}, u32[]{:S(2)}) collective-permute-start(f32[48,48]{0,1:T(8,128)S(1)} %add_add_fusion.2), channel_id=1, source_target_pairs={{0,64},{16,80},{32,96},{48,112},{64,0},{80,16},{96,32},{112,48},{1... | collective-permute-start | bytes 27656 | tf_op jit(solution)/shard_map/ppermute | solution.py:25
  95.4 7.2 %collective-permute-start.22 = (f32[48,48]{0,1:T(8,128)S(1)}, f32[48,48]{0,1:T(8,128)S(1)}, u32[]{:S(2)}, u32[]{:S(2)}) collective-permute-start(f32[48,48]{0,1:T(8,128)S(1)} %add_add_fusion.2), channel_id=1, source_target_pairs={{0,128},{16,144},{32,160},{48,176},{64,192},{80,208},{96,224},{112... | collective-permute-start | bytes 27656 | tf_op jit(solution)/shard_map/ppermute | solution.py:25
  104.4 4.2 %collective-permute-done.23 = f32[48,48]{0,1:T(8,128)S(1)} collective-permute-done((f32[48,48]{0,1:T(8,128)S(1)}, f32[48,48]{0,1:T(8,128)S(1)}, u32[]{:S(2)}, u32[]{:S(2)}) %collective-permute-start.23) | collective-permute-done | bytes 9248 | tf_op jit(solution)/shard_map/ppermute | solution.py:25
  108.8 4.4 %cholesky.31 = f32[48,48]{1,0:T(8,128)S(1)} custom-call(f32[48,48]{1,0:T(8,128)S(1)} %fusion.28), custom_call_target="Cholesky" | custom-call | tf_op jit(solution)/shard_map/jit(cholesky)/cholesky | solution.py:211
  115.2 2.4 %custom-call.14 = f32[1,32,32]{1,2,0:T(8,128)S(1)} custom-call(f32[1,32,32]{2,1,0:T(8,128)S(1)} %fusion.36), custom_call_target="InvertDiagBlocksLowerTriangular" | custom-call | tf_op jit(solution)/shard_map/triangular_solve | solution.py:214
  118.5 2.9 %cholesky.59 = f32[32,32]{1,0:T(8,128)S(1)} custom-call(f32[32,32]{1,0:T(8,128)S(1)} %fusion.41), custom_call_target="Cholesky" | custom-call | tf_op jit(solution)/shard_map/jit(cholesky)/cholesky | solution.py:60
  122.7 2.4 %custom-call.15 = f32[1,32,32]{1,2,0:T(8,128)S(1)} custom-call(f32[1,32,32]{2,1,0:T(8,128)S(1)} %fusion.33), custom_call_target="InvertDiagBlocksLowerTriangular" | custom-call | tf_op jit(solution)/shard_map/triangular_solve | solution.py:62
  (193 shorter events, 52.1 us)
Async XLA Ops:
  3.3 20.8 %collective-permute-start.1 = (f32[17,16,64]{2,0,1:T(8,128)S(1)}, f32[17,16,64]{2,0,1:T(8,128)}, u32[]{:S(2)}, u32[]{:S(2)}) collective-permute-start(f32[17,16,64]{2,0,1:T(8,128)S(1)} %pad_maximum_fusion), channel_id=1, source_target_pairs={{0,1},{1,2},{2,3},{3,4},{4,5},{5,6},{6,7},{7,8},{8,9},{9,10},{10,1... | collective-permute-start | bytes 208904 | tf_op jit(solution)/shard_map/ppermute | solution.py:107
  7.5 15.1 %collective-permute-start = (f32[17,1,512]{2,0,1:T(8,128)S(1)}, f32[17,1,512]{2,0,1:T(8,128)}, u32[]{:S(2)}, u32[]{:S(2)}) collective-permute-start(f32[17,1,512]{2,0,1:T(8,128)S(1)} %pad_maximum_fusion.1), channel_id=1, source_target_pairs={{0,16},{16,32},{32,48},{48,64},{64,80},{80,96},{96,112},{112,128},... | collective-permute-start | bytes 104456 | tf_op jit(solution)/shard_map/ppermute | solution.py:107
  9.4 17.9 %collective-permute-start.3 = (f32[16,16,64]{2,0,1:T(8,128)S(1)}, f32[16,16,64]{2,0,1:T(8,128)}, u32[]{:S(2)}, u32[]{:S(2)}) collective-permute-start(f32[16,16,64]{2,0,1:T(8,128)S(1)} %get-tuple-element.39), channel_id=1, source_target_pairs={{1,0},{2,1},{3,2},{4,3},{5,4},{6,5},{7,6},{8,7},{9,8},{10,9},{11,1... | collective-permute-start | bytes 196616 | tf_op jit(solution)/shard_map/ppermute | solution.py:111
  14.0 13.3 %collective-permute-start.2 = (f32[16,1,512]{2,0,1:T(8,128)}, f32[16,1,512]{2,0,1:T(8,128)S(1)}, u32[]{:S(2)}, u32[]{:S(2)}) collective-permute-start(f32[16,1,512]{2,0,1:T(8,128)} %get-tuple-element.35), channel_id=1, source_target_pairs={{16,0},{32,16},{48,32},{64,48},{80,64},{96,80},{112,96},{128,112},... | collective-permute-start | bytes 98312 | tf_op jit(solution)/shard_map/ppermute | solution.py:111
  34.7 13.0 %collective-permute-start.6 = (f32[16,16,64]{2,0,1:T(8,128)S(1)}, f32[16,16,64]{2,0,1:T(8,128)S(1)}, u32[]{:S(2)}, u32[]{:S(2)}) collective-permute-start(f32[16,16,64]{2,0,1:T(8,128)S(1)} %get-tuple-element.29), channel_id=1, source_target_pairs={{1,0},{2,1},{3,2},{4,3},{5,4},{6,5},{7,6},{8,7},{9,8},{10,9},{11,1... | collective-permute-start | bytes 196616 | tf_op jit(solution)/shard_map/ppermute | solution.py:111
  37.2 10.6 %collective-permute-start.7 = (f32[16,16,64]{2,0,1:T(8,128)S(1)}, f32[16,16,64]{2,0,1:T(8,128)S(1)}, u32[]{:S(2)}, u32[]{:S(2)}) collective-permute-start(f32[16,16,64]{2,0,1:T(8,128)S(1)} %get-tuple-element.30), channel_id=1, source_target_pairs={{0,1},{1,2},{2,3},{3,4},{4,5},{5,6},{6,7},{7,8},{8,9},{9,10},{10,1... | collective-permute-start | bytes 196616 | tf_op jit(solution)/shard_map/ppermute | solution.py:107
  40.6 4.6 %collective-permute-start.4 = (f32[16,1,512]{2,0,1:T(8,128)S(1)}, f32[16,1,512]{2,0,1:T(8,128)S(1)}, u32[]{:S(2)}, u32[]{:S(2)}) collective-permute-start(f32[16,1,512]{2,0,1:T(8,128)S(1)} %get-tuple-element.25), channel_id=1, source_target_pairs={{16,0},{32,16},{48,32},{64,48},{80,64},{96,80},{112,96},{128,112},... | collective-permute-start | bytes 98312 | tf_op jit(solution)/shard_map/ppermute | solution.py:111
  42.5 5.2 %collective-permute-start.5 = (f32[16,1,512]{2,0,1:T(8,128)S(1)}, f32[16,1,512]{2,0,1:T(8,128)S(1)}, u32[]{:S(2)}, u32[]{:S(2)}) collective-permute-start(f32[16,1,512]{2,0,1:T(8,128)S(1)} %get-tuple-element.26), channel_id=1, source_target_pairs={{0,16},{16,32},{32,48},{48,64},{64,80},{80,96},{96,112},{112,128},... | collective-permute-start | bytes 98312 | tf_op jit(solution)/shard_map/ppermute | solution.py:107
  54.0 13.7 %collective-permute-start.10 = (f32[16,16,64]{2,0,1:T(8,128)S(1)}, f32[16,16,64]{2,0,1:T(8,128)S(1)}, u32[]{:S(2)}, u32[]{:S(2)}) collective-permute-start(f32[16,16,64]{2,0,1:T(8,128)S(1)} %get-tuple-element.19), channel_id=1, source_target_pairs={{1,0},{2,1},{3,2},{4,3},{5,4},{6,5},{7,6},{8,7},{9,8},{10,9},{11,1... | collective-permute-start | bytes 196616 | tf_op jit(solution)/shard_map/ppermute | solution.py:111
  58.6 9.1 %collective-permute-start.11 = (f32[16,16,64]{2,0,1:T(8,128)S(1)}, f32[16,16,64]{2,0,1:T(8,128)S(1)}, u32[]{:S(2)}, u32[]{:S(2)}) collective-permute-start(f32[16,16,64]{2,0,1:T(8,128)S(1)} %get-tuple-element.20), channel_id=1, source_target_pairs={{0,1},{1,2},{2,3},{3,4},{4,5},{5,6},{6,7},{7,8},{8,9},{9,10},{10,1... | collective-permute-start | bytes 196616 | tf_op jit(solution)/shard_map/ppermute | solution.py:107
  60.5 4.5 %collective-permute-start.8 = (f32[16,1,512]{2,0,1:T(8,128)S(1)}, f32[16,1,512]{2,0,1:T(8,128)S(1)}, u32[]{:S(2)}, u32[]{:S(2)}) collective-permute-start(f32[16,1,512]{2,0,1:T(8,128)S(1)} %get-tuple-element.15), channel_id=1, source_target_pairs={{16,0},{32,16},{48,32},{64,48},{80,64},{96,80},{112,96},{128,112},... | collective-permute-start | bytes 98312 | tf_op jit(solution)/shard_map/ppermute | solution.py:111
  62.5 5.2 %collective-permute-start.9 = (f32[16,1,512]{2,0,1:T(8,128)S(1)}, f32[16,1,512]{2,0,1:T(8,128)S(1)}, u32[]{:S(2)}, u32[]{:S(2)}) collective-permute-start(f32[16,1,512]{2,0,1:T(8,128)S(1)} %get-tuple-element.16), channel_id=1, source_target_pairs={{0,16},{16,32},{32,48},{48,64},{64,80},{80,96},{96,112},{112,128},... | collective-permute-start | bytes 98312 | tf_op jit(solution)/shard_map/ppermute | solution.py:107
  69.9 5.8 %collective-permute-start.12 = (f32[48,48]{0,1:T(8,128)S(1)}, f32[48,48]{0,1:T(8,128)S(1)}, u32[]{:S(2)}, u32[]{:S(2)}) collective-permute-start(f32[48,48]{0,1:T(8,128)S(1)} %fusion.6), channel_id=1, source_target_pairs={{0,1},{1,0},{2,3},{3,2},{4,5},{5,4},{6,7},{7,6},{8,9},{9,8},{10,11... | collective-permute-start | bytes 27656 | tf_op jit(solution)/shard_map/ppermute | solution.py:25
  70.0 7.7 %collective-permute-start.13 = (f32[48,48]{0,1:T(8,128)S(1)}, f32[48,48]{0,1:T(8,128)S(1)}, u32[]{:S(2)}, u32[]{:S(2)}) collective-permute-start(f32[48,48]{0,1:T(8,128)S(1)} %fusion.6), channel_id=1, source_target_pairs={{0,2},{1,3},{2,0},{3,1},{4,6},{5,7},{6,4},{7,5},{8,10},{9,11},{10,... | collective-permute-start | bytes 27656 | tf_op jit(solution)/shard_map/ppermute | solution.py:25
  75.6 5.0 %collective-permute-start.14 = (f32[48,48]{0,1:T(8,128)S(1)}, f32[48,48]{0,1:T(8,128)S(1)}, u32[]{:S(2)}, u32[]{:S(2)}) collective-permute-start(f32[48,48]{0,1:T(8,128)S(1)} %fusion.6), channel_id=1, source_target_pairs={{0,3},{1,2},{2,1},{3,0},{4,7},{5,6},{6,5},{7,4},{8,11},{9,10},{10,... | collective-permute-start | bytes 27656 | tf_op jit(solution)/shard_map/ppermute | solution.py:25
  80.7 3.9 %collective-permute-start.15 = (f32[48,48]{0,1:T(8,128)S(1)}, f32[48,48]{0,1:T(8,128)S(1)}, u32[]{:S(2)}, u32[]{:S(2)}) collective-permute-start(f32[48,48]{0,1:T(8,128)S(1)} %add_add_fusion.4), channel_id=1, source_target_pairs={{0,4},{1,5},{2,6},{3,7},{4,0},{5,1},{6,2},{7,3},{8,12},{9,13},{10,... | collective-permute-start | bytes 27656 | tf_op jit(solution)/shard_map/ppermute | solution.py:25
  81.2 5.3 %collective-permute-start.16 = (f32[48,48]{0,1:T(8,128)S(1)}, f32[48,48]{0,1:T(8,128)S(1)}, u32[]{:S(2)}, u32[]{:S(2)}) collective-permute-start(f32[48,48]{0,1:T(8,128)S(1)} %add_add_fusion.4), channel_id=1, source_target_pairs={{0,8},{1,9},{2,10},{3,11},{4,12},{5,13},{6,14},{7,15},{8,0},{9,1},... | collective-permute-start | bytes 27656 | tf_op jit(solution)/shard_map/ppermute | solution.py:25
  83.8 3.8 %collective-permute-start.17 = (f32[48,48]{0,1:T(8,128)S(1)}, f32[48,48]{0,1:T(8,128)S(1)}, u32[]{:S(2)}, u32[]{:S(2)}) collective-permute-start(f32[48,48]{0,1:T(8,128)S(1)} %add_add_fusion.4), channel_id=1, source_target_pairs={{0,12},{1,13},{2,14},{3,15},{4,8},{5,9},{6,10},{7,11},{8,4},{9,5},... | collective-permute-start | bytes 27656 | tf_op jit(solution)/shard_map/ppermute | solution.py:25
  87.7 2.0 %collective-permute-start.18 = (f32[48,48]{0,1:T(8,128)S(1)}, f32[48,48]{0,1:T(8,128)S(1)}, u32[]{:S(2)}, u32[]{:S(2)}) collective-permute-start(f32[48,48]{0,1:T(8,128)S(1)} %add_add_fusion.3), channel_id=1, source_target_pairs={{0,16},{16,0},{32,48},{48,32},{64,80},{80,64},{96,112},{112,96},{1... | collective-permute-start | bytes 27656 | tf_op jit(solution)/shard_map/ppermute | solution.py:25
  87.8 4.1 %collective-permute-start.19 = (f32[48,48]{0,1:T(8,128)S(1)}, f32[48,48]{0,1:T(8,128)S(1)}, u32[]{:S(2)}, u32[]{:S(2)}) collective-permute-start(f32[48,48]{0,1:T(8,128)S(1)} %add_add_fusion.3), channel_id=1, source_target_pairs={{0,32},{16,48},{32,0},{48,16},{64,96},{80,112},{96,64},{112,80},{1... | collective-permute-start | bytes 27656 | tf_op jit(solution)/shard_map/ppermute | solution.py:25
  88.1 3.8 %collective-permute-start.20 = (f32[48,48]{0,1:T(8,128)S(1)}, f32[48,48]{0,1:T(8,128)S(1)}, u32[]{:S(2)}, u32[]{:S(2)}) collective-permute-start(f32[48,48]{0,1:T(8,128)S(1)} %add_add_fusion.3), channel_id=1, source_target_pairs={{0,48},{16,32},{32,16},{48,0},{64,112},{80,96},{96,80},{112,64},{1... | collective-permute-start | bytes 27656 | tf_op jit(solution)/shard_map/ppermute | solution.py:25
  91.9 11.2 %collective-permute-start.21 = (f32[48,48]{0,1:T(8,128)S(1)}, f32[48,48]{0,1:T(8,128)S(1)}, u32[]{:S(2)}, u32[]{:S(2)}) collective-permute-start(f32[48,48]{0,1:T(8,128)S(1)} %add_add_fusion.2), channel_id=1, source_target_pairs={{0,64},{16,80},{32,96},{48,112},{64,0},{80,16},{96,32},{112,48},{1... | collective-permute-start | bytes 27656 | tf_op jit(solution)/shard_map/ppermute | solution.py:25
  95.4 9.0 %collective-permute-start.22 = (f32[48,48]{0,1:T(8,128)S(1)}, f32[48,48]{0,1:T(8,128)S(1)}, u32[]{:S(2)}, u32[]{:S(2)}) collective-permute-start(f32[48,48]{0,1:T(8,128)S(1)} %add_add_fusion.2), channel_id=1, source_target_pairs={{0,128},{16,144},{32,160},{48,176},{64,192},{80,208},{96,224},{112... | collective-permute-start | bytes 27656 | tf_op jit(solution)/shard_map/ppermute | solution.py:25
  102.6 6.0 %collective-permute-start.23 = (f32[48,48]{0,1:T(8,128)S(1)}, f32[48,48]{0,1:T(8,128)S(1)}, u32[]{:S(2)}, u32[]{:S(2)}) collective-permute-start(f32[48,48]{0,1:T(8,128)S(1)} %add_add_fusion.2), channel_id=1, source_target_pairs={{0,192},{16,208},{32,224},{48,240},{64,128},{80,144},{96,160},{112... | collective-permute-start | bytes 27656 | tf_op jit(solution)/shard_map/ppermute | solution.py:25
  (13 other events, 31.5 us)

commit v8 on v5

--- a/solution.py
+++ b/solution.py
@@ -204,8 +204,19 @@
         precond_set.append(turned)
         applied_set.append(apply_op(turned, turned_edges))
         krylov.append(applied_set[-1] - SHIFT * krylov[-1])
-    stacked = jnp.concatenate(krylov, axis=0)
-    span_gram = mesh_sum(block_gram(stacked, stacked))
+    leading = jnp.concatenate(krylov[:-1], axis=0)
+    leading_gram = block_gram(leading, leading)
+    last_cols = block_gram(leading, krylov[-1])
+    last_gram = block_gram(krylov[-1], krylov[-1])
+    span_gram = mesh_sum(
+        jnp.concatenate(
+            [
+                jnp.concatenate([leading_gram, last_cols], axis=1),
+                jnp.concatenate([last_cols.T, last_gram], axis=1),
+            ],
+            axis=0,
+        )
+    )
     width = span_gram.shape[0]
 
     full_low = jnp.linalg.cholesky(span_gram)

time: 134 us -> 137 us (1.022)
  other arithmetic: 26 us -> 27.8 us
    unnamed x30, local copies, waits for them, and re-layouts: 0.98 us -> 3.09 us
  transfers between devices with their start and end apart: 24 -> 24, of which waited for: 10 -> 10; matrix products, arithmetic and copies ran while one was open for 8% -> 7% of each run, Pallas kernels for 0% -> 0%
where the time goes in v8:
time: 137 us; the launch traced here: 135 us
  starting transfers between devices  56.9 us (42%)
  other arithmetic  27.8 us (20%)
  local copies, waits for them, and re-layouts  21.3 us (16%)
  waiting for transfers between devices  20.5 us (15%)
  matrix products  6.65 us (5%)
  between operations  1.56 us (1%)
    ppermute x12, starting transfers between devices, mesh_sum(): lax.ppermute(block, axis, [(i, i ^ step * m) for i in range(count)])  22.4 us
    ppermute x6, starting transfers between devices, backward(): return lax.ppermute(block, axis, [(i + 1, i) for i in range(count - 1)])  18.8 us
    ppermute x12, waiting for transfers between devices, mesh_sum(): lax.ppermute(block, axis, [(i, i ^ step * m) for i in range(count)])  16.3 us
    ppermute x6, starting transfers between devices, forward(): return lax.ppermute(block, axis, [(i, i + 1) for i in range(count - 1)])  15.8 us
    slice x27, local copies, waits for them, and re-layouts, up_along(): lax.slice_in_dim(values, width, count, axis=axis)  5.09 us
    another operation x3, other arithmetic, body(): full_low = jnp.linalg.cholesky(span_gram)  5.05 us
    ppermute x6, waiting for transfers between devices, forward(): return lax.ppermute(block, axis, [(i, i + 1) for i in range(count - 1)])  4.24 us
    mul x2, other arithmetic, precondition(): lower_sol = inv_piv * source  3.64 us
  transfers between devices with their start and end apart: 24, of which 10 were waited for; matrix products, arithmetic and copies ran while one was open for 7% of the time, Pallas kernels for 0%

profile of v8, /device:TPU:40, one launch (start us, length us, event | category | flops | bytes accessed | tf_op | source)
XLA Modules:
  0.0 134.7 jit_solution(14930716984831290265)
XLA Ops:
  4.3 3.5 %collective-permute-start.1 = (f32[17,16,64]{2,0,1:T(8,128)}, f32[17,16,64]{2,0,1:T(8,128)}, u32[]{:S(2)}, u32[]{:S(2)}) collective-permute-start(f32[17,16,64]{2,0,1:T(8,128)} %pad_maximum_fusion.3), channel_id=1, source_target_pairs={{0,1},{1,2},{2,3},{3,4},{4,5},{5,6},{6,7},{7,8},{8,9},{9,10},{10,1... | collective-permute-start | bytes 208904 | tf_op jit(solution)/shard_map/ppermute | solution.py:107
  10.5 4.6 %collective-permute-start.3 = (f32[16,16,64]{2,0,1:T(8,128)}, f32[16,16,64]{2,0,1:T(8,128)}, u32[]{:S(2)}, u32[]{:S(2)}) collective-permute-start(f32[16,16,64]{2,0,1:T(8,128)} %get-tuple-element.37), channel_id=1, source_target_pairs={{1,0},{2,1},{3,2},{4,3},{5,4},{6,5},{7,6},{8,7},{9,8},{10,9},{11,1... | collective-permute-start | bytes 196616 | tf_op jit(solution)/shard_map/ppermute | solution.py:111
  15.1 3.4 %collective-permute-start.2 = (f32[16,1,512]{2,0,1:T(8,128)}, f32[16,1,512]{2,0,1:T(8,128)S(1)}, u32[]{:S(2)}, u32[]{:S(2)}) collective-permute-start(f32[16,1,512]{2,0,1:T(8,128)} %get-tuple-element.33), channel_id=1, source_target_pairs={{16,0},{32,16},{48,32},{64,48},{80,64},{96,80},{112,96},{128,112},... | collective-permute-start | bytes 98312 | tf_op jit(solution)/shard_map/ppermute | solution.py:111
  28.7 2.1 %broadcast_multiply_fusion.1 = (f32[16,16,512]{2,0,1:T(8,128)S(1)}, f32[16,16,512]{2,0,1:T(8,128)S(1)}) fusion(f32[16,512]{1,0:T(8,128)S(1)} %bitcast.113, f32[16,16,512]{2,0,1:T(8,128)S(1)} %reshape.194, f32[512]{0:T(512)S(1)} %fusion.44, f32[16,16,511]{2,0,1:T(8,128)S(1)} %copy-done.3, f32[16,512]{1,0:T(8,128)S(1)} %get-tuple-element.45, ...), kind=kLoop, calls=%fused_computation.58 | loop fusion | flops 2752512 | bytes 5507072 | tf_op jit(solution)/shard_map/mul | solution.py:174
  36.3 2.4 %collective-permute-start.6 = (f32[16,16,64]{2,0,1:T(8,128)S(1)}, f32[16,16,64]{2,0,1:T(8,128)S(1)}, u32[]{:S(2)}, u32[]{:S(2)}) collective-permute-start(f32[16,16,64]{2,0,1:T(8,128)S(1)} %get-tuple-element.27), channel_id=1, source_target_pairs={{1,0},{2,1},{3,2},{4,3},{5,4},{6,5},{7,6},{8,7},{9,8},{10,9},{11,1... | collective-permute-start | bytes 196616 | tf_op jit(solution)/shard_map/ppermute | solution.py:111
  38.7 3.4 %collective-permute-start.7 = (f32[16,16,64]{2,0,1:T(8,128)S(1)}, f32[16,16,64]{2,0,1:T(8,128)S(1)}, u32[]{:S(2)}, u32[]{:S(2)}) collective-permute-start(f32[16,16,64]{2,0,1:T(8,128)S(1)} %get-tuple-element.28), channel_id=1, source_target_pairs={{0,1},{1,2},{2,3},{3,4},{4,5},{5,6},{6,7},{7,8},{8,9},{9,10},{10,1... | collective-permute-start | bytes 196616 | tf_op jit(solution)/shard_map/ppermute | solution.py:107
  44.0 2.6 %collective-permute-start.5 = (f32[16,1,512]{2,0,1:T(8,128)S(1)}, f32[16,1,512]{2,0,1:T(8,128)S(1)}, u32[]{:S(2)}, u32[]{:S(2)}) collective-permute-start(f32[16,1,512]{2,0,1:T(8,128)S(1)} %get-tuple-element.24), channel_id=1, source_target_pairs={{0,16},{16,32},{32,48},{48,64},{64,80},{80,96},{96,112},{112,128},... | collective-permute-start | bytes 98312 | tf_op jit(solution)/shard_map/ppermute | solution.py:107
  46.8 2.5 %collective-permute-done.5 = f32[16,1,512]{2,0,1:T(8,128)S(1)} collective-permute-done((f32[16,1,512]{2,0,1:T(8,128)S(1)}, f32[16,1,512]{2,0,1:T(8,128)S(1)}, u32[]{:S(2)}, u32[]{:S(2)}) %collective-permute-start.5) | collective-permute-done | bytes 32800 | tf_op jit(solution)/shard_map/ppermute | solution.py:107
  56.3 4.6 %collective-permute-start.10 = (f32[16,16,64]{2,0,1:T(8,128)S(1)}, f32[16,16,64]{2,0,1:T(8,128)S(1)}, u32[]{:S(2)}, u32[]{:S(2)}) collective-permute-start(f32[16,16,64]{2,0,1:T(8,128)S(1)} %get-tuple-element.14), channel_id=1, source_target_pairs={{1,0},{2,1},{3,2},{4,3},{5,4},{6,5},{7,6},{8,7},{9,8},{10,9},{11,1... | collective-permute-start | bytes 196616 | tf_op jit(solution)/shard_map/ppermute | solution.py:111
  64.7 2.4 %collective-permute-start.9 = (f32[16,1,512]{2,0,1:T(8,128)S(1)}, f32[16,1,512]{2,0,1:T(8,128)S(1)}, u32[]{:S(2)}, u32[]{:S(2)}) collective-permute-start(f32[16,1,512]{2,0,1:T(8,128)S(1)} %get-tuple-element.17), channel_id=1, source_target_pairs={{0,16},{16,32},{32,48},{48,64},{64,80},{80,96},{96,112},{112,128},... | collective-permute-start | bytes 98312 | tf_op jit(solution)/shard_map/ppermute | solution.py:107
  74.7 2.0 %collective-permute-done.13 = f32[48,48]{0,1:T(8,128)S(1)} collective-permute-done((f32[48,48]{0,1:T(8,128)S(1)}, f32[48,48]{0,1:T(8,128)S(1)}, u32[]{:S(2)}, u32[]{:S(2)}) %collective-permute-start.13) | collective-permute-done | bytes 9248 | tf_op jit(solution)/shard_map/ppermute | solution.py:25
  76.8 6.7 %collective-permute-start.15 = (f32[48,48]{0,1:T(8,128)S(1)}, f32[48,48]{0,1:T(8,128)S(1)}, u32[]{:S(2)}, u32[]{:S(2)}) collective-permute-start(f32[48,48]{0,1:T(8,128)S(1)} %add_add_fusion.4), channel_id=1, source_target_pairs={{0,64},{16,80},{32,96},{48,112},{64,0},{80,16},{96,32},{112,48},{1... | collective-permute-start | bytes 27656 | tf_op jit(solution)/shard_map/ppermute | solution.py:25
  83.5 3.8 %collective-permute-start.16 = (f32[48,48]{0,1:T(8,128)S(1)}, f32[48,48]{0,1:T(8,128)S(1)}, u32[]{:S(2)}, u32[]{:S(2)}) collective-permute-start(f32[48,48]{0,1:T(8,128)S(1)} %add_add_fusion.4), channel_id=1, source_target_pairs={{0,128},{16,144},{32,160},{48,176},{64,192},{80,208},{96,224},{112... | collective-permute-start | bytes 27656 | tf_op jit(solution)/shard_map/ppermute | solution.py:25
  87.8 3.5 %collective-permute-done.16 = f32[48,48]{0,1:T(8,128)S(1)} collective-permute-done((f32[48,48]{0,1:T(8,128)S(1)}, f32[48,48]{0,1:T(8,128)S(1)}, u32[]{:S(2)}, u32[]{:S(2)}) %collective-permute-start.16) | collective-permute-done | bytes 9248 | tf_op jit(solution)/shard_map/ppermute | solution.py:25
  91.3 2.2 %collective-permute-done.17 = f32[48,48]{0,1:T(8,128)S(1)} collective-permute-done((f32[48,48]{0,1:T(8,128)S(1)}, f32[48,48]{0,1:T(8,128)S(1)}, u32[]{:S(2)}, u32[]{:S(2)}) %collective-permute-start.17) | collective-permute-done | bytes 9248 | tf_op jit(solution)/shard_map/ppermute | solution.py:25
  93.8 5.6 %collective-permute-start.19 = (f32[48,48]{0,1:T(8,128)S(1)}, f32[48,48]{0,1:T(8,128)S(1)}, u32[]{:S(2)}, u32[]{:S(2)}) collective-permute-start(f32[48,48]{0,1:T(8,128)S(1)} %add_add_fusion.3), channel_id=1, source_target_pairs={{0,2},{1,3},{2,0},{3,1},{4,6},{5,7},{6,4},{7,5},{8,10},{9,11},{10,... | collective-permute-start | bytes 27656 | tf_op jit(solution)/shard_map/ppermute | solution.py:25
  99.4 2.1 %collective-permute-done.19 = f32[48,48]{0,1:T(8,128)S(1)} collective-permute-done((f32[48,48]{0,1:T(8,128)S(1)}, f32[48,48]{0,1:T(8,128)S(1)}, u32[]{:S(2)}, u32[]{:S(2)}) %collective-permute-start.19) | collective-permute-done | bytes 9248 | tf_op jit(solution)/shard_map/ppermute | solution.py:25
  101.5 3.0 %collective-permute-done.20 = f32[48,48]{0,1:T(8,128)S(1)} collective-permute-done((f32[48,48]{0,1:T(8,128)S(1)}, f32[48,48]{0,1:T(8,128)S(1)}, u32[]{:S(2)}, u32[]{:S(2)}) %collective-permute-start.20) | collective-permute-done | bytes 9248 | tf_op jit(solution)/shard_map/ppermute | solution.py:25
  105.1 2.6 %collective-permute-start.22 = (f32[48,48]{0,1:T(8,128)S(1)}, f32[48,48]{0,1:T(8,128)S(1)}, u32[]{:S(2)}, u32[]{:S(2)}) collective-permute-start(f32[48,48]{0,1:T(8,128)S(1)} %add_add_fusion.2), channel_id=1, source_target_pairs={{0,8},{1,9},{2,10},{3,11},{4,12},{5,13},{6,14},{7,15},{8,0},{9,1},... | collective-permute-start | bytes 27656 | tf_op jit(solution)/shard_map/ppermute | solution.py:25
  108.4 2.0 %collective-permute-done.22 = f32[48,48]{0,1:T(8,128)S(1)} collective-permute-done((f32[48,48]{0,1:T(8,128)S(1)}, f32[48,48]{0,1:T(8,128)S(1)}, u32[]{:S(2)}, u32[]{:S(2)}) %collective-permute-start.22) | collective-permute-done | bytes 9248 | tf_op jit(solution)/shard_map/ppermute | solution.py:25
  111.6 4.4 %cholesky.31 = f32[48,48]{1,0:T(8,128)S(1)} custom-call(f32[48,48]{1,0:T(8,128)S(1)} %fusion.22), custom_call_target="Cholesky" | custom-call | tf_op jit(solution)/shard_map/jit(cholesky)/cholesky | solution.py:222
  118.0 2.4 %custom-call.14 = f32[1,32,32]{1,2,0:T(8,128)S(1)} custom-call(f32[1,32,32]{2,1,0:T(8,128)S(1)} %fusion.30), custom_call_target="InvertDiagBlocksLowerTriangular" | custom-call | tf_op jit(solution)/shard_map/triangular_solve | solution.py:225
  121.3 2.9 %cholesky.59 = f32[32,32]{1,0:T(8,128)S(1)} custom-call(f32[32,32]{1,0:T(8,128)S(1)} %fusion.35), custom_call_target="Cholesky" | custom-call | tf_op jit(solution)/shard_map/jit(cholesky)/cholesky | solution.py:60
  125.6 2.4 %custom-call.15 = f32[1,32,32]{1,2,0:T(8,128)S(1)} custom-call(f32[1,32,32]{2,1,0:T(8,128)S(1)} %fusion.27), custom_call_target="InvertDiagBlocksLowerTriangular" | custom-call | tf_op jit(solution)/shard_map/triangular_solve | solution.py:62
  (199 shorter events, 56.0 us)
Async XLA Ops:
  4.3 21.4 %collective-permute-start.1 = (f32[17,16,64]{2,0,1:T(8,128)}, f32[17,16,64]{2,0,1:T(8,128)}, u32[]{:S(2)}, u32[]{:S(2)}) collective-permute-start(f32[17,16,64]{2,0,1:T(8,128)} %pad_maximum_fusion.3), channel_id=1, source_target_pairs={{0,1},{1,2},{2,3},{3,4},{4,5},{5,6},{6,7},{7,8},{8,9},{9,10},{10,1... | collective-permute-start | bytes 208904 | tf_op jit(solution)/shard_map/ppermute | solution.py:107
  8.6 16.4 %collective-permute-start = (f32[17,1,512]{2,0,1:T(8,128)S(1)}, f32[17,1,512]{2,0,1:T(8,128)S(1)}, u32[]{:S(2)}, u32[]{:S(2)}) collective-permute-start(f32[17,1,512]{2,0,1:T(8,128)S(1)} %pad_maximum_fusion.4), channel_id=1, source_target_pairs={{0,16},{16,32},{32,48},{48,64},{64,80},{80,96},{96,112},{112,128},... | collective-permute-start | bytes 104456 | tf_op jit(solution)/shard_map/ppermute | solution.py:107
  10.5 18.2 %collective-permute-start.3 = (f32[16,16,64]{2,0,1:T(8,128)}, f32[16,16,64]{2,0,1:T(8,128)}, u32[]{:S(2)}, u32[]{:S(2)}) collective-permute-start(f32[16,16,64]{2,0,1:T(8,128)} %get-tuple-element.37), channel_id=1, source_target_pairs={{1,0},{2,1},{3,2},{4,3},{5,4},{6,5},{7,6},{8,7},{9,8},{10,9},{11,1... | collective-permute-start | bytes 196616 | tf_op jit(solution)/shard_map/ppermute | solution.py:111
  15.1 13.6 %collective-permute-start.2 = (f32[16,1,512]{2,0,1:T(8,128)}, f32[16,1,512]{2,0,1:T(8,128)S(1)}, u32[]{:S(2)}, u32[]{:S(2)}) collective-permute-start(f32[16,1,512]{2,0,1:T(8,128)} %get-tuple-element.33), channel_id=1, source_target_pairs={{16,0},{32,16},{48,32},{64,48},{80,64},{96,80},{112,96},{128,112},... | collective-permute-start | bytes 98312 | tf_op jit(solution)/shard_map/ppermute | solution.py:111
  36.3 13.0 %collective-permute-start.6 = (f32[16,16,64]{2,0,1:T(8,128)S(1)}, f32[16,16,64]{2,0,1:T(8,128)S(1)}, u32[]{:S(2)}, u32[]{:S(2)}) collective-permute-start(f32[16,16,64]{2,0,1:T(8,128)S(1)} %get-tuple-element.27), channel_id=1, source_target_pairs={{1,0},{2,1},{3,2},{4,3},{5,4},{6,5},{7,6},{8,7},{9,8},{10,9},{11,1... | collective-permute-start | bytes 196616 | tf_op jit(solution)/shard_map/ppermute | solution.py:111
  38.7 10.6 %collective-permute-start.7 = (f32[16,16,64]{2,0,1:T(8,128)S(1)}, f32[16,16,64]{2,0,1:T(8,128)S(1)}, u32[]{:S(2)}, u32[]{:S(2)}) collective-permute-start(f32[16,16,64]{2,0,1:T(8,128)S(1)} %get-tuple-element.28), channel_id=1, source_target_pairs={{0,1},{1,2},{2,3},{3,4},{4,5},{5,6},{6,7},{7,8},{8,9},{9,10},{10,1... | collective-permute-start | bytes 196616 | tf_op jit(solution)/shard_map/ppermute | solution.py:107
  42.1 4.6 %collective-permute-start.4 = (f32[16,1,512]{2,0,1:T(8,128)S(1)}, f32[16,1,512]{2,0,1:T(8,128)S(1)}, u32[]{:S(2)}, u32[]{:S(2)}) collective-permute-start(f32[16,1,512]{2,0,1:T(8,128)S(1)} %get-tuple-element.23), channel_id=1, source_target_pairs={{16,0},{32,16},{48,32},{64,48},{80,64},{96,80},{112,96},{128,112},... | collective-permute-start | bytes 98312 | tf_op jit(solution)/shard_map/ppermute | solution.py:111
  44.0 5.2 %collective-permute-start.5 = (f32[16,1,512]{2,0,1:T(8,128)S(1)}, f32[16,1,512]{2,0,1:T(8,128)S(1)}, u32[]{:S(2)}, u32[]{:S(2)}) collective-permute-start(f32[16,1,512]{2,0,1:T(8,128)S(1)} %get-tuple-element.24), channel_id=1, source_target_pairs={{0,16},{16,32},{32,48},{48,64},{64,80},{80,96},{96,112},{112,128},... | collective-permute-start | bytes 98312 | tf_op jit(solution)/shard_map/ppermute | solution.py:107
  56.3 13.7 %collective-permute-start.10 = (f32[16,16,64]{2,0,1:T(8,128)S(1)}, f32[16,16,64]{2,0,1:T(8,128)S(1)}, u32[]{:S(2)}, u32[]{:S(2)}) collective-permute-start(f32[16,16,64]{2,0,1:T(8,128)S(1)} %get-tuple-element.14), channel_id=1, source_target_pairs={{1,0},{2,1},{3,2},{4,3},{5,4},{6,5},{7,6},{8,7},{9,8},{10,9},{11,1... | collective-permute-start | bytes 196616 | tf_op jit(solution)/shard_map/ppermute | solution.py:111
  60.9 9.1 %collective-permute-start.11 = (f32[16,16,64]{2,0,1:T(8,128)S(1)}, f32[16,16,64]{2,0,1:T(8,128)S(1)}, u32[]{:S(2)}, u32[]{:S(2)}) collective-permute-start(f32[16,16,64]{2,0,1:T(8,128)S(1)} %get-tuple-element.13), channel_id=1, source_target_pairs={{0,1},{1,2},{2,3},{3,4},{4,5},{5,6},{6,7},{7,8},{8,9},{9,10},{10,1... | collective-permute-start | bytes 196616 | tf_op jit(solution)/shard_map/ppermute | solution.py:107
  62.8 5.4 %collective-permute-start.8 = (f32[16,1,512]{2,0,1:T(8,128)S(1)}, f32[16,1,512]{2,0,1:T(8,128)S(1)}, u32[]{:S(2)}, u32[]{:S(2)}) collective-permute-start(f32[16,1,512]{2,0,1:T(8,128)S(1)} %get-tuple-element.18), channel_id=1, source_target_pairs={{16,0},{32,16},{48,32},{64,48},{80,64},{96,80},{112,96},{128,112},... | collective-permute-start | bytes 98312 | tf_op jit(solution)/shard_map/ppermute | solution.py:111
  64.7 5.2 %collective-permute-start.9 = (f32[16,1,512]{2,0,1:T(8,128)S(1)}, f32[16,1,512]{2,0,1:T(8,128)S(1)}, u32[]{:S(2)}, u32[]{:S(2)}) collective-permute-start(f32[16,1,512]{2,0,1:T(8,128)S(1)} %get-tuple-element.17), channel_id=1, source_target_pairs={{0,16},{16,32},{32,48},{48,64},{64,80},{80,96},{96,112},{112,128},... | collective-permute-start | bytes 98312 | tf_op jit(solution)/shard_map/ppermute | solution.py:107
  72.8 1.9 %collective-permute-start.12 = (f32[48,48]{0,1:T(8,128)S(1)}, f32[48,48]{0,1:T(8,128)S(1)}, u32[]{:S(2)}, u32[]{:S(2)}) collective-permute-start(f32[48,48]{0,1:T(8,128)S(1)} %pad_maximum_fusion.7), channel_id=1, source_target_pairs={{0,16},{16,0},{32,48},{48,32},{64,80},{80,64},{96,112},{112,96},{1... | collective-permute-start | bytes 27656 | tf_op jit(solution)/shard_map/ppermute | solution.py:25
  72.8 3.9 %collective-permute-start.13 = (f32[48,48]{0,1:T(8,128)S(1)}, f32[48,48]{0,1:T(8,128)S(1)}, u32[]{:S(2)}, u32[]{:S(2)}) collective-permute-start(f32[48,48]{0,1:T(8,128)S(1)} %pad_maximum_fusion.7), channel_id=1, source_target_pairs={{0,32},{16,48},{32,0},{48,16},{64,96},{80,112},{96,64},{112,80},{1... | collective-permute-start | bytes 27656 | tf_op jit(solution)/shard_map/ppermute | solution.py:25
  72.9 3.8 %collective-permute-start.14 = (f32[48,48]{0,1:T(8,128)S(1)}, f32[48,48]{0,1:T(8,128)S(1)}, u32[]{:S(2)}, u32[]{:S(2)}) collective-permute-start(f32[48,48]{0,1:T(8,128)S(1)} %pad_maximum_fusion.7), channel_id=1, source_target_pairs={{0,48},{16,32},{32,16},{48,0},{64,112},{80,96},{96,80},{112,64},{1... | collective-permute-start | bytes 27656 | tf_op jit(solution)/shard_map/ppermute | solution.py:25
  76.8 11.0 %collective-permute-start.15 = (f32[48,48]{0,1:T(8,128)S(1)}, f32[48,48]{0,1:T(8,128)S(1)}, u32[]{:S(2)}, u32[]{:S(2)}) collective-permute-start(f32[48,48]{0,1:T(8,128)S(1)} %add_add_fusion.4), channel_id=1, source_target_pairs={{0,64},{16,80},{32,96},{48,112},{64,0},{80,16},{96,32},{112,48},{1... | collective-permute-start | bytes 27656 | tf_op jit(solution)/shard_map/ppermute | solution.py:25
  83.5 7.8 %collective-permute-start.16 = (f32[48,48]{0,1:T(8,128)S(1)}, f32[48,48]{0,1:T(8,128)S(1)}, u32[]{:S(2)}, u32[]{:S(2)}) collective-permute-start(f32[48,48]{0,1:T(8,128)S(1)} %add_add_fusion.4), channel_id=1, source_target_pairs={{0,128},{16,144},{32,160},{48,176},{64,192},{80,208},{96,224},{112... | collective-permute-start | bytes 27656 | tf_op jit(solution)/shard_map/ppermute | solution.py:25
  87.3 6.2 %collective-permute-start.17 = (f32[48,48]{0,1:T(8,128)S(1)}, f32[48,48]{0,1:T(8,128)S(1)}, u32[]{:S(2)}, u32[]{:S(2)}) collective-permute-start(f32[48,48]{0,1:T(8,128)S(1)} %add_add_fusion.4), channel_id=1, source_target_pairs={{0,192},{16,208},{32,224},{48,240},{64,128},{80,144},{96,160},{112... | collective-permute-start | bytes 27656 | tf_op jit(solution)/shard_map/ppermute | solution.py:25
  93.5 5.9 %collective-permute-start.18 = (f32[48,48]{0,1:T(8,128)S(1)}, f32[48,48]{0,1:T(8,128)S(1)}, u32[]{:S(2)}, u32[]{:S(2)}) collective-permute-start(f32[48,48]{0,1:T(8,128)S(1)} %add_add_fusion.3), channel_id=1, source_target_pairs={{0,1},{1,0},{2,3},{3,2},{4,5},{5,4},{6,7},{7,6},{8,9},{9,8},{10,11... | collective-permute-start | bytes 27656 | tf_op jit(solution)/shard_map/ppermute | solution.py:25
  93.8 7.7 %collective-permute-start.19 = (f32[48,48]{0,1:T(8,128)S(1)}, f32[48,48]{0,1:T(8,128)S(1)}, u32[]{:S(2)}, u32[]{:S(2)}) collective-permute-start(f32[48,48]{0,1:T(8,128)S(1)} %add_add_fusion.3), channel_id=1, source_target_pairs={{0,2},{1,3},{2,0},{3,1},{4,6},{5,7},{6,4},{7,5},{8,10},{9,11},{10,... | collective-permute-start | bytes 27656 | tf_op jit(solution)/shard_map/ppermute | solution.py:25
  99.4 5.0 %collective-permute-start.20 = (f32[48,48]{0,1:T(8,128)S(1)}, f32[48,48]{0,1:T(8,128)S(1)}, u32[]{:S(2)}, u32[]{:S(2)}) collective-permute-start(f32[48,48]{0,1:T(8,128)S(1)} %add_add_fusion.3), channel_id=1, source_target_pairs={{0,3},{1,2},{2,1},{3,0},{4,7},{5,6},{6,5},{7,4},{8,11},{9,10},{10,... | collective-permute-start | bytes 27656 | tf_op jit(solution)/shard_map/ppermute | solution.py:25
  104.5 3.9 %collective-permute-start.21 = (f32[48,48]{0,1:T(8,128)S(1)}, f32[48,48]{0,1:T(8,128)S(1)}, u32[]{:S(2)}, u32[]{:S(2)}) collective-permute-start(f32[48,48]{0,1:T(8,128)S(1)} %add_add_fusion.2), channel_id=1, source_target_pairs={{0,4},{1,5},{2,6},{3,7},{4,0},{5,1},{6,2},{7,3},{8,12},{9,13},{10,... | collective-permute-start | bytes 27656 | tf_op jit(solution)/shard_map/ppermute | solution.py:25
  105.1 5.3 %collective-permute-start.22 = (f32[48,48]{0,1:T(8,128)S(1)}, f32[48,48]{0,1:T(8,128)S(1)}, u32[]{:S(2)}, u32[]{:S(2)}) collective-permute-start(f32[48,48]{0,1:T(8,128)S(1)} %add_add_fusion.2), channel_id=1, source_target_pairs={{0,8},{1,9},{2,10},{3,11},{4,12},{5,13},{6,14},{7,15},{8,0},{9,1},... | collective-permute-start | bytes 27656 | tf_op jit(solution)/shard_map/ppermute | solution.py:25
  107.7 3.8 %collective-permute-start.23 = (f32[48,48]{0,1:T(8,128)S(1)}, f32[48,48]{0,1:T(8,128)S(1)}, u32[]{:S(2)}, u32[]{:S(2)}) collective-permute-start(f32[48,48]{0,1:T(8,128)S(1)} %add_add_fusion.2), channel_id=1, source_target_pairs={{0,12},{1,13},{2,14},{3,15},{4,8},{5,9},{6,10},{7,11},{8,4},{9,5},... | collective-permute-start | bytes 27656 | tf_op jit(solution)/shard_map/ppermute | solution.py:25
  (14 other events, 22.3 us)

commit v9 on v5

--- a/solution.py
+++ b/solution.py
@@ -166,6 +166,8 @@
             - lows[2] * lows[2] * low_z(inv_now)
         )
     inv_piv = 1.0 / pivots
+    inv_rev = inv_piv[:, :, ::-1]
+    ups_rev = tuple(coupling[:, :, ::-1] for coupling in ups)
 
     def total_gram(former, latter):
         return mesh_sum(block_gram(former, latter))
@@ -179,14 +181,15 @@
                 + lows[1] * low_y(lower_sol)
                 + lows[2] * low_z(lower_sol)
             )
-        upper_sol = lower_sol
+        lower_rev = lower_sol[:, :, ::-1]
+        upper_rev = lower_rev
         for precondition_repeat in range(SWEEPS):
-            upper_sol = lower_sol + inv_piv * (
-                ups[0] * up_x(upper_sol)
-                + ups[1] * up_y(upper_sol)
-                + ups[2] * up_z(upper_sol)
+            upper_rev = lower_rev + inv_rev * (
+                ups_rev[0] * up_x(upper_rev)
+                + ups_rev[1] * low_y(upper_rev)
+                + ups_rev[2] * low_z(upper_rev)
             )
-        return upper_sol
+        return upper_rev[:, :, ::-1]
 
     start_edges = (
         joint_x[:count_rhs],

time: 134 us -> 212 us (1.58)
  local copies, waits for them, and re-layouts: 20.2 us -> 90.6 us
  other arithmetic: 26 us -> 36.2 us
  waiting for transfers between devices: 21.4 us -> 14.9 us
    unnamed x30 -> x68, local copies, waits for them, and re-layouts: 0.98 us -> 39.1 us
    slice x3 -> x5, local copies, waits for them, and re-layouts: 1.29 us -> 10.1 us  [apply_op(): next_x = jnp.concatenate([values[:, 1:], from_high_x], axis=1)]
    slice x0 -> x6, local copies, waits for them, and re-layouts: none -> 7.77 us  [the longest x2 3.41 us: apply_op(): prev_x = jnp.concatenate([from_low_x, values[:, :-1]], axis=1)]
    ppermute x6, waiting for transfers between devices: 5.21 us -> 0.02 us  [forward(): return lax.ppermute(block, axis, [(i, i + 1) for i in range(count - 1)])]
    rev x0 -> x7, local copies, waits for them, and re-layouts: none -> 4.54 us  [the longest x3 2.54 us: body(): ups_rev = tuple((coupling[:, :, ::-1] for coupling in ups))]
    add x8, other arithmetic: 2.51 us -> 5.76 us  [precondition(): lower_rev + inv_rev * (ups_rev[0] * up_x(upper_rev) + ups_rev[1] * low_y(...]
    slice x11 -> x15, local copies, waits for them, and re-layouts: 0.28 us -> 3.48 us  [low_along(): lax.slice_in_dim(values, 0, count - width, axis=axis)]
    slice x2 -> x4, local copies, waits for them, and re-layouts: 0.01 us -> 2.9 us  [halos(): values[:, :1]]
  transfers between devices with their start and end apart: 24 -> 24, of which waited for: 10 -> 7; matrix products, arithmetic and copies ran while one was open for 8% -> 27% of each run, Pallas kernels for 0% -> 0%
where the time goes in v9:
time: 212 us; the launch traced here: 209 us
  local copies, waits for them, and re-layouts  90.6 us (43%)
  starting transfers between devices  58.3 us (28%)
  other arithmetic  36.2 us (17%)
  waiting for transfers between devices  14.9 us (7%)
  matrix products  7.09 us (3%)
    unnamed x68, local copies, waits for them, and re-layouts  39.1 us
    ppermute x12, starting transfers between devices, mesh_sum(): lax.ppermute(block, axis, [(i, i ^ step * m) for i in range(count)])  23.2 us
    ppermute x6, starting transfers between devices, backward(): return lax.ppermute(block, axis, [(i + 1, i) for i in range(count - 1)])  19.7 us
    ppermute x6, starting transfers between devices, forward(): return lax.ppermute(block, axis, [(i, i + 1) for i in range(count - 1)])  15.4 us
    ppermute x12, waiting for transfers between devices, mesh_sum(): lax.ppermute(block, axis, [(i, i ^ step * m) for i in range(count)])  14.9 us
    slice x5, local copies, waits for them, and re-layouts, apply_op(): next_x = jnp.concatenate([values[:, 1:], from_high_x], axis=1)  10.1 us
    slice x15, local copies, waits for them, and re-layouts, up_along(): lax.slice_in_dim(values, width, count, axis=axis)  6.86 us
    add x8, other arithmetic, precondition(): lower_rev + inv_rev * (ups_rev[0] * up_x(upper_rev) + ups_rev[1] * low_y(...  5.76 us
  transfers between devices with their start and end apart: 24, of which 7 were waited for; matrix products, arithmetic and copies ran while one was open for 27% of the time, Pallas kernels for 0%

profile of v9, /device:TPU:40, one launch (start us, length us, event | category | flops | bytes accessed | tf_op | source)
XLA Modules:
  0.0 208.8 jit_solution(6285580456353920010)
XLA Ops:
  4.2 3.4 %collective-permute-start.1 = (f32[17,16,64]{2,0,1:T(8,128)}, f32[17,16,64]{2,0,1:T(8,128)}, u32[]{:S(2)}, u32[]{:S(2)}) collective-permute-start(f32[17,16,64]{2,0,1:T(8,128)} %pad_maximum_fusion), channel_id=1, source_target_pairs={{0,1},{1,2},{2,3},{3,4},{4,5},{5,6},{6,7},{7,8},{8,9},{9,10},{10,1... | collective-permute-start | bytes 208904 | tf_op jit(solution)/shard_map/ppermute | solution.py:107
  10.2 4.6 %collective-permute-start.3 = (f32[16,16,64]{2,0,1:T(8,128)}, f32[16,16,64]{2,0,1:T(8,128)}, u32[]{:S(2)}, u32[]{:S(2)}) collective-permute-start(f32[16,16,64]{2,0,1:T(8,128)} %get-tuple-element.41), channel_id=1, source_target_pairs={{1,0},{2,1},{3,2},{4,3},{5,4},{6,5},{7,6},{8,7},{9,8},{10,9},{11,1... | collective-permute-start | bytes 196616 | tf_op jit(solution)/shard_map/ppermute | solution.py:111
  14.8 3.4 %collective-permute-start.2 = (f32[16,1,512]{2,0,1:T(8,128)}, f32[16,1,512]{2,0,1:T(8,128)}, u32[]{:S(2)}, u32[]{:S(2)}) collective-permute-start(f32[16,1,512]{2,0,1:T(8,128)} %get-tuple-element.37), channel_id=1, source_target_pairs={{16,0},{32,16},{48,32},{64,48},{80,64},{96,80},{112,96},{128,112},... | collective-permute-start | bytes 98312 | tf_op jit(solution)/shard_map/ppermute | solution.py:111
  51.9 2.4 %collective-permute-start.6 = (f32[16,16,64]{2,0,1:T(8,128)S(1)}, f32[16,16,64]{2,0,1:T(8,128)S(1)}, u32[]{:S(2)}, u32[]{:S(2)}) collective-permute-start(f32[16,16,64]{2,0,1:T(8,128)S(1)} %slice.473), channel_id=1, source_target_pairs={{1,0},{2,1},{3,2},{4,3},{5,4},{6,5},{7,6},{8,7},{9,8},{10,9},{11,1... | collective-permute-start | bytes 196616 | tf_op jit(solution)/shard_map/ppermute | solution.py:111
  55.1 3.4 %collective-permute-start.7 = (f32[16,16,64]{2,0,1:T(8,128)}, f32[16,16,64]{2,0,1:T(8,128)S(1)}, u32[]{:S(2)}, u32[]{:S(2)}) collective-permute-start(f32[16,16,64]{2,0,1:T(8,128)} %slice.475), channel_id=1, source_target_pairs={{0,1},{1,2},{2,3},{3,4},{4,5},{5,6},{6,7},{7,8},{8,9},{9,10},{10,1... | collective-permute-start | bytes 196616 | tf_op jit(solution)/shard_map/ppermute | solution.py:107
  63.3 2.6 %collective-permute-start.5 = (f32[16,1,512]{2,0,1:T(8,128)}, f32[16,1,512]{2,0,1:T(8,128)S(1)}, u32[]{:S(2)}, u32[]{:S(2)}) collective-permute-start(f32[16,1,512]{2,0,1:T(8,128)} %slice.467), channel_id=1, source_target_pairs={{0,16},{16,32},{32,48},{48,64},{64,80},{80,96},{96,112},{112,128},... | collective-permute-start | bytes 98312 | tf_op jit(solution)/shard_map/ppermute | solution.py:107
  78.4 3.4 %slice.463 = f32[16,15,512]{2,0,1:T(8,128)} reverse(f32[16,15,512]{2,0,1:T(8,128)} %get-tuple-element.25), dimensions={2} | reverse | bytes 983040 | tf_op jit(solution)/shard_map/slice | solution.py:139
  83.6 3.2 %broadcast_multiply_fusion = (f32[16,16,512]{2,0,1:T(8,128)S(1)}, f32[16,16,512]{2,0,1:T(8,128)S(1)}, f32[16,16,512]{2,0,1:T(8,128)}) fusion(f32[16,512]{1,0:T(8,128)S(1)} %bitcast.181, f32[16,16,512]{2,0,1:T(8,128)S(1)} %get-tuple-element.8, f32[512]{0:T(512)S(1)} %fusion.50, f32[16,16,511]{2,0,1:T(8,128)} %slice.652, f32[16,512]{1,0:T(8,128)S(1)} %get-tuple-element.52, ...), kind=kLoop, calls=%fused_computation.60 | loop fusion | flops 2752512 | bytes 6031360 | tf_op jit(solution)/shard_map/mul | solution.py:176
  94.3 3.4 %reverse.37 = f32[16,16,512]{2,0,1:T(8,128)} reverse(f32[16,16,512]{2,0,1:T(8,128)} %bitcast.187), dimensions={2} | reverse | bytes 1048576
  107.7 4.5 %collective-permute-start.10 = (f32[16,16,64]{2,0,1:T(8,128)}, f32[16,16,64]{2,0,1:T(8,128)}, u32[]{:S(2)}, u32[]{:S(2)}) collective-permute-start(f32[16,16,64]{2,0,1:T(8,128)} %slice.520), channel_id=1, source_target_pairs={{1,0},{2,1},{3,2},{4,3},{5,4},{6,5},{7,6},{8,7},{9,8},{10,9},{11,1... | collective-permute-start | bytes 196616 | tf_op jit(solution)/shard_map/ppermute | solution.py:111
  116.4 2.9 %collective-permute-start.8 = (f32[16,1,512]{2,0,1:T(8,128)}, f32[16,1,512]{2,0,1:T(8,128)S(1)}, u32[]{:S(2)}, u32[]{:S(2)}) collective-permute-start(f32[16,1,512]{2,0,1:T(8,128)} %slice.512), channel_id=1, source_target_pairs={{16,0},{32,16},{48,32},{64,48},{80,64},{96,80},{112,96},{128,112},... | collective-permute-start | bytes 98312 | tf_op jit(solution)/shard_map/ppermute | solution.py:111
  137.0 3.4 %slice.510 = f32[16,15,512]{2,0,1:T(8,128)} reverse(f32[16,15,512]{2,0,1:T(8,128)} %get-tuple-element.15), dimensions={2} | reverse | bytes 983040 | tf_op jit(solution)/shard_map/slice | solution.py:139
  142.1 2.6 %fusion.54 = (f32[16,16,512]{2,0,1:T(8,128)S(1)}, f32[16,16,512]{2,0,1:T(8,128)S(1)}) fusion(f32[16,16,512]{2,0,1:T(8,128)S(1)} %get-tuple-element.5, f32[512]{0:T(512)S(1)} %fusion.50, f32[16,16,511]{2,0,1:T(8,128)} %slice.658, f32[16,512]{1,0:T(8,128)S(1)} %get-tuple-element.52, f32[512]{0:T(512)S(1)} %fusion.51, f32[16,16,511]{2,0,1:T(8,128)} %slice.659, ...), kind=kLoop, calls=%fused_computation.135 | loop fusion | flops 2621440 | bytes 5474304 | tf_op jit(solution)/shard_map/sub | solution.py:209
  149.4 2.4 %collective-permute-done.13 = f32[48,48]{0,1:T(8,128)S(1)} collective-permute-done((f32[48,48]{0,1:T(8,128)S(1)}, f32[48,48]{0,1:T(8,128)S(1)}, u32[]{:S(2)}, u32[]{:S(2)}) %collective-permute-start.13) | collective-permute-done | bytes 9248 | tf_op jit(solution)/shard_map/ppermute | solution.py:25
  151.8 7.2 %collective-permute-start.15 = (f32[48,48]{0,1:T(8,128)S(1)}, f32[48,48]{0,1:T(8,128)S(1)}, u32[]{:S(2)}, u32[]{:S(2)}) collective-permute-start(f32[48,48]{0,1:T(8,128)S(1)} %add_add_fusion.4), channel_id=1, source_target_pairs={{0,64},{16,80},{32,96},{48,112},{64,0},{80,16},{96,32},{112,48},{1... | collective-permute-start | bytes 27656 | tf_op jit(solution)/shard_map/ppermute | solution.py:25
  159.6 3.0 %collective-permute-start.17 = (f32[48,48]{0,1:T(8,128)S(1)}, f32[48,48]{0,1:T(8,128)S(1)}, u32[]{:S(2)}, u32[]{:S(2)}) collective-permute-start(f32[48,48]{0,1:T(8,128)S(1)} %add_add_fusion.4), channel_id=1, source_target_pairs={{0,192},{16,208},{32,224},{48,240},{64,128},{80,144},{96,160},{112... | collective-permute-start | bytes 27656 | tf_op jit(solution)/shard_map/ppermute | solution.py:25
  162.6 4.1 %collective-permute-done.16 = f32[48,48]{0,1:T(8,128)S(1)} collective-permute-done((f32[48,48]{0,1:T(8,128)S(1)}, f32[48,48]{0,1:T(8,128)S(1)}, u32[]{:S(2)}, u32[]{:S(2)}) %collective-permute-start.16) | collective-permute-done | bytes 9248 | tf_op jit(solution)/shard_map/ppermute | solution.py:25
  166.8 5.4 %collective-permute-start.19 = (f32[48,48]{0,1:T(8,128)S(1)}, f32[48,48]{0,1:T(8,128)S(1)}, u32[]{:S(2)}, u32[]{:S(2)}) collective-permute-start(f32[48,48]{0,1:T(8,128)S(1)} %add_add_fusion.3), channel_id=1, source_target_pairs={{0,2},{1,3},{2,0},{3,1},{4,6},{5,7},{6,4},{7,5},{8,10},{9,11},{10,... | collective-permute-start | bytes 27656 | tf_op jit(solution)/shard_map/ppermute | solution.py:25
  174.3 3.0 %collective-permute-done.20 = f32[48,48]{0,1:T(8,128)S(1)} collective-permute-done((f32[48,48]{0,1:T(8,128)S(1)}, f32[48,48]{0,1:T(8,128)S(1)}, u32[]{:S(2)}, u32[]{:S(2)}) %collective-permute-start.20) | collective-permute-done | bytes 9248 | tf_op jit(solution)/shard_map/ppermute | solution.py:25
  177.8 2.6 %collective-permute-start.22 = (f32[48,48]{0,1:T(8,128)S(1)}, f32[48,48]{0,1:T(8,128)S(1)}, u32[]{:S(2)}, u32[]{:S(2)}) collective-permute-start(f32[48,48]{0,1:T(8,128)S(1)} %add_add_fusion.2), channel_id=1, source_target_pairs={{0,8},{1,9},{2,10},{3,11},{4,12},{5,13},{6,14},{7,15},{8,0},{9,1},... | collective-permute-start | bytes 27656 | tf_op jit(solution)/shard_map/ppermute | solution.py:25
  184.3 4.4 %cholesky.31 = f32[48,48]{1,0:T(8,128)S(1)} custom-call(f32[48,48]{1,0:T(8,128)S(1)} %fusion.28), custom_call_target="Cholesky" | custom-call | tf_op jit(solution)/shard_map/jit(cholesky)/cholesky | solution.py:214
  190.7 2.4 %custom-call.14 = f32[1,32,32]{1,2,0:T(8,128)S(1)} custom-call(f32[1,32,32]{2,1,0:T(8,128)S(1)} %fusion.36), custom_call_target="InvertDiagBlocksLowerTriangular" | custom-call | tf_op jit(solution)/shard_map/triangular_solve | solution.py:217
  194.1 2.9 %cholesky.59 = f32[32,32]{1,0:T(8,128)S(1)} custom-call(f32[32,32]{1,0:T(8,128)S(1)} %fusion.41), custom_call_target="Cholesky" | custom-call | tf_op jit(solution)/shard_map/jit(cholesky)/cholesky | solution.py:60
  198.3 2.4 %custom-call.15 = f32[1,32,32]{1,2,0:T(8,128)S(1)} custom-call(f32[1,32,32]{2,1,0:T(8,128)S(1)} %fusion.33), custom_call_target="InvertDiagBlocksLowerTriangular" | custom-call | tf_op jit(solution)/shard_map/triangular_solve | solution.py:62
  (242 shorter events, 124.1 us)
Async XLA Ops:
  4.2 21.6 %collective-permute-start.1 = (f32[17,16,64]{2,0,1:T(8,128)}, f32[17,16,64]{2,0,1:T(8,128)}, u32[]{:S(2)}, u32[]{:S(2)}) collective-permute-start(f32[17,16,64]{2,0,1:T(8,128)} %pad_maximum_fusion), channel_id=1, source_target_pairs={{0,1},{1,2},{2,3},{3,4},{4,5},{5,6},{6,7},{7,8},{8,9},{9,10},{10,1... | collective-permute-start | bytes 208904 | tf_op jit(solution)/shard_map/ppermute | solution.py:107
  8.3 16.0 %collective-permute-start = (f32[17,1,512]{2,0,1:T(8,128)S(1)}, f32[17,1,512]{2,0,1:T(8,128)}, u32[]{:S(2)}, u32[]{:S(2)}) collective-permute-start(f32[17,1,512]{2,0,1:T(8,128)S(1)} %pad_maximum_fusion.1), channel_id=1, source_target_pairs={{0,16},{16,32},{32,48},{48,64},{64,80},{80,96},{96,112},{112,128},... | collective-permute-start | bytes 104456 | tf_op jit(solution)/shard_map/ppermute | solution.py:107
  10.2 20.7 %collective-permute-start.3 = (f32[16,16,64]{2,0,1:T(8,128)}, f32[16,16,64]{2,0,1:T(8,128)}, u32[]{:S(2)}, u32[]{:S(2)}) collective-permute-start(f32[16,16,64]{2,0,1:T(8,128)} %get-tuple-element.41), channel_id=1, source_target_pairs={{1,0},{2,1},{3,2},{4,3},{5,4},{6,5},{7,6},{8,7},{9,8},{10,9},{11,1... | collective-permute-start | bytes 196616 | tf_op jit(solution)/shard_map/ppermute | solution.py:111
  14.8 16.1 %collective-permute-start.2 = (f32[16,1,512]{2,0,1:T(8,128)}, f32[16,1,512]{2,0,1:T(8,128)}, u32[]{:S(2)}, u32[]{:S(2)}) collective-permute-start(f32[16,1,512]{2,0,1:T(8,128)} %get-tuple-element.37), channel_id=1, source_target_pairs={{16,0},{32,16},{48,32},{64,48},{80,64},{96,80},{112,96},{128,112},... | collective-permute-start | bytes 98312 | tf_op jit(solution)/shard_map/ppermute | solution.py:111
  51.9 31.7 %collective-permute-start.6 = (f32[16,16,64]{2,0,1:T(8,128)S(1)}, f32[16,16,64]{2,0,1:T(8,128)S(1)}, u32[]{:S(2)}, u32[]{:S(2)}) collective-permute-start(f32[16,16,64]{2,0,1:T(8,128)S(1)} %slice.473), channel_id=1, source_target_pairs={{1,0},{2,1},{3,2},{4,3},{5,4},{6,5},{7,6},{8,7},{9,8},{10,9},{11,1... | collective-permute-start | bytes 196616 | tf_op jit(solution)/shard_map/ppermute | solution.py:111
  55.1 28.5 %collective-permute-start.7 = (f32[16,16,64]{2,0,1:T(8,128)}, f32[16,16,64]{2,0,1:T(8,128)S(1)}, u32[]{:S(2)}, u32[]{:S(2)}) collective-permute-start(f32[16,16,64]{2,0,1:T(8,128)} %slice.475), channel_id=1, source_target_pairs={{0,1},{1,2},{2,3},{3,4},{4,5},{5,6},{6,7},{7,8},{8,9},{9,10},{10,1... | collective-permute-start | bytes 196616 | tf_op jit(solution)/shard_map/ppermute | solution.py:107
  60.0 23.6 %collective-permute-start.4 = (f32[16,1,512]{2,0,1:T(8,128)}, f32[16,1,512]{2,0,1:T(8,128)S(1)}, u32[]{:S(2)}, u32[]{:S(2)}) collective-permute-start(f32[16,1,512]{2,0,1:T(8,128)} %slice.465), channel_id=1, source_target_pairs={{16,0},{32,16},{48,32},{64,48},{80,64},{96,80},{112,96},{128,112},... | collective-permute-start | bytes 98312 | tf_op jit(solution)/shard_map/ppermute | solution.py:111
  63.3 20.3 %collective-permute-start.5 = (f32[16,1,512]{2,0,1:T(8,128)}, f32[16,1,512]{2,0,1:T(8,128)S(1)}, u32[]{:S(2)}, u32[]{:S(2)}) collective-permute-start(f32[16,1,512]{2,0,1:T(8,128)} %slice.467), channel_id=1, source_target_pairs={{0,16},{16,32},{32,48},{48,64},{64,80},{80,96},{96,112},{112,128},... | collective-permute-start | bytes 98312 | tf_op jit(solution)/shard_map/ppermute | solution.py:107
  107.7 34.4 %collective-permute-start.10 = (f32[16,16,64]{2,0,1:T(8,128)}, f32[16,16,64]{2,0,1:T(8,128)}, u32[]{:S(2)}, u32[]{:S(2)}) collective-permute-start(f32[16,16,64]{2,0,1:T(8,128)} %slice.520), channel_id=1, source_target_pairs={{1,0},{2,1},{3,2},{4,3},{5,4},{6,5},{7,6},{8,7},{9,8},{10,9},{11,1... | collective-permute-start | bytes 196616 | tf_op jit(solution)/shard_map/ppermute | solution.py:111
  113.0 29.1 %collective-permute-start.11 = (f32[16,16,64]{2,0,1:T(8,128)}, f32[16,16,64]{2,0,1:T(8,128)S(1)}, u32[]{:S(2)}, u32[]{:S(2)}) collective-permute-start(f32[16,16,64]{2,0,1:T(8,128)} %slice.522), channel_id=1, source_target_pairs={{0,1},{1,2},{2,3},{3,4},{4,5},{5,6},{6,7},{7,8},{8,9},{9,10},{10,1... | collective-permute-start | bytes 196616 | tf_op jit(solution)/shard_map/ppermute | solution.py:107
  116.4 25.7 %collective-permute-start.8 = (f32[16,1,512]{2,0,1:T(8,128)}, f32[16,1,512]{2,0,1:T(8,128)S(1)}, u32[]{:S(2)}, u32[]{:S(2)}) collective-permute-start(f32[16,1,512]{2,0,1:T(8,128)} %slice.512), channel_id=1, source_target_pairs={{16,0},{32,16},{48,32},{64,48},{80,64},{96,80},{112,96},{128,112},... | collective-permute-start | bytes 98312 | tf_op jit(solution)/shard_map/ppermute | solution.py:111
  120.7 21.4 %collective-permute-start.9 = (f32[16,1,512]{2,0,1:T(8,128)}, f32[16,1,512]{2,0,1:T(8,128)}, u32[]{:S(2)}, u32[]{:S(2)}) collective-permute-start(f32[16,1,512]{2,0,1:T(8,128)} %slice.514), channel_id=1, source_target_pairs={{0,16},{16,32},{32,48},{48,64},{64,80},{80,96},{96,112},{112,128},... | collective-permute-start | bytes 98312 | tf_op jit(solution)/shard_map/ppermute | solution.py:107
  146.1 3.3 %collective-permute-start.12 = (f32[48,48]{0,1:T(8,128)S(1)}, f32[48,48]{0,1:T(8,128)S(1)}, u32[]{:S(2)}, u32[]{:S(2)}) collective-permute-start(f32[48,48]{0,1:T(8,128)S(1)} %fusion.6), channel_id=1, source_target_pairs={{0,16},{16,0},{32,48},{48,32},{64,80},{80,64},{96,112},{112,96},{1... | collective-permute-start | bytes 27656 | tf_op jit(solution)/shard_map/ppermute | solution.py:25
  147.9 3.8 %collective-permute-start.13 = (f32[48,48]{0,1:T(8,128)S(1)}, f32[48,48]{0,1:T(8,128)S(1)}, u32[]{:S(2)}, u32[]{:S(2)}) collective-permute-start(f32[48,48]{0,1:T(8,128)S(1)} %fusion.6), channel_id=1, source_target_pairs={{0,32},{16,48},{32,0},{48,16},{64,96},{80,112},{96,64},{112,80},{1... | collective-permute-start | bytes 27656 | tf_op jit(solution)/shard_map/ppermute | solution.py:25
  148.0 3.7 %collective-permute-start.14 = (f32[48,48]{0,1:T(8,128)S(1)}, f32[48,48]{0,1:T(8,128)S(1)}, u32[]{:S(2)}, u32[]{:S(2)}) collective-permute-start(f32[48,48]{0,1:T(8,128)S(1)} %fusion.6), channel_id=1, source_target_pairs={{0,48},{16,32},{32,16},{48,0},{64,112},{80,96},{96,80},{112,64},{1... | collective-permute-start | bytes 27656 | tf_op jit(solution)/shard_map/ppermute | solution.py:25
  151.8 10.9 %collective-permute-start.15 = (f32[48,48]{0,1:T(8,128)S(1)}, f32[48,48]{0,1:T(8,128)S(1)}, u32[]{:S(2)}, u32[]{:S(2)}) collective-permute-start(f32[48,48]{0,1:T(8,128)S(1)} %add_add_fusion.4), channel_id=1, source_target_pairs={{0,64},{16,80},{32,96},{48,112},{64,0},{80,16},{96,32},{112,48},{1... | collective-permute-start | bytes 27656 | tf_op jit(solution)/shard_map/ppermute | solution.py:25
  159.0 7.8 %collective-permute-start.16 = (f32[48,48]{0,1:T(8,128)S(1)}, f32[48,48]{0,1:T(8,128)S(1)}, u32[]{:S(2)}, u32[]{:S(2)}) collective-permute-start(f32[48,48]{0,1:T(8,128)S(1)} %add_add_fusion.4), channel_id=1, source_target_pairs={{0,128},{16,144},{32,160},{48,176},{64,192},{80,208},{96,224},{112... | collective-permute-start | bytes 27656 | tf_op jit(solution)/shard_map/ppermute | solution.py:25
  159.6 7.1 %collective-permute-start.17 = (f32[48,48]{0,1:T(8,128)S(1)}, f32[48,48]{0,1:T(8,128)S(1)}, u32[]{:S(2)}, u32[]{:S(2)}) collective-permute-start(f32[48,48]{0,1:T(8,128)S(1)} %add_add_fusion.4), channel_id=1, source_target_pairs={{0,192},{16,208},{32,224},{48,240},{64,128},{80,144},{96,160},{112... | collective-permute-start | bytes 27656 | tf_op jit(solution)/shard_map/ppermute | solution.py:25
  166.7 5.5 %collective-permute-start.18 = (f32[48,48]{0,1:T(8,128)S(1)}, f32[48,48]{0,1:T(8,128)S(1)}, u32[]{:S(2)}, u32[]{:S(2)}) collective-permute-start(f32[48,48]{0,1:T(8,128)S(1)} %add_add_fusion.3), channel_id=1, source_target_pairs={{0,1},{1,0},{2,3},{3,2},{4,5},{5,4},{6,7},{7,6},{8,9},{9,8},{10,11... | collective-permute-start | bytes 27656 | tf_op jit(solution)/shard_map/ppermute | solution.py:25
  166.8 7.5 %collective-permute-start.19 = (f32[48,48]{0,1:T(8,128)S(1)}, f32[48,48]{0,1:T(8,128)S(1)}, u32[]{:S(2)}, u32[]{:S(2)}) collective-permute-start(f32[48,48]{0,1:T(8,128)S(1)} %add_add_fusion.3), channel_id=1, source_target_pairs={{0,2},{1,3},{2,0},{3,1},{4,6},{5,7},{6,4},{7,5},{8,10},{9,11},{10,... | collective-permute-start | bytes 27656 | tf_op jit(solution)/shard_map/ppermute | solution.py:25
  172.2 5.0 %collective-permute-start.20 = (f32[48,48]{0,1:T(8,128)S(1)}, f32[48,48]{0,1:T(8,128)S(1)}, u32[]{:S(2)}, u32[]{:S(2)}) collective-permute-start(f32[48,48]{0,1:T(8,128)S(1)} %add_add_fusion.3), channel_id=1, source_target_pairs={{0,3},{1,2},{2,1},{3,0},{4,7},{5,6},{6,5},{7,4},{8,11},{9,10},{10,... | collective-permute-start | bytes 27656 | tf_op jit(solution)/shard_map/ppermute | solution.py:25
  177.3 3.9 %collective-permute-start.21 = (f32[48,48]{0,1:T(8,128)S(1)}, f32[48,48]{0,1:T(8,128)S(1)}, u32[]{:S(2)}, u32[]{:S(2)}) collective-permute-start(f32[48,48]{0,1:T(8,128)S(1)} %add_add_fusion.2), channel_id=1, source_target_pairs={{0,4},{1,5},{2,6},{3,7},{4,0},{5,1},{6,2},{7,3},{8,12},{9,13},{10,... | collective-permute-start | bytes 27656 | tf_op jit(solution)/shard_map/ppermute | solution.py:25
  177.8 5.3 %collective-permute-start.22 = (f32[48,48]{0,1:T(8,128)S(1)}, f32[48,48]{0,1:T(8,128)S(1)}, u32[]{:S(2)}, u32[]{:S(2)}) collective-permute-start(f32[48,48]{0,1:T(8,128)S(1)} %add_add_fusion.2), channel_id=1, source_target_pairs={{0,8},{1,9},{2,10},{3,11},{4,12},{5,13},{6,14},{7,15},{8,0},{9,1},... | collective-permute-start | bytes 27656 | tf_op jit(solution)/shard_map/ppermute | solution.py:25
  180.4 3.8 %collective-permute-start.23 = (f32[48,48]{0,1:T(8,128)S(1)}, f32[48,48]{0,1:T(8,128)S(1)}, u32[]{:S(2)}, u32[]{:S(2)}) collective-permute-start(f32[48,48]{0,1:T(8,128)S(1)} %add_add_fusion.2), channel_id=1, source_target_pairs={{0,12},{1,13},{2,14},{3,15},{4,8},{5,9},{6,10},{7,11},{8,4},{9,5},... | collective-permute-start | bytes 27656 | tf_op jit(solution)/shard_map/ppermute | solution.py:25
  (21 other events, 73.8 us)

commit v10 on v5

--- a/solution.py
+++ b/solution.py
@@ -57,7 +57,7 @@
     count_rhs = first_factor.shape[0]
     target = jnp.dot(hessen[:count_rhs].T, first_factor, precision=HIGH)
     normal = jnp.dot(hessen.T, hessen, precision=HIGH)
-    low_factor = jnp.linalg.cholesky(normal)
+    low_factor = lax.linalg.cholesky(normal, symmetrize_input=False)
     partial_sol = lax.linalg.triangular_solve(low_factor, target, left_side=True, lower=True)
     return lax.linalg.triangular_solve(
         low_factor, partial_sol, left_side=True, lower=True, transpose_a=True
@@ -208,7 +208,7 @@
     span_gram = mesh_sum(block_gram(stacked, stacked))
     width = span_gram.shape[0]
 
-    full_low = jnp.linalg.cholesky(span_gram)
+    full_low = lax.linalg.cholesky(span_gram, symmetrize_input=False)
     upper = full_low.T
     head = ITERS * count_rhs
     head_inv = lax.linalg.triangular_solve(

time: 134 us -> 134 us (level)
  no operation moved by 1% of the time
where the time goes in v10:
time: 134 us; the launch traced here: 132 us
  starting transfers between devices  56.7 us (42%)
  other arithmetic  26 us (19%)
  waiting for transfers between devices  21.4 us (16%)
  local copies, waits for them, and re-layouts  20 us (15%)
  matrix products  6.07 us (5%)
  between operations  1.54 us (1%)
    ppermute x12, starting transfers between devices, mesh_sum(): lax.ppermute(block, axis, [(i, i ^ step * m) for i in range(count)])  22.3 us
    ppermute x6, starting transfers between devices, backward(): return lax.ppermute(block, axis, [(i + 1, i) for i in range(count - 1)])  18.8 us
    ppermute x12, waiting for transfers between devices, mesh_sum(): lax.ppermute(block, axis, [(i, i ^ step * m) for i in range(count)])  16.2 us
    ppermute x6, starting transfers between devices, forward(): return lax.ppermute(block, axis, [(i, i + 1) for i in range(count - 1)])  15.6 us
    ppermute x6, waiting for transfers between devices, forward(): return lax.ppermute(block, axis, [(i, i + 1) for i in range(count - 1)])  5.21 us
    slice x27, local copies, waits for them, and re-layouts, up_along(): lax.slice_in_dim(values, width, count, axis=axis)  5.1 us
    another operation x3, other arithmetic, body(): full_low = lax.linalg.cholesky(span_gram, symmetrize_input=False)  5.05 us
    another operation x3, other arithmetic, solve_small(): low_factor = lax.linalg.cholesky(normal, symmetrize_input=False)  3.6 us
  transfers between devices with their start and end apart: 24, of which 10 were waited for; matrix products, arithmetic and copies ran while one was open for 8% of the time, Pallas kernels for 0%

profile of v10, /device:TPU:40, one launch (start us, length us, event | category | flops | bytes accessed | tf_op | source)
XLA Modules:
  0.0 131.8 jit_solution(10576604790211235870)
XLA Ops:
  3.3 3.4 %collective-permute-start.1 = (f32[17,16,64]{2,0,1:T(8,128)S(1)}, f32[17,16,64]{2,0,1:T(8,128)}, u32[]{:S(2)}, u32[]{:S(2)}) collective-permute-start(f32[17,16,64]{2,0,1:T(8,128)S(1)} %pad_maximum_fusion), channel_id=1, source_target_pairs={{0,1},{1,2},{2,3},{3,4},{4,5},{5,6},{6,7},{7,8},{8,9},{9,10},{10,1... | collective-permute-start | bytes 208904 | tf_op jit(solution)/shard_map/ppermute | solution.py:107
  9.4 4.6 %collective-permute-start.3 = (f32[16,16,64]{2,0,1:T(8,128)S(1)}, f32[16,16,64]{2,0,1:T(8,128)}, u32[]{:S(2)}, u32[]{:S(2)}) collective-permute-start(f32[16,16,64]{2,0,1:T(8,128)S(1)} %get-tuple-element.39), channel_id=1, source_target_pairs={{1,0},{2,1},{3,2},{4,3},{5,4},{6,5},{7,6},{8,7},{9,8},{10,9},{11,1... | collective-permute-start | bytes 196616 | tf_op jit(solution)/shard_map/ppermute | solution.py:111
  14.0 3.4 %collective-permute-start.2 = (f32[16,1,512]{2,0,1:T(8,128)}, f32[16,1,512]{2,0,1:T(8,128)S(1)}, u32[]{:S(2)}, u32[]{:S(2)}) collective-permute-start(f32[16,1,512]{2,0,1:T(8,128)} %get-tuple-element.35), channel_id=1, source_target_pairs={{16,0},{32,16},{48,32},{64,48},{80,64},{96,80},{112,96},{128,112},... | collective-permute-start | bytes 98312 | tf_op jit(solution)/shard_map/ppermute | solution.py:111
  34.7 2.4 %collective-permute-start.6 = (f32[16,16,64]{2,0,1:T(8,128)S(1)}, f32[16,16,64]{2,0,1:T(8,128)S(1)}, u32[]{:S(2)}, u32[]{:S(2)}) collective-permute-start(f32[16,16,64]{2,0,1:T(8,128)S(1)} %get-tuple-element.29), channel_id=1, source_target_pairs={{1,0},{2,1},{3,2},{4,3},{5,4},{6,5},{7,6},{8,7},{9,8},{10,9},{11,1... | collective-permute-start | bytes 196616 | tf_op jit(solution)/shard_map/ppermute | solution.py:111
  37.2 3.4 %collective-permute-start.7 = (f32[16,16,64]{2,0,1:T(8,128)S(1)}, f32[16,16,64]{2,0,1:T(8,128)S(1)}, u32[]{:S(2)}, u32[]{:S(2)}) collective-permute-start(f32[16,16,64]{2,0,1:T(8,128)S(1)} %get-tuple-element.30), channel_id=1, source_target_pairs={{0,1},{1,2},{2,3},{3,4},{4,5},{5,6},{6,7},{7,8},{8,9},{9,10},{10,1... | collective-permute-start | bytes 196616 | tf_op jit(solution)/shard_map/ppermute | solution.py:107
  42.5 2.6 %collective-permute-start.5 = (f32[16,1,512]{2,0,1:T(8,128)S(1)}, f32[16,1,512]{2,0,1:T(8,128)S(1)}, u32[]{:S(2)}, u32[]{:S(2)}) collective-permute-start(f32[16,1,512]{2,0,1:T(8,128)S(1)} %get-tuple-element.26), channel_id=1, source_target_pairs={{0,16},{16,32},{32,48},{48,64},{64,80},{80,96},{96,112},{112,128},... | collective-permute-start | bytes 98312 | tf_op jit(solution)/shard_map/ppermute | solution.py:107
  45.3 2.5 %collective-permute-done.5 = f32[16,1,512]{2,0,1:T(8,128)S(1)} collective-permute-done((f32[16,1,512]{2,0,1:T(8,128)S(1)}, f32[16,1,512]{2,0,1:T(8,128)S(1)}, u32[]{:S(2)}, u32[]{:S(2)}) %collective-permute-start.5) | collective-permute-done | bytes 32800 | tf_op jit(solution)/shard_map/ppermute | solution.py:107
  54.0 4.6 %collective-permute-start.10 = (f32[16,16,64]{2,0,1:T(8,128)S(1)}, f32[16,16,64]{2,0,1:T(8,128)S(1)}, u32[]{:S(2)}, u32[]{:S(2)}) collective-permute-start(f32[16,16,64]{2,0,1:T(8,128)S(1)} %get-tuple-element.19), channel_id=1, source_target_pairs={{1,0},{2,1},{3,2},{4,3},{5,4},{6,5},{7,6},{8,7},{9,8},{10,9},{11,1... | collective-permute-start | bytes 196616 | tf_op jit(solution)/shard_map/ppermute | solution.py:111
  62.5 2.4 %collective-permute-start.9 = (f32[16,1,512]{2,0,1:T(8,128)S(1)}, f32[16,1,512]{2,0,1:T(8,128)S(1)}, u32[]{:S(2)}, u32[]{:S(2)}) collective-permute-start(f32[16,1,512]{2,0,1:T(8,128)S(1)} %get-tuple-element.16), channel_id=1, source_target_pairs={{0,16},{16,32},{32,48},{48,64},{64,80},{80,96},{96,112},{112,128},... | collective-permute-start | bytes 98312 | tf_op jit(solution)/shard_map/ppermute | solution.py:107
  65.0 2.7 %collective-permute-done.9 = f32[16,1,512]{2,0,1:T(8,128)S(1)} collective-permute-done((f32[16,1,512]{2,0,1:T(8,128)S(1)}, f32[16,1,512]{2,0,1:T(8,128)S(1)}, u32[]{:S(2)}, u32[]{:S(2)}) %collective-permute-start.9) | collective-permute-done | bytes 32800 | tf_op jit(solution)/shard_map/ppermute | solution.py:107
  71.8 2.0 %collective-permute-done.13 = f32[48,48]{1,0:T(8,128)S(1)} collective-permute-done((f32[48,48]{1,0:T(8,128)S(1)}, f32[48,48]{1,0:T(8,128)S(1)}, u32[]{:S(2)}, u32[]{:S(2)}) %collective-permute-start.13) | collective-permute-done | bytes 9248 | tf_op jit(solution)/shard_map/ppermute | solution.py:25
  73.9 6.6 %collective-permute-start.15 = (f32[48,48]{1,0:T(8,128)S(1)}, f32[48,48]{1,0:T(8,128)S(1)}, u32[]{:S(2)}, u32[]{:S(2)}) collective-permute-start(f32[48,48]{1,0:T(8,128)S(1)} %add_add_fusion.4), channel_id=1, source_target_pairs={{0,64},{16,80},{32,96},{48,112},{64,0},{80,16},{96,32},{112,48},{1... | collective-permute-start | bytes 27656 | tf_op jit(solution)/shard_map/ppermute | solution.py:25
  80.5 3.9 %collective-permute-start.16 = (f32[48,48]{1,0:T(8,128)S(1)}, f32[48,48]{1,0:T(8,128)S(1)}, u32[]{:S(2)}, u32[]{:S(2)}) collective-permute-start(f32[48,48]{1,0:T(8,128)S(1)} %add_add_fusion.4), channel_id=1, source_target_pairs={{0,128},{16,144},{32,160},{48,176},{64,192},{80,208},{96,224},{112... | collective-permute-start | bytes 27656 | tf_op jit(solution)/shard_map/ppermute | solution.py:25
  84.9 3.5 %collective-permute-done.16 = f32[48,48]{1,0:T(8,128)S(1)} collective-permute-done((f32[48,48]{1,0:T(8,128)S(1)}, f32[48,48]{1,0:T(8,128)S(1)}, u32[]{:S(2)}, u32[]{:S(2)}) %collective-permute-start.16) | collective-permute-done | bytes 9248 | tf_op jit(solution)/shard_map/ppermute | solution.py:25
  88.4 2.2 %collective-permute-done.17 = f32[48,48]{1,0:T(8,128)S(1)} collective-permute-done((f32[48,48]{1,0:T(8,128)S(1)}, f32[48,48]{1,0:T(8,128)S(1)}, u32[]{:S(2)}, u32[]{:S(2)}) %collective-permute-start.17) | collective-permute-done | bytes 9248 | tf_op jit(solution)/shard_map/ppermute | solution.py:25
  90.7 5.7 %collective-permute-start.19 = (f32[48,48]{1,0:T(8,128)S(1)}, f32[48,48]{1,0:T(8,128)S(1)}, u32[]{:S(2)}, u32[]{:S(2)}) collective-permute-start(f32[48,48]{1,0:T(8,128)S(1)} %add_add_fusion.3), channel_id=1, source_target_pairs={{0,2},{1,3},{2,0},{3,1},{4,6},{5,7},{6,4},{7,5},{8,10},{9,11},{10,... | collective-permute-start | bytes 27656 | tf_op jit(solution)/shard_map/ppermute | solution.py:25
  96.4 2.1 %collective-permute-done.19 = f32[48,48]{1,0:T(8,128)S(1)} collective-permute-done((f32[48,48]{1,0:T(8,128)S(1)}, f32[48,48]{1,0:T(8,128)S(1)}, u32[]{:S(2)}, u32[]{:S(2)}) %collective-permute-start.19) | collective-permute-done | bytes 9248 | tf_op jit(solution)/shard_map/ppermute | solution.py:25
  98.5 3.0 %collective-permute-done.20 = f32[48,48]{1,0:T(8,128)S(1)} collective-permute-done((f32[48,48]{1,0:T(8,128)S(1)}, f32[48,48]{1,0:T(8,128)S(1)}, u32[]{:S(2)}, u32[]{:S(2)}) %collective-permute-start.20) | collective-permute-done | bytes 9248 | tf_op jit(solution)/shard_map/ppermute | solution.py:25
  102.0 2.6 %collective-permute-start.22 = (f32[48,48]{1,0:T(8,128)S(1)}, f32[48,48]{1,0:T(8,128)S(1)}, u32[]{:S(2)}, u32[]{:S(2)}) collective-permute-start(f32[48,48]{1,0:T(8,128)S(1)} %add_add_fusion.2), channel_id=1, source_target_pairs={{0,8},{1,9},{2,10},{3,11},{4,12},{5,13},{6,14},{7,15},{8,0},{9,1},... | collective-permute-start | bytes 27656 | tf_op jit(solution)/shard_map/ppermute | solution.py:25
  105.4 2.0 %collective-permute-done.22 = f32[48,48]{1,0:T(8,128)S(1)} collective-permute-done((f32[48,48]{1,0:T(8,128)S(1)}, f32[48,48]{1,0:T(8,128)S(1)}, u32[]{:S(2)}, u32[]{:S(2)}) %collective-permute-start.22) | collective-permute-done | bytes 9248 | tf_op jit(solution)/shard_map/ppermute | solution.py:25
  108.4 4.4 %cholesky.31 = f32[48,48]{1,0:T(8,128)S(1)} custom-call(f32[48,48]{1,0:T(8,128)S(1)} %add_add_fusion.1), custom_call_target="Cholesky" | custom-call | tf_op jit(solution)/shard_map/cholesky | solution.py:211
  114.8 2.4 %custom-call.12 = f32[1,32,32]{1,2,0:T(8,128)S(1)} custom-call(f32[1,32,32]{2,1,0:T(8,128)S(1)} %fusion.35), custom_call_target="InvertDiagBlocksLowerTriangular" | custom-call | tf_op jit(solution)/shard_map/triangular_solve | solution.py:214
  118.1 2.9 %cholesky.59 = f32[32,32]{1,0:T(8,128)S(1)} custom-call(f32[32,32]{1,0:T(8,128)S(1)} %fusion.73), custom_call_target="Cholesky" | custom-call | tf_op jit(solution)/shard_map/cholesky | solution.py:60
  122.3 2.4 %custom-call.13 = f32[1,32,32]{1,2,0:T(8,128)S(1)} custom-call(f32[1,32,32]{2,1,0:T(8,128)S(1)} %fusion.32), custom_call_target="InvertDiagBlocksLowerTriangular" | custom-call | tf_op jit(solution)/shard_map/triangular_solve | solution.py:62
  (189 shorter events, 52.6 us)
Async XLA Ops:
  3.3 20.8 %collective-permute-start.1 = (f32[17,16,64]{2,0,1:T(8,128)S(1)}, f32[17,16,64]{2,0,1:T(8,128)}, u32[]{:S(2)}, u32[]{:S(2)}) collective-permute-start(f32[17,16,64]{2,0,1:T(8,128)S(1)} %pad_maximum_fusion), channel_id=1, source_target_pairs={{0,1},{1,2},{2,3},{3,4},{4,5},{5,6},{6,7},{7,8},{8,9},{9,10},{10,1... | collective-permute-start | bytes 208904 | tf_op jit(solution)/shard_map/ppermute | solution.py:107
  7.5 15.1 %collective-permute-start = (f32[17,1,512]{2,0,1:T(8,128)S(1)}, f32[17,1,512]{2,0,1:T(8,128)}, u32[]{:S(2)}, u32[]{:S(2)}) collective-permute-start(f32[17,1,512]{2,0,1:T(8,128)S(1)} %pad_maximum_fusion.1), channel_id=1, source_target_pairs={{0,16},{16,32},{32,48},{48,64},{64,80},{80,96},{96,112},{112,128},... | collective-permute-start | bytes 104456 | tf_op jit(solution)/shard_map/ppermute | solution.py:107
  9.4 17.9 %collective-permute-start.3 = (f32[16,16,64]{2,0,1:T(8,128)S(1)}, f32[16,16,64]{2,0,1:T(8,128)}, u32[]{:S(2)}, u32[]{:S(2)}) collective-permute-start(f32[16,16,64]{2,0,1:T(8,128)S(1)} %get-tuple-element.39), channel_id=1, source_target_pairs={{1,0},{2,1},{3,2},{4,3},{5,4},{6,5},{7,6},{8,7},{9,8},{10,9},{11,1... | collective-permute-start | bytes 196616 | tf_op jit(solution)/shard_map/ppermute | solution.py:111
  14.0 13.3 %collective-permute-start.2 = (f32[16,1,512]{2,0,1:T(8,128)}, f32[16,1,512]{2,0,1:T(8,128)S(1)}, u32[]{:S(2)}, u32[]{:S(2)}) collective-permute-start(f32[16,1,512]{2,0,1:T(8,128)} %get-tuple-element.35), channel_id=1, source_target_pairs={{16,0},{32,16},{48,32},{64,48},{80,64},{96,80},{112,96},{128,112},... | collective-permute-start | bytes 98312 | tf_op jit(solution)/shard_map/ppermute | solution.py:111
  34.7 13.0 %collective-permute-start.6 = (f32[16,16,64]{2,0,1:T(8,128)S(1)}, f32[16,16,64]{2,0,1:T(8,128)S(1)}, u32[]{:S(2)}, u32[]{:S(2)}) collective-permute-start(f32[16,16,64]{2,0,1:T(8,128)S(1)} %get-tuple-element.29), channel_id=1, source_target_pairs={{1,0},{2,1},{3,2},{4,3},{5,4},{6,5},{7,6},{8,7},{9,8},{10,9},{11,1... | collective-permute-start | bytes 196616 | tf_op jit(solution)/shard_map/ppermute | solution.py:111
  37.2 10.6 %collective-permute-start.7 = (f32[16,16,64]{2,0,1:T(8,128)S(1)}, f32[16,16,64]{2,0,1:T(8,128)S(1)}, u32[]{:S(2)}, u32[]{:S(2)}) collective-permute-start(f32[16,16,64]{2,0,1:T(8,128)S(1)} %get-tuple-element.30), channel_id=1, source_target_pairs={{0,1},{1,2},{2,3},{3,4},{4,5},{5,6},{6,7},{7,8},{8,9},{9,10},{10,1... | collective-permute-start | bytes 196616 | tf_op jit(solution)/shard_map/ppermute | solution.py:107
  40.6 4.6 %collective-permute-start.4 = (f32[16,1,512]{2,0,1:T(8,128)S(1)}, f32[16,1,512]{2,0,1:T(8,128)S(1)}, u32[]{:S(2)}, u32[]{:S(2)}) collective-permute-start(f32[16,1,512]{2,0,1:T(8,128)S(1)} %get-tuple-element.25), channel_id=1, source_target_pairs={{16,0},{32,16},{48,32},{64,48},{80,64},{96,80},{112,96},{128,112},... | collective-permute-start | bytes 98312 | tf_op jit(solution)/shard_map/ppermute | solution.py:111
  42.5 5.2 %collective-permute-start.5 = (f32[16,1,512]{2,0,1:T(8,128)S(1)}, f32[16,1,512]{2,0,1:T(8,128)S(1)}, u32[]{:S(2)}, u32[]{:S(2)}) collective-permute-start(f32[16,1,512]{2,0,1:T(8,128)S(1)} %get-tuple-element.26), channel_id=1, source_target_pairs={{0,16},{16,32},{32,48},{48,64},{64,80},{80,96},{96,112},{112,128},... | collective-permute-start | bytes 98312 | tf_op jit(solution)/shard_map/ppermute | solution.py:107
  54.0 13.7 %collective-permute-start.10 = (f32[16,16,64]{2,0,1:T(8,128)S(1)}, f32[16,16,64]{2,0,1:T(8,128)S(1)}, u32[]{:S(2)}, u32[]{:S(2)}) collective-permute-start(f32[16,16,64]{2,0,1:T(8,128)S(1)} %get-tuple-element.19), channel_id=1, source_target_pairs={{1,0},{2,1},{3,2},{4,3},{5,4},{6,5},{7,6},{8,7},{9,8},{10,9},{11,1... | collective-permute-start | bytes 196616 | tf_op jit(solution)/shard_map/ppermute | solution.py:111
  58.6 9.1 %collective-permute-start.11 = (f32[16,16,64]{2,0,1:T(8,128)S(1)}, f32[16,16,64]{2,0,1:T(8,128)S(1)}, u32[]{:S(2)}, u32[]{:S(2)}) collective-permute-start(f32[16,16,64]{2,0,1:T(8,128)S(1)} %get-tuple-element.20), channel_id=1, source_target_pairs={{0,1},{1,2},{2,3},{3,4},{4,5},{5,6},{6,7},{7,8},{8,9},{9,10},{10,1... | collective-permute-start | bytes 196616 | tf_op jit(solution)/shard_map/ppermute | solution.py:107
  60.5 4.5 %collective-permute-start.8 = (f32[16,1,512]{2,0,1:T(8,128)S(1)}, f32[16,1,512]{2,0,1:T(8,128)S(1)}, u32[]{:S(2)}, u32[]{:S(2)}) collective-permute-start(f32[16,1,512]{2,0,1:T(8,128)S(1)} %get-tuple-element.15), channel_id=1, source_target_pairs={{16,0},{32,16},{48,32},{64,48},{80,64},{96,80},{112,96},{128,112},... | collective-permute-start | bytes 98312 | tf_op jit(solution)/shard_map/ppermute | solution.py:111
  62.5 5.2 %collective-permute-start.9 = (f32[16,1,512]{2,0,1:T(8,128)S(1)}, f32[16,1,512]{2,0,1:T(8,128)S(1)}, u32[]{:S(2)}, u32[]{:S(2)}) collective-permute-start(f32[16,1,512]{2,0,1:T(8,128)S(1)} %get-tuple-element.16), channel_id=1, source_target_pairs={{0,16},{16,32},{32,48},{48,64},{64,80},{80,96},{96,112},{112,128},... | collective-permute-start | bytes 98312 | tf_op jit(solution)/shard_map/ppermute | solution.py:107
  69.9 2.0 %collective-permute-start.12 = (f32[48,48]{1,0:T(8,128)S(1)}, f32[48,48]{1,0:T(8,128)S(1)}, u32[]{:S(2)}, u32[]{:S(2)}) collective-permute-start(f32[48,48]{1,0:T(8,128)S(1)} %fusion.6), channel_id=1, source_target_pairs={{0,16},{16,0},{32,48},{48,32},{64,80},{80,64},{96,112},{112,96},{1... | collective-permute-start | bytes 27656 | tf_op jit(solution)/shard_map/ppermute | solution.py:25
  70.0 3.9 %collective-permute-start.13 = (f32[48,48]{1,0:T(8,128)S(1)}, f32[48,48]{1,0:T(8,128)S(1)}, u32[]{:S(2)}, u32[]{:S(2)}) collective-permute-start(f32[48,48]{1,0:T(8,128)S(1)} %fusion.6), channel_id=1, source_target_pairs={{0,32},{16,48},{32,0},{48,16},{64,96},{80,112},{96,64},{112,80},{1... | collective-permute-start | bytes 27656 | tf_op jit(solution)/shard_map/ppermute | solution.py:25
  70.1 3.8 %collective-permute-start.14 = (f32[48,48]{1,0:T(8,128)S(1)}, f32[48,48]{1,0:T(8,128)S(1)}, u32[]{:S(2)}, u32[]{:S(2)}) collective-permute-start(f32[48,48]{1,0:T(8,128)S(1)} %fusion.6), channel_id=1, source_target_pairs={{0,48},{16,32},{32,16},{48,0},{64,112},{80,96},{96,80},{112,64},{1... | collective-permute-start | bytes 27656 | tf_op jit(solution)/shard_map/ppermute | solution.py:25
  73.9 11.0 %collective-permute-start.15 = (f32[48,48]{1,0:T(8,128)S(1)}, f32[48,48]{1,0:T(8,128)S(1)}, u32[]{:S(2)}, u32[]{:S(2)}) collective-permute-start(f32[48,48]{1,0:T(8,128)S(1)} %add_add_fusion.4), channel_id=1, source_target_pairs={{0,64},{16,80},{32,96},{48,112},{64,0},{80,16},{96,32},{112,48},{1... | collective-permute-start | bytes 27656 | tf_op jit(solution)/shard_map/ppermute | solution.py:25
  80.5 7.9 %collective-permute-start.16 = (f32[48,48]{1,0:T(8,128)S(1)}, f32[48,48]{1,0:T(8,128)S(1)}, u32[]{:S(2)}, u32[]{:S(2)}) collective-permute-start(f32[48,48]{1,0:T(8,128)S(1)} %add_add_fusion.4), channel_id=1, source_target_pairs={{0,128},{16,144},{32,160},{48,176},{64,192},{80,208},{96,224},{112... | collective-permute-start | bytes 27656 | tf_op jit(solution)/shard_map/ppermute | solution.py:25
  84.4 6.2 %collective-permute-start.17 = (f32[48,48]{1,0:T(8,128)S(1)}, f32[48,48]{1,0:T(8,128)S(1)}, u32[]{:S(2)}, u32[]{:S(2)}) collective-permute-start(f32[48,48]{1,0:T(8,128)S(1)} %add_add_fusion.4), channel_id=1, source_target_pairs={{0,192},{16,208},{32,224},{48,240},{64,128},{80,144},{96,160},{112... | collective-permute-start | bytes 27656 | tf_op jit(solution)/shard_map/ppermute | solution.py:25
  90.6 5.8 %collective-permute-start.18 = (f32[48,48]{1,0:T(8,128)S(1)}, f32[48,48]{1,0:T(8,128)S(1)}, u32[]{:S(2)}, u32[]{:S(2)}) collective-permute-start(f32[48,48]{1,0:T(8,128)S(1)} %add_add_fusion.3), channel_id=1, source_target_pairs={{0,1},{1,0},{2,3},{3,2},{4,5},{5,4},{6,7},{7,6},{8,9},{9,8},{10,11... | collective-permute-start | bytes 27656 | tf_op jit(solution)/shard_map/ppermute | solution.py:25
  90.7 7.7 %collective-permute-start.19 = (f32[48,48]{1,0:T(8,128)S(1)}, f32[48,48]{1,0:T(8,128)S(1)}, u32[]{:S(2)}, u32[]{:S(2)}) collective-permute-start(f32[48,48]{1,0:T(8,128)S(1)} %add_add_fusion.3), channel_id=1, source_target_pairs={{0,2},{1,3},{2,0},{3,1},{4,6},{5,7},{6,4},{7,5},{8,10},{9,11},{10,... | collective-permute-start | bytes 27656 | tf_op jit(solution)/shard_map/ppermute | solution.py:25
  96.4 5.0 %collective-permute-start.20 = (f32[48,48]{1,0:T(8,128)S(1)}, f32[48,48]{1,0:T(8,128)S(1)}, u32[]{:S(2)}, u32[]{:S(2)}) collective-permute-start(f32[48,48]{1,0:T(8,128)S(1)} %add_add_fusion.3), channel_id=1, source_target_pairs={{0,3},{1,2},{2,1},{3,0},{4,7},{5,6},{6,5},{7,4},{8,11},{9,10},{10,... | collective-permute-start | bytes 27656 | tf_op jit(solution)/shard_map/ppermute | solution.py:25
  101.5 3.9 %collective-permute-start.21 = (f32[48,48]{1,0:T(8,128)S(1)}, f32[48,48]{1,0:T(8,128)S(1)}, u32[]{:S(2)}, u32[]{:S(2)}) collective-permute-start(f32[48,48]{1,0:T(8,128)S(1)} %add_add_fusion.2), channel_id=1, source_target_pairs={{0,4},{1,5},{2,6},{3,7},{4,0},{5,1},{6,2},{7,3},{8,12},{9,13},{10,... | collective-permute-start | bytes 27656 | tf_op jit(solution)/shard_map/ppermute | solution.py:25
  102.0 5.3 %collective-permute-start.22 = (f32[48,48]{1,0:T(8,128)S(1)}, f32[48,48]{1,0:T(8,128)S(1)}, u32[]{:S(2)}, u32[]{:S(2)}) collective-permute-start(f32[48,48]{1,0:T(8,128)S(1)} %add_add_fusion.2), channel_id=1, source_target_pairs={{0,8},{1,9},{2,10},{3,11},{4,12},{5,13},{6,14},{7,15},{8,0},{9,1},... | collective-permute-start | bytes 27656 | tf_op jit(solution)/shard_map/ppermute | solution.py:25
  104.6 3.8 %collective-permute-start.23 = (f32[48,48]{1,0:T(8,128)S(1)}, f32[48,48]{1,0:T(8,128)S(1)}, u32[]{:S(2)}, u32[]{:S(2)}) collective-permute-start(f32[48,48]{1,0:T(8,128)S(1)} %add_add_fusion.2), channel_id=1, source_target_pairs={{0,12},{1,13},{2,14},{3,15},{4,8},{5,9},{6,10},{7,11},{8,4},{9,5},... | collective-permute-start | bytes 27656 | tf_op jit(solution)/shard_map/ppermute | solution.py:25
  (13 other events, 31.5 us)

commit v11 on v5

--- a/solution.py
+++ b/solution.py
@@ -39,9 +39,9 @@
 
 
 def up_along(values, axis, width):
-    count = values.shape[axis]
-    blank = jnp.zeros_like(lax.slice_in_dim(values, 0, width, axis=axis))
-    return jnp.concatenate([lax.slice_in_dim(values, width, count, axis=axis), blank], axis=axis)
+    config = [(0, 0, 0)] * values.ndim
+    config[axis] = (-width, width, 0)
+    return lax.pad(values, jnp.zeros((), values.dtype), config)
 
 
 def block_gram(former, latter):

time: 134 us -> 129 us (0.963)
  local copies, waits for them, and re-layouts: 20.2 us -> 14.5 us
    slice x27 -> x0, local copies, waits for them, and re-layouts: 5.1 us -> none  [up_along(): lax.slice_in_dim(values, width, count, axis=axis)]
  transfers between devices with their start and end apart: 24 -> 24, of which waited for: 10 -> 10; matrix products, arithmetic and copies ran while one was open for 8% -> 7% of each run, Pallas kernels for 0% -> 0%
where the time goes in v11:
time: 129 us; the launch traced here: 127 us
  starting transfers between devices  56.9 us (44%)
  other arithmetic  26.5 us (21%)
  waiting for transfers between devices  21.4 us (17%)
  local copies, waits for them, and re-layouts  14.5 us (11%)
  matrix products  6.09 us (5%)
  between operations  1.47 us (1%)
    ppermute x12, starting transfers between devices, mesh_sum(): lax.ppermute(block, axis, [(i, i ^ step * m) for i in range(count)])  22.5 us
    ppermute x6, starting transfers between devices, backward(): return lax.ppermute(block, axis, [(i + 1, i) for i in range(count - 1)])  18.8 us
    ppermute x12, waiting for transfers between devices, mesh_sum(): lax.ppermute(block, axis, [(i, i ^ step * m) for i in range(count)])  16.2 us
    ppermute x6, starting transfers between devices, forward(): return lax.ppermute(block, axis, [(i, i + 1) for i in range(count - 1)])  15.6 us
    ppermute x6, waiting for transfers between devices, forward(): return lax.ppermute(block, axis, [(i, i + 1) for i in range(count - 1)])  5.2 us
    another operation x3, other arithmetic, body(): full_low = jnp.linalg.cholesky(span_gram)  5.05 us
    another operation x3, other arithmetic, solve_small(): low_factor = jnp.linalg.cholesky(normal)  3.6 us
    mul x8, other arithmetic, precondition(): inv_piv * (source + lows[0] * low_x(lower_sol) + lows[1] * low_y(lower_so...  3.34 us
  transfers between devices with their start and end apart: 24, of which 10 were waited for; matrix products, arithmetic and copies ran while one was open for 7% of the time, Pallas kernels for 0%

profile of v11, /device:TPU:40, one launch (start us, length us, event | category | flops | bytes accessed | tf_op | source)
XLA Modules:
  0.0 126.9 jit_solution(5804282563619649354)
XLA Ops:
  3.3 3.4 %collective-permute-start.1 = (f32[17,16,64]{2,0,1:T(8,128)S(1)}, f32[17,16,64]{2,0,1:T(8,128)}, u32[]{:S(2)}, u32[]{:S(2)}) collective-permute-start(f32[17,16,64]{2,0,1:T(8,128)S(1)} %pad_maximum_fusion), channel_id=1, source_target_pairs={{0,1},{1,2},{2,3},{3,4},{4,5},{5,6},{6,7},{7,8},{8,9},{9,10},{10,1... | collective-permute-start | bytes 208904 | tf_op jit(solution)/shard_map/ppermute | solution.py:107
  9.4 4.6 %collective-permute-start.3 = (f32[16,16,64]{2,0,1:T(8,128)S(1)}, f32[16,16,64]{2,0,1:T(8,128)}, u32[]{:S(2)}, u32[]{:S(2)}) collective-permute-start(f32[16,16,64]{2,0,1:T(8,128)S(1)} %get-tuple-element.35), channel_id=1, source_target_pairs={{1,0},{2,1},{3,2},{4,3},{5,4},{6,5},{7,6},{8,7},{9,8},{10,9},{11,1... | collective-permute-start | bytes 196616 | tf_op jit(solution)/shard_map/ppermute | solution.py:111
  14.0 3.4 %collective-permute-start.2 = (f32[16,1,512]{2,0,1:T(8,128)}, f32[16,1,512]{2,0,1:T(8,128)S(1)}, u32[]{:S(2)}, u32[]{:S(2)}) collective-permute-start(f32[16,1,512]{2,0,1:T(8,128)} %get-tuple-element.31), channel_id=1, source_target_pairs={{16,0},{32,16},{48,32},{64,48},{80,64},{96,80},{112,96},{128,112},... | collective-permute-start | bytes 98312 | tf_op jit(solution)/shard_map/ppermute | solution.py:111
  31.1 2.4 %collective-permute-start.6 = (f32[16,16,64]{2,0,1:T(8,128)S(1)}, f32[16,16,64]{2,0,1:T(8,128)S(1)}, u32[]{:S(2)}, u32[]{:S(2)}) collective-permute-start(f32[16,16,64]{2,0,1:T(8,128)S(1)} %get-tuple-element.27), channel_id=1, source_target_pairs={{1,0},{2,1},{3,2},{4,3},{5,4},{6,5},{7,6},{8,7},{9,8},{10,9},{11,1... | collective-permute-start | bytes 196616 | tf_op jit(solution)/shard_map/ppermute | solution.py:111
  33.6 3.4 %collective-permute-start.7 = (f32[16,16,64]{2,0,1:T(8,128)S(1)}, f32[16,16,64]{2,0,1:T(8,128)S(1)}, u32[]{:S(2)}, u32[]{:S(2)}) collective-permute-start(f32[16,16,64]{2,0,1:T(8,128)S(1)} %get-tuple-element.28), channel_id=1, source_target_pairs={{0,1},{1,2},{2,3},{3,4},{4,5},{5,6},{6,7},{7,8},{8,9},{9,10},{10,1... | collective-permute-start | bytes 196616 | tf_op jit(solution)/shard_map/ppermute | solution.py:107
  38.9 2.6 %collective-permute-start.5 = (f32[16,1,512]{2,0,1:T(8,128)S(1)}, f32[16,1,512]{2,0,1:T(8,128)S(1)}, u32[]{:S(2)}, u32[]{:S(2)}) collective-permute-start(f32[16,1,512]{2,0,1:T(8,128)S(1)} %get-tuple-element.24), channel_id=1, source_target_pairs={{0,16},{16,32},{32,48},{48,64},{64,80},{80,96},{96,112},{112,128},... | collective-permute-start | bytes 98312 | tf_op jit(solution)/shard_map/ppermute | solution.py:107
  41.6 2.5 %collective-permute-done.5 = f32[16,1,512]{2,0,1:T(8,128)S(1)} collective-permute-done((f32[16,1,512]{2,0,1:T(8,128)S(1)}, f32[16,1,512]{2,0,1:T(8,128)S(1)}, u32[]{:S(2)}, u32[]{:S(2)}) %collective-permute-start.5) | collective-permute-done | bytes 32800 | tf_op jit(solution)/shard_map/ppermute | solution.py:107
  48.7 4.6 %collective-permute-start.10 = (f32[16,16,64]{2,0,1:T(8,128)S(1)}, f32[16,16,64]{2,0,1:T(8,128)S(1)}, u32[]{:S(2)}, u32[]{:S(2)}) collective-permute-start(f32[16,16,64]{2,0,1:T(8,128)S(1)} %get-tuple-element.19), channel_id=1, source_target_pairs={{1,0},{2,1},{3,2},{4,3},{5,4},{6,5},{7,6},{8,7},{9,8},{10,9},{11,1... | collective-permute-start | bytes 196616 | tf_op jit(solution)/shard_map/ppermute | solution.py:111
  57.1 2.4 %collective-permute-start.9 = (f32[16,1,512]{2,0,1:T(8,128)S(1)}, f32[16,1,512]{2,0,1:T(8,128)S(1)}, u32[]{:S(2)}, u32[]{:S(2)}) collective-permute-start(f32[16,1,512]{2,0,1:T(8,128)S(1)} %get-tuple-element.16), channel_id=1, source_target_pairs={{0,16},{16,32},{32,48},{48,64},{64,80},{80,96},{96,112},{112,128},... | collective-permute-start | bytes 98312 | tf_op jit(solution)/shard_map/ppermute | solution.py:107
  59.7 2.7 %collective-permute-done.9 = f32[16,1,512]{2,0,1:T(8,128)S(1)} collective-permute-done((f32[16,1,512]{2,0,1:T(8,128)S(1)}, f32[16,1,512]{2,0,1:T(8,128)S(1)}, u32[]{:S(2)}, u32[]{:S(2)}) %collective-permute-start.9) | collective-permute-done | bytes 32800 | tf_op jit(solution)/shard_map/ppermute | solution.py:107
  66.5 2.0 %collective-permute-done.13 = f32[48,48]{0,1:T(8,128)S(1)} collective-permute-done((f32[48,48]{0,1:T(8,128)S(1)}, f32[48,48]{0,1:T(8,128)S(1)}, u32[]{:S(2)}, u32[]{:S(2)}) %collective-permute-start.13) | collective-permute-done | bytes 9248 | tf_op jit(solution)/shard_map/ppermute | solution.py:25
  68.6 6.6 %collective-permute-start.15 = (f32[48,48]{0,1:T(8,128)S(1)}, f32[48,48]{0,1:T(8,128)S(1)}, u32[]{:S(2)}, u32[]{:S(2)}) collective-permute-start(f32[48,48]{0,1:T(8,128)S(1)} %add_add_fusion.4), channel_id=1, source_target_pairs={{0,64},{16,80},{32,96},{48,112},{64,0},{80,16},{96,32},{112,48},{1... | collective-permute-start | bytes 27656 | tf_op jit(solution)/shard_map/ppermute | solution.py:25
  75.2 3.9 %collective-permute-start.16 = (f32[48,48]{0,1:T(8,128)S(1)}, f32[48,48]{0,1:T(8,128)S(1)}, u32[]{:S(2)}, u32[]{:S(2)}) collective-permute-start(f32[48,48]{0,1:T(8,128)S(1)} %add_add_fusion.4), channel_id=1, source_target_pairs={{0,128},{16,144},{32,160},{48,176},{64,192},{80,208},{96,224},{112... | collective-permute-start | bytes 27656 | tf_op jit(solution)/shard_map/ppermute | solution.py:25
  79.6 3.5 %collective-permute-done.16 = f32[48,48]{0,1:T(8,128)S(1)} collective-permute-done((f32[48,48]{0,1:T(8,128)S(1)}, f32[48,48]{0,1:T(8,128)S(1)}, u32[]{:S(2)}, u32[]{:S(2)}) %collective-permute-start.16) | collective-permute-done | bytes 9248 | tf_op jit(solution)/shard_map/ppermute | solution.py:25
  83.1 2.2 %collective-permute-done.17 = f32[48,48]{0,1:T(8,128)S(1)} collective-permute-done((f32[48,48]{0,1:T(8,128)S(1)}, f32[48,48]{0,1:T(8,128)S(1)}, u32[]{:S(2)}, u32[]{:S(2)}) %collective-permute-start.17) | collective-permute-done | bytes 9248 | tf_op jit(solution)/shard_map/ppermute | solution.py:25
  85.4 5.7 %collective-permute-start.19 = (f32[48,48]{0,1:T(8,128)S(1)}, f32[48,48]{0,1:T(8,128)S(1)}, u32[]{:S(2)}, u32[]{:S(2)}) collective-permute-start(f32[48,48]{0,1:T(8,128)S(1)} %add_add_fusion.3), channel_id=1, source_target_pairs={{0,2},{1,3},{2,0},{3,1},{4,6},{5,7},{6,4},{7,5},{8,10},{9,11},{10,... | collective-permute-start | bytes 27656 | tf_op jit(solution)/shard_map/ppermute | solution.py:25
  91.1 2.1 %collective-permute-done.19 = f32[48,48]{0,1:T(8,128)S(1)} collective-permute-done((f32[48,48]{0,1:T(8,128)S(1)}, f32[48,48]{0,1:T(8,128)S(1)}, u32[]{:S(2)}, u32[]{:S(2)}) %collective-permute-start.19) | collective-permute-done | bytes 9248 | tf_op jit(solution)/shard_map/ppermute | solution.py:25
  93.2 3.0 %collective-permute-done.20 = f32[48,48]{0,1:T(8,128)S(1)} collective-permute-done((f32[48,48]{0,1:T(8,128)S(1)}, f32[48,48]{0,1:T(8,128)S(1)}, u32[]{:S(2)}, u32[]{:S(2)}) %collective-permute-start.20) | collective-permute-done | bytes 9248 | tf_op jit(solution)/shard_map/ppermute | solution.py:25
  96.9 2.6 %collective-permute-start.22 = (f32[48,48]{0,1:T(8,128)S(1)}, f32[48,48]{0,1:T(8,128)S(1)}, u32[]{:S(2)}, u32[]{:S(2)}) collective-permute-start(f32[48,48]{0,1:T(8,128)S(1)} %add_add_fusion.2), channel_id=1, source_target_pairs={{0,8},{1,9},{2,10},{3,11},{4,12},{5,13},{6,14},{7,15},{8,0},{9,1},... | collective-permute-start | bytes 27656 | tf_op jit(solution)/shard_map/ppermute | solution.py:25
  100.3 2.0 %collective-permute-done.22 = f32[48,48]{0,1:T(8,128)S(1)} collective-permute-done((f32[48,48]{0,1:T(8,128)S(1)}, f32[48,48]{0,1:T(8,128)S(1)}, u32[]{:S(2)}, u32[]{:S(2)}) %collective-permute-start.22) | collective-permute-done | bytes 9248 | tf_op jit(solution)/shard_map/ppermute | solution.py:25
  103.4 4.4 %cholesky.31 = f32[48,48]{1,0:T(8,128)S(1)} custom-call(f32[48,48]{1,0:T(8,128)S(1)} %fusion.100), custom_call_target="Cholesky" | custom-call | tf_op jit(solution)/shard_map/jit(cholesky)/cholesky | solution.py:211
  109.8 2.4 %custom-call.14 = f32[1,32,32]{1,2,0:T(8,128)S(1)} custom-call(f32[1,32,32]{2,1,0:T(8,128)S(1)} %fusion.108), custom_call_target="InvertDiagBlocksLowerTriangular" | custom-call | tf_op jit(solution)/shard_map/triangular_solve | solution.py:214
  113.2 2.9 %cholesky.59 = f32[32,32]{1,0:T(8,128)S(1)} custom-call(f32[32,32]{1,0:T(8,128)S(1)} %fusion.113), custom_call_target="Cholesky" | custom-call | tf_op jit(solution)/shard_map/jit(cholesky)/cholesky | solution.py:60
  117.4 2.4 %custom-call.15 = f32[1,32,32]{1,2,0:T(8,128)S(1)} custom-call(f32[1,32,32]{2,1,0:T(8,128)S(1)} %fusion.105), custom_call_target="InvertDiagBlocksLowerTriangular" | custom-call | tf_op jit(solution)/shard_map/triangular_solve | solution.py:62
  (160 shorter events, 47.8 us)
Async XLA Ops:
  3.3 19.1 %collective-permute-start.1 = (f32[17,16,64]{2,0,1:T(8,128)S(1)}, f32[17,16,64]{2,0,1:T(8,128)}, u32[]{:S(2)}, u32[]{:S(2)}) collective-permute-start(f32[17,16,64]{2,0,1:T(8,128)S(1)} %pad_maximum_fusion), channel_id=1, source_target_pairs={{0,1},{1,2},{2,3},{3,4},{4,5},{5,6},{6,7},{7,8},{8,9},{9,10},{10,1... | collective-permute-start | bytes 208904 | tf_op jit(solution)/shard_map/ppermute | solution.py:107
  7.5 13.5 %collective-permute-start = (f32[17,1,512]{2,0,1:T(8,128)S(1)}, f32[17,1,512]{2,0,1:T(8,128)}, u32[]{:S(2)}, u32[]{:S(2)}) collective-permute-start(f32[17,1,512]{2,0,1:T(8,128)S(1)} %pad_maximum_fusion.1), channel_id=1, source_target_pairs={{0,16},{16,32},{32,48},{48,64},{64,80},{80,96},{96,112},{112,128},... | collective-permute-start | bytes 104456 | tf_op jit(solution)/shard_map/ppermute | solution.py:107
  9.4 16.2 %collective-permute-start.3 = (f32[16,16,64]{2,0,1:T(8,128)S(1)}, f32[16,16,64]{2,0,1:T(8,128)}, u32[]{:S(2)}, u32[]{:S(2)}) collective-permute-start(f32[16,16,64]{2,0,1:T(8,128)S(1)} %get-tuple-element.35), channel_id=1, source_target_pairs={{1,0},{2,1},{3,2},{4,3},{5,4},{6,5},{7,6},{8,7},{9,8},{10,9},{11,1... | collective-permute-start | bytes 196616 | tf_op jit(solution)/shard_map/ppermute | solution.py:111
  14.0 11.6 %collective-permute-start.2 = (f32[16,1,512]{2,0,1:T(8,128)}, f32[16,1,512]{2,0,1:T(8,128)S(1)}, u32[]{:S(2)}, u32[]{:S(2)}) collective-permute-start(f32[16,1,512]{2,0,1:T(8,128)} %get-tuple-element.31), channel_id=1, source_target_pairs={{16,0},{32,16},{48,32},{64,48},{80,64},{96,80},{112,96},{128,112},... | collective-permute-start | bytes 98312 | tf_op jit(solution)/shard_map/ppermute | solution.py:111
  31.1 13.0 %collective-permute-start.6 = (f32[16,16,64]{2,0,1:T(8,128)S(1)}, f32[16,16,64]{2,0,1:T(8,128)S(1)}, u32[]{:S(2)}, u32[]{:S(2)}) collective-permute-start(f32[16,16,64]{2,0,1:T(8,128)S(1)} %get-tuple-element.27), channel_id=1, source_target_pairs={{1,0},{2,1},{3,2},{4,3},{5,4},{6,5},{7,6},{8,7},{9,8},{10,9},{11,1... | collective-permute-start | bytes 196616 | tf_op jit(solution)/shard_map/ppermute | solution.py:111
  33.6 10.6 %collective-permute-start.7 = (f32[16,16,64]{2,0,1:T(8,128)S(1)}, f32[16,16,64]{2,0,1:T(8,128)S(1)}, u32[]{:S(2)}, u32[]{:S(2)}) collective-permute-start(f32[16,16,64]{2,0,1:T(8,128)S(1)} %get-tuple-element.28), channel_id=1, source_target_pairs={{0,1},{1,2},{2,3},{3,4},{4,5},{5,6},{6,7},{7,8},{8,9},{9,10},{10,1... | collective-permute-start | bytes 196616 | tf_op jit(solution)/shard_map/ppermute | solution.py:107
  37.0 4.6 %collective-permute-start.4 = (f32[16,1,512]{2,0,1:T(8,128)S(1)}, f32[16,1,512]{2,0,1:T(8,128)S(1)}, u32[]{:S(2)}, u32[]{:S(2)}) collective-permute-start(f32[16,1,512]{2,0,1:T(8,128)S(1)} %get-tuple-element.23), channel_id=1, source_target_pairs={{16,0},{32,16},{48,32},{64,48},{80,64},{96,80},{112,96},{128,112},... | collective-permute-start | bytes 98312 | tf_op jit(solution)/shard_map/ppermute | solution.py:111
  38.9 5.2 %collective-permute-start.5 = (f32[16,1,512]{2,0,1:T(8,128)S(1)}, f32[16,1,512]{2,0,1:T(8,128)S(1)}, u32[]{:S(2)}, u32[]{:S(2)}) collective-permute-start(f32[16,1,512]{2,0,1:T(8,128)S(1)} %get-tuple-element.24), channel_id=1, source_target_pairs={{0,16},{16,32},{32,48},{48,64},{64,80},{80,96},{96,112},{112,128},... | collective-permute-start | bytes 98312 | tf_op jit(solution)/shard_map/ppermute | solution.py:107
  48.7 13.7 %collective-permute-start.10 = (f32[16,16,64]{2,0,1:T(8,128)S(1)}, f32[16,16,64]{2,0,1:T(8,128)S(1)}, u32[]{:S(2)}, u32[]{:S(2)}) collective-permute-start(f32[16,16,64]{2,0,1:T(8,128)S(1)} %get-tuple-element.19), channel_id=1, source_target_pairs={{1,0},{2,1},{3,2},{4,3},{5,4},{6,5},{7,6},{8,7},{9,8},{10,9},{11,1... | collective-permute-start | bytes 196616 | tf_op jit(solution)/shard_map/ppermute | solution.py:111
  53.2 9.1 %collective-permute-start.11 = (f32[16,16,64]{2,0,1:T(8,128)S(1)}, f32[16,16,64]{2,0,1:T(8,128)S(1)}, u32[]{:S(2)}, u32[]{:S(2)}) collective-permute-start(f32[16,16,64]{2,0,1:T(8,128)S(1)} %get-tuple-element.20), channel_id=1, source_target_pairs={{0,1},{1,2},{2,3},{3,4},{4,5},{5,6},{6,7},{7,8},{8,9},{9,10},{10,1... | collective-permute-start | bytes 196616 | tf_op jit(solution)/shard_map/ppermute | solution.py:107
  55.2 4.5 %collective-permute-start.8 = (f32[16,1,512]{2,0,1:T(8,128)S(1)}, f32[16,1,512]{2,0,1:T(8,128)S(1)}, u32[]{:S(2)}, u32[]{:S(2)}) collective-permute-start(f32[16,1,512]{2,0,1:T(8,128)S(1)} %get-tuple-element.15), channel_id=1, source_target_pairs={{16,0},{32,16},{48,32},{64,48},{80,64},{96,80},{112,96},{128,112},... | collective-permute-start | bytes 98312 | tf_op jit(solution)/shard_map/ppermute | solution.py:111
  57.1 5.2 %collective-permute-start.9 = (f32[16,1,512]{2,0,1:T(8,128)S(1)}, f32[16,1,512]{2,0,1:T(8,128)S(1)}, u32[]{:S(2)}, u32[]{:S(2)}) collective-permute-start(f32[16,1,512]{2,0,1:T(8,128)S(1)} %get-tuple-element.16), channel_id=1, source_target_pairs={{0,16},{16,32},{32,48},{48,64},{64,80},{80,96},{96,112},{112,128},... | collective-permute-start | bytes 98312 | tf_op jit(solution)/shard_map/ppermute | solution.py:107
  64.6 2.0 %collective-permute-start.12 = (f32[48,48]{0,1:T(8,128)S(1)}, f32[48,48]{0,1:T(8,128)S(1)}, u32[]{:S(2)}, u32[]{:S(2)}) collective-permute-start(f32[48,48]{0,1:T(8,128)S(1)} %fusion.6), channel_id=1, source_target_pairs={{0,16},{16,0},{32,48},{48,32},{64,80},{80,64},{96,112},{112,96},{1... | collective-permute-start | bytes 27656 | tf_op jit(solution)/shard_map/ppermute | solution.py:25
  64.7 3.9 %collective-permute-start.13 = (f32[48,48]{0,1:T(8,128)S(1)}, f32[48,48]{0,1:T(8,128)S(1)}, u32[]{:S(2)}, u32[]{:S(2)}) collective-permute-start(f32[48,48]{0,1:T(8,128)S(1)} %fusion.6), channel_id=1, source_target_pairs={{0,32},{16,48},{32,0},{48,16},{64,96},{80,112},{96,64},{112,80},{1... | collective-permute-start | bytes 27656 | tf_op jit(solution)/shard_map/ppermute | solution.py:25
  64.8 3.8 %collective-permute-start.14 = (f32[48,48]{0,1:T(8,128)S(1)}, f32[48,48]{0,1:T(8,128)S(1)}, u32[]{:S(2)}, u32[]{:S(2)}) collective-permute-start(f32[48,48]{0,1:T(8,128)S(1)} %fusion.6), channel_id=1, source_target_pairs={{0,48},{16,32},{32,16},{48,0},{64,112},{80,96},{96,80},{112,64},{1... | collective-permute-start | bytes 27656 | tf_op jit(solution)/shard_map/ppermute | solution.py:25
  68.6 11.0 %collective-permute-start.15 = (f32[48,48]{0,1:T(8,128)S(1)}, f32[48,48]{0,1:T(8,128)S(1)}, u32[]{:S(2)}, u32[]{:S(2)}) collective-permute-start(f32[48,48]{0,1:T(8,128)S(1)} %add_add_fusion.4), channel_id=1, source_target_pairs={{0,64},{16,80},{32,96},{48,112},{64,0},{80,16},{96,32},{112,48},{1... | collective-permute-start | bytes 27656 | tf_op jit(solution)/shard_map/ppermute | solution.py:25
  75.2 7.9 %collective-permute-start.16 = (f32[48,48]{0,1:T(8,128)S(1)}, f32[48,48]{0,1:T(8,128)S(1)}, u32[]{:S(2)}, u32[]{:S(2)}) collective-permute-start(f32[48,48]{0,1:T(8,128)S(1)} %add_add_fusion.4), channel_id=1, source_target_pairs={{0,128},{16,144},{32,160},{48,176},{64,192},{80,208},{96,224},{112... | collective-permute-start | bytes 27656 | tf_op jit(solution)/shard_map/ppermute | solution.py:25
  79.1 6.2 %collective-permute-start.17 = (f32[48,48]{0,1:T(8,128)S(1)}, f32[48,48]{0,1:T(8,128)S(1)}, u32[]{:S(2)}, u32[]{:S(2)}) collective-permute-start(f32[48,48]{0,1:T(8,128)S(1)} %add_add_fusion.4), channel_id=1, source_target_pairs={{0,192},{16,208},{32,224},{48,240},{64,128},{80,144},{96,160},{112... | collective-permute-start | bytes 27656 | tf_op jit(solution)/shard_map/ppermute | solution.py:25
  85.3 5.8 %collective-permute-start.18 = (f32[48,48]{0,1:T(8,128)S(1)}, f32[48,48]{0,1:T(8,128)S(1)}, u32[]{:S(2)}, u32[]{:S(2)}) collective-permute-start(f32[48,48]{0,1:T(8,128)S(1)} %add_add_fusion.3), channel_id=1, source_target_pairs={{0,1},{1,0},{2,3},{3,2},{4,5},{5,4},{6,7},{7,6},{8,9},{9,8},{10,11... | collective-permute-start | bytes 27656 | tf_op jit(solution)/shard_map/ppermute | solution.py:25
  85.4 7.8 %collective-permute-start.19 = (f32[48,48]{0,1:T(8,128)S(1)}, f32[48,48]{0,1:T(8,128)S(1)}, u32[]{:S(2)}, u32[]{:S(2)}) collective-permute-start(f32[48,48]{0,1:T(8,128)S(1)} %add_add_fusion.3), channel_id=1, source_target_pairs={{0,2},{1,3},{2,0},{3,1},{4,6},{5,7},{6,4},{7,5},{8,10},{9,11},{10,... | collective-permute-start | bytes 27656 | tf_op jit(solution)/shard_map/ppermute | solution.py:25
  91.1 5.0 %collective-permute-start.20 = (f32[48,48]{0,1:T(8,128)S(1)}, f32[48,48]{0,1:T(8,128)S(1)}, u32[]{:S(2)}, u32[]{:S(2)}) collective-permute-start(f32[48,48]{0,1:T(8,128)S(1)} %add_add_fusion.3), channel_id=1, source_target_pairs={{0,3},{1,2},{2,1},{3,0},{4,7},{5,6},{6,5},{7,4},{8,11},{9,10},{10,... | collective-permute-start | bytes 27656 | tf_op jit(solution)/shard_map/ppermute | solution.py:25
  96.2 4.1 %collective-permute-start.21 = (f32[48,48]{0,1:T(8,128)S(1)}, f32[48,48]{0,1:T(8,128)S(1)}, u32[]{:S(2)}, u32[]{:S(2)}) collective-permute-start(f32[48,48]{0,1:T(8,128)S(1)} %add_add_fusion.2), channel_id=1, source_target_pairs={{0,4},{1,5},{2,6},{3,7},{4,0},{5,1},{6,2},{7,3},{8,12},{9,13},{10,... | collective-permute-start | bytes 27656 | tf_op jit(solution)/shard_map/ppermute | solution.py:25
  96.9 5.3 %collective-permute-start.22 = (f32[48,48]{0,1:T(8,128)S(1)}, f32[48,48]{0,1:T(8,128)S(1)}, u32[]{:S(2)}, u32[]{:S(2)}) collective-permute-start(f32[48,48]{0,1:T(8,128)S(1)} %add_add_fusion.2), channel_id=1, source_target_pairs={{0,8},{1,9},{2,10},{3,11},{4,12},{5,13},{6,14},{7,15},{8,0},{9,1},... | collective-permute-start | bytes 27656 | tf_op jit(solution)/shard_map/ppermute | solution.py:25
  99.5 3.8 %collective-permute-start.23 = (f32[48,48]{0,1:T(8,128)S(1)}, f32[48,48]{0,1:T(8,128)S(1)}, u32[]{:S(2)}, u32[]{:S(2)}) collective-permute-start(f32[48,48]{0,1:T(8,128)S(1)} %add_add_fusion.2), channel_id=1, source_target_pairs={{0,12},{1,13},{2,14},{3,15},{4,8},{5,9},{6,10},{7,11},{8,4},{9,5},... | collective-permute-start | bytes 27656 | tf_op jit(solution)/shard_map/ppermute | solution.py:25
  (10 other events, 20.2 us)

commit v12 on v11

--- a/solution.py
+++ b/solution.py
@@ -33,9 +33,9 @@
 
 
 def low_along(values, axis, width):
-    count = values.shape[axis]
-    blank = jnp.zeros_like(lax.slice_in_dim(values, 0, width, axis=axis))
-    return jnp.concatenate([blank, lax.slice_in_dim(values, 0, count - width, axis=axis)], axis=axis)
+    config = [(0, 0, 0)] * values.ndim
+    config[axis] = (width, -width, 0)
+    return lax.pad(values, jnp.zeros((), values.dtype), config)
 
 
 def up_along(values, axis, width):

time: 129 us -> 130 us (level)
  transfers between devices with their start and end apart: 24 -> 24, of which waited for: 10 -> 10; matrix products, arithmetic and copies ran while one was open for 7% -> 8% of each run, Pallas kernels for 0% -> 0%
where the time goes in v12:
time: 130 us; the launch traced here: 127 us
  starting transfers between devices  56.7 us (44%)
  other arithmetic  27.6 us (21%)
  waiting for transfers between devices  21.4 us (16%)
  local copies, waits for them, and re-layouts  14.9 us (11%)
  matrix products  5.28 us (4%)
  between operations  1.44 us (1%)
    ppermute x12, starting transfers between devices, mesh_sum(): lax.ppermute(block, axis, [(i, i ^ step * m) for i in range(count)])  22.3 us
    ppermute x6, starting transfers between devices, backward(): return lax.ppermute(block, axis, [(i + 1, i) for i in range(count - 1)])  18.8 us
    ppermute x12, waiting for transfers between devices, mesh_sum(): lax.ppermute(block, axis, [(i, i ^ step * m) for i in range(count)])  16.2 us
    ppermute x6, starting transfers between devices, forward(): return lax.ppermute(block, axis, [(i, i + 1) for i in range(count - 1)])  15.6 us
    ppermute x6, waiting for transfers between devices, forward(): return lax.ppermute(block, axis, [(i, i + 1) for i in range(count - 1)])  5.2 us
    another operation x3, other arithmetic, body(): full_low = jnp.linalg.cholesky(span_gram)  5.05 us
    another operation x3, other arithmetic, solve_small(): low_factor = jnp.linalg.cholesky(normal)  3.6 us
    another operation x2, other arithmetic, solve_small(): lax.linalg.triangular_solve(low_factor, partial_sol, left_side=True, lowe...  3.09 us
  transfers between devices with their start and end apart: 24, of which 10 were waited for; matrix products, arithmetic and copies ran while one was open for 8% of the time, Pallas kernels for 0%

profile of v12, /device:TPU:40, one launch (start us, length us, event | category | flops | bytes accessed | tf_op | source)
XLA Modules:
  0.0 127.4 jit_solution(15594160047263788311)
XLA Ops:
  3.5 3.4 %collective-permute-start.1 = (f32[17,16,64]{2,0,1:T(8,128)S(1)}, f32[17,16,64]{2,0,1:T(8,128)}, u32[]{:S(2)}, u32[]{:S(2)}) collective-permute-start(f32[17,16,64]{2,0,1:T(8,128)S(1)} %pad_maximum_fusion), channel_id=1, source_target_pairs={{0,1},{1,2},{2,3},{3,4},{4,5},{5,6},{6,7},{7,8},{8,9},{9,10},{10,1... | collective-permute-start | bytes 208904 | tf_op jit(solution)/shard_map/ppermute | solution.py:107
  10.2 4.6 %collective-permute-start.3 = (f32[16,16,64]{2,0,1:T(8,128)}, f32[16,16,64]{2,0,1:T(8,128)}, u32[]{:S(2)}, u32[]{:S(2)}) collective-permute-start(f32[16,16,64]{2,0,1:T(8,128)} %get-tuple-element.35), channel_id=1, source_target_pairs={{1,0},{2,1},{3,2},{4,3},{5,4},{6,5},{7,6},{8,7},{9,8},{10,9},{11,1... | collective-permute-start | bytes 196616 | tf_op jit(solution)/shard_map/ppermute | solution.py:111
  14.7 3.4 %collective-permute-start.2 = (f32[16,1,512]{2,0,1:T(8,128)}, f32[16,1,512]{2,0,1:T(8,128)}, u32[]{:S(2)}, u32[]{:S(2)}) collective-permute-start(f32[16,1,512]{2,0,1:T(8,128)} %get-tuple-element.31), channel_id=1, source_target_pairs={{16,0},{32,16},{48,32},{64,48},{80,64},{96,80},{112,96},{128,112},... | collective-permute-start | bytes 98312 | tf_op jit(solution)/shard_map/ppermute | solution.py:111
  31.8 2.4 %collective-permute-start.6 = (f32[16,16,64]{2,0,1:T(8,128)S(1)}, f32[16,16,64]{2,0,1:T(8,128)S(1)}, u32[]{:S(2)}, u32[]{:S(2)}) collective-permute-start(f32[16,16,64]{2,0,1:T(8,128)S(1)} %get-tuple-element.27), channel_id=1, source_target_pairs={{1,0},{2,1},{3,2},{4,3},{5,4},{6,5},{7,6},{8,7},{9,8},{10,9},{11,1... | collective-permute-start | bytes 196616 | tf_op jit(solution)/shard_map/ppermute | solution.py:111
  34.2 3.4 %collective-permute-start.7 = (f32[16,16,64]{2,0,1:T(8,128)S(1)}, f32[16,16,64]{2,0,1:T(8,128)S(1)}, u32[]{:S(2)}, u32[]{:S(2)}) collective-permute-start(f32[16,16,64]{2,0,1:T(8,128)S(1)} %get-tuple-element.28), channel_id=1, source_target_pairs={{0,1},{1,2},{2,3},{3,4},{4,5},{5,6},{6,7},{7,8},{8,9},{9,10},{10,1... | collective-permute-start | bytes 196616 | tf_op jit(solution)/shard_map/ppermute | solution.py:107
  39.5 2.6 %collective-permute-start.5 = (f32[16,1,512]{2,0,1:T(8,128)S(1)}, f32[16,1,512]{2,0,1:T(8,128)S(1)}, u32[]{:S(2)}, u32[]{:S(2)}) collective-permute-start(f32[16,1,512]{2,0,1:T(8,128)S(1)} %get-tuple-element.24), channel_id=1, source_target_pairs={{0,16},{16,32},{32,48},{48,64},{64,80},{80,96},{96,112},{112,128},... | collective-permute-start | bytes 98312 | tf_op jit(solution)/shard_map/ppermute | solution.py:107
  42.3 2.5 %collective-permute-done.5 = f32[16,1,512]{2,0,1:T(8,128)S(1)} collective-permute-done((f32[16,1,512]{2,0,1:T(8,128)S(1)}, f32[16,1,512]{2,0,1:T(8,128)S(1)}, u32[]{:S(2)}, u32[]{:S(2)}) %collective-permute-start.5) | collective-permute-done | bytes 32800 | tf_op jit(solution)/shard_map/ppermute | solution.py:107
  49.0 4.6 %collective-permute-start.10 = (f32[16,16,64]{2,0,1:T(8,128)S(1)}, f32[16,16,64]{2,0,1:T(8,128)S(1)}, u32[]{:S(2)}, u32[]{:S(2)}) collective-permute-start(f32[16,16,64]{2,0,1:T(8,128)S(1)} %get-tuple-element.19), channel_id=1, source_target_pairs={{1,0},{2,1},{3,2},{4,3},{5,4},{6,5},{7,6},{8,7},{9,8},{10,9},{11,1... | collective-permute-start | bytes 196616 | tf_op jit(solution)/shard_map/ppermute | solution.py:111
  57.4 2.4 %collective-permute-start.9 = (f32[16,1,512]{2,0,1:T(8,128)S(1)}, f32[16,1,512]{2,0,1:T(8,128)S(1)}, u32[]{:S(2)}, u32[]{:S(2)}) collective-permute-start(f32[16,1,512]{2,0,1:T(8,128)S(1)} %get-tuple-element.16), channel_id=1, source_target_pairs={{0,16},{16,32},{32,48},{48,64},{64,80},{80,96},{96,112},{112,128},... | collective-permute-start | bytes 98312 | tf_op jit(solution)/shard_map/ppermute | solution.py:107
  60.0 2.7 %collective-permute-done.9 = f32[16,1,512]{2,0,1:T(8,128)S(1)} collective-permute-done((f32[16,1,512]{2,0,1:T(8,128)S(1)}, f32[16,1,512]{2,0,1:T(8,128)S(1)}, u32[]{:S(2)}, u32[]{:S(2)}) %collective-permute-start.9) | collective-permute-done | bytes 32800 | tf_op jit(solution)/shard_map/ppermute | solution.py:107
  67.6 2.0 %collective-permute-done.13 = f32[48,48]{0,1:T(8,128)S(1)} collective-permute-done((f32[48,48]{0,1:T(8,128)S(1)}, f32[48,48]{0,1:T(8,128)S(1)}, u32[]{:S(2)}, u32[]{:S(2)}) %collective-permute-start.13) | collective-permute-done | bytes 9248 | tf_op jit(solution)/shard_map/ppermute | solution.py:25
  69.6 6.6 %collective-permute-start.15 = (f32[48,48]{0,1:T(8,128)S(1)}, f32[48,48]{0,1:T(8,128)S(1)}, u32[]{:S(2)}, u32[]{:S(2)}) collective-permute-start(f32[48,48]{0,1:T(8,128)S(1)} %add_add_fusion.4), channel_id=1, source_target_pairs={{0,64},{16,80},{32,96},{48,112},{64,0},{80,16},{96,32},{112,48},{1... | collective-permute-start | bytes 27656 | tf_op jit(solution)/shard_map/ppermute | solution.py:25
  76.2 3.9 %collective-permute-start.16 = (f32[48,48]{0,1:T(8,128)S(1)}, f32[48,48]{0,1:T(8,128)S(1)}, u32[]{:S(2)}, u32[]{:S(2)}) collective-permute-start(f32[48,48]{0,1:T(8,128)S(1)} %add_add_fusion.4), channel_id=1, source_target_pairs={{0,128},{16,144},{32,160},{48,176},{64,192},{80,208},{96,224},{112... | collective-permute-start | bytes 27656 | tf_op jit(solution)/shard_map/ppermute | solution.py:25
  80.6 3.5 %collective-permute-done.16 = f32[48,48]{0,1:T(8,128)S(1)} collective-permute-done((f32[48,48]{0,1:T(8,128)S(1)}, f32[48,48]{0,1:T(8,128)S(1)}, u32[]{:S(2)}, u32[]{:S(2)}) %collective-permute-start.16) | collective-permute-done | bytes 9248 | tf_op jit(solution)/shard_map/ppermute | solution.py:25
  84.1 2.2 %collective-permute-done.17 = f32[48,48]{0,1:T(8,128)S(1)} collective-permute-done((f32[48,48]{0,1:T(8,128)S(1)}, f32[48,48]{0,1:T(8,128)S(1)}, u32[]{:S(2)}, u32[]{:S(2)}) %collective-permute-start.17) | collective-permute-done | bytes 9248 | tf_op jit(solution)/shard_map/ppermute | solution.py:25
  86.5 5.7 %collective-permute-start.19 = (f32[48,48]{0,1:T(8,128)S(1)}, f32[48,48]{0,1:T(8,128)S(1)}, u32[]{:S(2)}, u32[]{:S(2)}) collective-permute-start(f32[48,48]{0,1:T(8,128)S(1)} %add_add_fusion.3), channel_id=1, source_target_pairs={{0,2},{1,3},{2,0},{3,1},{4,6},{5,7},{6,4},{7,5},{8,10},{9,11},{10,... | collective-permute-start | bytes 27656 | tf_op jit(solution)/shard_map/ppermute | solution.py:25
  92.2 2.1 %collective-permute-done.19 = f32[48,48]{0,1:T(8,128)S(1)} collective-permute-done((f32[48,48]{0,1:T(8,128)S(1)}, f32[48,48]{0,1:T(8,128)S(1)}, u32[]{:S(2)}, u32[]{:S(2)}) %collective-permute-start.19) | collective-permute-done | bytes 9248 | tf_op jit(solution)/shard_map/ppermute | solution.py:25
  94.2 3.0 %collective-permute-done.20 = f32[48,48]{0,1:T(8,128)S(1)} collective-permute-done((f32[48,48]{0,1:T(8,128)S(1)}, f32[48,48]{0,1:T(8,128)S(1)}, u32[]{:S(2)}, u32[]{:S(2)}) %collective-permute-start.20) | collective-permute-done | bytes 9248 | tf_op jit(solution)/shard_map/ppermute | solution.py:25
  97.8 2.6 %collective-permute-start.22 = (f32[48,48]{0,1:T(8,128)S(1)}, f32[48,48]{0,1:T(8,128)S(1)}, u32[]{:S(2)}, u32[]{:S(2)}) collective-permute-start(f32[48,48]{0,1:T(8,128)S(1)} %add_add_fusion.2), channel_id=1, source_target_pairs={{0,8},{1,9},{2,10},{3,11},{4,12},{5,13},{6,14},{7,15},{8,0},{9,1},... | collective-permute-start | bytes 27656 | tf_op jit(solution)/shard_map/ppermute | solution.py:25
  101.1 2.0 %collective-permute-done.22 = f32[48,48]{0,1:T(8,128)S(1)} collective-permute-done((f32[48,48]{0,1:T(8,128)S(1)}, f32[48,48]{0,1:T(8,128)S(1)}, u32[]{:S(2)}, u32[]{:S(2)}) %collective-permute-start.22) | collective-permute-done | bytes 9248 | tf_op jit(solution)/shard_map/ppermute | solution.py:25
  104.3 4.4 %cholesky.31 = f32[48,48]{1,0:T(8,128)S(1)} custom-call(f32[48,48]{1,0:T(8,128)S(1)} %fusion.195), custom_call_target="Cholesky" | custom-call | tf_op jit(solution)/shard_map/jit(cholesky)/cholesky | solution.py:211
  110.7 2.4 %custom-call.14 = f32[1,32,32]{1,2,0:T(8,128)S(1)} custom-call(f32[1,32,32]{2,1,0:T(8,128)S(1)} %fusion.203), custom_call_target="InvertDiagBlocksLowerTriangular" | custom-call | tf_op jit(solution)/shard_map/triangular_solve | solution.py:214
  114.0 2.9 %cholesky.59 = f32[32,32]{1,0:T(8,128)S(1)} custom-call(f32[32,32]{1,0:T(8,128)S(1)} %fusion.208), custom_call_target="Cholesky" | custom-call | tf_op jit(solution)/shard_map/jit(cholesky)/cholesky | solution.py:60
  118.2 2.4 %custom-call.15 = f32[1,32,32]{1,2,0:T(8,128)S(1)} custom-call(f32[1,32,32]{2,1,0:T(8,128)S(1)} %fusion.200), custom_call_target="InvertDiagBlocksLowerTriangular" | custom-call | tf_op jit(solution)/shard_map/triangular_solve | solution.py:62
  (154 shorter events, 48.3 us)
Async XLA Ops:
  3.5 19.9 %collective-permute-start.1 = (f32[17,16,64]{2,0,1:T(8,128)S(1)}, f32[17,16,64]{2,0,1:T(8,128)}, u32[]{:S(2)}, u32[]{:S(2)}) collective-permute-start(f32[17,16,64]{2,0,1:T(8,128)S(1)} %pad_maximum_fusion), channel_id=1, source_target_pairs={{0,1},{1,2},{2,3},{3,4},{4,5},{5,6},{6,7},{7,8},{8,9},{9,10},{10,1... | collective-permute-start | bytes 208904 | tf_op jit(solution)/shard_map/ppermute | solution.py:107
  8.3 13.5 %collective-permute-start = (f32[17,1,512]{2,0,1:T(8,128)}, f32[17,1,512]{2,0,1:T(8,128)}, u32[]{:S(2)}, u32[]{:S(2)}) collective-permute-start(f32[17,1,512]{2,0,1:T(8,128)} %pad_maximum_fusion.1), channel_id=1, source_target_pairs={{0,16},{16,32},{32,48},{48,64},{64,80},{80,96},{96,112},{112,128},... | collective-permute-start | bytes 104456 | tf_op jit(solution)/shard_map/ppermute | solution.py:107
  10.2 16.3 %collective-permute-start.3 = (f32[16,16,64]{2,0,1:T(8,128)}, f32[16,16,64]{2,0,1:T(8,128)}, u32[]{:S(2)}, u32[]{:S(2)}) collective-permute-start(f32[16,16,64]{2,0,1:T(8,128)} %get-tuple-element.35), channel_id=1, source_target_pairs={{1,0},{2,1},{3,2},{4,3},{5,4},{6,5},{7,6},{8,7},{9,8},{10,9},{11,1... | collective-permute-start | bytes 196616 | tf_op jit(solution)/shard_map/ppermute | solution.py:111
  14.7 11.8 %collective-permute-start.2 = (f32[16,1,512]{2,0,1:T(8,128)}, f32[16,1,512]{2,0,1:T(8,128)}, u32[]{:S(2)}, u32[]{:S(2)}) collective-permute-start(f32[16,1,512]{2,0,1:T(8,128)} %get-tuple-element.31), channel_id=1, source_target_pairs={{16,0},{32,16},{48,32},{64,48},{80,64},{96,80},{112,96},{128,112},... | collective-permute-start | bytes 98312 | tf_op jit(solution)/shard_map/ppermute | solution.py:111
  31.8 13.0 %collective-permute-start.6 = (f32[16,16,64]{2,0,1:T(8,128)S(1)}, f32[16,16,64]{2,0,1:T(8,128)S(1)}, u32[]{:S(2)}, u32[]{:S(2)}) collective-permute-start(f32[16,16,64]{2,0,1:T(8,128)S(1)} %get-tuple-element.27), channel_id=1, source_target_pairs={{1,0},{2,1},{3,2},{4,3},{5,4},{6,5},{7,6},{8,7},{9,8},{10,9},{11,1... | collective-permute-start | bytes 196616 | tf_op jit(solution)/shard_map/ppermute | solution.py:111
  34.2 10.6 %collective-permute-start.7 = (f32[16,16,64]{2,0,1:T(8,128)S(1)}, f32[16,16,64]{2,0,1:T(8,128)S(1)}, u32[]{:S(2)}, u32[]{:S(2)}) collective-permute-start(f32[16,16,64]{2,0,1:T(8,128)S(1)} %get-tuple-element.28), channel_id=1, source_target_pairs={{0,1},{1,2},{2,3},{3,4},{4,5},{5,6},{6,7},{7,8},{8,9},{9,10},{10,1... | collective-permute-start | bytes 196616 | tf_op jit(solution)/shard_map/ppermute | solution.py:107
  37.6 4.6 %collective-permute-start.4 = (f32[16,1,512]{2,0,1:T(8,128)S(1)}, f32[16,1,512]{2,0,1:T(8,128)S(1)}, u32[]{:S(2)}, u32[]{:S(2)}) collective-permute-start(f32[16,1,512]{2,0,1:T(8,128)S(1)} %get-tuple-element.23), channel_id=1, source_target_pairs={{16,0},{32,16},{48,32},{64,48},{80,64},{96,80},{112,96},{128,112},... | collective-permute-start | bytes 98312 | tf_op jit(solution)/shard_map/ppermute | solution.py:111
  39.5 5.2 %collective-permute-start.5 = (f32[16,1,512]{2,0,1:T(8,128)S(1)}, f32[16,1,512]{2,0,1:T(8,128)S(1)}, u32[]{:S(2)}, u32[]{:S(2)}) collective-permute-start(f32[16,1,512]{2,0,1:T(8,128)S(1)} %get-tuple-element.24), channel_id=1, source_target_pairs={{0,16},{16,32},{32,48},{48,64},{64,80},{80,96},{96,112},{112,128},... | collective-permute-start | bytes 98312 | tf_op jit(solution)/shard_map/ppermute | solution.py:107
  49.0 13.7 %collective-permute-start.10 = (f32[16,16,64]{2,0,1:T(8,128)S(1)}, f32[16,16,64]{2,0,1:T(8,128)S(1)}, u32[]{:S(2)}, u32[]{:S(2)}) collective-permute-start(f32[16,16,64]{2,0,1:T(8,128)S(1)} %get-tuple-element.19), channel_id=1, source_target_pairs={{1,0},{2,1},{3,2},{4,3},{5,4},{6,5},{7,6},{8,7},{9,8},{10,9},{11,1... | collective-permute-start | bytes 196616 | tf_op jit(solution)/shard_map/ppermute | solution.py:111
  53.5 9.1 %collective-permute-start.11 = (f32[16,16,64]{2,0,1:T(8,128)S(1)}, f32[16,16,64]{2,0,1:T(8,128)S(1)}, u32[]{:S(2)}, u32[]{:S(2)}) collective-permute-start(f32[16,16,64]{2,0,1:T(8,128)S(1)} %get-tuple-element.20), channel_id=1, source_target_pairs={{0,1},{1,2},{2,3},{3,4},{4,5},{5,6},{6,7},{7,8},{8,9},{9,10},{10,1... | collective-permute-start | bytes 196616 | tf_op jit(solution)/shard_map/ppermute | solution.py:107
  55.5 4.5 %collective-permute-start.8 = (f32[16,1,512]{2,0,1:T(8,128)S(1)}, f32[16,1,512]{2,0,1:T(8,128)S(1)}, u32[]{:S(2)}, u32[]{:S(2)}) collective-permute-start(f32[16,1,512]{2,0,1:T(8,128)S(1)} %get-tuple-element.15), channel_id=1, source_target_pairs={{16,0},{32,16},{48,32},{64,48},{80,64},{96,80},{112,96},{128,112},... | collective-permute-start | bytes 98312 | tf_op jit(solution)/shard_map/ppermute | solution.py:111
  57.4 5.2 %collective-permute-start.9 = (f32[16,1,512]{2,0,1:T(8,128)S(1)}, f32[16,1,512]{2,0,1:T(8,128)S(1)}, u32[]{:S(2)}, u32[]{:S(2)}) collective-permute-start(f32[16,1,512]{2,0,1:T(8,128)S(1)} %get-tuple-element.16), channel_id=1, source_target_pairs={{0,16},{16,32},{32,48},{48,64},{64,80},{80,96},{96,112},{112,128},... | collective-permute-start | bytes 98312 | tf_op jit(solution)/shard_map/ppermute | solution.py:107
  65.6 2.0 %collective-permute-start.12 = (f32[48,48]{0,1:T(8,128)S(1)}, f32[48,48]{0,1:T(8,128)S(1)}, u32[]{:S(2)}, u32[]{:S(2)}) collective-permute-start(f32[48,48]{0,1:T(8,128)S(1)} %fusion.6), channel_id=1, source_target_pairs={{0,16},{16,0},{32,48},{48,32},{64,80},{80,64},{96,112},{112,96},{1... | collective-permute-start | bytes 27656 | tf_op jit(solution)/shard_map/ppermute | solution.py:25
  65.7 3.9 %collective-permute-start.13 = (f32[48,48]{0,1:T(8,128)S(1)}, f32[48,48]{0,1:T(8,128)S(1)}, u32[]{:S(2)}, u32[]{:S(2)}) collective-permute-start(f32[48,48]{0,1:T(8,128)S(1)} %fusion.6), channel_id=1, source_target_pairs={{0,32},{16,48},{32,0},{48,16},{64,96},{80,112},{96,64},{112,80},{1... | collective-permute-start | bytes 27656 | tf_op jit(solution)/shard_map/ppermute | solution.py:25
  65.8 3.8 %collective-permute-start.14 = (f32[48,48]{0,1:T(8,128)S(1)}, f32[48,48]{0,1:T(8,128)S(1)}, u32[]{:S(2)}, u32[]{:S(2)}) collective-permute-start(f32[48,48]{0,1:T(8,128)S(1)} %fusion.6), channel_id=1, source_target_pairs={{0,48},{16,32},{32,16},{48,0},{64,112},{80,96},{96,80},{112,64},{1... | collective-permute-start | bytes 27656 | tf_op jit(solution)/shard_map/ppermute | solution.py:25
  69.6 11.0 %collective-permute-start.15 = (f32[48,48]{0,1:T(8,128)S(1)}, f32[48,48]{0,1:T(8,128)S(1)}, u32[]{:S(2)}, u32[]{:S(2)}) collective-permute-start(f32[48,48]{0,1:T(8,128)S(1)} %add_add_fusion.4), channel_id=1, source_target_pairs={{0,64},{16,80},{32,96},{48,112},{64,0},{80,16},{96,32},{112,48},{1... | collective-permute-start | bytes 27656 | tf_op jit(solution)/shard_map/ppermute | solution.py:25
  76.2 7.9 %collective-permute-start.16 = (f32[48,48]{0,1:T(8,128)S(1)}, f32[48,48]{0,1:T(8,128)S(1)}, u32[]{:S(2)}, u32[]{:S(2)}) collective-permute-start(f32[48,48]{0,1:T(8,128)S(1)} %add_add_fusion.4), channel_id=1, source_target_pairs={{0,128},{16,144},{32,160},{48,176},{64,192},{80,208},{96,224},{112... | collective-permute-start | bytes 27656 | tf_op jit(solution)/shard_map/ppermute | solution.py:25
  80.2 6.2 %collective-permute-start.17 = (f32[48,48]{0,1:T(8,128)S(1)}, f32[48,48]{0,1:T(8,128)S(1)}, u32[]{:S(2)}, u32[]{:S(2)}) collective-permute-start(f32[48,48]{0,1:T(8,128)S(1)} %add_add_fusion.4), channel_id=1, source_target_pairs={{0,192},{16,208},{32,224},{48,240},{64,128},{80,144},{96,160},{112... | collective-permute-start | bytes 27656 | tf_op jit(solution)/shard_map/ppermute | solution.py:25
  86.4 5.8 %collective-permute-start.18 = (f32[48,48]{0,1:T(8,128)S(1)}, f32[48,48]{0,1:T(8,128)S(1)}, u32[]{:S(2)}, u32[]{:S(2)}) collective-permute-start(f32[48,48]{0,1:T(8,128)S(1)} %add_add_fusion.3), channel_id=1, source_target_pairs={{0,1},{1,0},{2,3},{3,2},{4,5},{5,4},{6,7},{7,6},{8,9},{9,8},{10,11... | collective-permute-start | bytes 27656 | tf_op jit(solution)/shard_map/ppermute | solution.py:25
  86.5 7.7 %collective-permute-start.19 = (f32[48,48]{0,1:T(8,128)S(1)}, f32[48,48]{0,1:T(8,128)S(1)}, u32[]{:S(2)}, u32[]{:S(2)}) collective-permute-start(f32[48,48]{0,1:T(8,128)S(1)} %add_add_fusion.3), channel_id=1, source_target_pairs={{0,2},{1,3},{2,0},{3,1},{4,6},{5,7},{6,4},{7,5},{8,10},{9,11},{10,... | collective-permute-start | bytes 27656 | tf_op jit(solution)/shard_map/ppermute | solution.py:25
  92.2 5.0 %collective-permute-start.20 = (f32[48,48]{0,1:T(8,128)S(1)}, f32[48,48]{0,1:T(8,128)S(1)}, u32[]{:S(2)}, u32[]{:S(2)}) collective-permute-start(f32[48,48]{0,1:T(8,128)S(1)} %add_add_fusion.3), channel_id=1, source_target_pairs={{0,3},{1,2},{2,1},{3,0},{4,7},{5,6},{6,5},{7,4},{8,11},{9,10},{10,... | collective-permute-start | bytes 27656 | tf_op jit(solution)/shard_map/ppermute | solution.py:25
  97.2 3.9 %collective-permute-start.21 = (f32[48,48]{0,1:T(8,128)S(1)}, f32[48,48]{0,1:T(8,128)S(1)}, u32[]{:S(2)}, u32[]{:S(2)}) collective-permute-start(f32[48,48]{0,1:T(8,128)S(1)} %add_add_fusion.2), channel_id=1, source_target_pairs={{0,4},{1,5},{2,6},{3,7},{4,0},{5,1},{6,2},{7,3},{8,12},{9,13},{10,... | collective-permute-start | bytes 27656 | tf_op jit(solution)/shard_map/ppermute | solution.py:25
  97.8 5.3 %collective-permute-start.22 = (f32[48,48]{0,1:T(8,128)S(1)}, f32[48,48]{0,1:T(8,128)S(1)}, u32[]{:S(2)}, u32[]{:S(2)}) collective-permute-start(f32[48,48]{0,1:T(8,128)S(1)} %add_add_fusion.2), channel_id=1, source_target_pairs={{0,8},{1,9},{2,10},{3,11},{4,12},{5,13},{6,14},{7,15},{8,0},{9,1},... | collective-permute-start | bytes 27656 | tf_op jit(solution)/shard_map/ppermute | solution.py:25
  100.3 3.8 %collective-permute-start.23 = (f32[48,48]{0,1:T(8,128)S(1)}, f32[48,48]{0,1:T(8,128)S(1)}, u32[]{:S(2)}, u32[]{:S(2)}) collective-permute-start(f32[48,48]{0,1:T(8,128)S(1)} %add_add_fusion.2), channel_id=1, source_target_pairs={{0,12},{1,13},{2,14},{3,15},{4,8},{5,9},{6,10},{7,11},{8,4},{9,5},... | collective-permute-start | bytes 27656 | tf_op jit(solution)/shard_map/ppermute | solution.py:25
  (13 other events, 49.1 us)
